TPU v7x, 256 devices: a whole 4x4x8 slice. The times are simulated.
256 devices in a mesh: tm: 32 (over y, x, core), inner: 8 (over z).
Axes of the slice: x: 4, y: 4, z: 8, core: 2. Of those that a mesh axis runs over, the one named last changes fastest.
Arguments:
- query_input: bfloat16 [32768, 1792], P(('tm', 'inner')), may hold values from -6 to 6
- key_input: bfloat16 [32768, 1792], P(('tm', 'inner')), may hold values from -6 to 6
- value_input: bfloat16 [32768, 1792], P(('tm', 'inner')), may hold values from -6 to 6
- cotangent: bfloat16 [32768, 1792], P(('tm', 'inner')), may hold values from -6 to 6
- span_labels: int32 [32768], P(('tm', 'inner')), may hold values from 0 to 6, as said below
Outputs:
- query_gradient: bfloat16 [32768, 1792], P(('tm', 'inner'))
- key_gradient: bfloat16 [32768, 1792], P(('tm', 'inner'))
- value_gradient: bfloat16 [32768, 1792], P(('tm', 'inner'))
Inputs may be any that keep to these rules, and one draw needn't show every extreme that they name: `span_labels`: span labels never fall along the tokens; each of the 7 spans holds 1 to 8 whole frames of 1024 tokens and begins at a multiple of 1024; one span holds exactly 8192 tokens.
All inputs are finite; a program needn't handle non-finite values.
Results may differ from a plain program's by a relative error of at most 0.008.
Values may be sent and summed in bfloat16 or wider, within the bound.
No kernel may reach another device: no remote copies, remote signals or barrier semaphores. Data moves between devices by JAX's collectives and lax.ppermute only.
A program may use at most 192 MiB of HBM per device.

v0:
```python
import jax
import jax.numpy as jnp
from jax import lax
from jax.sharding import PartitionSpec as P

DH = 112
SPANS = 7
TOK_DEV = 128


loss_scale = 1024.0
exact = lax.Precision.HIGHEST


def prefix(part, axis, combine, identity, reverse):
    count = lax.axis_size(axis)
    place = lax.axis_index(axis)
    ahead = count - 1 - place if reverse else place
    gathered = jax.tree.map(lambda a: lax.all_gather(a, axis), part)
    state = jax.tree.map(lambda a, e: jnp.zeros_like(a) + jnp.asarray(e, a.dtype), part, identity)

    def one(hop, state):
        source = count - 1 - hop if reverse else hop
        return combine(
            state, jax.tree.map(lambda a: lax.dynamic_index_in_dim(a, source, 0, False), gathered)
        )

    return lax.fori_loop(0, ahead, one, state)


def prefix_2(x, axis, combine, identity):
    size, index = (lax.axis_size(axis), lax.axis_index(axis))
    everything = jax.tree.map(
        lambda part, kind: lax.all_gather(part.astype(kind), axis),
        x,
        jax.tree.map(lambda a: jnp.bfloat16 if a.dtype == jnp.float32 else a.dtype, x),
    )
    start = jax.tree.map(
        lambda part, zero: jnp.broadcast_to(jnp.asarray(zero, part.dtype), part.shape), x, identity
    )

    def hop(k, before):
        reached = k < index
        new = combine(
            before, jax.tree.map(lambda part, own: part[k].astype(own.dtype), everything, x)
        )
        return jax.tree.map(lambda a, b: jnp.where(reached, a, b), new, before)

    return lax.fori_loop(0, size, hop, start)


def reverse_cumsum(pieces):
    return jnp.flip(jnp.cumsum(jnp.flip(pieces, 0), 0), 0)


def add_pairs(earlier, later):
    return jax.tree.map(jnp.add, earlier, later)


def zero_tree(pieces):
    return jax.tree.map(jnp.zeros_like, pieces)


def empty_segment(pieces):
    return (jnp.full_like(pieces[0], -1.0), jnp.zeros_like(pieces[1]), jnp.zeros_like(pieces[2]))


def front_join(first_part, second_part):
    is_empty = first_part[0] < 0
    is_same = second_part[0] == first_part[0]
    joined_label = jnp.where(is_empty, second_part[0], first_part[0])
    joined_state = jnp.where(
        is_empty, second_part[1], first_part[1] + jnp.where(is_same, second_part[1], 0.0)
    )
    joined_mass = jnp.where(
        is_empty, second_part[2], first_part[2] + jnp.where(is_same, second_part[2], 0.0)
    )
    return (joined_label, joined_state, joined_mass)


def back_join(first_part, second_part):
    is_empty = second_part[0] < 0
    is_same = first_part[0] == second_part[0]
    joined_label = jnp.where(is_empty, first_part[0], second_part[0])
    joined_state = jnp.where(
        is_empty, first_part[1], second_part[1] + jnp.where(is_same, first_part[1], 0.0)
    )
    joined_mass = jnp.where(
        is_empty, first_part[2], second_part[2] + jnp.where(is_same, first_part[2], 0.0)
    )
    return (joined_label, joined_state, joined_mass)


def key_tail_join(earlier, later):
    return front_join(later, earlier)


def key_visible_scan(state_part, mass_part, labels, prefix_fn, tail_fn):
    levels = jnp.arange(state_part.shape[0], dtype=jnp.float32)
    first_label = jnp.min(labels)
    last_label = jnp.max(labels)
    lead_mask = (levels == first_label).astype(jnp.float32)
    lead_state = jnp.sum(lead_mask[:, None, None, None] * state_part, axis=0)
    lead_mass = jnp.sum(lead_mask[:, None, None] * mass_part, axis=0)
    before_state, before_mass = prefix_fn((jnp.sum(state_part, axis=0), jnp.sum(mass_part, axis=0)))
    tail_label, tail_state, tail_mass = tail_fn((first_label.reshape(1), lead_state, lead_mass))
    trail_mask = ((levels == last_label) & (tail_label[0] == last_label)).astype(jnp.float32)
    state_vis = (
        before_state[None]
        + jnp.cumsum(state_part, axis=0)
        + trail_mask[:, None, None, None] * tail_state[None]
    )
    mass_vis = (
        before_mass[None]
        + jnp.cumsum(mass_part, axis=0)
        + trail_mask[:, None, None] * tail_mass[None]
    )
    return (state_vis, mass_vis)


def query_visible_scan(state_part, mass_part, labels, suffix_fn, head_fn):
    levels = jnp.arange(state_part.shape[0], dtype=jnp.float32)
    first_label = jnp.min(labels)
    last_label = jnp.max(labels)
    trail_mask = (levels == last_label).astype(jnp.float32)
    trail_state = jnp.sum(trail_mask[:, None, None, None] * state_part, axis=0)
    trail_mass = jnp.sum(trail_mask[:, None, None] * mass_part, axis=0)
    after_state, after_mass = suffix_fn((jnp.sum(state_part, axis=0), jnp.sum(mass_part, axis=0)))
    head_label, head_state, head_mass = head_fn((last_label.reshape(1), trail_state, trail_mass))
    lead_mask = ((levels == first_label) & (head_label[0] == first_label)).astype(jnp.float32)
    state_vis = (
        after_state[None]
        + reverse_cumsum(state_part)
        + lead_mask[:, None, None, None] * head_state[None]
    )
    mass_vis = (
        after_mass[None] + reverse_cumsum(mass_part) + lead_mask[:, None, None] * head_mass[None]
    )
    return (state_vis, mass_vis)


def local_backward(
    query_flat, key_flat, value_flat, cotangent_flat, labels, key_chain, query_chain
):
    token_count = query_flat.shape[0]
    head_count = query_flat.shape[1] // DH
    block_count = token_count // TOK_DEV

    def to_heads(flat):
        return jnp.transpose(flat.reshape(block_count, TOK_DEV, head_count, DH), (0, 2, 1, 3))

    def to_rows(heads):
        return jnp.transpose(heads, (0, 2, 1, 3)).reshape(token_count, head_count * DH)

    query_heads = to_heads(query_flat)
    key_heads = to_heads(key_flat)
    value_heads = to_heads(value_flat)
    cotangent_heads = to_heads(cotangent_flat)
    feat_query = jnp.maximum(query_heads, 0)
    feat_key = jnp.maximum(key_heads, 0)
    block_labels = labels.reshape(block_count, TOK_DEV)[:, 0]
    levels = jnp.arange(SPANS, dtype=jnp.float32)
    block_onehot = (block_labels[:, None] == levels[None, :]).astype(jnp.float32)
    block_state = jnp.einsum(
        "bhtk,bhtv->bhkv", feat_key, value_heads, preferred_element_type=jnp.float32
    )
    block_mass = jnp.sum(feat_key, axis=2, dtype=jnp.float32)
    state_part = jnp.einsum("bc,bhkv->chkv", block_onehot, block_state, precision=exact)
    mass_part = jnp.einsum("bc,bhk->chk", block_onehot, block_mass, precision=exact)
    state_vis, mass_vis = key_chain(state_part, mass_part, labels)
    state_low = jnp.einsum("bc,chkv->bhkv", block_onehot, state_vis, precision=exact).astype(
        jnp.bfloat16
    )
    mass_low = jnp.einsum("bc,chk->bhk", block_onehot, mass_vis, precision=exact).astype(
        jnp.bfloat16
    )
    numerator = jnp.einsum(
        "bhtk,bhkv->bhtv", feat_query, state_low, preferred_element_type=jnp.float32
    )
    weight = jnp.einsum("bhtk,bhk->bht", feat_query, mass_low, preferred_element_type=jnp.float32)
    denominator = weight / DH + 1.0
    output = numerator / (DH * denominator[..., None])
    scaled = cotangent_heads.astype(jnp.float32) * loss_scale
    numer_back = (scaled / (DH * denominator[..., None])).astype(jnp.bfloat16)
    weight_back = (-jnp.sum(scaled * output, axis=-1) / (DH * denominator)).astype(jnp.bfloat16)
    block_adjoint = jnp.einsum(
        "bhtk,bhtv->bhkv", feat_query, numer_back, preferred_element_type=jnp.float32
    )
    block_adjoint_mass = jnp.einsum(
        "bhtk,bht->bhk", feat_query, weight_back, preferred_element_type=jnp.float32
    )
    adjoint_part = jnp.einsum("bc,bhkv->chkv", block_onehot, block_adjoint, precision=exact)
    adjoint_mass = jnp.einsum("bc,bhk->chk", block_onehot, block_adjoint_mass, precision=exact)
    adjoint_vis, adjoint_mass_vis = query_chain(adjoint_part, adjoint_mass, labels)
    adjoint_low = jnp.einsum("bc,chkv->bhkv", block_onehot, adjoint_vis, precision=exact).astype(
        jnp.bfloat16
    )
    adjoint_mass_low = jnp.einsum(
        "bc,chk->bhk", block_onehot, adjoint_mass_vis, precision=exact
    ).astype(jnp.bfloat16)
    query_feat = jnp.einsum(
        "bhtv,bhkv->bhtk", numer_back, state_low, preferred_element_type=jnp.float32
    )
    query_feat = (
        query_feat
        + mass_low.astype(jnp.float32)[:, :, None, :] * weight_back.astype(jnp.float32)[..., None]
    )
    key_feat = jnp.einsum(
        "bhtv,bhkv->bhtk", value_heads, adjoint_low, preferred_element_type=jnp.float32
    )
    key_feat = key_feat + adjoint_mass_low.astype(jnp.float32)[:, :, None, :]
    value_back = jnp.einsum(
        "bhtk,bhkv->bhtv", feat_key, adjoint_low, preferred_element_type=jnp.float32
    )
    query_back = to_rows(jnp.where(query_heads > 0, query_feat, 0.0).astype(jnp.bfloat16))
    key_back = to_rows(jnp.where(key_heads > 0, key_feat, 0.0).astype(jnp.bfloat16))
    return (query_back, key_back, to_rows(value_back.astype(jnp.bfloat16)))


def local(query_input, key_input, value_input, cotangent, span_labels):
    groups = lax.axis_size("inner")
    label_cols = jnp.broadcast_to(
        span_labels.astype(jnp.bfloat16)[:, None], (span_labels.shape[0], groups)
    )
    query_rows, key_rows, value_rows, cotangent_rows, label_rows = (
        lax.all_to_all(query_input, "inner", split_axis=1, concat_axis=0, tiled=True),
        lax.all_to_all(key_input, "inner", split_axis=1, concat_axis=0, tiled=True),
        lax.all_to_all(value_input, "inner", split_axis=1, concat_axis=0, tiled=True),
        lax.all_to_all(cotangent, "inner", split_axis=1, concat_axis=0, tiled=True),
        lax.all_to_all(label_cols, "inner", split_axis=1, concat_axis=0, tiled=True),
    )
    labels = label_rows[:, 0].astype(jnp.float32)
    key_chain = lambda state_in, mass_in, labels_in: key_visible_scan(
        state_in,
        mass_in,
        labels_in,
        lambda pieces: prefix(pieces, "tm", add_pairs, zero_tree(pieces), False),
        lambda pieces: prefix(pieces, "tm", key_tail_join, empty_segment(pieces), True),
    )
    query_chain = lambda state_in, mass_in, labels_in: query_visible_scan(
        state_in,
        mass_in,
        labels_in,
        lambda pieces: prefix(pieces, "tm", add_pairs, zero_tree(pieces), True),
        lambda pieces: prefix_2(pieces, "tm", back_join, empty_segment(pieces)),
    )
    query_back, key_back, value_back = local_backward(
        query_rows, key_rows, value_rows, cotangent_rows, labels, key_chain, query_chain
    )
    return (
        lax.all_to_all(query_back, "inner", split_axis=0, concat_axis=1, tiled=True),
        lax.all_to_all(key_back, "inner", split_axis=0, concat_axis=1, tiled=True),
        lax.all_to_all(value_back, "inner", split_axis=0, concat_axis=1, tiled=True),
    )


def solution(mesh):
    return jax.shard_map(
        local,
        mesh=mesh,
        in_specs=(
            P(("tm", "inner"), None),
            P(("tm", "inner"), None),
            P(("tm", "inner"), None),
            P(("tm", "inner"), None),
            P(("tm", "inner")),
        ),
        out_specs=(P(("tm", "inner"), None), P(("tm", "inner"), None), P(("tm", "inner"), None)),
        check_vma=False,
    )
```

profile of v0, /device:TPU:2, one launch (start us, length us, event | category | flops | bytes accessed | tf_op | source)
XLA Modules:
  0.0 638.7 jit_solution(8772264290364809481)
XLA Ops:
  8.4 8.5 %all-to-all-start.2 = ((bf16[128,8,1]{0,2,1:T(2,128)(2,1)}), bf16[128,8,1]{0,2,1:T(2,128)(2,1)S(1)}, u32[]{:S(2)}, u32[]{:S(2)}) async-start(bf16[128,8,1]{0,2,1:T(2,128)(2,1)} %broadcast_in_dim.171), calls=%async_computation.2 | async-start | bytes 8192 | tf_op jit(solution)/shard_map/all_to_all | solution.py:230
  16.9 2.0 copy.65
  18.9 5.6 all-to-all-done.2
  24.5 3.5 all-to-all-start.3
  28.0 2.0 copy.66
  30.0 12.8 %all-to-all-done.3 = bf16[128,8,224]{0,2,1:T(8,128)(2,1)S(1)} async-done(((bf16[128,8,224]{0,2,1:T(8,128)(2,1)}), bf16[128,8,224]{0,2,1:T(8,128)(2,1)S(1)}, u32[]{:S(2)}, u32[]{:S(2)}) %all-to-all-start.3) | async-done | bytes 458784 | tf_op jit(solution)/shard_map/all_to_all | solution.py:227
  42.8 3.5 all-to-all-start.4
  47.7 12.2 %all-to-all-done.4 = bf16[128,8,224]{0,2,1:T(8,128)(2,1)S(1)} async-done(((bf16[128,8,224]{0,2,1:T(8,128)(2,1)}), bf16[128,8,224]{0,2,1:T(8,128)(2,1)S(1)}, u32[]{:S(2)}, u32[]{:S(2)}) %all-to-all-start.4) | async-done | bytes 458784 | tf_op jit(solution)/shard_map/all_to_all | solution.py:228
  60.3 2.3 fusion.70
  64.4 3.5 all-to-all-start
  68.8 11.5 %all-to-all-done = bf16[128,8,224]{0,2,1:T(8,128)(2,1)S(1)} async-done(((bf16[128,8,224]{0,2,1:T(8,128)(2,1)}), bf16[128,8,224]{0,2,1:T(8,128)(2,1)S(1)}, u32[]{:S(2)}, u32[]{:S(2)}) %all-to-all-start) | async-done | bytes 458784 | tf_op jit(solution)/shard_map/all_to_all | solution.py:226
  80.4 4.1 all-to-all-start.1
  87.6 57.8 %all-reduce = f32[32]{0:T(128)S(1)} all-reduce(f32[32]{0:T(128)S(1)} %dynamic-update-slice), channel_id=1, replica_groups=mesh['tm'=32,'inner'=8] {'tm'}, use_global_device_ids=true, to_apply=%add | all-reduce | flops 32 | bytes 256
  145.9 26.7 %all-gather.9 = f32[32,2,112]{2,1,0:T(2,128)S(1)} all-gather(f32[1,2,112]{2,1,0:T(2,128)S(1)} %bitcast.218), channel_id=5, replica_groups=mesh['tm'=32,'inner'=8] {'tm'}, dimensions={0}, use_global_device_ids=true | all-gather | bytes 29568 | tf_op jit(solution)/shard_map/all_gather | solution.py:19
  172.6 21.4 %all-gather.8 = f32[32,2,112]{2,1,0:T(2,128)S(1)} all-gather(f32[1,2,112]{2,1,0:T(2,128)S(1)} %bitcast.217), channel_id=3, replica_groups=mesh['tm'=32,'inner'=8] {'tm'}, dimensions={0}, use_global_device_ids=true | all-gather | bytes 29568 | tf_op jit(solution)/shard_map/all_gather | solution.py:19
  194.1 2.0 convert_multiply_fusion
  196.1 102.0 %while.61 = (s32[]{:T(128)}, f32[1]{0:T(128)}, f32[2,112,112]{2,1,0:T(8,128)S(1)}, f32[2,112]{1,0:T(2,128)S(1)}, s32[]{:T(128)}, /*index=5*/f32[32,1]{0,1:T(1,12...) while((s32[]{:T(128)}, f32[1]{0:T(128)}, ...), condition=%wide.region_11.12_spmd, body=%wide.region_10.11_spmd.sunk | while | flops 75945 | bytes 303986 | solution.py:28
  298.7 1.9 while.60
  303.1 3.2 fusion.69
  306.9 2.4 dynamic-update-slice.1
  309.4 66.0 %all-reduce.1 = bf16[32]{0:T(256)(128)(2,1)} all-reduce(bf16[32]{0:T(256)(128)(2,1)} %dynamic-update-slice.1), channel_id=1, replica_groups=mesh['tm'=32,'inner'=8] {'tm'}, use_global_device_ids=true, to_apply=%add.1 | all-reduce | flops 32 | bytes 128
  379.9 1.9 convolution_convert_fusion.2
  385.3 7.0 %all-to-all-start.5 = ((bf16[8,128,224]{1,2,0:T(8,128)(2,1)}), bf16[8,128,224]{1,2,0:T(8,128)(2,1)}, u32[]{:S(2)}, u32[]{:S(2)}) async-start(bf16[8,128,224]{1,2,0:T(8,128)(2,1)} %bitcast.53), calls=%async_computation.5 | async-start | bytes 917504 | tf_op jit(solution)/shard_map/all_to_all | solution.py:251
  396.9 23.7 %all-gather.11 = bf16[32,2,112]{2,1,0:T(2,128)(2,1)S(1)} all-gather(bf16[1,2,112]{2,1,0:T(2,128)(2,1)S(1)} %bitcast.219), channel_id=9, replica_groups=mesh['tm'=32,'inner'=8] {'tm'}, dimensions={0}, use_global_device_ids=true | all-gather | bytes 14784 | tf_op jit(solution)/shard_map/all_gather | solution.py:34
  420.6 21.1 %all-gather.10 = f32[32,2,112]{2,1,0:T(2,128)S(1)} all-gather(f32[1,2,112]{2,1,0:T(2,128)S(1)} %bitcast.216), channel_id=7, replica_groups=mesh['tm'=32,'inner'=8] {'tm'}, dimensions={0}, use_global_device_ids=true | all-gather | bytes 29568 | tf_op jit(solution)/shard_map/all_gather | solution.py:19
  441.7 116.9 %while.63 = (s32[]{:T(128)}, f32[1]{0:T(128)}, f32[2,112,112]{2,1,0:T(8,128)S(1)}, f32[2,112]{1,0:T(2,128)S(1)}, s32[]{:T(128)}, /*index=5*/bf16[32,1]{0,1:T(2,1...) while((s32[]{:T(128)}, f32[1]{0:T(128)}, ...), condition=%wide.region_22.23_spmd.clone, body=%wide.region_21.22_spmd.clone.sunk | while | flops 151880 | bytes 253325 | solution.py:49
  559.8 28.1 %while.62 = (s32[]{:T(128)}, f32[2,112,112]{2,1,0:T(8,128)S(1)}, f32[2,112]{1,0:T(2,128)S(1)}, s32[]{:T(128)}, f32[32,2,112,112]{3,2,1,0:T(8,128)}, /*index=5*/f...) while((s32[]{:T(128)}, f32[2,112,112]{2,1,0:T(8,128)S(1)}, ...), condition=%wide.region_17.18_spmd, body=%wide.region_16.17_spmd.sunk | while | flops 25318 | bytes 303907 | solution.py:28
  590.5 7.0 %all-to-all-start.6 = ((bf16[8,128,224]{1,2,0:T(8,128)(2,1)}), bf16[8,128,224]{1,2,0:T(8,128)(2,1)S(1)}, u32[]{:S(2)}, u32[]{:S(2)}) async-start(bf16[8,128,224]{1,2,0:T(8,128)(2,1)} %bitcast.73), calls=%async_computation.6 | async-start | bytes 917504 | tf_op jit(solution)/shard_map/all_to_all | solution.py:252
  598.6 14.5 %all-to-all-done.6 = bf16[8,128,224]{1,2,0:T(8,128)(2,1)S(1)} async-done(((bf16[8,128,224]{1,2,0:T(8,128)(2,1)}), bf16[8,128,224]{1,2,0:T(8,128)(2,1)S(1)}, u32[]{:S(2)}, u32[]{:S(2)}) %all-to-all-start.6) | async-done | bytes 458784 | tf_op jit(solution)/shard_map/all_to_all | solution.py:252
  613.1 3.5 all-to-all-start.7
  616.6 2.0 copy.80
  619.5 11.7 %all-to-all-done.7 = bf16[8,128,224]{1,2,0:T(8,128)(2,1)S(1)} async-done(((bf16[8,128,224]{1,2,0:T(8,128)(2,1)}), bf16[8,128,224]{1,2,0:T(8,128)(2,1)S(1)}, u32[]{:S(2)}, u32[]{:S(2)}) %all-to-all-start.7) | async-done | bytes 458784 | tf_op jit(solution)/shard_map/all_to_all | solution.py:253
  (360 shorter events, 154.8 us)
Async XLA Ops:
  8.4 16.1 %all-to-all-start.2 = ((bf16[128,8,1]{0,2,1:T(2,128)(2,1)}), bf16[128,8,1]{0,2,1:T(2,128)(2,1)S(1)}, u32[]{:S(2)}, u32[]{:S(2)}) async-start(bf16[128,8,1]{0,2,1:T(2,128)(2,1)} %broadcast_in_dim.171), calls=%async_computation.2 | async-start | bytes 8192 | tf_op jit(solution)/shard_map/all_to_all | solution.py:230
  24.5 18.3 %all-to-all-start.3 = ((bf16[128,8,224]{0,2,1:T(8,128)(2,1)}), bf16[128,8,224]{0,2,1:T(8,128)(2,1)S(1)}, u32[]{:S(2)}, u32[]{:S(2)}) async-start(bf16[128,8,224]{0,2,1:T(8,128)(2,1)} %bitcast.23), calls=%async_computation.3 | async-start | bytes 917504 | tf_op jit(solution)/shard_map/all_to_all | solution.py:227
  28.0 35.4 %copy-start.3 = (bf16[128,1792]{1,0:T(8,128)(2,1)S(1)}, bf16[128,1792]{1,0:T(8,128)(2,1)}, u32[]{:S(2)}) copy-start(bf16[128,1792]{1,0:T(8,128)(2,1)} %param.13) | copy-start | bytes 1376260
  42.8 17.1 %all-to-all-start.4 = ((bf16[128,8,224]{0,2,1:T(8,128)(2,1)}), bf16[128,8,224]{0,2,1:T(8,128)(2,1)S(1)}, u32[]{:S(2)}, u32[]{:S(2)}) async-start(bf16[128,8,224]{0,2,1:T(8,128)(2,1)} %bitcast.27), calls=%async_computation.4 | async-start | bytes 917504 | tf_op jit(solution)/shard_map/all_to_all | solution.py:228
  46.3 21.5 %copy-start.4 = (bf16[128,1792]{1,0:T(8,128)(2,1)S(1)}, bf16[128,1792]{1,0:T(8,128)(2,1)}, u32[]{:S(2)}) copy-start(bf16[128,1792]{1,0:T(8,128)(2,1)} %param.16) | copy-start | bytes 1376260
  46.3 149.7 %all-gather.19.cloned.1.call-start = ((), (), s32[]{:S(2)}) async-start(), calls=%async_computation.9 | async-start | bytes 3784704 | tf_op jit(solution)/shard_map/all_gather | solution.py:19
  47.6 255.4 %copy-start.12 = (f32[8]{0:T(128)}, f32[8]{0:T(128)S(1)}, u32[]{:S(2)}) copy-start(f32[8]{0:T(128)S(1)} %convert_reduce_fusion.1) | copy-start | bytes 100
  59.9 24.6 %copy-start.20 = (u32[256]{0:T(256)S(1)}, u32[256]{0:T(256)}, u32[]{:S(2)}) copy-start(u32[256]{0:T(256)} %constant.161) | copy-start | bytes 3076
  62.6 236.0 %all-gather.17.cloned.1.call-start = ((), (), s32[]{:S(2)}) async-start(), calls=%async_computation.8 | async-start | bytes 3784704 | tf_op jit(solution)/shard_map/all_gather | solution.py:19
  64.4 16.0 %all-to-all-start = ((bf16[128,8,224]{0,2,1:T(8,128)(2,1)}), bf16[128,8,224]{0,2,1:T(8,128)(2,1)S(1)}, u32[]{:S(2)}, u32[]{:S(2)}) async-start(bf16[128,8,224]{0,2,1:T(8,128)(2,1)} %bitcast.9), calls=%async_computation | async-start | bytes 917504 | tf_op jit(solution)/shard_map/all_to_all | solution.py:226
  80.4 113.7 %all-to-all-start.1 = ((bf16[128,8,224]{0,2,1:T(8,128)(2,1)}), bf16[128,8,224]{0,2,1:T(8,128)(2,1)}, u32[]{:S(2)}, u32[]{:S(2)}) async-start(bf16[128,8,224]{0,2,1:T(8,128)(2,1)} %bitcast.12), calls=%async_computation.1 | async-start | bytes 917504 | tf_op jit(solution)/shard_map/all_to_all | solution.py:229
  84.5 357.2 %all-gather.23.cloned.1.call-start = ((), (), s32[]{:S(2)}) async-start(), calls=%async_computation.11 | async-start | bytes 1892352 | tf_op jit(solution)/shard_map/all_gather | solution.py:34
  300.7 5.7 copy-start.17
  300.9 5.5 copy-start.9
  301.4 4.9 copy-start.7
  301.5 4.9 copy-start.15
  377.0 5.2 copy-start.1
  381.8 2.2 copy-start.6
  382.2 1.8 copy-start.2
  382.2 1.8 copy-start.14
  382.2 1.8 copy-start.16
  383.4 9.2 %copy-start = (f32[7,2,112,112]{3,0,2,1:T(8,128)S(1)}, f32[7,2,112,112]{3,0,2,1:T(8,128)}, u32[]{:S(2)}) copy-start(f32[7,2,112,112]{3,0,2,1:T(8,128)} %get-tuple-element.479) | copy-start | bytes 2107396
  385.3 10.9 %copy-start.10 = (bf16[8,2,128]{2,1,0:T(2,128)(2,1)S(1)}, bf16[8,2,128]{2,1,0:T(2,128)(2,1)}, u32[]{:S(2)}) copy-start(bf16[8,2,128]{2,1,0:T(2,128)(2,1)} %get-tuple-element.476) | copy-start | bytes 12292
  385.3 11.2 %copy-start.13 = (f32[8]{0:T(128)S(1)}, f32[8]{0:T(128)}, u32[]{:S(2)}) copy-start(f32[8]{0:T(128)} %copy-done.12) | copy-start | bytes 100
  385.3 11.2 %copy-start.18 = (f32[7]{0:T(128)S(1)}, f32[7]{0:T(128)}, u32[]{:S(2)}) copy-start(f32[7]{0:T(128)} %copy-done.17) | copy-start | bytes 88
  385.3 56.4 %copy-start.11 = (f32[2,112]{1,0:T(2,128)S(1)}, f32[2,112]{1,0:T(2,128)}, u32[]{:S(2)}) copy-start(f32[2,112]{1,0:T(2,128)} %custom-call.1) | copy-start | bytes 2692
  385.3 56.4 %copy-start.21 = (bf16[32]{0:T(256)(128)(2,1)S(1)}, bf16[32]{0:T(256)(128)(2,1)}, u32[]{:S(2)}) copy-start(bf16[32]{0:T(256)(128)(2,1)} %all-reduce.1) | copy-start | bytes 196
  385.3 205.1 %all-to-all-start.5 = ((bf16[8,128,224]{1,2,0:T(8,128)(2,1)}), bf16[8,128,224]{1,2,0:T(8,128)(2,1)}, u32[]{:S(2)}, u32[]{:S(2)}) async-start(bf16[8,128,224]{1,2,0:T(8,128)(2,1)} %bitcast.53), calls=%async_computation.5 | async-start | bytes 917504 | tf_op jit(solution)/shard_map/all_to_all | solution.py:251
  392.3 167.4 %all-gather.21.cloned.1.call-start = ((), (), s32[]{:S(2)}) async-start(), calls=%async_computation.10 | async-start | bytes 3784704 | tf_op jit(solution)/shard_map/all_gather | solution.py:19
  396.2 193.0 %copy-start.5 = (pred[128,8,224]{0,2,1:T(8,128)(4,1)S(1)}, pred[128,8,224]{0,2,1:T(8,128)(4,1)}, u32[]{:S(2)}) copy-start(pred[128,8,224]{0,2,1:T(8,128)(4,1)} %broadcast_compare_fusion) | copy-start | bytes 688132
  590.5 22.6 %all-to-all-start.6 = ((bf16[8,128,224]{1,2,0:T(8,128)(2,1)}), bf16[8,128,224]{1,2,0:T(8,128)(2,1)S(1)}, u32[]{:S(2)}, u32[]{:S(2)}) async-start(bf16[8,128,224]{1,2,0:T(8,128)(2,1)} %bitcast.73), calls=%async_computation.6 | async-start | bytes 917504 | tf_op jit(solution)/shard_map/all_to_all | solution.py:252
  613.1 18.1 %all-to-all-start.7 = ((bf16[8,128,224]{1,2,0:T(8,128)(2,1)}), bf16[8,128,224]{1,2,0:T(8,128)(2,1)S(1)}, u32[]{:S(2)}, u32[]{:S(2)}) async-start(bf16[8,128,224]{1,2,0:T(8,128)(2,1)} %bitcast.77), calls=%async_computation.7 | async-start | bytes 917504 | tf_op jit(solution)/shard_map/all_to_all | solution.py:253
  (2 other events, 1.8 us)
Sparse Core Ops, SparseCore 0:
  62.8 46.5 all-gather.18
  112.5 50.0 all-gather.16
  306.5 52.0 all-gather.22
  441.8 51.0 all-gather.20
where the time goes:
time: 648 us; the launch traced here: 639 us
  blocking collectives  217 us (33%)
  loops' own time  125 us (19%)
  other arithmetic  97.3 us (15%)
  waiting for transfers between devices  69.1 us (11%)
  local copies, waits for them, and re-layouts  57.7 us (9%)
  starting transfers between devices  40.8 us (6%)
  matrix products  16.4 us (3%)
  between operations  16 us (2%)
    unnamed x2, blocking collectives  124 us
    all_gather x3, blocking collectives, prefix(): gathered = jax.tree.map(lambda a: lax.all_gather(a, axis), part)  69.2 us
    another operation x1, loops' own time, prefix_2(): return lax.fori_loop(0, size, hop, start)  66.6 us
    another operation x3, loops' own time, prefix(): return lax.fori_loop(0, ahead, one, state)  58 us
    select_n x64, other arithmetic, hop(): return jax.tree.map(lambda a, b: jnp.where(reached, a, b), new, before)  29.5 us
    add x62, other arithmetic, add_pairs(): return jax.tree.map(jnp.add, earlier, later)  29.2 us
    select_n x29, other arithmetic, front_join(): jnp.where(is_empty, second_part[1], first_part[1] + jnp.where(is_same, se...  27.3 us
    all_gather x1, blocking collectives, prefix_2(): lax.all_gather(part.astype(kind), axis)  23.7 us
  transfers between devices with their start and end apart: 12, of which 6 were waited for; matrix products, arithmetic and copies ran while one was open for 25% of the time, Pallas kernels for 0%

commit v1 on v0

v1 whole, which is shorter than its diff:
```python
import jax
import jax.numpy as jnp
from jax import lax
from jax.sharding import PartitionSpec as P

DH = 112
SPANS = 7

loss_scale = 1024.0


def visible(part, label, later):
    own = lax.psum_scatter(part, "inner", scatter_dimension=0, tiled=True)
    levels = jnp.arange(SPANS, dtype=jnp.int32)
    onehot = (levels == label).astype(jnp.float32)
    spread = onehot[:, None, None, None] * own[None]
    totals = lax.psum(spread, "tm")
    keep = (levels >= label) if later else (levels <= label)
    seen = jnp.sum(jnp.where(keep[:, None, None, None], totals, 0.0), axis=0)
    return lax.all_gather(seen.astype(jnp.bfloat16), "inner", axis=0, tiled=True)


def local(query_input, key_input, value_input, cotangent, span_labels):
    tokens = query_input.shape[0]
    heads = query_input.shape[1] // DH

    def split(flat):
        return flat.reshape(tokens, heads, DH)

    query_heads = split(query_input)
    key_heads = split(key_input)
    value_heads = split(value_input)
    feat_query = jnp.maximum(query_heads, 0)
    feat_key = jnp.maximum(key_heads, 0)
    label = span_labels[0]
    ones = jnp.ones((tokens, heads, 1), jnp.bfloat16)
    value_aug = jnp.concatenate([value_heads, ones], axis=-1)
    state_part = jnp.einsum(
        "thk,thv->hkv", feat_key, value_aug, preferred_element_type=jnp.float32
    )
    state_vis = visible(state_part, label, False)
    both = jnp.einsum("thk,hkv->thv", feat_query, state_vis, preferred_element_type=jnp.float32)
    numerator = both[..., :DH]
    weight = both[..., DH]
    denominator = weight / DH + 1.0
    output = numerator / (DH * denominator[..., None])
    scaled = split(cotangent).astype(jnp.float32) * loss_scale
    numer_back = (scaled / (DH * denominator[..., None])).astype(jnp.bfloat16)
    weight_back = (-jnp.sum(scaled * output, axis=-1) / (DH * denominator)).astype(jnp.bfloat16)
    back_aug = jnp.concatenate([numer_back, weight_back[..., None]], axis=-1)
    adjoint_part = jnp.einsum(
        "thk,thv->hkv", feat_query, back_aug, preferred_element_type=jnp.float32
    )
    adjoint_vis = visible(adjoint_part, label, True)
    query_feat = jnp.einsum("thv,hkv->thk", back_aug, state_vis, preferred_element_type=jnp.float32)
    key_feat = jnp.einsum("thv,hkv->thk", value_aug, adjoint_vis, preferred_element_type=jnp.float32)
    value_back = jnp.einsum(
        "thk,hkv->thv", feat_key, adjoint_vis[..., :DH], preferred_element_type=jnp.float32
    )
    query_back = jnp.where(query_heads > 0, query_feat, 0.0).astype(jnp.bfloat16)
    key_back = jnp.where(key_heads > 0, key_feat, 0.0).astype(jnp.bfloat16)

    def merge(heads_arr):
        return heads_arr.reshape(tokens, heads * DH)

    return merge(query_back), merge(key_back), merge(value_back.astype(jnp.bfloat16))


def solution(mesh):
    row = P(("tm", "inner"), None)
    return jax.shard_map(
        local,
        mesh=mesh,
        in_specs=(row, row, row, row, P(("tm", "inner"))),
        out_specs=(row, row, row),
        check_vma=False,
    )
```

time: 648 us -> 387 us (0.60); the launches traced: 639 us -> 386 us
  waiting for transfers between devices: 69.1 us -> 298 us
  blocking collectives: 217 us -> 53.5 us
  loops' own time: 125 us -> 0 us
  other arithmetic: 97.3 us -> 7.08 us
  local copies, waits for them, and re-layouts: 57.7 us -> 9.54 us
  starting transfers between devices: 40.8 us -> 0.16 us
  matrix products: 16.4 us -> 4.24 us
    psum x0 -> x2, waiting for transfers between devices: none -> 223 us  [visible(): totals = lax.psum(spread, 'tm')]
    another operation x4 -> x0, loops' own time: 125 us -> none  [the longest x1 66.6 us: prefix_2(): return lax.fori_loop(0, size, hop, start)]
    unnamed x2 -> x0, blocking collectives: 124 us -> none
    reduce_scatter x0 -> x2, waiting for transfers between devices: none -> 74.3 us  [visible(): own = lax.psum_scatter(part, 'inner', scatter_dimension=0, tiled=True)]
    all_to_all x8 -> x0, waiting for transfers between devices: 68.3 us -> none  [the longest x1 14.5 us: local(): lax.all_to_all(key_back, 'inner', split_axis=0, concat_axis=1, tiled=True)]
    select_n x122 -> x0, other arithmetic: 57.3 us -> none  [the longest x64 29.5 us: hop(): return jax.tree.map(lambda a, b: jnp.where(reached, a, b), new, before)]
    all_to_all x8 -> x0, starting transfers between devices: 40.5 us -> none  [the longest x1 8.47 us: local(): lax.all_to_all(label_cols, 'inner', split_axis=1, concat_axis=0, tiled=True)]
    all_gather x4 -> x2, blocking collectives: 92.8 us -> 53.5 us  [visible(): lax.all_gather(seen.astype(jnp.bfloat16), 'inner', axis=0, tiled=True)]
  transfers between devices with their start and end apart: 12 -> 4, of which waited for: 6 -> 4; matrix products, arithmetic and copies ran while one was open for 25% -> 1% of each run, Pallas kernels for 0% -> 0%
where the time goes in v1:
time: 387 us; the launch traced here: 386 us
  waiting for transfers between devices  298 us (77%)
  blocking collectives  53.5 us (14%)
  between operations  14 us (4%)
  local copies, waits for them, and re-layouts  9.54 us (2%)
  other arithmetic  7.08 us (2%)
  matrix products  4.24 us (1%)
    psum x2, waiting for transfers between devices, visible(): totals = lax.psum(spread, 'tm')  223 us
    reduce_scatter x2, waiting for transfers between devices, visible(): own = lax.psum_scatter(part, 'inner', scatter_dimension=0, tiled=True)  74.3 us
    all_gather x2, blocking collectives, visible(): lax.all_gather(seen.astype(jnp.bfloat16), 'inner', axis=0, tiled=True)  53.5 us
    unnamed x22, local copies, waits for them, and re-layouts  9.25 us
  transfers between devices with their start and end apart: 4, of which 4 were waited for; matrix products, arithmetic and copies ran while one was open for 1% of the time, Pallas kernels for 0%

profile of v1, /device:TPU:2, one launch (start us, length us, event | category | flops | bytes accessed | tf_op | source)
XLA Modules:
  0.0 386.1 jit_solution(13692422102469256657)
XLA Ops:
  7.2 1.3 copy.41
  8.5 1.0 copy-done.4
  9.5 0.3 copy.42
  9.8 1.3 fusion.8
  11.2 0.9 copy-done.5
  12.1 0.3 copy.40
  12.5 0.3 copy.43
  12.8 0.7 copy-done.7
  13.5 38.9 %reduce-scatter.3.cloned.1.call-done = f32[2,112,113]{2,1,0:T(8,128)} async-done(((f32[16,112,113]{2,1,0:T(8,128)}), f32[2,112,113]{2,1,0:T(8,128)}) %reduce-scatter.3.cloned.1.call-update) | async-done | bytes 101264 | tf_op jit(solution)/shard_map/reduce_scatter | solution.py:13
  52.4 1.9 broadcast_multiply_fusion.1
  54.5 113.0 %all-reduce.4.cloned.1.call-done = f32[7,2,112,113]{3,2,1,0:T(8,128)} async-done(((f32[7,2,112,113]{3,2,1,0:T(8,128)}), f32[7,2,112,113]{3,2,1,0:T(8,128)}) %all-reduce.4.cloned.1.call-update) | async-done | bytes 708752 | tf_op jit(solution)/shard_map/psum | solution.py:17
  167.5 1.3 select_reduce_fusion.1
  168.8 26.8 %all_gather.6 = bf16[16,112,113]{2,1,0:T(8,128)(2,1)S(1)} all-gather(bf16[2,112,113]{2,1,0:T(8,128)(2,1)S(1)} %select_reduce_fusion.1), channel_id=1, replica_groups=mesh['tm'=32,'inner'=8] {'inner'}, dimensions={0}, use_global_device_ids=true | all-gather | bytes 455616 | tf_op jit(solution)/shard_map/all_gather | solution.py:20
  195.5 0.5 convolution_bitcast_fusion
  196.0 0.3 copy-done.2
  196.3 0.2 divide_convert_fusion
  196.5 1.3 fusion.10
  197.9 0.1 broadcast_compare_fusion.1
  198.1 0.1 broadcast_compare_fusion
  198.2 35.4 %reduce-scatter.5.cloned.1.call-done = f32[2,112,113]{2,1,0:T(8,128)} async-done(((f32[16,112,113]{2,1,0:T(8,128)}), f32[2,112,113]{2,1,0:T(8,128)}) %reduce-scatter.5.cloned.1.call-update) | async-done | bytes 101264 | tf_op jit(solution)/shard_map/reduce_scatter | solution.py:13
  233.6 1.9 broadcast_multiply_fusion
  235.6 0.9 copy-done.3
  236.5 0.4 fusion.2
  236.9 1.0 copy.47
  237.9 110.3 %all-reduce.6.cloned.1.call-done = f32[7,2,112,113]{3,2,1,0:T(8,128)} async-done(((f32[7,2,112,113]{3,2,1,0:T(8,128)}), f32[7,2,112,113]{3,2,1,0:T(8,128)}) %all-reduce.6.cloned.1.call-update) | async-done | bytes 708752 | tf_op jit(solution)/shard_map/psum | solution.py:17
  348.1 1.3 select_reduce_fusion
  349.4 26.8 %all_gather.7 = bf16[16,112,113]{2,1,0:T(8,128)(2,1)S(1)} all-gather(bf16[2,112,113]{2,1,0:T(8,128)(2,1)S(1)} %select_reduce_fusion), channel_id=1, replica_groups=mesh['tm'=32,'inner'=8] {'inner'}, dimensions={0}, use_global_device_ids=true | all-gather | bytes 455616 | tf_op jit(solution)/shard_map/all_gather | solution.py:20
  376.2 0.3 convolution_convert_fusion
  376.5 0.7 copy-done.1
  377.2 0.4 fusion.3
  377.6 1.0 copy.49
  378.6 1.0 copy.48
  (27 shorter events, 0.5 us)
Async XLA Ops:
  7.2 45.3 %reduce-scatter.3.cloned.1.call-start = ((), (), s32[]{:S(2)}) async-start(), calls=%async_computation.2 | async-start | bytes 1032192 | tf_op jit(solution)/shard_map/reduce_scatter | solution.py:13
  8.5 1.0 copy-start.4
  9.8 1.4 copy-start
  11.1 1.0 copy-start.5
  11.1 1.2 copy-start.6
  11.2 156.3 %all-reduce.4.cloned.1.call-start = ((), (), s32[]{:S(2)}) async-start(), calls=%async_computation.3 | async-start | bytes 1605632 | tf_op jit(solution)/shard_map/psum | solution.py:17
  12.8 0.7 copy-start.7
  54.4 179.2 %reduce-scatter.5.cloned.1.call-start = ((), (), s32[]{:S(2)}) async-start(), calls=%async_computation.4 | async-start | bytes 1032192 | tf_op jit(solution)/shard_map/reduce_scatter | solution.py:13
  195.5 0.8 copy-start.2
  197.9 150.3 %all-reduce.6.cloned.1.call-start = ((), (), s32[]{:S(2)}) async-start(), calls=%async_computation.5 | async-start | bytes 1605632 | tf_op jit(solution)/shard_map/psum | solution.py:17
  235.5 1.0 copy-start.3
  376.2 1.0 copy-start.1
Sparse Core Ops, SparseCore 0:
  11.3 41.1 reduce-scatter.2
  56.1 111.3 all-reduce.3
  198.0 35.5 reduce-scatter.4
  236.7 111.3 all-reduce.5

commit v2 on v1

--- a/solution.py
+++ b/solution.py
@@ -4,32 +4,38 @@
 from jax.sharding import PartitionSpec as P
 
 DH = 112
-SPANS = 7
 
 loss_scale = 1024.0
 
 
 def visible(part, label, later):
-    own = lax.psum_scatter(part, "inner", scatter_dimension=0, tiled=True)
-    levels = jnp.arange(SPANS, dtype=jnp.int32)
-    onehot = (levels == label).astype(jnp.float32)
-    spread = onehot[:, None, None, None] * own[None]
-    totals = lax.psum(spread, "tm")
-    keep = (levels >= label) if later else (levels <= label)
-    seen = jnp.sum(jnp.where(keep[:, None, None, None], totals, 0.0), axis=0)
-    return lax.all_gather(seen.astype(jnp.bfloat16), "inner", axis=0, tiled=True)
+    tag = jnp.broadcast_to(label.astype(jnp.float32), part.shape[:-1] + (1,))
+    packed = jnp.concatenate([part, tag], axis=-1)
+    every = lax.all_gather(packed, "tm", axis=0)
+    their = every[:, 0, 0, DH + 1]
+    keep = (their >= label) if later else (their <= label)
+    seen = jnp.sum(jnp.where(keep[:, None, None, None], every[..., : DH + 1], 0.0), axis=0)
+    return seen.astype(jnp.bfloat16)
 
 
 def local(query_input, key_input, value_input, cotangent, span_labels):
-    tokens = query_input.shape[0]
-    heads = query_input.shape[1] // DH
+    groups = lax.axis_size("inner")
+    rows, columns = query_input.shape
+    width = columns // groups
+    heads = width // DH
+    tokens = rows * groups
 
-    def split(flat):
-        return flat.reshape(tokens, heads, DH)
+    stacked = jnp.stack([query_input, key_input, value_input, cotangent])
+    outgoing = stacked.reshape(4, rows, groups, width).transpose(2, 0, 1, 3)
+    incoming = lax.all_to_all(outgoing, "inner", 0, 0, tiled=True)
+    arrived = incoming.transpose(1, 0, 2, 3).reshape(4, tokens, heads, DH)
+    query_heads, key_heads, value_heads, cotangent_heads = (
+        arrived[0],
+        arrived[1],
+        arrived[2],
+        arrived[3],
+    )
 
-    query_heads = split(query_input)
-    key_heads = split(key_input)
-    value_heads = split(value_input)
     feat_query = jnp.maximum(query_heads, 0)
     feat_key = jnp.maximum(key_heads, 0)
     label = span_labels[0]
@@ -44,7 +50,7 @@
     weight = both[..., DH]
     denominator = weight / DH + 1.0
     output = numerator / (DH * denominator[..., None])
-    scaled = split(cotangent).astype(jnp.float32) * loss_scale
+    scaled = cotangent_heads.astype(jnp.float32) * loss_scale
     numer_back = (scaled / (DH * denominator[..., None])).astype(jnp.bfloat16)
     weight_back = (-jnp.sum(scaled * output, axis=-1) / (DH * denominator)).astype(jnp.bfloat16)
     back_aug = jnp.concatenate([numer_back, weight_back[..., None]], axis=-1)
@@ -60,10 +66,11 @@
     query_back = jnp.where(query_heads > 0, query_feat, 0.0).astype(jnp.bfloat16)
     key_back = jnp.where(key_heads > 0, key_feat, 0.0).astype(jnp.bfloat16)
 
-    def merge(heads_arr):
-        return heads_arr.reshape(tokens, heads * DH)
-
-    return merge(query_back), merge(key_back), merge(value_back.astype(jnp.bfloat16))
+    results = jnp.stack([query_back, key_back, value_back.astype(jnp.bfloat16)])
+    leaving = results.reshape(3, groups, rows, width).transpose(1, 0, 2, 3)
+    returned = lax.all_to_all(leaving, "inner", 0, 0, tiled=True)
+    merged = returned.transpose(1, 2, 0, 3).reshape(3, rows, columns)
+    return merged[0], merged[1], merged[2]
 
 
 def solution(mesh):

time: 387 us -> 233 us (0.60)
  waiting for transfers between devices: 298 us -> 134 us
  local copies, waits for them, and re-layouts: 9.54 us -> 22.1 us
  blocking collectives: 53.5 us -> 43 us
  starting transfers between devices: 0.16 us -> 8.68 us
    psum x2 -> x0, waiting for transfers between devices: 223 us -> none  [visible(): totals = lax.psum(spread, 'tm')]
    all_gather x0 -> x2, waiting for transfers between devices: none -> 88.6 us  [visible(): every = lax.all_gather(packed, 'tm', axis=0)]
    reduce_scatter x2 -> x0, waiting for transfers between devices: 74.3 us -> none  [visible(): own = lax.psum_scatter(part, 'inner', scatter_dimension=0, tiled=True)]
    all_gather x2 -> x0, blocking collectives: 53.5 us -> none  [visible(): lax.all_gather(seen.astype(jnp.bfloat16), 'inner', axis=0, tiled=True)]
    all_to_all x0 -> x1, waiting for transfers between devices: none -> 45.5 us  [local(): incoming = lax.all_to_all(outgoing, 'inner', 0, 0, tiled=True)]
    all_to_all x0 -> x1, blocking collectives: none -> 43 us  [local(): returned = lax.all_to_all(leaving, 'inner', 0, 0, tiled=True)]
    all_to_all x0 -> x1, starting transfers between devices: none -> 8.6 us  [local(): incoming = lax.all_to_all(outgoing, 'inner', 0, 0, tiled=True)]
    max x0 -> x4, local copies, waits for them, and re-layouts: none -> 5.51 us  [the longest x2 3.95 us: local(): feat_query = jnp.maximum(query_heads, 0)]
  transfers between devices with their start and end apart: 4 -> 3, of which waited for: 4 -> 3; matrix products, arithmetic and copies ran while one was open for 1% -> 4% of each run, Pallas kernels for 0% -> 0%
where the time goes in v2:
time: 233 us; the launch traced here: 232 us
  waiting for transfers between devices  134 us (58%)
  blocking collectives  43 us (18%)
  local copies, waits for them, and re-layouts  22.1 us (9%)
  between operations  14.4 us (6%)
  starting transfers between devices  8.68 us (4%)
  other arithmetic  8.19 us (4%)
    all_gather x2, waiting for transfers between devices, visible(): every = lax.all_gather(packed, 'tm', axis=0)  88.6 us
    all_to_all x1, waiting for transfers between devices, local(): incoming = lax.all_to_all(outgoing, 'inner', 0, 0, tiled=True)  45.5 us
    all_to_all x1, blocking collectives, local(): returned = lax.all_to_all(leaving, 'inner', 0, 0, tiled=True)  43 us
    all_to_all x1, starting transfers between devices, local(): incoming = lax.all_to_all(outgoing, 'inner', 0, 0, tiled=True)  8.6 us
    unnamed x29, local copies, waits for them, and re-layouts  7.64 us
    reduce_sum x2, other arithmetic, visible(): jnp.sum(jnp.where(keep[:, None, None, None], every[..., :DH + 1], 0.0), a...  5.2 us
  transfers between devices with their start and end apart: 3, of which 3 were waited for; matrix products, arithmetic and copies ran while one was open for 4% of the time, Pallas kernels for 0%

profile of v2, /device:TPU:2, one launch (start us, length us, event | category | flops | bytes accessed | tf_op | source)
XLA Modules:
  0.0 232.3 jit_solution(4019059200682709887)
XLA Ops:
  7.2 1.4 copy.59
  8.5 1.3 copy.60
  10.1 1.0 copy.62
  11.1 1.2 maximum_bitcast_fusion
  12.3 1.4 copy.63
  13.7 8.6 %all-to-all-start = ((bf16[8,4,128,224]{2,3,1,0:T(8,128)(2,1)}), bf16[8,4,128,224]{2,3,1,0:T(8,128)(2,1)S(1)}, u32[]{:S(2)}, u32[]{:S(2)}) async-start(bf16[8,4,128,224]{2,3,1,0:T(8,128)(2,1)} %copy.63), calls=%async_computation | async-start | bytes 3670016 | tf_op jit(solution)/shard_map/all_to_all | solution.py:30
  22.4 45.5 %all-to-all-done = bf16[8,4,128,224]{2,3,1,0:T(8,128)(2,1)S(1)} async-done(((bf16[8,4,128,224]{2,3,1,0:T(8,128)(2,1)}), bf16[8,4,128,224]{2,3,1,0:T(8,128)(2,1)S(1)}, u32[]{:S(2)}, u32[]{:S(2)}) %all-to-all-start) | async-done | bytes 1835040 | tf_op jit(solution)/shard_map/all_to_all | solution.py:30
  67.9 1.0 fusion.22
  69.3 1.4 copy.65
  70.9 0.3 fusion.9
  71.2 0.7 concatenate.15
  72.0 1.5 copy.68
  73.5 1.3 mul.22
  74.8 2.0 copy.69
  76.8 2.0 max.15
  78.7 39.8 %all-gather.5.cloned.1.call-done = f32[64,112,114]{2,1,0:T(8,128)} async-done(((f32[2,112,114]{2,1,0:T(8,128)}), f32[64,112,114]{2,1,0:T(8,128)}) %all-gather.5.cloned.1.call-update) | async-done | bytes 3268624 | tf_op jit(solution)/shard_map/all_gather | solution.py:14
  118.5 1.0 slice.70
  119.6 2.6 %fusion.1 = bf16[2,112,113]{2,1,0:T(8,128)(2,1)S(1)} fusion(f32[32,2,112,114]{3,2,1,0:T(8,128)} %bitcast.98, pred[32]{0:T(512)(128)(4,1)S(1)} %compare_bitcast_fusion.1), kind=kLoop, calls=%fused_computation.3 | loop fusion | flops 1594656 | bytes 3290592 | tf_op jit(solution)/shard_map/reduce_sum | solution.py:17
  122.2 0.3 convolution_bitcast_fusion
  122.9 0.3 fusion.11
  123.2 0.4 copy-done.5
  123.6 0.7 concatenate.17
  125.3 0.3 fusion.5
  125.8 48.8 %all-gather.7.cloned.1.call-done = f32[64,112,114]{2,1,0:T(8,128)} async-done(((f32[2,112,114]{2,1,0:T(8,128)}), f32[64,112,114]{2,1,0:T(8,128)}) %all-gather.7.cloned.1.call-update) | async-done | bytes 3268624 | tf_op jit(solution)/shard_map/all_gather | solution.py:14
  174.5 1.0 slice.75
  175.6 2.6 %fusion = bf16[2,112,113]{2,1,0:T(8,128)(2,1)S(1)} fusion(f32[32,2,112,114]{3,2,1,0:T(8,128)} %bitcast.96, pred[32]{0:T(512)(128)(4,1)S(1)} %compare_bitcast_fusion), kind=kLoop, calls=%fused_computation.1 | loop fusion | flops 1594656 | bytes 3290592 | tf_op jit(solution)/shard_map/reduce_sum | solution.py:17
  178.2 0.3 convolution_convert_fusion
  178.6 0.3 fusion.4
  179.3 43.0 %all_to_all.10 = bf16[8,3,128,224]{2,3,1,0:T(8,128)(2,1)S(1)} all-to-all(bf16[8,3,128,224]{2,3,1,0:T(8,128)(2,1)S(1)} %maximum_bitcast_fusion.1), channel_id=1, replica_groups=mesh['tm'=32,'inner'=8] {'inner'}, dimensions={0} | all-to-all | bytes 2752512 | tf_op jit(solution)/shard_map/all_to_all | solution.py:71
  222.5 1.0 copy.79
  223.5 1.0 copy.78
  224.5 1.0 copy.77
  (47 shorter events, 3.2 us)
Async XLA Ops:
  7.2 2.7 %copy-start.3 = (bf16[128,1792]{1,0:T(8,128)(2,1)S(1)}, bf16[128,1792]{1,0:T(8,128)(2,1)}, u32[]{:S(2)}) copy-start(bf16[128,1792]{1,0:T(8,128)(2,1)} %param.7) | copy-start | bytes 1376260
  7.2 2.9 %copy-start.4 = (bf16[128,1792]{1,0:T(8,128)(2,1)S(1)}, bf16[128,1792]{1,0:T(8,128)(2,1)}, u32[]{:S(2)}) copy-start(bf16[128,1792]{1,0:T(8,128)(2,1)} %param.8) | copy-start | bytes 1376260
  13.7 8.6 %copy-start.7 = (s32[128]{0:T(128)S(1)}, s32[128]{0:T(128)}, u32[]{:S(2)}) copy-start(s32[128]{0:T(128)} %param.9) | copy-start | bytes 1540
  13.7 54.2 %all-to-all-start = ((bf16[8,4,128,224]{2,3,1,0:T(8,128)(2,1)}), bf16[8,4,128,224]{2,3,1,0:T(8,128)(2,1)S(1)}, u32[]{:S(2)}, u32[]{:S(2)}) async-start(bf16[8,4,128,224]{2,3,1,0:T(8,128)(2,1)} %copy.63), calls=%async_computation | async-start | bytes 3670016 | tf_op jit(solution)/shard_map/all_to_all | solution.py:30
  22.3 96.2 %all-gather.5.cloned.1.call-start = ((), (), s32[]{:S(2)}) async-start(), calls=%async_computation.2 | async-start | bytes 3784704 | tf_op jit(solution)/shard_map/all_gather | solution.py:14
  69.3 2.7 %copy-start = (bf16[1024,2,112]{0,2,1:T(8,128)(2,1)}, bf16[1024,2,112]{0,2,1:T(8,128)(2,1)S(1)}, u32[]{:S(2)}) copy-start(bf16[1024,2,112]{0,2,1:T(8,128)(2,1)S(1)} %squeeze.8) | copy-start | bytes 1376260
  71.9 102.6 %all-gather.7.cloned.1.call-start = ((), (), s32[]{:S(2)}) async-start(), calls=%async_computation.3 | async-start | bytes 3784704 | tf_op jit(solution)/shard_map/all_gather | solution.py:14
  119.6 2.6 %copy-start.2 = (bf16[1024,2,112]{0,2,1:T(8,128)(2,1)S(1)}, bf16[1024,2,112]{0,2,1:T(8,128)(2,1)}, u32[]{:S(2)}) copy-start(bf16[1024,2,112]{0,2,1:T(8,128)(2,1)} %max.15) | copy-start | bytes 1376260
  122.9 0.8 copy-start.5
  124.3 1.0 copy-start.6
  175.6 2.9 %copy-start.1 = (bf16[1024,2,112]{0,2,1:T(8,128)(2,1)S(1)}, bf16[1024,2,112]{0,2,1:T(8,128)(2,1)}, u32[]{:S(2)}) copy-start(bf16[1024,2,112]{0,2,1:T(8,128)(2,1)} %copy-done) | copy-start | bytes 1376260
Sparse Core Ops, SparseCore 0:
  72.0 46.5 all-gather.4
  124.4 50.0 all-gather.6

commit v3 on v2

--- a/solution.py
+++ b/solution.py
@@ -1,3 +1,5 @@
+import functools
+
 import jax
 import jax.numpy as jnp
 from jax import lax
@@ -8,13 +10,60 @@
 loss_scale = 1024.0
 
 
+ROW = 8
+
+
+def shifted(value, count, step):
+    total = lax.axis_size("tm")
+    pairs = []
+    for base in range(0, total, count):
+        for i in range(count):
+            pairs.append((base + i, base + (i + step) % count))
+    return lax.ppermute(value, "tm", pairs)
+
+
+def strided(value, stride, step):
+    total = lax.axis_size("tm")
+    rows = total // stride
+    pairs = []
+    for r in range(rows):
+        for j in range(stride):
+            pairs.append((r * stride + j, ((r + step) % rows) * stride + j))
+    return lax.ppermute(value, "tm", pairs)
+
+
 def visible(part, label, later):
-    tag = jnp.broadcast_to(label.astype(jnp.float32), part.shape[:-1] + (1,))
+    total = lax.axis_size("tm")
+    row = min(ROW, total)
+    rows = total // row
+    me = lax.axis_index("tm") // row
+    flabel = label.astype(jnp.float32)
+    tag = jnp.broadcast_to(flabel, part.shape[:-1] + (1,))
     packed = jnp.concatenate([part, tag], axis=-1)
-    every = lax.all_gather(packed, "tm", axis=0)
-    their = every[:, 0, 0, DH + 1]
-    keep = (their >= label) if later else (their <= label)
-    seen = jnp.sum(jnp.where(keep[:, None, None, None], every[..., : DH + 1], 0.0), axis=0)
+    frames = [packed] + [shifted(packed, row, s) for s in range(1, row)]
+    labels = [f[0, 0, DH + 1] for f in frames]
+    states = [f[..., : DH + 1] for f in frames]
+    keep = [(l >= flabel) if later else (l <= flabel) for l in labels]
+    seen = sum(jnp.where(k, s, 0.0) for k, s in zip(keep, states))
+    if rows > 1:
+        edge = functools.reduce(jnp.maximum, labels) if later else functools.reduce(jnp.minimum, labels)
+        whole = sum(states)
+        edge_sum = sum(jnp.where(l == edge, s, 0.0) for l, s in zip(labels, states))
+        etag = jnp.broadcast_to(edge, part.shape[:-1] + (1,))
+        summary = jnp.stack(
+            [jnp.concatenate([whole, etag], -1), jnp.concatenate([edge_sum, etag], -1)]
+        )
+        for s in range(1, rows):
+            got = strided(summary, row, s)
+            source = (me - s) % rows
+            their_edge = got[1, 0, 0, DH + 1]
+            full = (source > me) if later else (source < me)
+            part_only = ((source < me) if later else (source > me)) & (their_edge == flabel)
+            seen = (
+                seen
+                + jnp.where(full, got[0, ..., : DH + 1], 0.0)
+                + jnp.where(part_only, got[1, ..., : DH + 1], 0.0)
+            )
     return seen.astype(jnp.bfloat16)
 
 

time: 233 us -> 204 us (0.88)
  the two profiles are of different devices: /device:TPU:2 before, /device:TPU:25 now
where the time goes in v3:
time: 204 us; the launch traced here: 203 us
  waiting for transfers between devices  51.1 us (25%)
  blocking collectives  38.6 us (19%)
  starting transfers between devices  36.1 us (18%)
  local copies, waits for them, and re-layouts  35.9 us (18%)
  between operations  31.9 us (16%)
  other arithmetic  7.55 us (4%)
    all_to_all x1, waiting for transfers between devices, local(): incoming = lax.all_to_all(outgoing, 'inner', 0, 0, tiled=True)  46 us
    all_to_all x1, blocking collectives, local(): returned = lax.all_to_all(leaving, 'inner', 0, 0, tiled=True)  38.6 us
    ppermute x14, starting transfers between devices, shifted(): return lax.ppermute(value, 'tm', pairs)  20.6 us
    slice x14, local copies, waits for them, and re-layouts, visible(): labels = [f[0, 0, DH + 1] for f in frames]  9.34 us
    all_to_all x1, starting transfers between devices, local(): incoming = lax.all_to_all(outgoing, 'inner', 0, 0, tiled=True)  8.32 us
    slice x6, local copies, waits for them, and re-layouts, visible(): their_edge = got[1, 0, 0, DH + 1]  7.57 us
    ppermute x6, starting transfers between devices, strided(): return lax.ppermute(value, 'tm', pairs)  7.21 us
    unnamed x43, local copies, waits for them, and re-layouts  7.03 us
  transfers between devices with their start and end apart: 21, of which 4 were waited for; matrix products, arithmetic and copies ran while one was open for 10% of the time, Pallas kernels for 0%

profile of v3, /device:TPU:25, one launch (start us, length us, event | category | flops | bytes accessed | tf_op | source)
XLA Modules:
  0.0 203.0 jit_solution(4930737068033318955)
XLA Ops:
  0.7 1.4 copy.33
  2.0 1.3 copy.34
  4.1 1.4 copy.37
  5.5 8.3 %all-to-all-start = ((bf16[8,4,128,224]{2,3,1,0:T(8,128)(2,1)}), bf16[8,4,128,224]{2,3,1,0:T(8,128)(2,1)S(1)}, u32[]{:S(2)}, u32[]{:S(2)}) async-start(bf16[8,4,128,224]{2,3,1,0:T(8,128)(2,1)} %copy.37), calls=%async_computation | async-start | bytes 3670016 | tf_op jit(solution)/shard_map/all_to_all | solution.py:79
  13.8 46.0 %all-to-all-done = bf16[8,4,128,224]{2,3,1,0:T(8,128)(2,1)S(1)} async-done(((bf16[8,4,128,224]{2,3,1,0:T(8,128)(2,1)}), bf16[8,4,128,224]{2,3,1,0:T(8,128)(2,1)S(1)}, u32[]{:S(2)}, u32[]{:S(2)}) %all-to-all-start) | async-done | bytes 1835040 | tf_op jit(solution)/shard_map/all_to_all | solution.py:79
  61.2 1.4 copy.39
  65.0 1.9 collective-permute-start
  66.9 1.2 collective-permute-start.2
  68.6 2.3 %collective-permute-start.4 = (f32[2,112,114]{2,1,0:T(8,128)}, f32[2,112,114]{2,1,0:T(8,128)S(1)}, u32[]{:S(2)}, u32[]{:S(2)}) collective-permute-start(f32[2,112,114]{2,1,0:T(8,128)} %concatenate.27), channel_id=1, source_target_pairs={{0,40},{8,48},{16,56},{24,0},{32,8},{40,16},{48,24},{56,32},{64,10... | collective-permute-start | bytes 306440 | tf_op jit(solution)/shard_map/ppermute | solution.py:22
  71.6 1.7 collective-permute-start.6
  81.2 1.3 slice.252
  91.3 1.9 collective-permute-start.7
  93.3 1.5 copy.41
  94.8 1.3 mul.22
  96.1 2.0 copy.42
  98.1 2.0 max.36
  104.6 1.3 slice.261
  106.5 1.3 slice.258
  108.4 1.3 slice.255
  110.4 1.5 fusion.25
  115.4 2.1 %collective-permute-start.15 = (f32[2,112,114]{2,1,0:T(8,128)S(1)}, f32[2,112,114]{2,1,0:T(8,128)S(1)}, u32[]{:S(2)}, u32[]{:S(2)}) collective-permute-start(f32[2,112,114]{2,1,0:T(8,128)S(1)} %concatenate.31), channel_id=1, source_target_pairs={{0,48},{8,56},{16,0},{24,8},{32,16},{40,24},{48,32},{56,40},{64,11... | collective-permute-start | bytes 306440 | tf_op jit(solution)/shard_map/ppermute | solution.py:22
  117.5 2.1 %collective-permute-start.14 = (f32[2,112,114]{2,1,0:T(8,128)S(1)}, f32[2,112,114]{2,1,0:T(8,128)S(1)}, u32[]{:S(2)}, u32[]{:S(2)}) collective-permute-start(f32[2,112,114]{2,1,0:T(8,128)S(1)} %concatenate.31), channel_id=1, source_target_pairs={{0,40},{8,48},{16,56},{24,0},{32,8},{40,16},{48,24},{56,32},{64,10... | collective-permute-start | bytes 306440 | tf_op jit(solution)/shard_map/ppermute | solution.py:22
  119.6 1.6 collective-permute-start.13
  121.2 3.5 %collective-permute-start.12 = (f32[2,112,114]{2,1,0:T(8,128)S(1)}, f32[2,112,114]{2,1,0:T(8,128)S(1)}, u32[]{:S(2)}, u32[]{:S(2)}) collective-permute-start(f32[2,112,114]{2,1,0:T(8,128)S(1)} %concatenate.31), channel_id=1, source_target_pairs={{0,24},{8,32},{16,40},{24,48},{32,56},{40,0},{48,8},{56,16},{64,88... | collective-permute-start | bytes 306440 | tf_op jit(solution)/shard_map/ppermute | solution.py:22
  139.9 2.1 %collective-permute-start.18 = (f32[2,2,112,114]{3,2,1,0:T(8,128)S(1)}, f32[2,2,112,114]{3,2,1,0:T(8,128)}, u32[]{:S(2)}, u32[]{:S(2)}) collective-permute-start(f32[2,2,112,114]{3,2,1,0:T(8,128)S(1)} %pad_maximum_fusion.4), channel_id=1, source_target_pairs={{0,128},{8,136},{16,144},{24,152},{32,160},{40,168},{48,176},{56,1... | collective-permute-start | bytes 612872 | tf_op jit(solution)/shard_map/ppermute | solution.py:32
  142.1 2.0 collective-permute-start.17
  148.9 4.1 %collective-permute-done.19 = f32[2,2,112,114]{3,2,1,0:T(8,128)} collective-permute-done((f32[2,2,112,114]{3,2,1,0:T(8,128)S(1)}, f32[2,2,112,114]{3,2,1,0:T(8,128)}, u32[]{:S(2)}, u32[]{:S(2)}) %collective-permute-start.19) | collective-permute-done | bytes 204320 | tf_op jit(solution)/shard_map/ppermute | solution.py:32
  153.0 1.3 slice.287
  155.0 1.3 slice.284
  156.9 1.3 slice.281
  158.8 1.3 fusion.12
  161.2 38.6 %all_to_all.10 = bf16[8,3,128,224]{2,3,1,0:T(8,128)(2,1)S(1)} all-to-all(bf16[8,3,128,224]{2,3,1,0:T(8,128)(2,1)S(1)} %maximum_bitcast_fusion.1), channel_id=1, replica_groups=mesh['tm'=32,'inner'=8] {'inner'}, dimensions={0} | all-to-all | bytes 2752512 | tf_op jit(solution)/shard_map/all_to_all | solution.py:120
  (120 shorter events, 27.8 us)
Async XLA Ops:
  0.6 2.9 %copy-start.8 = (bf16[128,1792]{1,0:T(8,128)(2,1)S(1)}, bf16[128,1792]{1,0:T(8,128)(2,1)}, u32[]{:S(2)}) copy-start(bf16[128,1792]{1,0:T(8,128)(2,1)} %param.8) | copy-start | bytes 1376260
  5.5 8.3 %copy-start.15 = (s32[128]{0:T(128)S(1)}, s32[128]{0:T(128)}, u32[]{:S(2)}) copy-start(s32[128]{0:T(128)} %param.9) | copy-start | bytes 1540
  5.5 54.4 %all-to-all-start = ((bf16[8,4,128,224]{2,3,1,0:T(8,128)(2,1)}), bf16[8,4,128,224]{2,3,1,0:T(8,128)(2,1)S(1)}, u32[]{:S(2)}, u32[]{:S(2)}) async-start(bf16[8,4,128,224]{2,3,1,0:T(8,128)(2,1)} %copy.37), calls=%async_computation | async-start | bytes 3670016 | tf_op jit(solution)/shard_map/all_to_all | solution.py:79
  61.2 27.3 %copy-start = (bf16[1024,2,112]{0,2,1:T(8,128)(2,1)}, bf16[1024,2,112]{0,2,1:T(8,128)(2,1)S(1)}, u32[]{:S(2)}) copy-start(bf16[1024,2,112]{0,2,1:T(8,128)(2,1)S(1)} %squeeze.91) | copy-start | bytes 1376260
  63.8 7.2 %collective-permute-start.1 = (f32[2,112,114]{2,1,0:T(8,128)}, f32[2,112,114]{2,1,0:T(8,128)S(1)}, u32[]{:S(2)}, u32[]{:S(2)}) collective-permute-start(f32[2,112,114]{2,1,0:T(8,128)} %concatenate.27), channel_id=1, source_target_pairs={{0,16},{8,24},{16,32},{24,40},{32,48},{40,56},{48,0},{56,8},{64,80... | collective-permute-start | bytes 306440 | tf_op jit(solution)/shard_map/ppermute | solution.py:22
  65.0 6.6 %collective-permute-start = (f32[2,112,114]{2,1,0:T(8,128)}, f32[2,112,114]{2,1,0:T(8,128)S(1)}, u32[]{:S(2)}, u32[]{:S(2)}) collective-permute-start(f32[2,112,114]{2,1,0:T(8,128)} %concatenate.27), channel_id=1, source_target_pairs={{0,8},{8,16},{16,24},{24,32},{32,40},{40,48},{48,56},{56,0},{64,72... | collective-permute-start | bytes 306440 | tf_op jit(solution)/shard_map/ppermute | solution.py:22
  66.9 9.1 %collective-permute-start.2 = (f32[2,112,114]{2,1,0:T(8,128)}, f32[2,112,114]{2,1,0:T(8,128)S(1)}, u32[]{:S(2)}, u32[]{:S(2)}) collective-permute-start(f32[2,112,114]{2,1,0:T(8,128)} %concatenate.27), channel_id=1, source_target_pairs={{0,24},{8,32},{16,40},{24,48},{32,56},{40,0},{48,8},{56,16},{64,88... | collective-permute-start | bytes 306440 | tf_op jit(solution)/shard_map/ppermute | solution.py:22
  68.1 9.4 %collective-permute-start.3 = (f32[2,112,114]{2,1,0:T(8,128)}, f32[2,112,114]{2,1,0:T(8,128)S(1)}, u32[]{:S(2)}, u32[]{:S(2)}) collective-permute-start(f32[2,112,114]{2,1,0:T(8,128)} %concatenate.27), channel_id=1, source_target_pairs={{0,32},{8,40},{16,48},{24,56},{32,0},{40,8},{48,16},{56,24},{64,96... | collective-permute-start | bytes 306440 | tf_op jit(solution)/shard_map/ppermute | solution.py:22
  68.6 10.0 %collective-permute-start.4 = (f32[2,112,114]{2,1,0:T(8,128)}, f32[2,112,114]{2,1,0:T(8,128)S(1)}, u32[]{:S(2)}, u32[]{:S(2)}) collective-permute-start(f32[2,112,114]{2,1,0:T(8,128)} %concatenate.27), channel_id=1, source_target_pairs={{0,40},{8,48},{16,56},{24,0},{32,8},{40,16},{48,24},{56,32},{64,10... | collective-permute-start | bytes 306440 | tf_op jit(solution)/shard_map/ppermute | solution.py:22
  70.9 8.9 %collective-permute-start.5 = (f32[2,112,114]{2,1,0:T(8,128)}, f32[2,112,114]{2,1,0:T(8,128)S(1)}, u32[]{:S(2)}, u32[]{:S(2)}) collective-permute-start(f32[2,112,114]{2,1,0:T(8,128)} %concatenate.27), channel_id=1, source_target_pairs={{0,48},{8,56},{16,0},{24,8},{32,16},{40,24},{48,32},{56,40},{64,11... | collective-permute-start | bytes 306440 | tf_op jit(solution)/shard_map/ppermute | solution.py:22
  71.6 9.6 %collective-permute-start.6 = (f32[2,112,114]{2,1,0:T(8,128)}, f32[2,112,114]{2,1,0:T(8,128)}, u32[]{:S(2)}, u32[]{:S(2)}) collective-permute-start(f32[2,112,114]{2,1,0:T(8,128)} %concatenate.27), channel_id=1, source_target_pairs={{0,56},{8,0},{16,8},{24,16},{32,24},{40,32},{48,40},{56,48},{64,12... | collective-permute-start | bytes 306440 | tf_op jit(solution)/shard_map/ppermute | solution.py:22
  75.9 17.4 %copy-start.3 = (f32[2,112,114]{2,1,0:T(8,128)}, f32[2,112,114]{2,1,0:T(8,128)S(1)}, u32[]{:S(2)}) copy-start(f32[2,112,114]{2,1,0:T(8,128)S(1)} %collective-permute-done.2) | copy-start | bytes 306436
  77.5 15.8 %copy-start.4 = (f32[2,112,114]{2,1,0:T(8,128)}, f32[2,112,114]{2,1,0:T(8,128)S(1)}, u32[]{:S(2)}) copy-start(f32[2,112,114]{2,1,0:T(8,128)S(1)} %collective-permute-done.3) | copy-start | bytes 306436
  78.6 14.7 %copy-start.5 = (f32[2,112,114]{2,1,0:T(8,128)}, f32[2,112,114]{2,1,0:T(8,128)S(1)}, u32[]{:S(2)}) copy-start(f32[2,112,114]{2,1,0:T(8,128)S(1)} %collective-permute-done.4) | copy-start | bytes 306436
  79.8 13.5 %copy-start.6 = (f32[2,112,114]{2,1,0:T(8,128)}, f32[2,112,114]{2,1,0:T(8,128)S(1)}, u32[]{:S(2)}) copy-start(f32[2,112,114]{2,1,0:T(8,128)S(1)} %collective-permute-done.5) | copy-start | bytes 306436
  90.2 14.4 %collective-permute-start.9 = (f32[2,2,112,114]{3,2,1,0:T(8,128)}, f32[2,2,112,114]{3,2,1,0:T(8,128)}, u32[]{:S(2)}, u32[]{:S(2)}) collective-permute-start(f32[2,2,112,114]{3,2,1,0:T(8,128)} %pad_maximum_fusion.3), channel_id=1, source_target_pairs={{0,192},{8,200},{16,208},{24,216},{32,224},{40,232},{48,240},{56,2... | collective-permute-start | bytes 612872 | tf_op jit(solution)/shard_map/ppermute | solution.py:32
  90.7 15.8 %collective-permute-start.8 = (f32[2,2,112,114]{3,2,1,0:T(8,128)}, f32[2,2,112,114]{3,2,1,0:T(8,128)}, u32[]{:S(2)}, u32[]{:S(2)}) collective-permute-start(f32[2,2,112,114]{3,2,1,0:T(8,128)} %pad_maximum_fusion.3), channel_id=1, source_target_pairs={{0,128},{8,136},{16,144},{24,152},{32,160},{40,168},{48,176},{56,1... | collective-permute-start | bytes 612872 | tf_op jit(solution)/shard_map/ppermute | solution.py:32
  91.3 17.1 %collective-permute-start.7 = (f32[2,2,112,114]{3,2,1,0:T(8,128)}, f32[2,2,112,114]{3,2,1,0:T(8,128)}, u32[]{:S(2)}, u32[]{:S(2)}) collective-permute-start(f32[2,2,112,114]{3,2,1,0:T(8,128)} %pad_maximum_fusion.3), channel_id=1, source_target_pairs={{0,64},{8,72},{16,80},{24,88},{32,96},{40,104},{48,112},{56,120},{... | collective-permute-start | bytes 612872 | tf_op jit(solution)/shard_map/ppermute | solution.py:32
  113.5 6.1 %collective-permute-start.11 = (f32[2,112,114]{2,1,0:T(8,128)S(1)}, f32[2,112,114]{2,1,0:T(8,128)S(1)}, u32[]{:S(2)}, u32[]{:S(2)}) collective-permute-start(f32[2,112,114]{2,1,0:T(8,128)S(1)} %concatenate.31), channel_id=1, source_target_pairs={{0,16},{8,24},{16,32},{24,40},{32,48},{40,56},{48,0},{56,8},{64,80... | collective-permute-start | bytes 306440 | tf_op jit(solution)/shard_map/ppermute | solution.py:22
  114.2 7.0 %collective-permute-start.10 = (f32[2,112,114]{2,1,0:T(8,128)S(1)}, f32[2,112,114]{2,1,0:T(8,128)S(1)}, u32[]{:S(2)}, u32[]{:S(2)}) collective-permute-start(f32[2,112,114]{2,1,0:T(8,128)S(1)} %concatenate.31), channel_id=1, source_target_pairs={{0,8},{8,16},{16,24},{24,32},{32,40},{40,48},{48,56},{56,0},{64,72... | collective-permute-start | bytes 306440 | tf_op jit(solution)/shard_map/ppermute | solution.py:22
  115.4 18.6 %collective-permute-start.16 = (f32[2,112,114]{2,1,0:T(8,128)S(1)}, f32[2,112,114]{2,1,0:T(8,128)S(1)}, u32[]{:S(2)}, u32[]{:S(2)}) collective-permute-start(f32[2,112,114]{2,1,0:T(8,128)S(1)} %concatenate.31), channel_id=1, source_target_pairs={{0,56},{8,0},{16,8},{24,16},{32,24},{40,32},{48,40},{56,48},{64,12... | collective-permute-start | bytes 306440 | tf_op jit(solution)/shard_map/ppermute | solution.py:22
  115.4 17.3 %collective-permute-start.15 = (f32[2,112,114]{2,1,0:T(8,128)S(1)}, f32[2,112,114]{2,1,0:T(8,128)S(1)}, u32[]{:S(2)}, u32[]{:S(2)}) collective-permute-start(f32[2,112,114]{2,1,0:T(8,128)S(1)} %concatenate.31), channel_id=1, source_target_pairs={{0,48},{8,56},{16,0},{24,8},{32,16},{40,24},{48,32},{56,40},{64,11... | collective-permute-start | bytes 306440 | tf_op jit(solution)/shard_map/ppermute | solution.py:22
  117.5 14.0 %collective-permute-start.14 = (f32[2,112,114]{2,1,0:T(8,128)S(1)}, f32[2,112,114]{2,1,0:T(8,128)S(1)}, u32[]{:S(2)}, u32[]{:S(2)}) collective-permute-start(f32[2,112,114]{2,1,0:T(8,128)S(1)} %concatenate.31), channel_id=1, source_target_pairs={{0,40},{8,48},{16,56},{24,0},{32,8},{40,16},{48,24},{56,32},{64,10... | collective-permute-start | bytes 306440 | tf_op jit(solution)/shard_map/ppermute | solution.py:22
  119.6 10.5 %collective-permute-start.13 = (f32[2,112,114]{2,1,0:T(8,128)S(1)}, f32[2,112,114]{2,1,0:T(8,128)S(1)}, u32[]{:S(2)}, u32[]{:S(2)}) collective-permute-start(f32[2,112,114]{2,1,0:T(8,128)S(1)} %concatenate.31), channel_id=1, source_target_pairs={{0,32},{8,40},{16,48},{24,56},{32,0},{40,8},{48,16},{56,24},{64,96... | collective-permute-start | bytes 306440 | tf_op jit(solution)/shard_map/ppermute | solution.py:22
  121.2 7.8 %collective-permute-start.12 = (f32[2,112,114]{2,1,0:T(8,128)S(1)}, f32[2,112,114]{2,1,0:T(8,128)S(1)}, u32[]{:S(2)}, u32[]{:S(2)}) collective-permute-start(f32[2,112,114]{2,1,0:T(8,128)S(1)} %concatenate.31), channel_id=1, source_target_pairs={{0,24},{8,32},{16,40},{24,48},{32,56},{40,0},{48,8},{56,16},{64,88... | collective-permute-start | bytes 306440 | tf_op jit(solution)/shard_map/ppermute | solution.py:22
  125.4 18.7 %copy-start.10 = (bf16[1024,2,112]{0,2,1:T(8,128)(2,1)S(1)}, bf16[1024,2,112]{0,2,1:T(8,128)(2,1)}, u32[]{:S(2)}) copy-start(bf16[1024,2,112]{0,2,1:T(8,128)(2,1)} %copy-done.9) | copy-start | bytes 1376260
  125.4 18.6 %copy-start.12 = (bf16[2,112,113]{2,1,0:T(8,128)(2,1)S(1)}, bf16[2,112,113]{2,1,0:T(8,128)(2,1)}, u32[]{:S(2)}) copy-start(bf16[2,112,113]{2,1,0:T(8,128)(2,1)} %copy-done.11) | copy-start | bytes 151876
  125.4 18.6 %copy-start.14 = (bf16[1024,2,1]{0,2,1:T(2,128)(2,1)S(1)}, bf16[1024,2,1]{0,2,1:T(2,128)(2,1)}, u32[]{:S(2)}) copy-start(bf16[1024,2,1]{0,2,1:T(2,128)(2,1)} %copy-done.13) | copy-start | bytes 12292
  139.8 13.2 %collective-permute-start.19 = (f32[2,2,112,114]{3,2,1,0:T(8,128)S(1)}, f32[2,2,112,114]{3,2,1,0:T(8,128)}, u32[]{:S(2)}, u32[]{:S(2)}) collective-permute-start(f32[2,2,112,114]{3,2,1,0:T(8,128)S(1)} %pad_maximum_fusion.4), channel_id=1, source_target_pairs={{0,192},{8,200},{16,208},{24,216},{32,224},{40,232},{48,240},{56,2... | collective-permute-start | bytes 612872 | tf_op jit(solution)/shard_map/ppermute | solution.py:32
  139.9 15.0 %collective-permute-start.18 = (f32[2,2,112,114]{3,2,1,0:T(8,128)S(1)}, f32[2,2,112,114]{3,2,1,0:T(8,128)}, u32[]{:S(2)}, u32[]{:S(2)}) collective-permute-start(f32[2,2,112,114]{3,2,1,0:T(8,128)S(1)} %pad_maximum_fusion.4), channel_id=1, source_target_pairs={{0,128},{8,136},{16,144},{24,152},{32,160},{40,168},{48,176},{56,1... | collective-permute-start | bytes 612872 | tf_op jit(solution)/shard_map/ppermute | solution.py:32
  142.1 14.8 %collective-permute-start.17 = (f32[2,2,112,114]{3,2,1,0:T(8,128)S(1)}, f32[2,2,112,114]{3,2,1,0:T(8,128)}, u32[]{:S(2)}, u32[]{:S(2)}) collective-permute-start(f32[2,2,112,114]{3,2,1,0:T(8,128)S(1)} %pad_maximum_fusion.4), channel_id=1, source_target_pairs={{0,64},{8,72},{16,80},{24,88},{32,96},{40,104},{48,112},{56,120},{... | collective-permute-start | bytes 612872 | tf_op jit(solution)/shard_map/ppermute | solution.py:32
  144.4 16.0 %copy-start.1 = (bf16[1024,2,112]{0,2,1:T(8,128)(2,1)S(1)}, bf16[1024,2,112]{0,2,1:T(8,128)(2,1)}, u32[]{:S(2)}) copy-start(bf16[1024,2,112]{0,2,1:T(8,128)(2,1)} %copy-done) | copy-start | bytes 1376260
  (5 other events, 7.0 us)

commit v4 on v3

--- a/solution.py
+++ b/solution.py
@@ -74,16 +74,22 @@
     heads = width // DH
     tokens = rows * groups
 
-    stacked = jnp.stack([query_input, key_input, value_input, cotangent])
-    outgoing = stacked.reshape(4, rows, groups, width).transpose(2, 0, 1, 3)
-    incoming = lax.all_to_all(outgoing, "inner", 0, 0, tiled=True)
-    arrived = incoming.transpose(1, 0, 2, 3).reshape(4, tokens, heads, DH)
-    query_heads, key_heads, value_heads, cotangent_heads = (
-        arrived[0],
-        arrived[1],
-        arrived[2],
-        arrived[3],
-    )
+    def to_heads(arrays):
+        count = len(arrays)
+        outgoing = jnp.stack(arrays).reshape(count, rows, groups, width).transpose(2, 0, 1, 3)
+        incoming = lax.all_to_all(outgoing, "inner", 0, 0, tiled=True)
+        arrived = incoming.transpose(1, 0, 2, 3).reshape(count, tokens, heads, DH)
+        return [arrived[i] for i in range(count)]
+
+    def to_rows(arrays):
+        count = len(arrays)
+        leaving = jnp.stack(arrays).reshape(count, groups, rows, width).transpose(1, 0, 2, 3)
+        returned = lax.all_to_all(leaving, "inner", 0, 0, tiled=True)
+        merged = returned.transpose(1, 2, 0, 3).reshape(count, rows, columns)
+        return [merged[i] for i in range(count)]
+
+    key_heads, value_heads = to_heads([key_input, value_input])
+    query_heads, cotangent_heads = to_heads([query_input, cotangent])
 
     feat_query = jnp.maximum(query_heads, 0)
     feat_key = jnp.maximum(key_heads, 0)
@@ -106,20 +112,18 @@
     adjoint_part = jnp.einsum(
         "thk,thv->hkv", feat_query, back_aug, preferred_element_type=jnp.float32
     )
+    query_feat = jnp.einsum("thv,hkv->thk", back_aug, state_vis, preferred_element_type=jnp.float32)
+    query_back = jnp.where(query_heads > 0, query_feat, 0.0).astype(jnp.bfloat16)
     adjoint_vis = visible(adjoint_part, label, True)
-    query_feat = jnp.einsum("thv,hkv->thk", back_aug, state_vis, preferred_element_type=jnp.float32)
     key_feat = jnp.einsum("thv,hkv->thk", value_aug, adjoint_vis, preferred_element_type=jnp.float32)
     value_back = jnp.einsum(
         "thk,hkv->thv", feat_key, adjoint_vis[..., :DH], preferred_element_type=jnp.float32
     )
-    query_back = jnp.where(query_heads > 0, query_feat, 0.0).astype(jnp.bfloat16)
     key_back = jnp.where(key_heads > 0, key_feat, 0.0).astype(jnp.bfloat16)
 
-    results = jnp.stack([query_back, key_back, value_back.astype(jnp.bfloat16)])
-    leaving = results.reshape(3, groups, rows, width).transpose(1, 0, 2, 3)
-    returned = lax.all_to_all(leaving, "inner", 0, 0, tiled=True)
-    merged = returned.transpose(1, 2, 0, 3).reshape(3, rows, columns)
-    return merged[0], merged[1], merged[2]
+    (query_out,) = to_rows([query_back])
+    key_out, value_out = to_rows([key_back, value_back.astype(jnp.bfloat16)])
+    return query_out, key_out, value_out
 
 
 def solution(mesh):

time: 204 us -> 198 us (0.971)
  the two profiles are of different devices: /device:TPU:25 before, /device:TPU:2 now
where the time goes in v4:
time: 198 us; the launch traced here: 195 us
  waiting for transfers between devices  68.4 us (35%)
  starting transfers between devices  45.9 us (23%)
  local copies, waits for them, and re-layouts  39.4 us (20%)
  between operations  31.7 us (16%)
  other arithmetic  7.92 us (4%)
    all_to_all x2, waiting for transfers between devices, to_heads(): incoming = lax.all_to_all(outgoing, 'inner', 0, 0, tiled=True)  38.6 us
    all_to_all x2, waiting for transfers between devices, to_rows(): returned = lax.all_to_all(leaving, 'inner', 0, 0, tiled=True)  25 us
    ppermute x14, starting transfers between devices, shifted(): return lax.ppermute(value, 'tm', pairs)  15.5 us
    all_to_all x2, starting transfers between devices, to_heads(): incoming = lax.all_to_all(outgoing, 'inner', 0, 0, tiled=True)  12.1 us
    slice x14, local copies, waits for them, and re-layouts, visible(): labels = [f[0, 0, DH + 1] for f in frames]  12.1 us
    all_to_all x2, starting transfers between devices, to_rows(): returned = lax.all_to_all(leaving, 'inner', 0, 0, tiled=True)  9.56 us
    unnamed x33, local copies, waits for them, and re-layouts  8.73 us
    ppermute x6, starting transfers between devices, strided(): return lax.ppermute(value, 'tm', pairs)  8.65 us
  transfers between devices with their start and end apart: 24, of which 6 were waited for; matrix products, arithmetic and copies ran while one was open for 16% of the time, Pallas kernels for 0%

profile of v4, /device:TPU:2, one launch (start us, length us, event | category | flops | bytes accessed | tf_op | source)
XLA Modules:
  0.0 195.0 jit_solution(3787358399831300317)
XLA Ops:
  0.6 1.3 copy.37
  3.3 8.6 %all-to-all-start.1 = ((bf16[8,2,128,224]{2,3,1,0:T(8,128)(2,1)}), bf16[8,2,128,224]{2,3,1,0:T(8,128)(2,1)S(1)}, u32[]{:S(2)}, u32[]{:S(2)}) async-start(bf16[8,2,128,224]{2,3,1,0:T(8,128)(2,1)} %copy.39), calls=%async_computation.1 | async-start | bytes 1835008 | tf_op jit(solution)/shard_map/all_to_all | solution.py:80
  14.3 23.5 %all-to-all-done.1 = bf16[8,2,128,224]{2,3,1,0:T(8,128)(2,1)S(1)} async-done(((bf16[8,2,128,224]{2,3,1,0:T(8,128)(2,1)}), bf16[8,2,128,224]{2,3,1,0:T(8,128)(2,1)S(1)}, u32[]{:S(2)}, u32[]{:S(2)}) %all-to-all-start.1) | async-done | bytes 917536 | tf_op jit(solution)/shard_map/all_to_all | solution.py:80
  37.8 3.6 %all-to-all-start = ((bf16[8,2,128,224]{2,3,1,0:T(8,128)(2,1)}), bf16[8,2,128,224]{2,3,1,0:T(8,128)(2,1)S(1)}, u32[]{:S(2)}, u32[]{:S(2)}) async-start(bf16[8,2,128,224]{2,3,1,0:T(8,128)(2,1)} %copy.35), calls=%async_computation | async-start | bytes 1835008 | tf_op jit(solution)/shard_map/all_to_all | solution.py:80
  44.3 1.5 collective-permute-start.1
  45.8 1.7 collective-permute-start.6
  47.5 1.8 collective-permute-start.5
  50.2 2.5 %collective-permute-start.3 = (f32[2,112,114]{2,1,0:T(8,128)}, f32[2,112,114]{2,1,0:T(8,128)}, u32[]{:S(2)}, u32[]{:S(2)}) collective-permute-start(f32[2,112,114]{2,1,0:T(8,128)} %concatenate.28), channel_id=1, source_target_pairs={{0,32},{8,40},{16,48},{24,56},{32,0},{40,8},{48,16},{56,24},{64,96... | collective-permute-start | bytes 306440 | tf_op jit(solution)/shard_map/ppermute | solution.py:22
  52.6 15.1 %all-to-all-done = bf16[8,2,128,224]{2,3,1,0:T(8,128)(2,1)S(1)} async-done(((bf16[8,2,128,224]{2,3,1,0:T(8,128)(2,1)}), bf16[8,2,128,224]{2,3,1,0:T(8,128)(2,1)S(1)}, u32[]{:S(2)}, u32[]{:S(2)}) %all-to-all-start) | async-done | bytes 917536 | tf_op jit(solution)/shard_map/all_to_all | solution.py:80
  67.8 1.5 copy.42
  69.2 1.3 mul.22
  72.9 1.3 slice.239
  74.9 1.3 slice.241
  77.0 1.3 slice.243
  78.9 1.3 slice.245
  80.9 1.3 slice.247
  90.5 3.0 %collective-permute-start.9 = (f32[2,2,112,114]{3,2,1,0:T(8,128)}, f32[2,2,112,114]{3,2,1,0:T(8,128)}, u32[]{:S(2)}, u32[]{:S(2)}) collective-permute-start(f32[2,2,112,114]{3,2,1,0:T(8,128)} %pad_maximum_fusion.3), channel_id=1, source_target_pairs={{0,192},{8,200},{16,208},{24,216},{32,224},{40,232},{48,240},{56,2... | collective-permute-start | bytes 612872 | tf_op jit(solution)/shard_map/ppermute | solution.py:32
  96.1 2.0 %max.36 = bf16[1024,2,112]{0,2,1:T(8,128)(2,1)} reshape(bf16[1,8,128,224]{2,1,3,0:T(8,128)(2,1)} %copy.43) | data formatting | bytes 917504 | tf_op jit(solution)/shard_map/max | solution.py:94
  104.5 1.3 slice.253
  106.4 1.3 slice.250
  108.4 1.5 fusion.25
  111.6 1.6 collective-permute-start.11
  113.3 1.8 collective-permute-start.16
  115.0 1.7 collective-permute-start.15
  116.8 2.9 %collective-permute-start.13 = (f32[2,112,114]{2,1,0:T(8,128)S(1)}, f32[2,112,114]{2,1,0:T(8,128)S(1)}, u32[]{:S(2)}, u32[]{:S(2)}) collective-permute-start(f32[2,112,114]{2,1,0:T(8,128)S(1)} %concatenate.32), channel_id=1, source_target_pairs={{0,32},{8,40},{16,48},{24,56},{32,0},{40,8},{48,16},{56,24},{64,96... | collective-permute-start | bytes 306440 | tf_op jit(solution)/shard_map/ppermute | solution.py:22
  123.1 3.9 %collective-permute-done.12 = f32[2,112,114]{2,1,0:T(8,128)S(1)} collective-permute-done((f32[2,112,114]{2,1,0:T(8,128)S(1)}, f32[2,112,114]{2,1,0:T(8,128)S(1)}, u32[]{:S(2)}, u32[]{:S(2)}) %collective-permute-start.12) | collective-permute-done | bytes 102176 | tf_op jit(solution)/shard_map/ppermute | solution.py:22
  137.8 2.8 %collective-permute-start.19 = (f32[2,2,112,114]{3,2,1,0:T(8,128)S(1)}, f32[2,2,112,114]{3,2,1,0:T(8,128)}, u32[]{:S(2)}, u32[]{:S(2)}) collective-permute-start(f32[2,2,112,114]{3,2,1,0:T(8,128)S(1)} %pad_maximum_fusion.4), channel_id=1, source_target_pairs={{0,192},{8,200},{16,208},{24,216},{32,224},{40,232},{48,240},{56,2... | collective-permute-start | bytes 612872 | tf_op jit(solution)/shard_map/ppermute | solution.py:32
  143.1 3.5 %all-to-all-start.2 = ((bf16[8,1,128,224]{2,3,1,0:T(8,128)(2,1)}), bf16[8,1,128,224]{2,3,1,0:T(8,128)(2,1)S(1)}, u32[]{:S(2)}, u32[]{:S(2)}) async-start(bf16[8,1,128,224]{2,3,1,0:T(8,128)(2,1)} %copy.44), calls=%async_computation.2 | async-start | bytes 917504 | tf_op jit(solution)/shard_map/all_to_all | solution.py:87
  152.9 1.3 slice.279
  156.7 1.3 fusion.12
  162.1 6.0 %all-to-all-start.3 = ((bf16[8,2,128,224]{2,3,1,0:T(8,128)(2,1)}), bf16[8,2,128,224]{2,3,1,0:T(8,128)(2,1)S(1)}, u32[]{:S(2)}, u32[]{:S(2)}) async-start(bf16[8,2,128,224]{2,3,1,0:T(8,128)(2,1)} %maximum_bitcast_fusion.2), calls=%async_computation.3 | async-start | bytes 1835008 | tf_op jit(solution)/shard_map/all_to_all | solution.py:87
  169.1 23.8 %all-to-all-done.3 = bf16[8,2,128,224]{2,3,1,0:T(8,128)(2,1)S(1)} async-done(((bf16[8,2,128,224]{2,3,1,0:T(8,128)(2,1)}), bf16[8,2,128,224]{2,3,1,0:T(8,128)(2,1)S(1)}, u32[]{:S(2)}, u32[]{:S(2)}) %all-to-all-start.3) | async-done | bytes 917536 | tf_op jit(solution)/shard_map/all_to_all | solution.py:87
  (119 shorter events, 34.7 us)
Async XLA Ops:
  0.6 1.3 copy-start.3
  3.3 8.6 %copy-start.4 = (bf16[128,1792]{1,0:T(8,128)(2,1)S(1)}, bf16[128,1792]{1,0:T(8,128)(2,1)}, u32[]{:S(2)}) copy-start(bf16[128,1792]{1,0:T(8,128)(2,1)} %param.5) | copy-start | bytes 1376260
  3.3 34.5 %all-to-all-start.1 = ((bf16[8,2,128,224]{2,3,1,0:T(8,128)(2,1)}), bf16[8,2,128,224]{2,3,1,0:T(8,128)(2,1)S(1)}, u32[]{:S(2)}, u32[]{:S(2)}) async-start(bf16[8,2,128,224]{2,3,1,0:T(8,128)(2,1)} %copy.39), calls=%async_computation.1 | async-start | bytes 1835008 | tf_op jit(solution)/shard_map/all_to_all | solution.py:80
  11.9 1.0 copy-start.5
  37.8 29.9 %all-to-all-start = ((bf16[8,2,128,224]{2,3,1,0:T(8,128)(2,1)}), bf16[8,2,128,224]{2,3,1,0:T(8,128)(2,1)S(1)}, u32[]{:S(2)}, u32[]{:S(2)}) async-start(bf16[8,2,128,224]{2,3,1,0:T(8,128)(2,1)} %copy.35), calls=%async_computation | async-start | bytes 1835008 | tf_op jit(solution)/shard_map/all_to_all | solution.py:80
  42.6 0.8 copy-start
  44.3 5.9 %collective-permute-start.1 = (f32[2,112,114]{2,1,0:T(8,128)}, f32[2,112,114]{2,1,0:T(8,128)S(1)}, u32[]{:S(2)}, u32[]{:S(2)}) collective-permute-start(f32[2,112,114]{2,1,0:T(8,128)} %concatenate.28), channel_id=1, source_target_pairs={{0,16},{8,24},{16,32},{24,40},{32,48},{40,56},{48,0},{56,8},{64,80... | collective-permute-start | bytes 306440 | tf_op jit(solution)/shard_map/ppermute | solution.py:22
  45.8 6.9 %collective-permute-start = (f32[2,112,114]{2,1,0:T(8,128)}, f32[2,112,114]{2,1,0:T(8,128)S(1)}, u32[]{:S(2)}, u32[]{:S(2)}) collective-permute-start(f32[2,112,114]{2,1,0:T(8,128)} %concatenate.28), channel_id=1, source_target_pairs={{0,8},{8,16},{16,24},{24,32},{32,40},{40,48},{48,56},{56,0},{64,72... | collective-permute-start | bytes 306440 | tf_op jit(solution)/shard_map/ppermute | solution.py:22
  45.8 35.1 %collective-permute-start.6 = (f32[2,112,114]{2,1,0:T(8,128)}, f32[2,112,114]{2,1,0:T(8,128)}, u32[]{:S(2)}, u32[]{:S(2)}) collective-permute-start(f32[2,112,114]{2,1,0:T(8,128)} %concatenate.28), channel_id=1, source_target_pairs={{0,56},{8,0},{16,8},{24,16},{32,24},{40,32},{48,40},{56,48},{64,12... | collective-permute-start | bytes 306440 | tf_op jit(solution)/shard_map/ppermute | solution.py:22
  47.5 31.4 %collective-permute-start.5 = (f32[2,112,114]{2,1,0:T(8,128)}, f32[2,112,114]{2,1,0:T(8,128)}, u32[]{:S(2)}, u32[]{:S(2)}) collective-permute-start(f32[2,112,114]{2,1,0:T(8,128)} %concatenate.28), channel_id=1, source_target_pairs={{0,48},{8,56},{16,0},{24,8},{32,16},{40,24},{48,32},{56,40},{64,11... | collective-permute-start | bytes 306440 | tf_op jit(solution)/shard_map/ppermute | solution.py:22
  49.3 27.7 %collective-permute-start.4 = (f32[2,112,114]{2,1,0:T(8,128)}, f32[2,112,114]{2,1,0:T(8,128)}, u32[]{:S(2)}, u32[]{:S(2)}) collective-permute-start(f32[2,112,114]{2,1,0:T(8,128)} %concatenate.28), channel_id=1, source_target_pairs={{0,40},{8,48},{16,56},{24,0},{32,8},{40,16},{48,24},{56,32},{64,10... | collective-permute-start | bytes 306440 | tf_op jit(solution)/shard_map/ppermute | solution.py:22
  50.2 24.8 %collective-permute-start.3 = (f32[2,112,114]{2,1,0:T(8,128)}, f32[2,112,114]{2,1,0:T(8,128)}, u32[]{:S(2)}, u32[]{:S(2)}) collective-permute-start(f32[2,112,114]{2,1,0:T(8,128)} %concatenate.28), channel_id=1, source_target_pairs={{0,32},{8,40},{16,48},{24,56},{32,0},{40,8},{48,16},{56,24},{64,96... | collective-permute-start | bytes 306440 | tf_op jit(solution)/shard_map/ppermute | solution.py:22
  52.6 20.3 %collective-permute-start.2 = (f32[2,112,114]{2,1,0:T(8,128)}, f32[2,112,114]{2,1,0:T(8,128)}, u32[]{:S(2)}, u32[]{:S(2)}) collective-permute-start(f32[2,112,114]{2,1,0:T(8,128)} %concatenate.28), channel_id=1, source_target_pairs={{0,24},{8,32},{16,40},{24,48},{32,56},{40,0},{48,8},{56,16},{64,88... | collective-permute-start | bytes 306440 | tf_op jit(solution)/shard_map/ppermute | solution.py:22
  90.5 12.1 %collective-permute-start.9 = (f32[2,2,112,114]{3,2,1,0:T(8,128)}, f32[2,2,112,114]{3,2,1,0:T(8,128)}, u32[]{:S(2)}, u32[]{:S(2)}) collective-permute-start(f32[2,2,112,114]{3,2,1,0:T(8,128)} %pad_maximum_fusion.3), channel_id=1, source_target_pairs={{0,192},{8,200},{16,208},{24,216},{32,224},{40,232},{48,240},{56,2... | collective-permute-start | bytes 612872 | tf_op jit(solution)/shard_map/ppermute | solution.py:32
  93.5 11.0 %collective-permute-start.8 = (f32[2,2,112,114]{3,2,1,0:T(8,128)}, f32[2,2,112,114]{3,2,1,0:T(8,128)}, u32[]{:S(2)}, u32[]{:S(2)}) collective-permute-start(f32[2,2,112,114]{3,2,1,0:T(8,128)} %pad_maximum_fusion.3), channel_id=1, source_target_pairs={{0,128},{8,136},{16,144},{24,152},{32,160},{40,168},{48,176},{56,1... | collective-permute-start | bytes 612872 | tf_op jit(solution)/shard_map/ppermute | solution.py:32
  94.2 12.3 %collective-permute-start.7 = (f32[2,2,112,114]{3,2,1,0:T(8,128)}, f32[2,2,112,114]{3,2,1,0:T(8,128)}, u32[]{:S(2)}, u32[]{:S(2)}) collective-permute-start(f32[2,2,112,114]{3,2,1,0:T(8,128)} %pad_maximum_fusion.3), channel_id=1, source_target_pairs={{0,64},{8,72},{16,80},{24,88},{32,96},{40,104},{48,112},{56,120},{... | collective-permute-start | bytes 612872 | tf_op jit(solution)/shard_map/ppermute | solution.py:32
  108.4 1.5 copy-start.2
  111.6 5.2 %collective-permute-start.11 = (f32[2,112,114]{2,1,0:T(8,128)S(1)}, f32[2,112,114]{2,1,0:T(8,128)S(1)}, u32[]{:S(2)}, u32[]{:S(2)}) collective-permute-start(f32[2,112,114]{2,1,0:T(8,128)S(1)} %concatenate.32), channel_id=1, source_target_pairs={{0,16},{8,24},{16,32},{24,40},{32,48},{40,56},{48,0},{56,8},{64,80... | collective-permute-start | bytes 306440 | tf_op jit(solution)/shard_map/ppermute | solution.py:22
  113.1 6.6 %collective-permute-start.10 = (f32[2,112,114]{2,1,0:T(8,128)S(1)}, f32[2,112,114]{2,1,0:T(8,128)S(1)}, u32[]{:S(2)}, u32[]{:S(2)}) collective-permute-start(f32[2,112,114]{2,1,0:T(8,128)S(1)} %concatenate.32), channel_id=1, source_target_pairs={{0,8},{8,16},{16,24},{24,32},{32,40},{40,48},{48,56},{56,0},{64,72... | collective-permute-start | bytes 306440 | tf_op jit(solution)/shard_map/ppermute | solution.py:22
  113.3 18.7 %collective-permute-start.16 = (f32[2,112,114]{2,1,0:T(8,128)S(1)}, f32[2,112,114]{2,1,0:T(8,128)S(1)}, u32[]{:S(2)}, u32[]{:S(2)}) collective-permute-start(f32[2,112,114]{2,1,0:T(8,128)S(1)} %concatenate.32), channel_id=1, source_target_pairs={{0,56},{8,0},{16,8},{24,16},{32,24},{40,32},{48,40},{56,48},{64,12... | collective-permute-start | bytes 306440 | tf_op jit(solution)/shard_map/ppermute | solution.py:22
  115.0 15.7 %collective-permute-start.15 = (f32[2,112,114]{2,1,0:T(8,128)S(1)}, f32[2,112,114]{2,1,0:T(8,128)S(1)}, u32[]{:S(2)}, u32[]{:S(2)}) collective-permute-start(f32[2,112,114]{2,1,0:T(8,128)S(1)} %concatenate.32), channel_id=1, source_target_pairs={{0,48},{8,56},{16,0},{24,8},{32,16},{40,24},{48,32},{56,40},{64,11... | collective-permute-start | bytes 306440 | tf_op jit(solution)/shard_map/ppermute | solution.py:22
  116.8 12.6 %collective-permute-start.14 = (f32[2,112,114]{2,1,0:T(8,128)S(1)}, f32[2,112,114]{2,1,0:T(8,128)S(1)}, u32[]{:S(2)}, u32[]{:S(2)}) collective-permute-start(f32[2,112,114]{2,1,0:T(8,128)S(1)} %concatenate.32), channel_id=1, source_target_pairs={{0,40},{8,48},{16,56},{24,0},{32,8},{40,16},{48,24},{56,32},{64,10... | collective-permute-start | bytes 306440 | tf_op jit(solution)/shard_map/ppermute | solution.py:22
  116.8 11.5 %collective-permute-start.13 = (f32[2,112,114]{2,1,0:T(8,128)S(1)}, f32[2,112,114]{2,1,0:T(8,128)S(1)}, u32[]{:S(2)}, u32[]{:S(2)}) collective-permute-start(f32[2,112,114]{2,1,0:T(8,128)S(1)} %concatenate.32), channel_id=1, source_target_pairs={{0,32},{8,40},{16,48},{24,56},{32,0},{40,8},{48,16},{56,24},{64,96... | collective-permute-start | bytes 306440 | tf_op jit(solution)/shard_map/ppermute | solution.py:22
  119.7 7.3 %collective-permute-start.12 = (f32[2,112,114]{2,1,0:T(8,128)S(1)}, f32[2,112,114]{2,1,0:T(8,128)S(1)}, u32[]{:S(2)}, u32[]{:S(2)}) collective-permute-start(f32[2,112,114]{2,1,0:T(8,128)S(1)} %concatenate.32), channel_id=1, source_target_pairs={{0,24},{8,32},{16,40},{24,48},{32,56},{40,0},{48,8},{56,16},{64,88... | collective-permute-start | bytes 306440 | tf_op jit(solution)/shard_map/ppermute | solution.py:22
  137.8 4.1 %copy-start.7 = (bf16[1024,2,112]{0,2,1:T(8,128)(2,1)S(1)}, bf16[1024,2,112]{0,2,1:T(8,128)(2,1)}, u32[]{:S(2)}) copy-start(bf16[1024,2,112]{0,2,1:T(8,128)(2,1)} %copy-done.6) | copy-start | bytes 1376260
  137.8 4.1 %copy-start.9 = (bf16[2,112,113]{2,1,0:T(8,128)(2,1)S(1)}, bf16[2,112,113]{2,1,0:T(8,128)(2,1)}, u32[]{:S(2)}) copy-start(bf16[2,112,113]{2,1,0:T(8,128)(2,1)} %copy-done.8) | copy-start | bytes 151876
  137.8 13.1 %collective-permute-start.19 = (f32[2,2,112,114]{3,2,1,0:T(8,128)S(1)}, f32[2,2,112,114]{3,2,1,0:T(8,128)}, u32[]{:S(2)}, u32[]{:S(2)}) collective-permute-start(f32[2,2,112,114]{3,2,1,0:T(8,128)S(1)} %pad_maximum_fusion.4), channel_id=1, source_target_pairs={{0,192},{8,200},{16,208},{24,216},{32,224},{40,232},{48,240},{56,2... | collective-permute-start | bytes 612872 | tf_op jit(solution)/shard_map/ppermute | solution.py:32
  140.6 12.2 %collective-permute-start.18 = (f32[2,2,112,114]{3,2,1,0:T(8,128)S(1)}, f32[2,2,112,114]{3,2,1,0:T(8,128)}, u32[]{:S(2)}, u32[]{:S(2)}) collective-permute-start(f32[2,2,112,114]{3,2,1,0:T(8,128)S(1)} %pad_maximum_fusion.4), channel_id=1, source_target_pairs={{0,128},{8,136},{16,144},{24,152},{32,160},{40,168},{48,176},{56,1... | collective-permute-start | bytes 612872 | tf_op jit(solution)/shard_map/ppermute | solution.py:32
  141.9 12.9 %collective-permute-start.17 = (f32[2,2,112,114]{3,2,1,0:T(8,128)S(1)}, f32[2,2,112,114]{3,2,1,0:T(8,128)}, u32[]{:S(2)}, u32[]{:S(2)}) collective-permute-start(f32[2,2,112,114]{3,2,1,0:T(8,128)S(1)} %pad_maximum_fusion.4), channel_id=1, source_target_pairs={{0,64},{8,72},{16,80},{24,88},{32,96},{40,104},{48,112},{56,120},{... | collective-permute-start | bytes 612872 | tf_op jit(solution)/shard_map/ppermute | solution.py:32
  143.1 19.0 %all-to-all-start.2 = ((bf16[8,1,128,224]{2,3,1,0:T(8,128)(2,1)}), bf16[8,1,128,224]{2,3,1,0:T(8,128)(2,1)S(1)}, u32[]{:S(2)}, u32[]{:S(2)}) async-start(bf16[8,1,128,224]{2,3,1,0:T(8,128)(2,1)} %copy.44), calls=%async_computation.2 | async-start | bytes 917504 | tf_op jit(solution)/shard_map/all_to_all | solution.py:87
  158.4 1.0 copy-start.1
  162.1 30.8 %all-to-all-start.3 = ((bf16[8,2,128,224]{2,3,1,0:T(8,128)(2,1)}), bf16[8,2,128,224]{2,3,1,0:T(8,128)(2,1)S(1)}, u32[]{:S(2)}, u32[]{:S(2)}) async-start(bf16[8,2,128,224]{2,3,1,0:T(8,128)(2,1)} %maximum_bitcast_fusion.2), calls=%async_computation.3 | async-start | bytes 1835008 | tf_op jit(solution)/shard_map/all_to_all | solution.py:87
  (3 other events, 2.1 us)

commit v5 on v4

--- a/solution.py
+++ b/solution.py
@@ -38,33 +38,28 @@
     rows = total // row
     me = lax.axis_index("tm") // row
     flabel = label.astype(jnp.float32)
-    tag = jnp.broadcast_to(flabel, part.shape[:-1] + (1,))
-    packed = jnp.concatenate([part, tag], axis=-1)
+    lanes = 128
+    spare = jnp.zeros(part.shape[:-1] + (lanes - DH - 1,), jnp.float32)
+    lane = lax.broadcasted_iota(jnp.int32, part.shape[:-1] + (lanes,), 2)
+    is_tag = lane == DH + 1
+    packed = jnp.where(is_tag, flabel, jnp.concatenate([part, spare], axis=-1))
     frames = [packed] + [shifted(packed, row, s) for s in range(1, row)]
     labels = [f[0, 0, DH + 1] for f in frames]
-    states = [f[..., : DH + 1] for f in frames]
     keep = [(l >= flabel) if later else (l <= flabel) for l in labels]
-    seen = sum(jnp.where(k, s, 0.0) for k, s in zip(keep, states))
+    seen = sum(jnp.where(k, f, 0.0) for k, f in zip(keep, frames))
     if rows > 1:
         edge = functools.reduce(jnp.maximum, labels) if later else functools.reduce(jnp.minimum, labels)
-        whole = sum(states)
-        edge_sum = sum(jnp.where(l == edge, s, 0.0) for l, s in zip(labels, states))
-        etag = jnp.broadcast_to(edge, part.shape[:-1] + (1,))
-        summary = jnp.stack(
-            [jnp.concatenate([whole, etag], -1), jnp.concatenate([edge_sum, etag], -1)]
-        )
+        whole = jnp.where(is_tag, edge, sum(frames))
+        edge_sum = jnp.where(is_tag, edge, sum(jnp.where(l == edge, f, 0.0) for l, f in zip(labels, frames)))
+        summary = jnp.stack([whole, edge_sum])
         for s in range(1, rows):
             got = strided(summary, row, s)
             source = (me - s) % rows
             their_edge = got[1, 0, 0, DH + 1]
             full = (source > me) if later else (source < me)
             part_only = ((source < me) if later else (source > me)) & (their_edge == flabel)
-            seen = (
-                seen
-                + jnp.where(full, got[0, ..., : DH + 1], 0.0)
-                + jnp.where(part_only, got[1, ..., : DH + 1], 0.0)
-            )
-    return seen.astype(jnp.bfloat16)
+            seen = seen + jnp.where(full, got[0], 0.0) + jnp.where(part_only, got[1], 0.0)
+    return seen[..., : DH + 1].astype(jnp.bfloat16)
 
 
 def local(query_input, key_input, value_input, cotangent, span_labels):

time: 198 us -> 201 us (1.015)
  waiting for transfers between devices: 68.4 us -> 62.7 us
  between operations: 31.7 us -> 35.2 us
  starting transfers between devices: 45.9 us -> 48.1 us
    ppermute x14, waiting for transfers between devices: 4.84 us -> 0.04 us  [shifted(): return lax.ppermute(value, 'tm', pairs)]
    ppermute x14, starting transfers between devices: 15.5 us -> 19.3 us  [shifted(): return lax.ppermute(value, 'tm', pairs)]
    select_n x0 -> x5, other arithmetic: none -> 3.53 us  [the longest x2 1.95 us: visible(): jnp.where(full, got[0], 0.0)]
    convert_element_type x2 -> x0, other arithmetic: 2.83 us -> none  [visible(): return seen.astype(jnp.bfloat16)]
    another operation x2 -> x6, other arithmetic: 0.75 us -> 2.92 us  [the longest x4 2.74 us: visible(): summary = jnp.stack([whole, edge_sum])]
    slice x14 -> x16, local copies, waits for them, and re-layouts: 12.1 us -> 13.8 us  [visible(): labels = [f[0, 0, DH + 1] for f in frames]]
    unnamed x33 -> x37, local copies, waits for them, and re-layouts: 8.73 us -> 9.46 us
  transfers between devices with their start and end apart: 24 -> 24, of which waited for: 6 -> 4; matrix products, arithmetic and copies ran while one was open for 16% -> 16% of each run, Pallas kernels for 0% -> 0%
where the time goes in v5:
time: 201 us; the launch traced here: 197 us
  waiting for transfers between devices  62.7 us (31%)
  starting transfers between devices  48.1 us (24%)
  local copies, waits for them, and re-layouts  39.8 us (20%)
  between operations  35.2 us (18%)
  other arithmetic  9.59 us (5%)
    all_to_all x2, waiting for transfers between devices, to_heads(): incoming = lax.all_to_all(outgoing, 'inner', 0, 0, tiled=True)  37.4 us
    all_to_all x2, waiting for transfers between devices, to_rows(): returned = lax.all_to_all(leaving, 'inner', 0, 0, tiled=True)  25.2 us
    ppermute x14, starting transfers between devices, shifted(): return lax.ppermute(value, 'tm', pairs)  19.3 us
    slice x16, local copies, waits for them, and re-layouts, visible(): labels = [f[0, 0, DH + 1] for f in frames]  13.8 us
    all_to_all x2, starting transfers between devices, to_heads(): incoming = lax.all_to_all(outgoing, 'inner', 0, 0, tiled=True)  12.1 us
    unnamed x37, local copies, waits for them, and re-layouts  9.46 us
    ppermute x6, starting transfers between devices, strided(): return lax.ppermute(value, 'tm', pairs)  8.51 us
    all_to_all x2, starting transfers between devices, to_rows(): returned = lax.all_to_all(leaving, 'inner', 0, 0, tiled=True)  8.12 us
  transfers between devices with their start and end apart: 24, of which 4 were waited for; matrix products, arithmetic and copies ran while one was open for 16% of the time, Pallas kernels for 0%

profile of v5, /device:TPU:2, one launch (start us, length us, event | category | flops | bytes accessed | tf_op | source)
XLA Modules:
  0.0 197.1 jit_solution(10539152354121257928)
XLA Ops:
  0.6 1.3 copy.37
  3.3 8.6 %all-to-all-start.1 = ((bf16[8,2,128,224]{2,3,1,0:T(8,128)(2,1)}), bf16[8,2,128,224]{2,3,1,0:T(8,128)(2,1)S(1)}, u32[]{:S(2)}, u32[]{:S(2)}) async-start(bf16[8,2,128,224]{2,3,1,0:T(8,128)(2,1)} %copy.39), calls=%async_computation.1 | async-start | bytes 1835008 | tf_op jit(solution)/shard_map/all_to_all | solution.py:75
  14.3 23.5 %all-to-all-done.1 = bf16[8,2,128,224]{2,3,1,0:T(8,128)(2,1)S(1)} async-done(((bf16[8,2,128,224]{2,3,1,0:T(8,128)(2,1)}), bf16[8,2,128,224]{2,3,1,0:T(8,128)(2,1)S(1)}, u32[]{:S(2)}, u32[]{:S(2)}) %all-to-all-start.1) | async-done | bytes 917536 | tf_op jit(solution)/shard_map/all_to_all | solution.py:75
  37.8 3.6 %all-to-all-start = ((bf16[8,2,128,224]{2,3,1,0:T(8,128)(2,1)}), bf16[8,2,128,224]{2,3,1,0:T(8,128)(2,1)S(1)}, u32[]{:S(2)}, u32[]{:S(2)}) async-start(bf16[8,2,128,224]{2,3,1,0:T(8,128)(2,1)} %copy.35), calls=%async_computation | async-start | bytes 1835008 | tf_op jit(solution)/shard_map/all_to_all | solution.py:75
  44.3 1.5 collective-permute-start.1
  46.3 2.0 %collective-permute-start.4 = (f32[2,112,128]{2,1,0:T(8,128)}, f32[2,112,128]{2,1,0:T(8,128)}, u32[]{:S(2)}, u32[]{:S(2)}) collective-permute-start(f32[2,112,128]{2,1,0:T(8,128)} %pad_select_fusion.1), channel_id=1, source_target_pairs={{0,40},{8,48},{16,56},{24,0},{32,8},{40,16},{48,24},{56,32},{64,10... | collective-permute-start | bytes 344072 | tf_op jit(solution)/shard_map/ppermute | solution.py:22
  48.4 2.4 %collective-permute-start.3 = (f32[2,112,128]{2,1,0:T(8,128)}, f32[2,112,128]{2,1,0:T(8,128)}, u32[]{:S(2)}, u32[]{:S(2)}) collective-permute-start(f32[2,112,128]{2,1,0:T(8,128)} %pad_select_fusion.1), channel_id=1, source_target_pairs={{0,32},{8,40},{16,48},{24,56},{32,0},{40,8},{48,16},{56,24},{64,96... | collective-permute-start | bytes 344072 | tf_op jit(solution)/shard_map/ppermute | solution.py:22
  50.8 3.0 %collective-permute-start.6 = (f32[2,112,128]{2,1,0:T(8,128)}, f32[2,112,128]{2,1,0:T(8,128)}, u32[]{:S(2)}, u32[]{:S(2)}) collective-permute-start(f32[2,112,128]{2,1,0:T(8,128)} %pad_select_fusion.1), channel_id=1, source_target_pairs={{0,56},{8,0},{16,8},{24,16},{32,24},{40,32},{48,40},{56,48},{64,12... | collective-permute-start | bytes 344072 | tf_op jit(solution)/shard_map/ppermute | solution.py:22
  53.8 13.9 %all-to-all-done = bf16[8,2,128,224]{2,3,1,0:T(8,128)(2,1)S(1)} async-done(((bf16[8,2,128,224]{2,3,1,0:T(8,128)(2,1)}), bf16[8,2,128,224]{2,3,1,0:T(8,128)(2,1)S(1)}, u32[]{:S(2)}, u32[]{:S(2)}) %all-to-all-start) | async-done | bytes 917536 | tf_op jit(solution)/shard_map/all_to_all | solution.py:75
  67.8 1.3 slice.196
  69.7 1.5 copy.42
  71.1 1.3 mul.22
  75.8 1.2 slice.199
  77.6 1.3 slice.200
  79.5 1.3 slice.201
  81.3 1.3 slice.202
  83.2 1.3 slice.203
  92.0 3.0 %collective-permute-start.9 = (f32[2,2,112,128]{3,2,1,0:T(8,128)}, f32[2,2,112,128]{3,2,1,0:T(8,128)}, u32[]{:S(2)}, u32[]{:S(2)}) collective-permute-start(f32[2,2,112,128]{3,2,1,0:T(8,128)} %pad_maximum_fusion.3), channel_id=1, source_target_pairs={{0,192},{8,200},{16,208},{24,216},{32,224},{40,232},{48,240},{56,2... | collective-permute-start | bytes 688136 | tf_op jit(solution)/shard_map/ppermute | solution.py:32
  97.6 2.0 %max.36 = bf16[1024,2,112]{0,2,1:T(8,128)(2,1)} reshape(bf16[1,8,128,224]{2,1,3,0:T(8,128)(2,1)} %copy.43) | data formatting | bytes 917504 | tf_op jit(solution)/shard_map/max | solution.py:89
  104.0 1.3 slice.211
  105.9 1.3 slice.208
  107.8 1.3 slice.205
  112.6 1.3 fusion.30
  116.3 1.6 collective-permute-start.11
  118.8 2.0 %collective-permute-start.14 = (f32[2,112,128]{2,1,0:T(8,128)S(1)}, f32[2,112,128]{2,1,0:T(8,128)S(1)}, u32[]{:S(2)}, u32[]{:S(2)}) collective-permute-start(f32[2,112,128]{2,1,0:T(8,128)S(1)} %pad_select_fusion), channel_id=1, source_target_pairs={{0,40},{8,48},{16,56},{24,0},{32,8},{40,16},{48,24},{56,32},{64,10... | collective-permute-start | bytes 344072 | tf_op jit(solution)/shard_map/ppermute | solution.py:22
  120.8 2.4 %collective-permute-start.13 = (f32[2,112,128]{2,1,0:T(8,128)S(1)}, f32[2,112,128]{2,1,0:T(8,128)S(1)}, u32[]{:S(2)}, u32[]{:S(2)}) collective-permute-start(f32[2,112,128]{2,1,0:T(8,128)S(1)} %pad_select_fusion), channel_id=1, source_target_pairs={{0,32},{8,40},{16,48},{24,56},{32,0},{40,8},{48,16},{56,24},{64,96... | collective-permute-start | bytes 344072 | tf_op jit(solution)/shard_map/ppermute | solution.py:22
  123.3 3.0 %collective-permute-start.16 = (f32[2,112,128]{2,1,0:T(8,128)S(1)}, f32[2,112,128]{2,1,0:T(8,128)S(1)}, u32[]{:S(2)}, u32[]{:S(2)}) collective-permute-start(f32[2,112,128]{2,1,0:T(8,128)S(1)} %pad_select_fusion), channel_id=1, source_target_pairs={{0,56},{8,0},{16,8},{24,16},{32,24},{40,32},{48,40},{56,48},{64,12... | collective-permute-start | bytes 344072 | tf_op jit(solution)/shard_map/ppermute | solution.py:22
  144.3 2.9 %collective-permute-start.19 = (f32[2,2,112,128]{3,2,1,0:T(8,128)}, f32[2,2,112,128]{3,2,1,0:T(8,128)S(1)}, u32[]{:S(2)}, u32[]{:S(2)}) collective-permute-start(f32[2,2,112,128]{3,2,1,0:T(8,128)} %pad_maximum_fusion.4), channel_id=1, source_target_pairs={{0,192},{8,200},{16,208},{24,216},{32,224},{40,232},{48,240},{56,2... | collective-permute-start | bytes 688136 | tf_op jit(solution)/shard_map/ppermute | solution.py:32
  149.4 3.6 %all-to-all-start.2 = ((bf16[8,1,128,224]{2,3,1,0:T(8,128)(2,1)}), bf16[8,1,128,224]{2,3,1,0:T(8,128)(2,1)S(1)}, u32[]{:S(2)}, u32[]{:S(2)}) async-start(bf16[8,1,128,224]{2,3,1,0:T(8,128)(2,1)} %copy.44), calls=%async_computation.2 | async-start | bytes 917504 | tf_op jit(solution)/shard_map/all_to_all | solution.py:82
  164.4 2.7 %all-to-all-done.2 = bf16[8,1,128,224]{2,3,1,0:T(8,128)(2,1)S(1)} async-done(((bf16[8,1,128,224]{2,3,1,0:T(8,128)(2,1)}), bf16[8,1,128,224]{2,3,1,0:T(8,128)(2,1)S(1)}, u32[]{:S(2)}, u32[]{:S(2)}) %all-to-all-start.2) | async-done | bytes 458784 | tf_op jit(solution)/shard_map/all_to_all | solution.py:82
  167.1 4.5 %all-to-all-start.3 = ((bf16[8,2,128,224]{2,3,1,0:T(8,128)(2,1)}), bf16[8,2,128,224]{2,3,1,0:T(8,128)(2,1)S(1)}, u32[]{:S(2)}, u32[]{:S(2)}) async-start(bf16[8,2,128,224]{2,3,1,0:T(8,128)(2,1)} %maximum_bitcast_fusion.2), calls=%async_computation.3 | async-start | bytes 1835008 | tf_op jit(solution)/shard_map/all_to_all | solution.py:82
  172.6 22.4 %all-to-all-done.3 = bf16[8,2,128,224]{2,3,1,0:T(8,128)(2,1)S(1)} async-done(((bf16[8,2,128,224]{2,3,1,0:T(8,128)(2,1)}), bf16[8,2,128,224]{2,3,1,0:T(8,128)(2,1)S(1)}, u32[]{:S(2)}, u32[]{:S(2)}) %all-to-all-start.3) | async-done | bytes 917536 | tf_op jit(solution)/shard_map/all_to_all | solution.py:82
  (125 shorter events, 36.4 us)
Async XLA Ops:
  0.6 1.3 copy-start.3
  3.3 8.6 %copy-start.4 = (bf16[128,1792]{1,0:T(8,128)(2,1)S(1)}, bf16[128,1792]{1,0:T(8,128)(2,1)}, u32[]{:S(2)}) copy-start(bf16[128,1792]{1,0:T(8,128)(2,1)} %param.5) | copy-start | bytes 1376260
  3.3 34.5 %all-to-all-start.1 = ((bf16[8,2,128,224]{2,3,1,0:T(8,128)(2,1)}), bf16[8,2,128,224]{2,3,1,0:T(8,128)(2,1)S(1)}, u32[]{:S(2)}, u32[]{:S(2)}) async-start(bf16[8,2,128,224]{2,3,1,0:T(8,128)(2,1)} %copy.39), calls=%async_computation.1 | async-start | bytes 1835008 | tf_op jit(solution)/shard_map/all_to_all | solution.py:75
  11.9 1.0 copy-start.5
  37.8 29.9 %all-to-all-start = ((bf16[8,2,128,224]{2,3,1,0:T(8,128)(2,1)}), bf16[8,2,128,224]{2,3,1,0:T(8,128)(2,1)S(1)}, u32[]{:S(2)}, u32[]{:S(2)}) async-start(bf16[8,2,128,224]{2,3,1,0:T(8,128)(2,1)} %copy.35), calls=%async_computation | async-start | bytes 1835008 | tf_op jit(solution)/shard_map/all_to_all | solution.py:75
  42.1 1.5 copy-start.9
  44.3 6.5 %collective-permute-start.1 = (f32[2,112,128]{2,1,0:T(8,128)}, f32[2,112,128]{2,1,0:T(8,128)S(1)}, u32[]{:S(2)}, u32[]{:S(2)}) collective-permute-start(f32[2,112,128]{2,1,0:T(8,128)} %pad_select_fusion.1), channel_id=1, source_target_pairs={{0,16},{8,24},{16,32},{24,40},{32,48},{40,56},{48,0},{56,8},{64,80... | collective-permute-start | bytes 344072 | tf_op jit(solution)/shard_map/ppermute | solution.py:22
  45.8 5.0 %collective-permute-start = (f32[2,112,128]{2,1,0:T(8,128)}, f32[2,112,128]{2,1,0:T(8,128)S(1)}, u32[]{:S(2)}, u32[]{:S(2)}) collective-permute-start(f32[2,112,128]{2,1,0:T(8,128)} %pad_select_fusion.1), channel_id=1, source_target_pairs={{0,8},{8,16},{16,24},{24,32},{32,40},{40,48},{48,56},{56,0},{64,72... | collective-permute-start | bytes 344072 | tf_op jit(solution)/shard_map/ppermute | solution.py:22
  45.8 35.5 %collective-permute-start.5 = (f32[2,112,128]{2,1,0:T(8,128)}, f32[2,112,128]{2,1,0:T(8,128)}, u32[]{:S(2)}, u32[]{:S(2)}) collective-permute-start(f32[2,112,128]{2,1,0:T(8,128)} %pad_select_fusion.1), channel_id=1, source_target_pairs={{0,48},{8,56},{16,0},{24,8},{32,16},{40,24},{48,32},{56,40},{64,11... | collective-permute-start | bytes 344072 | tf_op jit(solution)/shard_map/ppermute | solution.py:22
  46.3 33.1 %collective-permute-start.4 = (f32[2,112,128]{2,1,0:T(8,128)}, f32[2,112,128]{2,1,0:T(8,128)}, u32[]{:S(2)}, u32[]{:S(2)}) collective-permute-start(f32[2,112,128]{2,1,0:T(8,128)} %pad_select_fusion.1), channel_id=1, source_target_pairs={{0,40},{8,48},{16,56},{24,0},{32,8},{40,16},{48,24},{56,32},{64,10... | collective-permute-start | bytes 344072 | tf_op jit(solution)/shard_map/ppermute | solution.py:22
  48.4 29.2 %collective-permute-start.3 = (f32[2,112,128]{2,1,0:T(8,128)}, f32[2,112,128]{2,1,0:T(8,128)}, u32[]{:S(2)}, u32[]{:S(2)}) collective-permute-start(f32[2,112,128]{2,1,0:T(8,128)} %pad_select_fusion.1), channel_id=1, source_target_pairs={{0,32},{8,40},{16,48},{24,56},{32,0},{40,8},{48,16},{56,24},{64,96... | collective-permute-start | bytes 344072 | tf_op jit(solution)/shard_map/ppermute | solution.py:22
  50.8 25.0 %collective-permute-start.2 = (f32[2,112,128]{2,1,0:T(8,128)}, f32[2,112,128]{2,1,0:T(8,128)}, u32[]{:S(2)}, u32[]{:S(2)}) collective-permute-start(f32[2,112,128]{2,1,0:T(8,128)} %pad_select_fusion.1), channel_id=1, source_target_pairs={{0,24},{8,32},{16,40},{24,48},{32,56},{40,0},{48,8},{56,16},{64,88... | collective-permute-start | bytes 344072 | tf_op jit(solution)/shard_map/ppermute | solution.py:22
  50.8 32.4 %collective-permute-start.6 = (f32[2,112,128]{2,1,0:T(8,128)}, f32[2,112,128]{2,1,0:T(8,128)}, u32[]{:S(2)}, u32[]{:S(2)}) collective-permute-start(f32[2,112,128]{2,1,0:T(8,128)} %pad_select_fusion.1), channel_id=1, source_target_pairs={{0,56},{8,0},{16,8},{24,16},{32,24},{40,32},{48,40},{56,48},{64,12... | collective-permute-start | bytes 344072 | tf_op jit(solution)/shard_map/ppermute | solution.py:22
  92.0 11.9 %collective-permute-start.9 = (f32[2,2,112,128]{3,2,1,0:T(8,128)}, f32[2,2,112,128]{3,2,1,0:T(8,128)}, u32[]{:S(2)}, u32[]{:S(2)}) collective-permute-start(f32[2,2,112,128]{3,2,1,0:T(8,128)} %pad_maximum_fusion.3), channel_id=1, source_target_pairs={{0,192},{8,200},{16,208},{24,216},{32,224},{40,232},{48,240},{56,2... | collective-permute-start | bytes 688136 | tf_op jit(solution)/shard_map/ppermute | solution.py:32
  95.1 10.8 %collective-permute-start.8 = (f32[2,2,112,128]{3,2,1,0:T(8,128)}, f32[2,2,112,128]{3,2,1,0:T(8,128)}, u32[]{:S(2)}, u32[]{:S(2)}) collective-permute-start(f32[2,2,112,128]{3,2,1,0:T(8,128)} %pad_maximum_fusion.3), channel_id=1, source_target_pairs={{0,128},{8,136},{16,144},{24,152},{32,160},{40,168},{48,176},{56,1... | collective-permute-start | bytes 688136 | tf_op jit(solution)/shard_map/ppermute | solution.py:32
  95.7 12.1 %collective-permute-start.7 = (f32[2,2,112,128]{3,2,1,0:T(8,128)}, f32[2,2,112,128]{3,2,1,0:T(8,128)}, u32[]{:S(2)}, u32[]{:S(2)}) collective-permute-start(f32[2,2,112,128]{3,2,1,0:T(8,128)} %pad_maximum_fusion.3), channel_id=1, source_target_pairs={{0,64},{8,72},{16,80},{24,88},{32,96},{40,104},{48,112},{56,120},{... | collective-permute-start | bytes 688136 | tf_op jit(solution)/shard_map/ppermute | solution.py:32
  113.9 1.0 copy-start.2
  116.3 7.0 %collective-permute-start.11 = (f32[2,112,128]{2,1,0:T(8,128)S(1)}, f32[2,112,128]{2,1,0:T(8,128)S(1)}, u32[]{:S(2)}, u32[]{:S(2)}) collective-permute-start(f32[2,112,128]{2,1,0:T(8,128)S(1)} %pad_select_fusion), channel_id=1, source_target_pairs={{0,16},{8,24},{16,32},{24,40},{32,48},{40,56},{48,0},{56,8},{64,80... | collective-permute-start | bytes 344072 | tf_op jit(solution)/shard_map/ppermute | solution.py:22
  117.9 5.4 %collective-permute-start.10 = (f32[2,112,128]{2,1,0:T(8,128)S(1)}, f32[2,112,128]{2,1,0:T(8,128)S(1)}, u32[]{:S(2)}, u32[]{:S(2)}) collective-permute-start(f32[2,112,128]{2,1,0:T(8,128)S(1)} %pad_select_fusion), channel_id=1, source_target_pairs={{0,8},{8,16},{16,24},{24,32},{32,40},{40,48},{48,56},{56,0},{64,72... | collective-permute-start | bytes 344072 | tf_op jit(solution)/shard_map/ppermute | solution.py:22
  118.0 17.8 %collective-permute-start.15 = (f32[2,112,128]{2,1,0:T(8,128)S(1)}, f32[2,112,128]{2,1,0:T(8,128)S(1)}, u32[]{:S(2)}, u32[]{:S(2)}) collective-permute-start(f32[2,112,128]{2,1,0:T(8,128)S(1)} %pad_select_fusion), channel_id=1, source_target_pairs={{0,48},{8,56},{16,0},{24,8},{32,16},{40,24},{48,32},{56,40},{64,11... | collective-permute-start | bytes 344072 | tf_op jit(solution)/shard_map/ppermute | solution.py:22
  118.8 15.8 %collective-permute-start.14 = (f32[2,112,128]{2,1,0:T(8,128)S(1)}, f32[2,112,128]{2,1,0:T(8,128)S(1)}, u32[]{:S(2)}, u32[]{:S(2)}) collective-permute-start(f32[2,112,128]{2,1,0:T(8,128)S(1)} %pad_select_fusion), channel_id=1, source_target_pairs={{0,40},{8,48},{16,56},{24,0},{32,8},{40,16},{48,24},{56,32},{64,10... | collective-permute-start | bytes 344072 | tf_op jit(solution)/shard_map/ppermute | solution.py:22
  120.8 12.4 %collective-permute-start.13 = (f32[2,112,128]{2,1,0:T(8,128)S(1)}, f32[2,112,128]{2,1,0:T(8,128)S(1)}, u32[]{:S(2)}, u32[]{:S(2)}) collective-permute-start(f32[2,112,128]{2,1,0:T(8,128)S(1)} %pad_select_fusion), channel_id=1, source_target_pairs={{0,32},{8,40},{16,48},{24,56},{32,0},{40,8},{48,16},{56,24},{64,96... | collective-permute-start | bytes 344072 | tf_op jit(solution)/shard_map/ppermute | solution.py:22
  123.3 8.9 %collective-permute-start.12 = (f32[2,112,128]{2,1,0:T(8,128)S(1)}, f32[2,112,128]{2,1,0:T(8,128)S(1)}, u32[]{:S(2)}, u32[]{:S(2)}) collective-permute-start(f32[2,112,128]{2,1,0:T(8,128)S(1)} %pad_select_fusion), channel_id=1, source_target_pairs={{0,24},{8,32},{16,40},{24,48},{32,56},{40,0},{48,8},{56,16},{64,88... | collective-permute-start | bytes 344072 | tf_op jit(solution)/shard_map/ppermute | solution.py:22
  123.3 13.8 %collective-permute-start.16 = (f32[2,112,128]{2,1,0:T(8,128)S(1)}, f32[2,112,128]{2,1,0:T(8,128)S(1)}, u32[]{:S(2)}, u32[]{:S(2)}) collective-permute-start(f32[2,112,128]{2,1,0:T(8,128)S(1)} %pad_select_fusion), channel_id=1, source_target_pairs={{0,56},{8,0},{16,8},{24,16},{32,24},{40,32},{48,40},{56,48},{64,12... | collective-permute-start | bytes 344072 | tf_op jit(solution)/shard_map/ppermute | solution.py:22
  143.6 4.6 %copy-start.7 = (bf16[1024,2,112]{0,2,1:T(8,128)(2,1)S(1)}, bf16[1024,2,112]{0,2,1:T(8,128)(2,1)}, u32[]{:S(2)}) copy-start(bf16[1024,2,112]{0,2,1:T(8,128)(2,1)} %copy-done.6) | copy-start | bytes 1376260
  144.3 13.1 %collective-permute-start.19 = (f32[2,2,112,128]{3,2,1,0:T(8,128)}, f32[2,2,112,128]{3,2,1,0:T(8,128)S(1)}, u32[]{:S(2)}, u32[]{:S(2)}) collective-permute-start(f32[2,2,112,128]{3,2,1,0:T(8,128)} %pad_maximum_fusion.4), channel_id=1, source_target_pairs={{0,192},{8,200},{16,208},{24,216},{32,224},{40,232},{48,240},{56,2... | collective-permute-start | bytes 688136 | tf_op jit(solution)/shard_map/ppermute | solution.py:32
  147.1 11.6 %collective-permute-start.18 = (f32[2,2,112,128]{3,2,1,0:T(8,128)}, f32[2,2,112,128]{3,2,1,0:T(8,128)S(1)}, u32[]{:S(2)}, u32[]{:S(2)}) collective-permute-start(f32[2,2,112,128]{3,2,1,0:T(8,128)} %pad_maximum_fusion.4), channel_id=1, source_target_pairs={{0,128},{8,136},{16,144},{24,152},{32,160},{40,168},{48,176},{56,1... | collective-permute-start | bytes 688136 | tf_op jit(solution)/shard_map/ppermute | solution.py:32
  148.2 11.9 %collective-permute-start.17 = (f32[2,2,112,128]{3,2,1,0:T(8,128)}, f32[2,2,112,128]{3,2,1,0:T(8,128)S(1)}, u32[]{:S(2)}, u32[]{:S(2)}) collective-permute-start(f32[2,2,112,128]{3,2,1,0:T(8,128)} %pad_maximum_fusion.4), channel_id=1, source_target_pairs={{0,64},{8,72},{16,80},{24,88},{32,96},{40,104},{48,112},{56,120},{... | collective-permute-start | bytes 688136 | tf_op jit(solution)/shard_map/ppermute | solution.py:32
  149.4 17.7 %all-to-all-start.2 = ((bf16[8,1,128,224]{2,3,1,0:T(8,128)(2,1)}), bf16[8,1,128,224]{2,3,1,0:T(8,128)(2,1)S(1)}, u32[]{:S(2)}, u32[]{:S(2)}) async-start(bf16[8,1,128,224]{2,3,1,0:T(8,128)(2,1)} %copy.44), calls=%async_computation.2 | async-start | bytes 917504 | tf_op jit(solution)/shard_map/all_to_all | solution.py:82
  161.9 1.0 copy-start.1
  161.9 1.1 copy-start.8
  167.1 27.9 %all-to-all-start.3 = ((bf16[8,2,128,224]{2,3,1,0:T(8,128)(2,1)}), bf16[8,2,128,224]{2,3,1,0:T(8,128)(2,1)S(1)}, u32[]{:S(2)}, u32[]{:S(2)}) async-start(bf16[8,2,128,224]{2,3,1,0:T(8,128)(2,1)} %maximum_bitcast_fusion.2), calls=%async_computation.3 | async-start | bytes 1835008 | tf_op jit(solution)/shard_map/all_to_all | solution.py:82
  (5 other events, 3.9 us)

commit v6 on v5

--- a/solution.py
+++ b/solution.py
@@ -1,5 +1,3 @@
-import functools
-
 import jax
 import jax.numpy as jnp
 from jax import lax
@@ -43,22 +41,26 @@
     lane = lax.broadcasted_iota(jnp.int32, part.shape[:-1] + (lanes,), 2)
     is_tag = lane == DH + 1
     packed = jnp.where(is_tag, flabel, jnp.concatenate([part, spare], axis=-1))
-    frames = [packed] + [shifted(packed, row, s) for s in range(1, row)]
-    labels = [f[0, 0, DH + 1] for f in frames]
-    keep = [(l >= flabel) if later else (l <= flabel) for l in labels]
-    seen = sum(jnp.where(k, f, 0.0) for k, f in zip(keep, frames))
+    frames = jnp.stack([packed] + [shifted(packed, row, s) for s in range(1, row)])
+    labels = frames[:, 0, 0, DH + 1]
+    keep = (labels >= flabel) if later else (labels <= flabel)
+    seen = jnp.sum(jnp.where(keep[:, None, None, None], frames, 0.0), axis=0)
     if rows > 1:
-        edge = functools.reduce(jnp.maximum, labels) if later else functools.reduce(jnp.minimum, labels)
-        whole = jnp.where(is_tag, edge, sum(frames))
-        edge_sum = jnp.where(is_tag, edge, sum(jnp.where(l == edge, f, 0.0) for l, f in zip(labels, frames)))
+        edge = jnp.max(labels) if later else jnp.min(labels)
+        whole = jnp.where(is_tag, edge, jnp.sum(frames, axis=0))
+        on_edge = (labels == edge)[:, None, None, None]
+        edge_sum = jnp.where(is_tag, edge, jnp.sum(jnp.where(on_edge, frames, 0.0), axis=0))
         summary = jnp.stack([whole, edge_sum])
-        for s in range(1, rows):
-            got = strided(summary, row, s)
-            source = (me - s) % rows
-            their_edge = got[1, 0, 0, DH + 1]
-            full = (source > me) if later else (source < me)
-            part_only = ((source < me) if later else (source > me)) & (their_edge == flabel)
-            seen = seen + jnp.where(full, got[0], 0.0) + jnp.where(part_only, got[1], 0.0)
+        got = jnp.stack([strided(summary, row, s) for s in range(1, rows)])
+        source = (me - jnp.arange(1, rows)) % rows
+        their_edge = got[:, 1, 0, 0, DH + 1]
+        full = (source > me) if later else (source < me)
+        part_only = ((source < me) if later else (source > me)) & (their_edge == flabel)
+        seen = seen + jnp.sum(
+            jnp.where(full[:, None, None, None], got[:, 0], 0.0)
+            + jnp.where(part_only[:, None, None, None], got[:, 1], 0.0),
+            axis=0,
+        )
     return seen[..., : DH + 1].astype(jnp.bfloat16)
 
 

time: 201 us -> 212 us (1.055)
  the two profiles are of different devices: /device:TPU:2 before, /device:TPU:16 now
where the time goes in v6:
time: 212 us; the launch traced here: 211 us
  waiting for transfers between devices  121 us (57%)
  starting transfers between devices  41.3 us (19%)
  local copies, waits for them, and re-layouts  29.4 us (14%)
  other arithmetic  15.7 us (7%)
    all_to_all x2, waiting for transfers between devices, to_heads(): incoming = lax.all_to_all(outgoing, 'inner', 0, 0, tiled=True)  47.2 us
    all_to_all x2, waiting for transfers between devices, to_rows(): returned = lax.all_to_all(leaving, 'inner', 0, 0, tiled=True)  33 us
    ppermute x14, waiting for transfers between devices, shifted(): return lax.ppermute(value, 'tm', pairs)  24.9 us
    unnamed x51, local copies, waits for them, and re-layouts  17.4 us
    ppermute x6, waiting for transfers between devices, strided(): return lax.ppermute(value, 'tm', pairs)  16 us
    ppermute x14, starting transfers between devices, shifted(): return lax.ppermute(value, 'tm', pairs)  13.1 us
    all_to_all x2, starting transfers between devices, to_heads(): incoming = lax.all_to_all(outgoing, 'inner', 0, 0, tiled=True)  12.1 us
    ppermute x6, starting transfers between devices, strided(): return lax.ppermute(value, 'tm', pairs)  9.04 us
  transfers between devices with their start and end apart: 24, of which 13 were waited for; matrix products, arithmetic and copies ran while one was open for 11% of the time, Pallas kernels for 0%

profile of v6, /device:TPU:16, one launch (start us, length us, event | category | flops | bytes accessed | tf_op | source)
XLA Modules:
  0.0 210.5 jit_solution(1448724772864192759)
XLA Ops:
  3.3 8.6 %all-to-all-start.1 = ((bf16[8,2,128,224]{2,3,1,0:T(8,128)(2,1)}), bf16[8,2,128,224]{2,3,1,0:T(8,128)(2,1)S(1)}, u32[]{:S(2)}, u32[]{:S(2)}) async-start(bf16[8,2,128,224]{2,3,1,0:T(8,128)(2,1)} %copy.47), calls=%async_computation.1 | async-start | bytes 1835008 | tf_op jit(solution)/shard_map/all_to_all | solution.py:77
  14.3 23.5 %all-to-all-done.1 = bf16[8,2,128,224]{2,3,1,0:T(8,128)(2,1)S(1)} async-done(((bf16[8,2,128,224]{2,3,1,0:T(8,128)(2,1)}), bf16[8,2,128,224]{2,3,1,0:T(8,128)(2,1)S(1)}, u32[]{:S(2)}, u32[]{:S(2)}) %all-to-all-start.1) | async-done | bytes 917536 | tf_op jit(solution)/shard_map/all_to_all | solution.py:77
  37.9 3.6 %all-to-all-start = ((bf16[8,2,128,224]{2,3,1,0:T(8,128)(2,1)}), bf16[8,2,128,224]{2,3,1,0:T(8,128)(2,1)S(1)}, u32[]{:S(2)}, u32[]{:S(2)}) async-start(bf16[8,2,128,224]{2,3,1,0:T(8,128)(2,1)} %copy.43), calls=%async_computation | async-start | bytes 1835008 | tf_op jit(solution)/shard_map/all_to_all | solution.py:77
  44.1 23.6 %all-to-all-done = bf16[8,2,128,224]{2,3,1,0:T(8,128)(2,1)S(1)} async-done(((bf16[8,2,128,224]{2,3,1,0:T(8,128)(2,1)}), bf16[8,2,128,224]{2,3,1,0:T(8,128)(2,1)S(1)}, u32[]{:S(2)}, u32[]{:S(2)}) %all-to-all-start) | async-done | bytes 917536 | tf_op jit(solution)/shard_map/all_to_all | solution.py:77
  69.6 3.0 %collective-permute-start.6 = (f32[2,112,128]{2,1,0:T(8,128)}, f32[2,112,128]{2,1,0:T(8,128)S(1)}, u32[]{:S(2)}, u32[]{:S(2)}) collective-permute-start(f32[2,112,128]{2,1,0:T(8,128)} %get-tuple-element.20), channel_id=1, source_target_pairs={{0,56},{8,0},{16,8},{24,16},{32,24},{40,32},{48,40},{56,48},{64,12... | collective-permute-start | bytes 344072 | tf_op jit(solution)/shard_map/ppermute | solution.py:20
  72.6 1.5 collective-permute-start.5
  74.1 1.7 collective-permute-start.3
  75.8 1.5 copy.52
  78.6 2.0 copy.53
  80.6 2.0 max.15
  83.5 6.2 %collective-permute-done.1 = f32[2,112,128]{2,1,0:T(8,128)S(1)} collective-permute-done((f32[2,112,128]{2,1,0:T(8,128)}, f32[2,112,128]{2,1,0:T(8,128)S(1)}, u32[]{:S(2)}, u32[]{:S(2)}) %collective-permute-start.1) | collective-permute-done | bytes 114720 | tf_op jit(solution)/shard_map/ppermute | solution.py:20
  90.4 5.4 %collective-permute-done.2 = f32[2,112,128]{2,1,0:T(8,128)S(1)} collective-permute-done((f32[2,112,128]{2,1,0:T(8,128)}, f32[2,112,128]{2,1,0:T(8,128)S(1)}, u32[]{:S(2)}, u32[]{:S(2)}) %collective-permute-start.2) | collective-permute-done | bytes 114720 | tf_op jit(solution)/shard_map/ppermute | solution.py:20
  96.4 1.5 bitcast_dynamic-update-slice_fusion.11
  98.0 1.5 bitcast_dynamic-update-slice_fusion.10
  100.8 1.4 slice_reduce_fusion.1
  102.3 1.8 compare_reduce_fusion.3
  106.8 1.7 select_bitcast_fusion.1
  109.1 2.9 %collective-permute-start.8 = (f32[2,2,112,128]{3,2,1,0:T(8,128)S(1)}, f32[2,2,112,128]{3,2,1,0:T(8,128)S(1)}, u32[]{:S(2)}, u32[]{:S(2)}) collective-permute-start(f32[2,2,112,128]{3,2,1,0:T(8,128)S(1)} %pad_maximum_fusion.5), channel_id=1, source_target_pairs={{0,128},{8,136},{16,144},{24,152},{32,160},{40,168},{48,176},{56,1... | collective-permute-start | bytes 688136 | tf_op jit(solution)/shard_map/ppermute | solution.py:30
  112.1 4.9 %collective-permute-done.9 = f32[2,2,112,128]{3,2,1,0:T(8,128)S(1)} collective-permute-done((f32[2,2,112,128]{3,2,1,0:T(8,128)S(1)}, f32[2,2,112,128]{3,2,1,0:T(8,128)S(1)}, u32[]{:S(2)}, u32[]{:S(2)}) %collective-permute-start.9) | collective-permute-done | bytes 229408 | tf_op jit(solution)/shard_map/ppermute | solution.py:30
  117.0 2.0 collective-permute-done.8
  119.0 4.3 %collective-permute-done.7 = f32[2,2,112,128]{3,2,1,0:T(8,128)S(1)} collective-permute-done((f32[2,2,112,128]{3,2,1,0:T(8,128)S(1)}, f32[2,2,112,128]{3,2,1,0:T(8,128)S(1)}, u32[]{:S(2)}, u32[]{:S(2)}) %collective-permute-start.7) | collective-permute-done | bytes 229408 | tf_op jit(solution)/shard_map/ppermute | solution.py:30
  127.9 2.9 %collective-permute-start.16 = (f32[2,112,128]{2,1,0:T(8,128)S(1)}, f32[2,112,128]{2,1,0:T(8,128)S(1)}, u32[]{:S(2)}, u32[]{:S(2)}) collective-permute-start(f32[2,112,128]{2,1,0:T(8,128)S(1)} %get-tuple-element.18), channel_id=1, source_target_pairs={{0,56},{8,0},{16,8},{24,16},{32,24},{40,32},{48,40},{56,48},{64,12... | collective-permute-start | bytes 344072 | tf_op jit(solution)/shard_map/ppermute | solution.py:20
  130.8 3.3 %collective-permute-start.13 = (f32[2,112,128]{2,1,0:T(8,128)S(1)}, f32[2,112,128]{2,1,0:T(8,128)S(1)}, u32[]{:S(2)}, u32[]{:S(2)}) collective-permute-start(f32[2,112,128]{2,1,0:T(8,128)S(1)} %get-tuple-element.18), channel_id=1, source_target_pairs={{0,32},{8,40},{16,48},{24,56},{32,0},{40,8},{48,16},{56,24},{64,96... | collective-permute-start | bytes 344072 | tf_op jit(solution)/shard_map/ppermute | solution.py:20
  134.2 7.8 %collective-permute-done.11 = f32[2,112,128]{2,1,0:T(8,128)S(1)} collective-permute-done((f32[2,112,128]{2,1,0:T(8,128)S(1)}, f32[2,112,128]{2,1,0:T(8,128)S(1)}, u32[]{:S(2)}, u32[]{:S(2)}) %collective-permute-start.11) | collective-permute-done | bytes 114720 | tf_op jit(solution)/shard_map/ppermute | solution.py:20
  142.2 5.6 %collective-permute-done.12 = f32[2,112,128]{2,1,0:T(8,128)S(1)} collective-permute-done((f32[2,112,128]{2,1,0:T(8,128)S(1)}, f32[2,112,128]{2,1,0:T(8,128)S(1)}, u32[]{:S(2)}, u32[]{:S(2)}) %collective-permute-start.12) | collective-permute-done | bytes 114720 | tf_op jit(solution)/shard_map/ppermute | solution.py:20
  152.6 2.9 %collective-permute-start.18 = (f32[2,2,112,128]{3,2,1,0:T(8,128)S(1)}, f32[2,2,112,128]{3,2,1,0:T(8,128)S(1)}, u32[]{:S(2)}, u32[]{:S(2)}) collective-permute-start(f32[2,2,112,128]{3,2,1,0:T(8,128)S(1)} %pad_maximum_fusion.6), channel_id=1, source_target_pairs={{0,128},{8,136},{16,144},{24,152},{32,160},{40,168},{48,176},{56,1... | collective-permute-start | bytes 688136 | tf_op jit(solution)/shard_map/ppermute | solution.py:30
  155.5 2.0 collective-permute-start.17
  158.7 3.5 %all-to-all-start.2 = ((bf16[8,1,128,224]{2,3,1,0:T(8,128)(2,1)}), bf16[8,1,128,224]{2,3,1,0:T(8,128)(2,1)S(1)}, u32[]{:S(2)}, u32[]{:S(2)}) async-start(bf16[8,1,128,224]{2,3,1,0:T(8,128)(2,1)} %copy.54), calls=%async_computation.2 | async-start | bytes 917504 | tf_op jit(solution)/shard_map/all_to_all | solution.py:84
  162.6 4.4 %collective-permute-done.17 = f32[2,2,112,128]{3,2,1,0:T(8,128)S(1)} collective-permute-done((f32[2,2,112,128]{3,2,1,0:T(8,128)S(1)}, f32[2,2,112,128]{3,2,1,0:T(8,128)S(1)}, u32[]{:S(2)}, u32[]{:S(2)}) %collective-permute-start.17) | collective-permute-done | bytes 229408 | tf_op jit(solution)/shard_map/ppermute | solution.py:30
  170.9 7.7 %all-to-all-done.2 = bf16[8,1,128,224]{2,3,1,0:T(8,128)(2,1)S(1)} async-done(((bf16[8,1,128,224]{2,3,1,0:T(8,128)(2,1)}), bf16[8,1,128,224]{2,3,1,0:T(8,128)(2,1)S(1)}, u32[]{:S(2)}, u32[]{:S(2)}) %all-to-all-start.2) | async-done | bytes 458784 | tf_op jit(solution)/shard_map/all_to_all | solution.py:84
  178.6 3.6 %all-to-all-start.3 = ((bf16[8,2,128,224]{2,3,1,0:T(8,128)(2,1)}), bf16[8,2,128,224]{2,3,1,0:T(8,128)(2,1)S(1)}, u32[]{:S(2)}, u32[]{:S(2)}) async-start(bf16[8,2,128,224]{2,3,1,0:T(8,128)(2,1)} %maximum_bitcast_fusion.2), calls=%async_computation.3 | async-start | bytes 1835008 | tf_op jit(solution)/shard_map/all_to_all | solution.py:84
  183.1 25.3 %all-to-all-done.3 = bf16[8,2,128,224]{2,3,1,0:T(8,128)(2,1)S(1)} async-done(((bf16[8,2,128,224]{2,3,1,0:T(8,128)(2,1)}), bf16[8,2,128,224]{2,3,1,0:T(8,128)(2,1)S(1)}, u32[]{:S(2)}, u32[]{:S(2)}) %all-to-all-start.3) | async-done | bytes 917536 | tf_op jit(solution)/shard_map/all_to_all | solution.py:84
  (133 shorter events, 35.5 us)
Async XLA Ops:
  0.6 1.3 copy-start.3
  3.3 8.6 %copy-start.4 = (bf16[128,1792]{1,0:T(8,128)(2,1)S(1)}, bf16[128,1792]{1,0:T(8,128)(2,1)}, u32[]{:S(2)}) copy-start(bf16[128,1792]{1,0:T(8,128)(2,1)} %param.5) | copy-start | bytes 1376260
  3.3 34.5 %all-to-all-start.1 = ((bf16[8,2,128,224]{2,3,1,0:T(8,128)(2,1)}), bf16[8,2,128,224]{2,3,1,0:T(8,128)(2,1)S(1)}, u32[]{:S(2)}, u32[]{:S(2)}) async-start(bf16[8,2,128,224]{2,3,1,0:T(8,128)(2,1)} %copy.47), calls=%async_computation.1 | async-start | bytes 1835008 | tf_op jit(solution)/shard_map/all_to_all | solution.py:77
  11.9 1.0 copy-start.5
  37.9 29.9 %all-to-all-start = ((bf16[8,2,128,224]{2,3,1,0:T(8,128)(2,1)}), bf16[8,2,128,224]{2,3,1,0:T(8,128)(2,1)S(1)}, u32[]{:S(2)}, u32[]{:S(2)}) async-start(bf16[8,2,128,224]{2,3,1,0:T(8,128)(2,1)} %copy.43), calls=%async_computation | async-start | bytes 1835008 | tf_op jit(solution)/shard_map/all_to_all | solution.py:77
  42.1 25.9 %copy-start.8 = (pred[128]{0:T(512)(128)(4,1)}, pred[128]{0:T(512)(128)(4,1)S(1)}, u32[]{:S(2)}) copy-start(pred[128]{0:T(512)(128)(4,1)S(1)} %iota_compare_fusion) | copy-start | bytes 388
  43.7 24.1 %copy-start = (bf16[1024,2,112]{0,2,1:T(8,128)(2,1)}, bf16[1024,2,112]{0,2,1:T(8,128)(2,1)S(1)}, u32[]{:S(2)}) copy-start(bf16[1024,2,112]{0,2,1:T(8,128)(2,1)S(1)} %squeeze.14) | copy-start | bytes 1376260
  68.8 13.8 %collective-permute-start = (f32[2,112,128]{2,1,0:T(8,128)}, f32[2,112,128]{2,1,0:T(8,128)S(1)}, u32[]{:S(2)}, u32[]{:S(2)}) collective-permute-start(f32[2,112,128]{2,1,0:T(8,128)} %get-tuple-element.20), channel_id=1, source_target_pairs={{0,8},{8,16},{16,24},{24,32},{32,40},{40,48},{48,56},{56,0},{64,72... | collective-permute-start | bytes 344072 | tf_op jit(solution)/shard_map/ppermute | solution.py:20
  69.6 30.6 %collective-permute-start.6 = (f32[2,112,128]{2,1,0:T(8,128)}, f32[2,112,128]{2,1,0:T(8,128)S(1)}, u32[]{:S(2)}, u32[]{:S(2)}) collective-permute-start(f32[2,112,128]{2,1,0:T(8,128)} %get-tuple-element.20), channel_id=1, source_target_pairs={{0,56},{8,0},{16,8},{24,16},{32,24},{40,32},{48,40},{56,48},{64,12... | collective-permute-start | bytes 344072 | tf_op jit(solution)/shard_map/ppermute | solution.py:20
  72.6 27.0 %collective-permute-start.5 = (f32[2,112,128]{2,1,0:T(8,128)}, f32[2,112,128]{2,1,0:T(8,128)S(1)}, u32[]{:S(2)}, u32[]{:S(2)}) collective-permute-start(f32[2,112,128]{2,1,0:T(8,128)} %get-tuple-element.20), channel_id=1, source_target_pairs={{0,48},{8,56},{16,0},{24,8},{32,16},{40,24},{48,32},{56,40},{64,11... | collective-permute-start | bytes 344072 | tf_op jit(solution)/shard_map/ppermute | solution.py:20
  74.1 23.9 %collective-permute-start.4 = (f32[2,112,128]{2,1,0:T(8,128)}, f32[2,112,128]{2,1,0:T(8,128)}, u32[]{:S(2)}, u32[]{:S(2)}) collective-permute-start(f32[2,112,128]{2,1,0:T(8,128)} %get-tuple-element.20), channel_id=1, source_target_pairs={{0,40},{8,48},{16,56},{24,0},{32,8},{40,16},{48,24},{56,32},{64,10... | collective-permute-start | bytes 344072 | tf_op jit(solution)/shard_map/ppermute | solution.py:20
  74.1 22.3 %collective-permute-start.3 = (f32[2,112,128]{2,1,0:T(8,128)}, f32[2,112,128]{2,1,0:T(8,128)}, u32[]{:S(2)}, u32[]{:S(2)}) collective-permute-start(f32[2,112,128]{2,1,0:T(8,128)} %get-tuple-element.20), channel_id=1, source_target_pairs={{0,32},{8,40},{16,48},{24,56},{32,0},{40,8},{48,16},{56,24},{64,96... | collective-permute-start | bytes 344072 | tf_op jit(solution)/shard_map/ppermute | solution.py:20
  82.6 7.1 %collective-permute-start.1 = (f32[2,112,128]{2,1,0:T(8,128)}, f32[2,112,128]{2,1,0:T(8,128)S(1)}, u32[]{:S(2)}, u32[]{:S(2)}) collective-permute-start(f32[2,112,128]{2,1,0:T(8,128)} %get-tuple-element.20), channel_id=1, source_target_pairs={{0,16},{8,24},{16,32},{24,40},{32,48},{40,56},{48,0},{56,8},{64,80... | collective-permute-start | bytes 344072 | tf_op jit(solution)/shard_map/ppermute | solution.py:20
  89.7 6.0 %collective-permute-start.2 = (f32[2,112,128]{2,1,0:T(8,128)}, f32[2,112,128]{2,1,0:T(8,128)S(1)}, u32[]{:S(2)}, u32[]{:S(2)}) collective-permute-start(f32[2,112,128]{2,1,0:T(8,128)} %get-tuple-element.20), channel_id=1, source_target_pairs={{0,24},{8,32},{16,40},{24,48},{32,56},{40,0},{48,8},{56,16},{64,88... | collective-permute-start | bytes 344072 | tf_op jit(solution)/shard_map/ppermute | solution.py:20
  108.5 8.5 %collective-permute-start.9 = (f32[2,2,112,128]{3,2,1,0:T(8,128)S(1)}, f32[2,2,112,128]{3,2,1,0:T(8,128)S(1)}, u32[]{:S(2)}, u32[]{:S(2)}) collective-permute-start(f32[2,2,112,128]{3,2,1,0:T(8,128)S(1)} %pad_maximum_fusion.5), channel_id=1, source_target_pairs={{0,192},{8,200},{16,208},{24,216},{32,224},{40,232},{48,240},{56,2... | collective-permute-start | bytes 688136 | tf_op jit(solution)/shard_map/ppermute | solution.py:30
  109.1 10.0 %collective-permute-start.8 = (f32[2,2,112,128]{3,2,1,0:T(8,128)S(1)}, f32[2,2,112,128]{3,2,1,0:T(8,128)S(1)}, u32[]{:S(2)}, u32[]{:S(2)}) collective-permute-start(f32[2,2,112,128]{3,2,1,0:T(8,128)S(1)} %pad_maximum_fusion.5), channel_id=1, source_target_pairs={{0,128},{8,136},{16,144},{24,152},{32,160},{40,168},{48,176},{56,1... | collective-permute-start | bytes 688136 | tf_op jit(solution)/shard_map/ppermute | solution.py:30
  112.0 11.4 %collective-permute-start.7 = (f32[2,2,112,128]{3,2,1,0:T(8,128)S(1)}, f32[2,2,112,128]{3,2,1,0:T(8,128)S(1)}, u32[]{:S(2)}, u32[]{:S(2)}) collective-permute-start(f32[2,2,112,128]{3,2,1,0:T(8,128)S(1)} %pad_maximum_fusion.5), channel_id=1, source_target_pairs={{0,64},{8,72},{16,80},{24,88},{32,96},{40,104},{48,112},{56,120},{... | collective-permute-start | bytes 688136 | tf_op jit(solution)/shard_map/ppermute | solution.py:30
  124.3 1.0 copy-start.2
  127.0 7.2 %collective-permute-start.10 = (f32[2,112,128]{2,1,0:T(8,128)S(1)}, f32[2,112,128]{2,1,0:T(8,128)S(1)}, u32[]{:S(2)}, u32[]{:S(2)}) collective-permute-start(f32[2,112,128]{2,1,0:T(8,128)S(1)} %get-tuple-element.18), channel_id=1, source_target_pairs={{0,8},{8,16},{16,24},{24,32},{32,40},{40,48},{48,56},{56,0},{64,72... | collective-permute-start | bytes 344072 | tf_op jit(solution)/shard_map/ppermute | solution.py:20
  127.9 20.0 %collective-permute-start.16 = (f32[2,112,128]{2,1,0:T(8,128)S(1)}, f32[2,112,128]{2,1,0:T(8,128)S(1)}, u32[]{:S(2)}, u32[]{:S(2)}) collective-permute-start(f32[2,112,128]{2,1,0:T(8,128)S(1)} %get-tuple-element.18), channel_id=1, source_target_pairs={{0,56},{8,0},{16,8},{24,16},{32,24},{40,32},{48,40},{56,48},{64,12... | collective-permute-start | bytes 344072 | tf_op jit(solution)/shard_map/ppermute | solution.py:20
  130.8 17.0 %collective-permute-start.15 = (f32[2,112,128]{2,1,0:T(8,128)S(1)}, f32[2,112,128]{2,1,0:T(8,128)S(1)}, u32[]{:S(2)}, u32[]{:S(2)}) collective-permute-start(f32[2,112,128]{2,1,0:T(8,128)S(1)} %get-tuple-element.18), channel_id=1, source_target_pairs={{0,48},{8,56},{16,0},{24,8},{32,16},{40,24},{48,32},{56,40},{64,11... | collective-permute-start | bytes 344072 | tf_op jit(solution)/shard_map/ppermute | solution.py:20
  130.8 17.0 %collective-permute-start.14 = (f32[2,112,128]{2,1,0:T(8,128)S(1)}, f32[2,112,128]{2,1,0:T(8,128)S(1)}, u32[]{:S(2)}, u32[]{:S(2)}) collective-permute-start(f32[2,112,128]{2,1,0:T(8,128)S(1)} %get-tuple-element.18), channel_id=1, source_target_pairs={{0,40},{8,48},{16,56},{24,0},{32,8},{40,16},{48,24},{56,32},{64,10... | collective-permute-start | bytes 344072 | tf_op jit(solution)/shard_map/ppermute | solution.py:20
  130.8 17.0 %collective-permute-start.13 = (f32[2,112,128]{2,1,0:T(8,128)S(1)}, f32[2,112,128]{2,1,0:T(8,128)S(1)}, u32[]{:S(2)}, u32[]{:S(2)}) collective-permute-start(f32[2,112,128]{2,1,0:T(8,128)S(1)} %get-tuple-element.18), channel_id=1, source_target_pairs={{0,32},{8,40},{16,48},{24,56},{32,0},{40,8},{48,16},{56,24},{64,96... | collective-permute-start | bytes 344072 | tf_op jit(solution)/shard_map/ppermute | solution.py:20
  134.2 7.8 %collective-permute-start.11 = (f32[2,112,128]{2,1,0:T(8,128)S(1)}, f32[2,112,128]{2,1,0:T(8,128)S(1)}, u32[]{:S(2)}, u32[]{:S(2)}) collective-permute-start(f32[2,112,128]{2,1,0:T(8,128)S(1)} %get-tuple-element.18), channel_id=1, source_target_pairs={{0,16},{8,24},{16,32},{24,40},{32,48},{40,56},{48,0},{56,8},{64,80... | collective-permute-start | bytes 344072 | tf_op jit(solution)/shard_map/ppermute | solution.py:20
  142.0 5.8 %collective-permute-start.12 = (f32[2,112,128]{2,1,0:T(8,128)S(1)}, f32[2,112,128]{2,1,0:T(8,128)S(1)}, u32[]{:S(2)}, u32[]{:S(2)}) collective-permute-start(f32[2,112,128]{2,1,0:T(8,128)S(1)} %get-tuple-element.18), channel_id=1, source_target_pairs={{0,24},{8,32},{16,40},{24,48},{32,56},{40,0},{48,8},{56,16},{64,88... | collective-permute-start | bytes 344072 | tf_op jit(solution)/shard_map/ppermute | solution.py:20
  151.9 5.7 %copy-start.7 = (bf16[1024,2,112]{0,2,1:T(8,128)(2,1)S(1)}, bf16[1024,2,112]{0,2,1:T(8,128)(2,1)}, u32[]{:S(2)}) copy-start(bf16[1024,2,112]{0,2,1:T(8,128)(2,1)} %copy-done.6) | copy-start | bytes 1376260
  151.9 10.3 %collective-permute-start.19 = (f32[2,2,112,128]{3,2,1,0:T(8,128)S(1)}, f32[2,2,112,128]{3,2,1,0:T(8,128)S(1)}, u32[]{:S(2)}, u32[]{:S(2)}) collective-permute-start(f32[2,2,112,128]{3,2,1,0:T(8,128)S(1)} %pad_maximum_fusion.6), channel_id=1, source_target_pairs={{0,192},{8,200},{16,208},{24,216},{32,224},{40,232},{48,240},{56,2... | collective-permute-start | bytes 688136 | tf_op jit(solution)/shard_map/ppermute | solution.py:30
  152.6 10.0 %collective-permute-start.18 = (f32[2,2,112,128]{3,2,1,0:T(8,128)S(1)}, f32[2,2,112,128]{3,2,1,0:T(8,128)S(1)}, u32[]{:S(2)}, u32[]{:S(2)}) collective-permute-start(f32[2,2,112,128]{3,2,1,0:T(8,128)S(1)} %pad_maximum_fusion.6), channel_id=1, source_target_pairs={{0,128},{8,136},{16,144},{24,152},{32,160},{40,168},{48,176},{56,1... | collective-permute-start | bytes 688136 | tf_op jit(solution)/shard_map/ppermute | solution.py:30
  155.5 11.5 %collective-permute-start.17 = (f32[2,2,112,128]{3,2,1,0:T(8,128)S(1)}, f32[2,2,112,128]{3,2,1,0:T(8,128)S(1)}, u32[]{:S(2)}, u32[]{:S(2)}) collective-permute-start(f32[2,2,112,128]{3,2,1,0:T(8,128)S(1)} %pad_maximum_fusion.6), channel_id=1, source_target_pairs={{0,64},{8,72},{16,80},{24,88},{32,96},{40,104},{48,112},{56,120},{... | collective-permute-start | bytes 688136 | tf_op jit(solution)/shard_map/ppermute | solution.py:30
  158.7 19.8 %all-to-all-start.2 = ((bf16[8,1,128,224]{2,3,1,0:T(8,128)(2,1)}), bf16[8,1,128,224]{2,3,1,0:T(8,128)(2,1)S(1)}, u32[]{:S(2)}, u32[]{:S(2)}) async-start(bf16[8,1,128,224]{2,3,1,0:T(8,128)(2,1)} %copy.54), calls=%async_computation.2 | async-start | bytes 917504 | tf_op jit(solution)/shard_map/all_to_all | solution.py:84
  168.4 1.0 copy-start.1
  178.6 29.9 %all-to-all-start.3 = ((bf16[8,2,128,224]{2,3,1,0:T(8,128)(2,1)}), bf16[8,2,128,224]{2,3,1,0:T(8,128)(2,1)S(1)}, u32[]{:S(2)}, u32[]{:S(2)}) async-start(bf16[8,2,128,224]{2,3,1,0:T(8,128)(2,1)} %maximum_bitcast_fusion.2), calls=%async_computation.3 | async-start | bytes 1835008 | tf_op jit(solution)/shard_map/all_to_all | solution.py:84
  (6 other events, 3.9 us)

commit v7 on v4

--- a/solution.py
+++ b/solution.py
@@ -115,14 +115,24 @@
     query_feat = jnp.einsum("thv,hkv->thk", back_aug, state_vis, preferred_element_type=jnp.float32)
     query_back = jnp.where(query_heads > 0, query_feat, 0.0).astype(jnp.bfloat16)
     adjoint_vis = visible(adjoint_part, label, True)
-    key_feat = jnp.einsum("thv,hkv->thk", value_aug, adjoint_vis, preferred_element_type=jnp.float32)
+    (query_out,) = to_rows([query_back])
+
+    copies = jnp.broadcast_to(adjoint_vis[None], (groups,) + adjoint_vis.shape)
+    adjoint_all = lax.all_to_all(copies, "inner", 0, 0, tiled=True).reshape(
+        groups * heads, DH, DH + 1
+    )
+    all_heads = groups * heads
+    own_key = key_input.reshape(rows, all_heads, DH)
+    own_value = value_input.reshape(rows, all_heads, DH)
+    own_feat_key = jnp.maximum(own_key, 0)
+    key_feat = jnp.einsum(
+        "thv,hkv->thk", own_value, adjoint_all[..., :DH], preferred_element_type=jnp.float32
+    ) + adjoint_all[..., DH].astype(jnp.float32)[None]
     value_back = jnp.einsum(
-        "thk,hkv->thv", feat_key, adjoint_vis[..., :DH], preferred_element_type=jnp.float32
+        "thk,hkv->thv", own_feat_key, adjoint_all[..., :DH], preferred_element_type=jnp.float32
     )
-    key_back = jnp.where(key_heads > 0, key_feat, 0.0).astype(jnp.bfloat16)
-
-    (query_out,) = to_rows([query_back])
-    key_out, value_out = to_rows([key_back, value_back.astype(jnp.bfloat16)])
+    key_out = jnp.where(own_key > 0, key_feat, 0.0).astype(jnp.bfloat16).reshape(rows, columns)
+    value_out = value_back.astype(jnp.bfloat16).reshape(rows, columns)
     return query_out, key_out, value_out
 
 

time: 198 us -> 184 us (0.929)
  local copies, waits for them, and re-layouts: 39.4 us -> 31.6 us
  waiting for transfers between devices: 68.4 us -> 62.2 us
  starting transfers between devices: 45.9 us -> 47.9 us
    all_to_all x2 -> x1, waiting for transfers between devices: 25 us -> 0.01 us  [to_rows(): returned = lax.all_to_all(leaving, 'inner', 0, 0, tiled=True)]
    all_to_all x0 -> x1, waiting for transfers between devices: none -> 14.8 us  [local(): lax.all_to_all(copies, 'inner', 0, 0, tiled=True)]
    ppermute x6, waiting for transfers between devices: 0.02 us -> 7.44 us  [strided(): return lax.ppermute(value, 'tm', pairs)]
    all_to_all x0 -> x1, starting transfers between devices: none -> 6.93 us  [local(): lax.all_to_all(copies, 'inner', 0, 0, tiled=True)]
    all_to_all x2 -> x1, starting transfers between devices: 9.56 us -> 3.82 us  [to_rows(): returned = lax.all_to_all(leaving, 'inner', 0, 0, tiled=True)]
    ppermute x14, waiting for transfers between devices: 4.84 us -> 0.92 us  [shifted(): return lax.ppermute(value, 'tm', pairs)]
    max x2, local copies, waits for them, and re-layouts: 2.93 us -> 0.38 us  [local(): feat_query = jnp.maximum(query_heads, 0)]
    mul x2, local copies, waits for them, and re-layouts: 2.79 us -> 0.68 us  [local(): scaled = cotangent_heads.astype(jnp.float32) * loss_scale]
  transfers between devices with their start and end apart: 24 -> 24, of which waited for: 6 -> 7; matrix products, arithmetic and copies ran while one was open for 16% -> 13% of each run, Pallas kernels for 0% -> 0%
where the time goes in v7:
time: 184 us; the launch traced here: 181 us
  waiting for transfers between devices  62.2 us (34%)
  starting transfers between devices  47.9 us (26%)
  local copies, waits for them, and re-layouts  31.6 us (17%)
  between operations  31.4 us (17%)
  other arithmetic  6.05 us (3%)
  matrix products  1.9 us (1%)
    all_to_all x2, waiting for transfers between devices, to_heads(): incoming = lax.all_to_all(outgoing, 'inner', 0, 0, tiled=True)  39 us
    ppermute x14, starting transfers between devices, shifted(): return lax.ppermute(value, 'tm', pairs)  15.7 us
    all_to_all x1, waiting for transfers between devices, local(): lax.all_to_all(copies, 'inner', 0, 0, tiled=True)  14.8 us
    all_to_all x2, starting transfers between devices, to_heads(): incoming = lax.all_to_all(outgoing, 'inner', 0, 0, tiled=True)  12.1 us
    slice x14, local copies, waits for them, and re-layouts, visible(): labels = [f[0, 0, DH + 1] for f in frames]  12 us
    ppermute x6, starting transfers between devices, strided(): return lax.ppermute(value, 'tm', pairs)  9.33 us
    ppermute x6, waiting for transfers between devices, strided(): return lax.ppermute(value, 'tm', pairs)  7.44 us
    unnamed x25, local copies, waits for them, and re-layouts  7.33 us
  transfers between devices with their start and end apart: 24, of which 7 were waited for; matrix products, arithmetic and copies ran while one was open for 13% of the time, Pallas kernels for 0%

profile of v7, /device:TPU:2, one launch (start us, length us, event | category | flops | bytes accessed | tf_op | source)
XLA Modules:
  0.0 181.0 jit_solution(7945267131648699940)
XLA Ops:
  0.6 1.3 copy.41
  2.8 1.0 copy.42
  3.8 8.6 %all-to-all-start.1 = ((bf16[8,2,128,224]{2,3,1,0:T(8,128)(2,1)}), bf16[8,2,128,224]{2,3,1,0:T(8,128)(2,1)S(1)}, u32[]{:S(2)}, u32[]{:S(2)}) async-start(bf16[8,2,128,224]{2,3,1,0:T(8,128)(2,1)} %copy.42), calls=%async_computation.1 | async-start | bytes 1835008 | tf_op jit(solution)/shard_map/all_to_all | solution.py:80
  14.8 23.5 %all-to-all-done.1 = bf16[8,2,128,224]{2,3,1,0:T(8,128)(2,1)S(1)} async-done(((bf16[8,2,128,224]{2,3,1,0:T(8,128)(2,1)}), bf16[8,2,128,224]{2,3,1,0:T(8,128)(2,1)S(1)}, u32[]{:S(2)}, u32[]{:S(2)}) %all-to-all-start.1) | async-done | bytes 917536 | tf_op jit(solution)/shard_map/all_to_all | solution.py:80
  38.4 3.6 %all-to-all-start = ((bf16[8,2,128,224]{2,3,1,0:T(8,128)(2,1)}), bf16[8,2,128,224]{2,3,1,0:T(8,128)(2,1)S(1)}, u32[]{:S(2)}, u32[]{:S(2)}) async-start(bf16[8,2,128,224]{2,3,1,0:T(8,128)(2,1)} %copy.38), calls=%async_computation | async-start | bytes 1835008 | tf_op jit(solution)/shard_map/all_to_all | solution.py:80
  44.4 1.5 collective-permute-start.1
  45.9 1.7 collective-permute-start.6
  47.7 1.8 collective-permute-start.5
  50.3 2.5 %collective-permute-start.3 = (f32[2,112,114]{2,1,0:T(8,128)}, f32[2,112,114]{2,1,0:T(8,128)}, u32[]{:S(2)}, u32[]{:S(2)}) collective-permute-start(f32[2,112,114]{2,1,0:T(8,128)} %concatenate.27), channel_id=1, source_target_pairs={{0,32},{8,40},{16,48},{24,56},{32,0},{40,8},{48,16},{56,24},{64,96... | collective-permute-start | bytes 306440 | tf_op jit(solution)/shard_map/ppermute | solution.py:22
  52.8 15.4 %all-to-all-done = bf16[8,2,128,224]{2,3,1,0:T(8,128)(2,1)S(1)} async-done(((bf16[8,2,128,224]{2,3,1,0:T(8,128)(2,1)}), bf16[8,2,128,224]{2,3,1,0:T(8,128)(2,1)S(1)}, u32[]{:S(2)}, u32[]{:S(2)}) %all-to-all-start) | async-done | bytes 917536 | tf_op jit(solution)/shard_map/all_to_all | solution.py:80
  71.5 1.2 slice.234
  73.3 1.3 slice.236
  75.4 1.3 slice.238
  77.3 1.3 slice.240
  79.2 1.3 slice.242
  85.7 1.2 add_add_fusion.1
  86.9 1.2 select_add_fusion.1
  88.8 3.0 %collective-permute-start.9 = (f32[2,2,112,114]{3,2,1,0:T(8,128)}, f32[2,2,112,114]{3,2,1,0:T(8,128)}, u32[]{:S(2)}, u32[]{:S(2)}) collective-permute-start(f32[2,2,112,114]{3,2,1,0:T(8,128)} %pad_maximum_fusion.3), channel_id=1, source_target_pairs={{0,192},{8,200},{16,208},{24,216},{32,224},{40,232},{48,240},{56,2... | collective-permute-start | bytes 612872 | tf_op jit(solution)/shard_map/ppermute | solution.py:32
  98.3 1.6 collective-permute-done.9
  99.9 1.3 slice.251
  101.7 1.2 slice.248
  103.6 1.3 slice.245
  105.5 1.5 fusion.27
  108.2 1.8 collective-permute-start.11
  110.5 1.8 collective-permute-start.16
  112.2 1.7 collective-permute-start.15
  114.0 2.5 %collective-permute-start.13 = (f32[2,112,114]{2,1,0:T(8,128)S(1)}, f32[2,112,114]{2,1,0:T(8,128)S(1)}, u32[]{:S(2)}, u32[]{:S(2)}) collective-permute-start(f32[2,112,114]{2,1,0:T(8,128)S(1)} %concatenate.31), channel_id=1, source_target_pairs={{0,32},{8,40},{16,48},{24,56},{32,0},{40,8},{48,16},{56,24},{64,96... | collective-permute-start | bytes 306440 | tf_op jit(solution)/shard_map/ppermute | solution.py:22
  118.2 3.8 %all-to-all-start.2 = ((bf16[8,1,128,224]{2,3,1,0:T(8,128)(2,1)}), bf16[8,1,128,224]{2,3,1,0:T(8,128)(2,1)S(1)}, u32[]{:S(2)}, u32[]{:S(2)}) async-start(bf16[8,1,128,224]{2,3,1,0:T(8,128)(2,1)} %copy.47), calls=%async_computation.2 | async-start | bytes 917504 | tf_op jit(solution)/shard_map/all_to_all | solution.py:87
  135.3 3.8 %collective-permute-start.19 = (f32[2,2,112,114]{3,2,1,0:T(8,128)S(1)}, f32[2,2,112,114]{3,2,1,0:T(8,128)S(1)}, u32[]{:S(2)}, u32[]{:S(2)}) collective-permute-start(f32[2,2,112,114]{3,2,1,0:T(8,128)S(1)} %pad_maximum_fusion.4), channel_id=1, source_target_pairs={{0,192},{8,200},{16,208},{24,216},{32,224},{40,232},{48,240},{56,2... | collective-permute-start | bytes 612872 | tf_op jit(solution)/shard_map/ppermute | solution.py:32
  144.3 5.0 %collective-permute-done.19 = f32[2,2,112,114]{3,2,1,0:T(8,128)S(1)} collective-permute-done((f32[2,2,112,114]{3,2,1,0:T(8,128)S(1)}, f32[2,2,112,114]{3,2,1,0:T(8,128)S(1)}, u32[]{:S(2)}, u32[]{:S(2)}) %collective-permute-start.19) | collective-permute-done | bytes 204320 | tf_op jit(solution)/shard_map/ppermute | solution.py:32
  155.0 6.9 %all-to-all-start.3 = ((bf16[8,2,112,113]{3,2,1,0:T(8,128)(2,1)}), bf16[8,2,112,113]{3,2,1,0:T(8,128)(2,1)S(1)}, u32[]{:S(2)}, u32[]{:S(2)}) async-start(bf16[8,2,112,113]{3,2,1,0:T(8,128)(2,1)} %broadcast_in_dim.75), calls=%async_computation.3 | async-start | bytes 917504 | tf_op jit(solution)/shard_map/all_to_all | solution.py:121
  163.1 14.8 %all-to-all-done.3 = bf16[8,2,112,113]{3,2,1,0:T(8,128)(2,1)S(1)} async-done(((bf16[8,2,112,113]{3,2,1,0:T(8,128)(2,1)}), bf16[8,2,112,113]{3,2,1,0:T(8,128)(2,1)S(1)}, u32[]{:S(2)}, u32[]{:S(2)}) %all-to-all-start.3) | async-done | bytes 405024 | tf_op jit(solution)/shard_map/all_to_all | solution.py:121
  (107 shorter events, 27.9 us)
Async XLA Ops:
  0.6 1.3 copy-start.2
  2.0 0.8 copy-start
  3.8 8.6 %copy-start.3 = (bf16[128,1792]{1,0:T(8,128)(2,1)S(1)}, bf16[128,1792]{1,0:T(8,128)(2,1)}, u32[]{:S(2)}) copy-start(bf16[128,1792]{1,0:T(8,128)(2,1)} %param.8) | copy-start | bytes 1376260
  3.8 34.5 %all-to-all-start.1 = ((bf16[8,2,128,224]{2,3,1,0:T(8,128)(2,1)}), bf16[8,2,128,224]{2,3,1,0:T(8,128)(2,1)S(1)}, u32[]{:S(2)}, u32[]{:S(2)}) async-start(bf16[8,2,128,224]{2,3,1,0:T(8,128)(2,1)} %copy.42), calls=%async_computation.1 | async-start | bytes 1835008 | tf_op jit(solution)/shard_map/all_to_all | solution.py:80
  12.4 1.0 copy-start.4
  38.4 29.9 %all-to-all-start = ((bf16[8,2,128,224]{2,3,1,0:T(8,128)(2,1)}), bf16[8,2,128,224]{2,3,1,0:T(8,128)(2,1)S(1)}, u32[]{:S(2)}, u32[]{:S(2)}) async-start(bf16[8,2,128,224]{2,3,1,0:T(8,128)(2,1)} %copy.38), calls=%async_computation | async-start | bytes 1835008 | tf_op jit(solution)/shard_map/all_to_all | solution.py:80
  41.9 0.7 copy-start.7
  44.4 5.9 %collective-permute-start.1 = (f32[2,112,114]{2,1,0:T(8,128)}, f32[2,112,114]{2,1,0:T(8,128)S(1)}, u32[]{:S(2)}, u32[]{:S(2)}) collective-permute-start(f32[2,112,114]{2,1,0:T(8,128)} %concatenate.27), channel_id=1, source_target_pairs={{0,16},{8,24},{16,32},{24,40},{32,48},{40,56},{48,0},{56,8},{64,80... | collective-permute-start | bytes 306440 | tf_op jit(solution)/shard_map/ppermute | solution.py:22
  45.9 6.9 %collective-permute-start = (f32[2,112,114]{2,1,0:T(8,128)}, f32[2,112,114]{2,1,0:T(8,128)S(1)}, u32[]{:S(2)}, u32[]{:S(2)}) collective-permute-start(f32[2,112,114]{2,1,0:T(8,128)} %concatenate.27), channel_id=1, source_target_pairs={{0,8},{8,16},{16,24},{24,32},{32,40},{40,48},{48,56},{56,0},{64,72... | collective-permute-start | bytes 306440 | tf_op jit(solution)/shard_map/ppermute | solution.py:22
  45.9 33.3 %collective-permute-start.6 = (f32[2,112,114]{2,1,0:T(8,128)}, f32[2,112,114]{2,1,0:T(8,128)}, u32[]{:S(2)}, u32[]{:S(2)}) collective-permute-start(f32[2,112,114]{2,1,0:T(8,128)} %concatenate.27), channel_id=1, source_target_pairs={{0,56},{8,0},{16,8},{24,16},{32,24},{40,32},{48,40},{56,48},{64,12... | collective-permute-start | bytes 306440 | tf_op jit(solution)/shard_map/ppermute | solution.py:22
  47.7 29.6 %collective-permute-start.5 = (f32[2,112,114]{2,1,0:T(8,128)}, f32[2,112,114]{2,1,0:T(8,128)}, u32[]{:S(2)}, u32[]{:S(2)}) collective-permute-start(f32[2,112,114]{2,1,0:T(8,128)} %concatenate.27), channel_id=1, source_target_pairs={{0,48},{8,56},{16,0},{24,8},{32,16},{40,24},{48,32},{56,40},{64,11... | collective-permute-start | bytes 306440 | tf_op jit(solution)/shard_map/ppermute | solution.py:22
  49.4 25.9 %collective-permute-start.4 = (f32[2,112,114]{2,1,0:T(8,128)}, f32[2,112,114]{2,1,0:T(8,128)}, u32[]{:S(2)}, u32[]{:S(2)}) collective-permute-start(f32[2,112,114]{2,1,0:T(8,128)} %concatenate.27), channel_id=1, source_target_pairs={{0,40},{8,48},{16,56},{24,0},{32,8},{40,16},{48,24},{56,32},{64,10... | collective-permute-start | bytes 306440 | tf_op jit(solution)/shard_map/ppermute | solution.py:22
  50.3 23.0 %collective-permute-start.3 = (f32[2,112,114]{2,1,0:T(8,128)}, f32[2,112,114]{2,1,0:T(8,128)}, u32[]{:S(2)}, u32[]{:S(2)}) collective-permute-start(f32[2,112,114]{2,1,0:T(8,128)} %concatenate.27), channel_id=1, source_target_pairs={{0,32},{8,40},{16,48},{24,56},{32,0},{40,8},{48,16},{56,24},{64,96... | collective-permute-start | bytes 306440 | tf_op jit(solution)/shard_map/ppermute | solution.py:22
  52.8 18.7 %collective-permute-start.2 = (f32[2,112,114]{2,1,0:T(8,128)}, f32[2,112,114]{2,1,0:T(8,128)}, u32[]{:S(2)}, u32[]{:S(2)}) collective-permute-start(f32[2,112,114]{2,1,0:T(8,128)} %concatenate.27), channel_id=1, source_target_pairs={{0,24},{8,32},{16,40},{24,48},{32,56},{40,0},{48,8},{56,16},{64,88... | collective-permute-start | bytes 306440 | tf_op jit(solution)/shard_map/ppermute | solution.py:22
  88.8 11.1 %collective-permute-start.9 = (f32[2,2,112,114]{3,2,1,0:T(8,128)}, f32[2,2,112,114]{3,2,1,0:T(8,128)}, u32[]{:S(2)}, u32[]{:S(2)}) collective-permute-start(f32[2,2,112,114]{3,2,1,0:T(8,128)} %pad_maximum_fusion.3), channel_id=1, source_target_pairs={{0,192},{8,200},{16,208},{24,216},{32,224},{40,232},{48,240},{56,2... | collective-permute-start | bytes 612872 | tf_op jit(solution)/shard_map/ppermute | solution.py:32
  91.8 9.9 %collective-permute-start.8 = (f32[2,2,112,114]{3,2,1,0:T(8,128)}, f32[2,2,112,114]{3,2,1,0:T(8,128)}, u32[]{:S(2)}, u32[]{:S(2)}) collective-permute-start(f32[2,2,112,114]{3,2,1,0:T(8,128)} %pad_maximum_fusion.3), channel_id=1, source_target_pairs={{0,128},{8,136},{16,144},{24,152},{32,160},{40,168},{48,176},{56,1... | collective-permute-start | bytes 612872 | tf_op jit(solution)/shard_map/ppermute | solution.py:32
  92.4 11.1 %collective-permute-start.7 = (f32[2,2,112,114]{3,2,1,0:T(8,128)}, f32[2,2,112,114]{3,2,1,0:T(8,128)}, u32[]{:S(2)}, u32[]{:S(2)}) collective-permute-start(f32[2,2,112,114]{3,2,1,0:T(8,128)} %pad_maximum_fusion.3), channel_id=1, source_target_pairs={{0,64},{8,72},{16,80},{24,88},{32,96},{40,104},{48,112},{56,120},{... | collective-permute-start | bytes 612872 | tf_op jit(solution)/shard_map/ppermute | solution.py:32
  107.0 0.6 copy-start.5
  108.2 5.8 %collective-permute-start.11 = (f32[2,112,114]{2,1,0:T(8,128)S(1)}, f32[2,112,114]{2,1,0:T(8,128)S(1)}, u32[]{:S(2)}, u32[]{:S(2)}) collective-permute-start(f32[2,112,114]{2,1,0:T(8,128)S(1)} %concatenate.31), channel_id=1, source_target_pairs={{0,16},{8,24},{16,32},{24,40},{32,48},{40,56},{48,0},{56,8},{64,80... | collective-permute-start | bytes 306440 | tf_op jit(solution)/shard_map/ppermute | solution.py:22
  110.0 6.6 %collective-permute-start.10 = (f32[2,112,114]{2,1,0:T(8,128)S(1)}, f32[2,112,114]{2,1,0:T(8,128)S(1)}, u32[]{:S(2)}, u32[]{:S(2)}) collective-permute-start(f32[2,112,114]{2,1,0:T(8,128)S(1)} %concatenate.31), channel_id=1, source_target_pairs={{0,8},{8,16},{16,24},{24,32},{32,40},{40,48},{48,56},{56,0},{64,72... | collective-permute-start | bytes 306440 | tf_op jit(solution)/shard_map/ppermute | solution.py:22
  110.2 6.8 %copy-start.6 = (bf16[2,112,113]{2,1,0:T(8,128)(2,1)S(1)}, bf16[2,112,113]{2,1,0:T(8,128)(2,1)}, u32[]{:S(2)}) copy-start(bf16[2,112,113]{2,1,0:T(8,128)(2,1)} %copy-done.5) | copy-start | bytes 151876
  110.5 19.0 %collective-permute-start.16 = (f32[2,112,114]{2,1,0:T(8,128)S(1)}, f32[2,112,114]{2,1,0:T(8,128)S(1)}, u32[]{:S(2)}, u32[]{:S(2)}) collective-permute-start(f32[2,112,114]{2,1,0:T(8,128)S(1)} %concatenate.31), channel_id=1, source_target_pairs={{0,56},{8,0},{16,8},{24,16},{32,24},{40,32},{48,40},{56,48},{64,12... | collective-permute-start | bytes 306440 | tf_op jit(solution)/shard_map/ppermute | solution.py:22
  112.2 16.1 %collective-permute-start.15 = (f32[2,112,114]{2,1,0:T(8,128)S(1)}, f32[2,112,114]{2,1,0:T(8,128)S(1)}, u32[]{:S(2)}, u32[]{:S(2)}) collective-permute-start(f32[2,112,114]{2,1,0:T(8,128)S(1)} %concatenate.31), channel_id=1, source_target_pairs={{0,48},{8,56},{16,0},{24,8},{32,16},{40,24},{48,32},{56,40},{64,11... | collective-permute-start | bytes 306440 | tf_op jit(solution)/shard_map/ppermute | solution.py:22
  114.0 13.0 %collective-permute-start.14 = (f32[2,112,114]{2,1,0:T(8,128)S(1)}, f32[2,112,114]{2,1,0:T(8,128)S(1)}, u32[]{:S(2)}, u32[]{:S(2)}) collective-permute-start(f32[2,112,114]{2,1,0:T(8,128)S(1)} %concatenate.31), channel_id=1, source_target_pairs={{0,40},{8,48},{16,56},{24,0},{32,8},{40,16},{48,24},{56,32},{64,10... | collective-permute-start | bytes 306440 | tf_op jit(solution)/shard_map/ppermute | solution.py:22
  114.0 11.7 %collective-permute-start.13 = (f32[2,112,114]{2,1,0:T(8,128)S(1)}, f32[2,112,114]{2,1,0:T(8,128)S(1)}, u32[]{:S(2)}, u32[]{:S(2)}) collective-permute-start(f32[2,112,114]{2,1,0:T(8,128)S(1)} %concatenate.31), channel_id=1, source_target_pairs={{0,32},{8,40},{16,48},{24,56},{32,0},{40,8},{48,16},{56,24},{64,96... | collective-permute-start | bytes 306440 | tf_op jit(solution)/shard_map/ppermute | solution.py:22
  116.5 8.0 %collective-permute-start.12 = (f32[2,112,114]{2,1,0:T(8,128)S(1)}, f32[2,112,114]{2,1,0:T(8,128)S(1)}, u32[]{:S(2)}, u32[]{:S(2)}) collective-permute-start(f32[2,112,114]{2,1,0:T(8,128)S(1)} %concatenate.31), channel_id=1, source_target_pairs={{0,24},{8,32},{16,40},{24,48},{32,56},{40,0},{48,8},{56,16},{64,88... | collective-permute-start | bytes 306440 | tf_op jit(solution)/shard_map/ppermute | solution.py:22
  118.2 36.0 %all-to-all-start.2 = ((bf16[8,1,128,224]{2,3,1,0:T(8,128)(2,1)}), bf16[8,1,128,224]{2,3,1,0:T(8,128)(2,1)S(1)}, u32[]{:S(2)}, u32[]{:S(2)}) async-start(bf16[8,1,128,224]{2,3,1,0:T(8,128)(2,1)} %copy.47), calls=%async_computation.2 | async-start | bytes 917504 | tf_op jit(solution)/shard_map/all_to_all | solution.py:87
  135.3 14.1 %collective-permute-start.19 = (f32[2,2,112,114]{3,2,1,0:T(8,128)S(1)}, f32[2,2,112,114]{3,2,1,0:T(8,128)S(1)}, u32[]{:S(2)}, u32[]{:S(2)}) collective-permute-start(f32[2,2,112,114]{3,2,1,0:T(8,128)S(1)} %pad_maximum_fusion.4), channel_id=1, source_target_pairs={{0,192},{8,200},{16,208},{24,216},{32,224},{40,232},{48,240},{56,2... | collective-permute-start | bytes 612872 | tf_op jit(solution)/shard_map/ppermute | solution.py:32
  139.0 11.6 %collective-permute-start.18 = (f32[2,2,112,114]{3,2,1,0:T(8,128)S(1)}, f32[2,2,112,114]{3,2,1,0:T(8,128)S(1)}, u32[]{:S(2)}, u32[]{:S(2)}) collective-permute-start(f32[2,2,112,114]{3,2,1,0:T(8,128)S(1)} %pad_maximum_fusion.4), channel_id=1, source_target_pairs={{0,128},{8,136},{16,144},{24,152},{32,160},{40,168},{48,176},{56,1... | collective-permute-start | bytes 612872 | tf_op jit(solution)/shard_map/ppermute | solution.py:32
  139.0 13.7 %collective-permute-start.17 = (f32[2,2,112,114]{3,2,1,0:T(8,128)S(1)}, f32[2,2,112,114]{3,2,1,0:T(8,128)S(1)}, u32[]{:S(2)}, u32[]{:S(2)}) collective-permute-start(f32[2,2,112,114]{3,2,1,0:T(8,128)S(1)} %pad_maximum_fusion.4), channel_id=1, source_target_pairs={{0,64},{8,72},{16,80},{24,88},{32,96},{40,104},{48,112},{56,120},{... | collective-permute-start | bytes 612872 | tf_op jit(solution)/shard_map/ppermute | solution.py:32
  155.0 22.9 %all-to-all-start.3 = ((bf16[8,2,112,113]{3,2,1,0:T(8,128)(2,1)}), bf16[8,2,112,113]{3,2,1,0:T(8,128)(2,1)S(1)}, u32[]{:S(2)}, u32[]{:S(2)}) async-start(bf16[8,2,112,113]{3,2,1,0:T(8,128)(2,1)} %broadcast_in_dim.75), calls=%async_computation.3 | async-start | bytes 917504 | tf_op jit(solution)/shard_map/all_to_all | solution.py:121
  163.1 15.2 %copy-start.1 = (bf16[128,1792]{0,1:T(8,128)(2,1)S(1)}, bf16[128,1792]{0,1:T(8,128)(2,1)}, u32[]{:S(2)}) copy-start(bf16[128,1792]{0,1:T(8,128)(2,1)} %copy-done) | copy-start | bytes 1376260

commit v8 on v7

--- a/solution.py
+++ b/solution.py
@@ -1,5 +1,3 @@
-import functools
-
 import jax
 import jax.numpy as jnp
 from jax import lax
@@ -41,22 +39,24 @@
     tag = jnp.broadcast_to(flabel, part.shape[:-1] + (1,))
     packed = jnp.concatenate([part, tag], axis=-1)
     frames = [packed] + [shifted(packed, row, s) for s in range(1, row)]
-    labels = [f[0, 0, DH + 1] for f in frames]
+    tags = [f[..., DH + 1 :] for f in frames]
     states = [f[..., : DH + 1] for f in frames]
-    keep = [(l >= flabel) if later else (l <= flabel) for l in labels]
+    keep = [(t >= flabel) if later else (t <= flabel) for t in tags]
     seen = sum(jnp.where(k, s, 0.0) for k, s in zip(keep, states))
     if rows > 1:
-        edge = functools.reduce(jnp.maximum, labels) if later else functools.reduce(jnp.minimum, labels)
+        pick = jnp.maximum if later else jnp.minimum
+        edge = tags[0]
+        for t in tags[1:]:
+            edge = pick(edge, t)
         whole = sum(states)
-        edge_sum = sum(jnp.where(l == edge, s, 0.0) for l, s in zip(labels, states))
-        etag = jnp.broadcast_to(edge, part.shape[:-1] + (1,))
+        edge_sum = sum(jnp.where(t == edge, s, 0.0) for t, s in zip(tags, states))
         summary = jnp.stack(
-            [jnp.concatenate([whole, etag], -1), jnp.concatenate([edge_sum, etag], -1)]
+            [jnp.concatenate([whole, edge], -1), jnp.concatenate([edge_sum, edge], -1)]
         )
         for s in range(1, rows):
             got = strided(summary, row, s)
             source = (me - s) % rows
-            their_edge = got[1, 0, 0, DH + 1]
+            their_edge = got[1, ..., DH + 1 :]
             full = (source > me) if later else (source < me)
             part_only = ((source < me) if later else (source > me)) & (their_edge == flabel)
             seen = (

time: 184 us -> 154 us (0.84); the launches traced: 181 us -> 153 us
  between operations: 31.4 us -> 1.27 us
  waiting for transfers between devices: 62.2 us -> 80.4 us
  local copies, waits for them, and re-layouts: 31.6 us -> 15.6 us
  starting transfers between devices: 47.9 us -> 43 us
  other arithmetic: 6.05 us -> 10.8 us
    slice x20 -> x0, local copies, waits for them, and re-layouts: 17.7 us -> none  [the longest x14 12 us: visible(): labels = [f[0, 0, DH + 1] for f in frames]]
    ppermute x6, waiting for transfers between devices: 7.44 us -> 15.3 us  [strided(): return lax.ppermute(value, 'tm', pairs)]
    ppermute x14, waiting for transfers between devices: 0.92 us -> 8.37 us  [shifted(): return lax.ppermute(value, 'tm', pairs)]
    and x0 -> x6, other arithmetic: none -> 2.93 us  [visible(): part_only = (source < me if later else source > me) & (their_edge == flabel)]
    all_to_all x1, starting transfers between devices: 6.93 us -> 4.73 us  [local(): lax.all_to_all(copies, 'inner', 0, 0, tiled=True)]
    all_to_all x1, waiting for transfers between devices: 0.01 us -> 2.09 us  [to_rows(): returned = lax.all_to_all(leaving, 'inner', 0, 0, tiled=True)]
    unnamed x25 -> x61, local copies, waits for them, and re-layouts: 7.33 us -> 8 us
  transfers between devices with their start and end apart: 24 -> 24, of which waited for: 7 -> 15; matrix products, arithmetic and copies ran while one was open for 13% -> 8% of each run, Pallas kernels for 0% -> 0%
where the time goes in v8:
time: 154 us; the launch traced here: 153 us
  waiting for transfers between devices  80.4 us (52%)
  starting transfers between devices  43 us (28%)
  local copies, waits for them, and re-layouts  15.6 us (10%)
  other arithmetic  10.8 us (7%)
  matrix products  1.89 us (1%)
    all_to_all x2, waiting for transfers between devices, to_heads(): incoming = lax.all_to_all(outgoing, 'inner', 0, 0, tiled=True)  40 us
    ppermute x6, waiting for transfers between devices, strided(): return lax.ppermute(value, 'tm', pairs)  15.3 us
    ppermute x14, starting transfers between devices, shifted(): return lax.ppermute(value, 'tm', pairs)  14.7 us
    all_to_all x1, waiting for transfers between devices, local(): lax.all_to_all(copies, 'inner', 0, 0, tiled=True)  14.6 us
    all_to_all x2, starting transfers between devices, to_heads(): incoming = lax.all_to_all(outgoing, 'inner', 0, 0, tiled=True)  12.1 us
    ppermute x14, waiting for transfers between devices, shifted(): return lax.ppermute(value, 'tm', pairs)  8.37 us
    unnamed x61, local copies, waits for them, and re-layouts  8 us
    ppermute x6, starting transfers between devices, strided(): return lax.ppermute(value, 'tm', pairs)  7.63 us
  transfers between devices with their start and end apart: 24, of which 15 were waited for; matrix products, arithmetic and copies ran while one was open for 8% of the time, Pallas kernels for 0%

profile of v8, /device:TPU:2, one launch (start us, length us, event | category | flops | bytes accessed | tf_op | source)
XLA Modules:
  0.0 153.0 jit_solution(4322691389887745232)
XLA Ops:
  0.6 1.3 copy.41
  2.8 1.0 copy.42
  3.9 8.6 %all-to-all-start.1 = ((bf16[8,2,128,224]{2,3,1,0:T(8,128)(2,1)}), bf16[8,2,128,224]{2,3,1,0:T(8,128)(2,1)S(1)}, u32[]{:S(2)}, u32[]{:S(2)}) async-start(bf16[8,2,128,224]{2,3,1,0:T(8,128)(2,1)} %copy.42), calls=%async_computation.1 | async-start | bytes 1835008 | tf_op jit(solution)/shard_map/all_to_all | solution.py:80
  14.8 23.6 %all-to-all-done.1 = bf16[8,2,128,224]{2,3,1,0:T(8,128)(2,1)S(1)} async-done(((bf16[8,2,128,224]{2,3,1,0:T(8,128)(2,1)}), bf16[8,2,128,224]{2,3,1,0:T(8,128)(2,1)S(1)}, u32[]{:S(2)}, u32[]{:S(2)}) %all-to-all-start.1) | async-done | bytes 917536 | tf_op jit(solution)/shard_map/all_to_all | solution.py:80
  38.4 3.6 %all-to-all-start = ((bf16[8,2,128,224]{2,3,1,0:T(8,128)(2,1)}), bf16[8,2,128,224]{2,3,1,0:T(8,128)(2,1)S(1)}, u32[]{:S(2)}, u32[]{:S(2)}) async-start(bf16[8,2,128,224]{2,3,1,0:T(8,128)(2,1)} %copy.38), calls=%async_computation | async-start | bytes 1835008 | tf_op jit(solution)/shard_map/all_to_all | solution.py:80
  44.0 2.8 %collective-permute-start.5 = (f32[2,112,114]{2,1,0:T(8,128)S(1)}, f32[2,112,114]{2,1,0:T(8,128)S(1)}, u32[]{:S(2)}, u32[]{:S(2)}) collective-permute-start(f32[2,112,114]{2,1,0:T(8,128)S(1)} %concatenate.27), channel_id=1, source_target_pairs={{0,48},{8,56},{16,0},{24,8},{32,16},{40,24},{48,32},{56,40},{64,11... | collective-permute-start | bytes 306440 | tf_op jit(solution)/shard_map/ppermute | solution.py:20
  47.7 1.3 collective-permute-start.2
  49.0 2.1 %collective-permute-start.1 = (f32[2,112,114]{2,1,0:T(8,128)S(1)}, f32[2,112,114]{2,1,0:T(8,128)S(1)}, u32[]{:S(2)}, u32[]{:S(2)}) collective-permute-start(f32[2,112,114]{2,1,0:T(8,128)S(1)} %concatenate.27), channel_id=1, source_target_pairs={{0,16},{8,24},{16,32},{24,40},{32,48},{40,56},{48,0},{56,8},{64,80... | collective-permute-start | bytes 306440 | tf_op jit(solution)/shard_map/ppermute | solution.py:20
  51.8 16.5 %all-to-all-done = bf16[8,2,128,224]{2,3,1,0:T(8,128)(2,1)S(1)} async-done(((bf16[8,2,128,224]{2,3,1,0:T(8,128)(2,1)}), bf16[8,2,128,224]{2,3,1,0:T(8,128)(2,1)S(1)}, u32[]{:S(2)}, u32[]{:S(2)}) %all-to-all-start) | async-done | bytes 917536 | tf_op jit(solution)/shard_map/all_to_all | solution.py:80
  68.5 1.4 compare_reduce_fusion.29
  71.1 3.0 %collective-permute-start.9 = (f32[2,2,112,114]{3,2,1,0:T(8,128)}, f32[2,2,112,114]{3,2,1,0:T(8,128)}, u32[]{:S(2)}, u32[]{:S(2)}) collective-permute-start(f32[2,2,112,114]{3,2,1,0:T(8,128)} %pad_maximum_fusion.3), channel_id=1, source_target_pairs={{0,192},{8,200},{16,208},{24,216},{32,224},{40,232},{48,240},{56,2... | collective-permute-start | bytes 612872 | tf_op jit(solution)/shard_map/ppermute | solution.py:30
  76.2 1.2 copy.46
  79.3 2.8 %collective-permute-done.9 = f32[2,2,112,114]{3,2,1,0:T(8,128)} collective-permute-done((f32[2,2,112,114]{3,2,1,0:T(8,128)}, f32[2,2,112,114]{3,2,1,0:T(8,128)}, u32[]{:S(2)}, u32[]{:S(2)}) %collective-permute-start.9) | collective-permute-done | bytes 204320 | tf_op jit(solution)/shard_map/ppermute | solution.py:30
  82.1 1.1 fusion.47
  84.1 1.1 fusion.48
  85.2 1.5 collective-permute-done.7
  87.6 1.4 fusion.27
  90.4 1.1 collective-permute-start.15
  91.4 1.7 %collective-permute-start.14 = (f32[2,112,114]{2,1,0:T(8,128)S(1)}, f32[2,112,114]{2,1,0:T(8,128)S(1)}, u32[]{:S(2)}, u32[]{:S(2)}) collective-permute-start(f32[2,112,114]{2,1,0:T(8,128)S(1)} %concatenate.31), channel_id=1, source_target_pairs={{0,40},{8,48},{16,56},{24,0},{32,8},{40,16},{48,24},{56,32},{64,10... | collective-permute-start | bytes 306440 | tf_op jit(solution)/shard_map/ppermute | solution.py:20
  93.1 1.1 collective-permute-start.13
  94.2 1.2 collective-permute-start.12
  95.5 1.8 %collective-permute-start.11 = (f32[2,112,114]{2,1,0:T(8,128)S(1)}, f32[2,112,114]{2,1,0:T(8,128)S(1)}, u32[]{:S(2)}, u32[]{:S(2)}) collective-permute-start(f32[2,112,114]{2,1,0:T(8,128)S(1)} %concatenate.31), channel_id=1, source_target_pairs={{0,16},{8,24},{16,32},{24,40},{32,48},{40,56},{48,0},{56,8},{64,80... | collective-permute-start | bytes 306440 | tf_op jit(solution)/shard_map/ppermute | solution.py:20
  98.8 4.7 %collective-permute-done.13 = f32[2,112,114]{2,1,0:T(8,128)S(1)} collective-permute-done((f32[2,112,114]{2,1,0:T(8,128)S(1)}, f32[2,112,114]{2,1,0:T(8,128)S(1)}, u32[]{:S(2)}, u32[]{:S(2)}) %collective-permute-start.13) | collective-permute-done | bytes 102176 | tf_op jit(solution)/shard_map/ppermute | solution.py:20
  103.8 1.8 %collective-permute-done.11 = f32[2,112,114]{2,1,0:T(8,128)S(1)} collective-permute-done((f32[2,112,114]{2,1,0:T(8,128)S(1)}, f32[2,112,114]{2,1,0:T(8,128)S(1)}, u32[]{:S(2)}, u32[]{:S(2)}) %collective-permute-start.11) | collective-permute-done | bytes 102176 | tf_op jit(solution)/shard_map/ppermute | solution.py:20
  107.3 1.5 collective-permute-start.19
  110.0 3.8 %all-to-all-start.2 = ((bf16[8,1,128,224]{2,3,1,0:T(8,128)(2,1)}), bf16[8,1,128,224]{2,3,1,0:T(8,128)(2,1)S(1)}, u32[]{:S(2)}, u32[]{:S(2)}) async-start(bf16[8,1,128,224]{2,3,1,0:T(8,128)(2,1)} %copy.47), calls=%async_computation.2 | async-start | bytes 917504 | tf_op jit(solution)/shard_map/all_to_all | solution.py:87
  113.8 1.5 %collective-permute-start.17 = (f32[2,2,112,114]{3,2,1,0:T(8,128)S(1)}, f32[2,2,112,114]{3,2,1,0:T(8,128)S(1)}, u32[]{:S(2)}, u32[]{:S(2)}) collective-permute-start(f32[2,2,112,114]{3,2,1,0:T(8,128)S(1)} %pad_maximum_fusion.4), channel_id=1, source_target_pairs={{0,64},{8,72},{16,80},{24,88},{32,96},{40,104},{48,112},{56,120},{... | collective-permute-start | bytes 612872 | tf_op jit(solution)/shard_map/ppermute | solution.py:30
  115.5 8.1 %collective-permute-done.18 = f32[2,2,112,114]{3,2,1,0:T(8,128)S(1)} collective-permute-done((f32[2,2,112,114]{3,2,1,0:T(8,128)S(1)}, f32[2,2,112,114]{3,2,1,0:T(8,128)S(1)}, u32[]{:S(2)}, u32[]{:S(2)}) %collective-permute-start.18) | collective-permute-done | bytes 204320 | tf_op jit(solution)/shard_map/ppermute | solution.py:30
  123.8 2.0 %collective-permute-done.17 = f32[2,2,112,114]{3,2,1,0:T(8,128)S(1)} collective-permute-done((f32[2,2,112,114]{3,2,1,0:T(8,128)S(1)}, f32[2,2,112,114]{3,2,1,0:T(8,128)S(1)}, u32[]{:S(2)}, u32[]{:S(2)}) %collective-permute-start.17) | collective-permute-done | bytes 204320 | tf_op jit(solution)/shard_map/ppermute | solution.py:30
  126.5 2.1 %all-to-all-done.2 = bf16[8,1,128,224]{2,3,1,0:T(8,128)(2,1)S(1)} async-done(((bf16[8,1,128,224]{2,3,1,0:T(8,128)(2,1)}), bf16[8,1,128,224]{2,3,1,0:T(8,128)(2,1)S(1)}, u32[]{:S(2)}, u32[]{:S(2)}) %all-to-all-start.2) | async-done | bytes 458784 | tf_op jit(solution)/shard_map/all_to_all | solution.py:87
  129.4 4.7 %all-to-all-start.3 = ((bf16[8,2,112,113]{3,2,1,0:T(8,128)(2,1)}), bf16[8,2,112,113]{3,2,1,0:T(8,128)(2,1)S(1)}, u32[]{:S(2)}, u32[]{:S(2)}) async-start(bf16[8,2,112,113]{3,2,1,0:T(8,128)(2,1)} %broadcast_in_dim.401), calls=%async_computation.3 | async-start | bytes 917504 | tf_op jit(solution)/shard_map/all_to_all | solution.py:121
  135.3 14.6 %all-to-all-done.3 = bf16[8,2,112,113]{3,2,1,0:T(8,128)(2,1)S(1)} async-done(((bf16[8,2,112,113]{3,2,1,0:T(8,128)(2,1)}), bf16[8,2,112,113]{3,2,1,0:T(8,128)(2,1)S(1)}, u32[]{:S(2)}, u32[]{:S(2)}) %all-to-all-start.3) | async-done | bytes 405024 | tf_op jit(solution)/shard_map/all_to_all | solution.py:121
  (130 shorter events, 25.7 us)
Async XLA Ops:
  3.9 8.6 %copy-start.14 = (bf16[128,1792]{1,0:T(8,128)(2,1)S(1)}, bf16[128,1792]{1,0:T(8,128)(2,1)}, u32[]{:S(2)}) copy-start(bf16[128,1792]{1,0:T(8,128)(2,1)} %param.8) | copy-start | bytes 1376260
  3.9 34.5 %all-to-all-start.1 = ((bf16[8,2,128,224]{2,3,1,0:T(8,128)(2,1)}), bf16[8,2,128,224]{2,3,1,0:T(8,128)(2,1)S(1)}, u32[]{:S(2)}, u32[]{:S(2)}) async-start(bf16[8,2,128,224]{2,3,1,0:T(8,128)(2,1)} %copy.42), calls=%async_computation.1 | async-start | bytes 1835008 | tf_op jit(solution)/shard_map/all_to_all | solution.py:80
  38.4 29.9 %all-to-all-start = ((bf16[8,2,128,224]{2,3,1,0:T(8,128)(2,1)}), bf16[8,2,128,224]{2,3,1,0:T(8,128)(2,1)S(1)}, u32[]{:S(2)}, u32[]{:S(2)}) async-start(bf16[8,2,128,224]{2,3,1,0:T(8,128)(2,1)} %copy.38), calls=%async_computation | async-start | bytes 1835008 | tf_op jit(solution)/shard_map/all_to_all | solution.py:80
  43.8 5.2 %collective-permute-start.6 = (f32[2,112,114]{2,1,0:T(8,128)S(1)}, f32[2,112,114]{2,1,0:T(8,128)S(1)}, u32[]{:S(2)}, u32[]{:S(2)}) collective-permute-start(f32[2,112,114]{2,1,0:T(8,128)S(1)} %concatenate.27), channel_id=1, source_target_pairs={{0,56},{8,0},{16,8},{24,16},{32,24},{40,32},{48,40},{56,48},{64,12... | collective-permute-start | bytes 306440 | tf_op jit(solution)/shard_map/ppermute | solution.py:20
  44.0 7.4 %collective-permute-start.5 = (f32[2,112,114]{2,1,0:T(8,128)S(1)}, f32[2,112,114]{2,1,0:T(8,128)S(1)}, u32[]{:S(2)}, u32[]{:S(2)}) collective-permute-start(f32[2,112,114]{2,1,0:T(8,128)S(1)} %concatenate.27), channel_id=1, source_target_pairs={{0,48},{8,56},{16,0},{24,8},{32,16},{40,24},{48,32},{56,40},{64,11... | collective-permute-start | bytes 306440 | tf_op jit(solution)/shard_map/ppermute | solution.py:20
  46.7 21.6 %collective-permute-start.4 = (f32[2,112,114]{2,1,0:T(8,128)S(1)}, f32[2,112,114]{2,1,0:T(8,128)S(1)}, u32[]{:S(2)}, u32[]{:S(2)}) collective-permute-start(f32[2,112,114]{2,1,0:T(8,128)S(1)} %concatenate.27), channel_id=1, source_target_pairs={{0,40},{8,48},{16,56},{24,0},{32,8},{40,16},{48,24},{56,32},{64,10... | collective-permute-start | bytes 306440 | tf_op jit(solution)/shard_map/ppermute | solution.py:20
  46.7 21.6 %collective-permute-start.3 = (f32[2,112,114]{2,1,0:T(8,128)S(1)}, f32[2,112,114]{2,1,0:T(8,128)S(1)}, u32[]{:S(2)}, u32[]{:S(2)}) collective-permute-start(f32[2,112,114]{2,1,0:T(8,128)S(1)} %concatenate.27), channel_id=1, source_target_pairs={{0,32},{8,40},{16,48},{24,56},{32,0},{40,8},{48,16},{56,24},{64,96... | collective-permute-start | bytes 306440 | tf_op jit(solution)/shard_map/ppermute | solution.py:20
  47.7 20.6 %collective-permute-start.2 = (f32[2,112,114]{2,1,0:T(8,128)S(1)}, f32[2,112,114]{2,1,0:T(8,128)S(1)}, u32[]{:S(2)}, u32[]{:S(2)}) collective-permute-start(f32[2,112,114]{2,1,0:T(8,128)S(1)} %concatenate.27), channel_id=1, source_target_pairs={{0,24},{8,32},{16,40},{24,48},{32,56},{40,0},{48,8},{56,16},{64,88... | collective-permute-start | bytes 306440 | tf_op jit(solution)/shard_map/ppermute | solution.py:20
  49.0 19.3 %collective-permute-start.1 = (f32[2,112,114]{2,1,0:T(8,128)S(1)}, f32[2,112,114]{2,1,0:T(8,128)S(1)}, u32[]{:S(2)}, u32[]{:S(2)}) collective-permute-start(f32[2,112,114]{2,1,0:T(8,128)S(1)} %concatenate.27), channel_id=1, source_target_pairs={{0,16},{8,24},{16,32},{24,40},{32,48},{40,56},{48,0},{56,8},{64,80... | collective-permute-start | bytes 306440 | tf_op jit(solution)/shard_map/ppermute | solution.py:20
  51.4 17.0 %collective-permute-start = (f32[2,112,114]{2,1,0:T(8,128)S(1)}, f32[2,112,114]{2,1,0:T(8,128)S(1)}, u32[]{:S(2)}, u32[]{:S(2)}) collective-permute-start(f32[2,112,114]{2,1,0:T(8,128)S(1)} %concatenate.27), channel_id=1, source_target_pairs={{0,8},{8,16},{16,24},{24,32},{32,40},{40,48},{48,56},{56,0},{64,72... | collective-permute-start | bytes 306440 | tf_op jit(solution)/shard_map/ppermute | solution.py:20
  68.3 1.6 %copy-start.2 = (f32[2,112,114]{2,1,0:T(8,128)}, f32[2,112,114]{2,1,0:T(8,128)S(1)}, u32[]{:S(2)}) copy-start(f32[2,112,114]{2,1,0:T(8,128)S(1)} %collective-permute-done.4) | copy-start | bytes 306436
  71.1 11.1 %collective-permute-start.9 = (f32[2,2,112,114]{3,2,1,0:T(8,128)}, f32[2,2,112,114]{3,2,1,0:T(8,128)}, u32[]{:S(2)}, u32[]{:S(2)}) collective-permute-start(f32[2,2,112,114]{3,2,1,0:T(8,128)} %pad_maximum_fusion.3), channel_id=1, source_target_pairs={{0,192},{8,200},{16,208},{24,216},{32,224},{40,232},{48,240},{56,2... | collective-permute-start | bytes 612872 | tf_op jit(solution)/shard_map/ppermute | solution.py:30
  74.1 10.1 %collective-permute-start.8 = (f32[2,2,112,114]{3,2,1,0:T(8,128)}, f32[2,2,112,114]{3,2,1,0:T(8,128)}, u32[]{:S(2)}, u32[]{:S(2)}) collective-permute-start(f32[2,2,112,114]{3,2,1,0:T(8,128)} %pad_maximum_fusion.3), channel_id=1, source_target_pairs={{0,128},{8,136},{16,144},{24,152},{32,160},{40,168},{48,176},{56,1... | collective-permute-start | bytes 612872 | tf_op jit(solution)/shard_map/ppermute | solution.py:30
  77.4 9.6 %copy-start.9 = (f32[2,112,114]{2,1,0:T(8,128)S(1)}, f32[2,112,114]{2,1,0:T(8,128)}, u32[]{:S(2)}) copy-start(f32[2,112,114]{2,1,0:T(8,128)} %copy-done.8) | copy-start | bytes 306436
  77.4 9.6 %copy-start.11 = (f32[2,112,114]{2,1,0:T(8,128)S(1)}, f32[2,112,114]{2,1,0:T(8,128)}, u32[]{:S(2)}) copy-start(f32[2,112,114]{2,1,0:T(8,128)} %copy-done.10) | copy-start | bytes 306436
  78.4 8.4 %collective-permute-start.7 = (f32[2,2,112,114]{3,2,1,0:T(8,128)}, f32[2,2,112,114]{3,2,1,0:T(8,128)S(1)}, u32[]{:S(2)}, u32[]{:S(2)}) collective-permute-start(f32[2,2,112,114]{3,2,1,0:T(8,128)} %pad_maximum_fusion.3), channel_id=1, source_target_pairs={{0,64},{8,72},{16,80},{24,88},{32,96},{40,104},{48,112},{56,120},{... | collective-permute-start | bytes 612872 | tf_op jit(solution)/shard_map/ppermute | solution.py:30
  82.1 4.9 %copy-start.7 = (f32[2,112,114]{2,1,0:T(8,128)S(1)}, f32[2,112,114]{2,1,0:T(8,128)}, u32[]{:S(2)}) copy-start(f32[2,112,114]{2,1,0:T(8,128)} %copy-done.6) | copy-start | bytes 306436
  83.3 3.8 %copy-start.3 = (f32[2,112,114]{2,1,0:T(8,128)S(1)}, f32[2,112,114]{2,1,0:T(8,128)}, u32[]{:S(2)}) copy-start(f32[2,112,114]{2,1,0:T(8,128)} %copy-done.2) | copy-start | bytes 306436
  83.3 3.8 %copy-start.5 = (f32[2,112,114]{2,1,0:T(8,128)S(1)}, f32[2,112,114]{2,1,0:T(8,128)}, u32[]{:S(2)}) copy-start(f32[2,112,114]{2,1,0:T(8,128)} %copy-done.4) | copy-start | bytes 306436
  90.3 5.1 %collective-permute-start.16 = (f32[2,112,114]{2,1,0:T(8,128)S(1)}, f32[2,112,114]{2,1,0:T(8,128)S(1)}, u32[]{:S(2)}, u32[]{:S(2)}) collective-permute-start(f32[2,112,114]{2,1,0:T(8,128)S(1)} %concatenate.31), channel_id=1, source_target_pairs={{0,56},{8,0},{16,8},{24,16},{32,24},{40,32},{48,40},{56,48},{64,12... | collective-permute-start | bytes 306440 | tf_op jit(solution)/shard_map/ppermute | solution.py:20
  90.4 7.8 %collective-permute-start.15 = (f32[2,112,114]{2,1,0:T(8,128)S(1)}, f32[2,112,114]{2,1,0:T(8,128)S(1)}, u32[]{:S(2)}, u32[]{:S(2)}) collective-permute-start(f32[2,112,114]{2,1,0:T(8,128)S(1)} %concatenate.31), channel_id=1, source_target_pairs={{0,48},{8,56},{16,0},{24,8},{32,16},{40,24},{48,32},{56,40},{64,11... | collective-permute-start | bytes 306440 | tf_op jit(solution)/shard_map/ppermute | solution.py:20
  91.4 7.4 %collective-permute-start.14 = (f32[2,112,114]{2,1,0:T(8,128)S(1)}, f32[2,112,114]{2,1,0:T(8,128)S(1)}, u32[]{:S(2)}, u32[]{:S(2)}) collective-permute-start(f32[2,112,114]{2,1,0:T(8,128)S(1)} %concatenate.31), channel_id=1, source_target_pairs={{0,40},{8,48},{16,56},{24,0},{32,8},{40,16},{48,24},{56,32},{64,10... | collective-permute-start | bytes 306440 | tf_op jit(solution)/shard_map/ppermute | solution.py:20
  93.1 10.4 %collective-permute-start.13 = (f32[2,112,114]{2,1,0:T(8,128)S(1)}, f32[2,112,114]{2,1,0:T(8,128)S(1)}, u32[]{:S(2)}, u32[]{:S(2)}) collective-permute-start(f32[2,112,114]{2,1,0:T(8,128)S(1)} %concatenate.31), channel_id=1, source_target_pairs={{0,32},{8,40},{16,48},{24,56},{32,0},{40,8},{48,16},{56,24},{64,96... | collective-permute-start | bytes 306440 | tf_op jit(solution)/shard_map/ppermute | solution.py:20
  94.2 9.6 %collective-permute-start.12 = (f32[2,112,114]{2,1,0:T(8,128)S(1)}, f32[2,112,114]{2,1,0:T(8,128)S(1)}, u32[]{:S(2)}, u32[]{:S(2)}) collective-permute-start(f32[2,112,114]{2,1,0:T(8,128)S(1)} %concatenate.31), channel_id=1, source_target_pairs={{0,24},{8,32},{16,40},{24,48},{32,56},{40,0},{48,8},{56,16},{64,88... | collective-permute-start | bytes 306440 | tf_op jit(solution)/shard_map/ppermute | solution.py:20
  95.5 10.2 %collective-permute-start.11 = (f32[2,112,114]{2,1,0:T(8,128)S(1)}, f32[2,112,114]{2,1,0:T(8,128)S(1)}, u32[]{:S(2)}, u32[]{:S(2)}) collective-permute-start(f32[2,112,114]{2,1,0:T(8,128)S(1)} %concatenate.31), channel_id=1, source_target_pairs={{0,16},{8,24},{16,32},{24,40},{32,48},{40,56},{48,0},{56,8},{64,80... | collective-permute-start | bytes 306440 | tf_op jit(solution)/shard_map/ppermute | solution.py:20
  98.2 7.7 %collective-permute-start.10 = (f32[2,112,114]{2,1,0:T(8,128)S(1)}, f32[2,112,114]{2,1,0:T(8,128)S(1)}, u32[]{:S(2)}, u32[]{:S(2)}) collective-permute-start(f32[2,112,114]{2,1,0:T(8,128)S(1)} %concatenate.31), channel_id=1, source_target_pairs={{0,8},{8,16},{16,24},{24,32},{32,40},{40,48},{48,56},{56,0},{64,72... | collective-permute-start | bytes 306440 | tf_op jit(solution)/shard_map/ppermute | solution.py:20
  107.3 8.0 %collective-permute-start.19 = (f32[2,2,112,114]{3,2,1,0:T(8,128)S(1)}, f32[2,2,112,114]{3,2,1,0:T(8,128)S(1)}, u32[]{:S(2)}, u32[]{:S(2)}) collective-permute-start(f32[2,2,112,114]{3,2,1,0:T(8,128)S(1)} %pad_maximum_fusion.4), channel_id=1, source_target_pairs={{0,192},{8,200},{16,208},{24,216},{32,224},{40,232},{48,240},{56,2... | collective-permute-start | bytes 612872 | tf_op jit(solution)/shard_map/ppermute | solution.py:30
  110.0 18.6 %all-to-all-start.2 = ((bf16[8,1,128,224]{2,3,1,0:T(8,128)(2,1)}), bf16[8,1,128,224]{2,3,1,0:T(8,128)(2,1)S(1)}, u32[]{:S(2)}, u32[]{:S(2)}) async-start(bf16[8,1,128,224]{2,3,1,0:T(8,128)(2,1)} %copy.47), calls=%async_computation.2 | async-start | bytes 917504 | tf_op jit(solution)/shard_map/all_to_all | solution.py:87
  113.8 9.8 %collective-permute-start.18 = (f32[2,2,112,114]{3,2,1,0:T(8,128)S(1)}, f32[2,2,112,114]{3,2,1,0:T(8,128)S(1)}, u32[]{:S(2)}, u32[]{:S(2)}) collective-permute-start(f32[2,2,112,114]{3,2,1,0:T(8,128)S(1)} %pad_maximum_fusion.4), channel_id=1, source_target_pairs={{0,128},{8,136},{16,144},{24,152},{32,160},{40,168},{48,176},{56,1... | collective-permute-start | bytes 612872 | tf_op jit(solution)/shard_map/ppermute | solution.py:30
  113.8 12.0 %collective-permute-start.17 = (f32[2,2,112,114]{3,2,1,0:T(8,128)S(1)}, f32[2,2,112,114]{3,2,1,0:T(8,128)S(1)}, u32[]{:S(2)}, u32[]{:S(2)}) collective-permute-start(f32[2,2,112,114]{3,2,1,0:T(8,128)S(1)} %pad_maximum_fusion.4), channel_id=1, source_target_pairs={{0,64},{8,72},{16,80},{24,88},{32,96},{40,104},{48,112},{56,120},{... | collective-permute-start | bytes 612872 | tf_op jit(solution)/shard_map/ppermute | solution.py:30
  129.4 20.5 %all-to-all-start.3 = ((bf16[8,2,112,113]{3,2,1,0:T(8,128)(2,1)}), bf16[8,2,112,113]{3,2,1,0:T(8,128)(2,1)S(1)}, u32[]{:S(2)}, u32[]{:S(2)}) async-start(bf16[8,2,112,113]{3,2,1,0:T(8,128)(2,1)} %broadcast_in_dim.401), calls=%async_computation.3 | async-start | bytes 917504 | tf_op jit(solution)/shard_map/all_to_all | solution.py:121
  135.3 15.0 %copy-start.1 = (bf16[128,1792]{0,1:T(8,128)(2,1)S(1)}, bf16[128,1792]{0,1:T(8,128)(2,1)}, u32[]{:S(2)}) copy-start(bf16[128,1792]{0,1:T(8,128)(2,1)} %copy-done) | copy-start | bytes 1376260
  (18 other events, 18.3 us)

commit v9 on v8

--- a/solution.py
+++ b/solution.py
@@ -38,32 +38,36 @@
     flabel = label.astype(jnp.float32)
     tag = jnp.broadcast_to(flabel, part.shape[:-1] + (1,))
     packed = jnp.concatenate([part, tag], axis=-1)
-    frames = [packed] + [shifted(packed, row, s) for s in range(1, row)]
-    tags = [f[..., DH + 1 :] for f in frames]
-    states = [f[..., : DH + 1] for f in frames]
-    keep = [(t >= flabel) if later else (t <= flabel) for t in tags]
-    seen = sum(jnp.where(k, s, 0.0) for k, s in zip(keep, states))
+    in_row = [list(range(base, base + row)) for base in range(0, total, row)]
+    frames = lax.all_to_all(
+        jnp.broadcast_to(packed[None], (row,) + packed.shape),
+        "tm", 0, 0, tiled=True, axis_index_groups=in_row,
+    )
+    tags = frames[..., DH + 1 :]
+    states = frames[..., : DH + 1]
+    keep = (tags >= flabel) if later else (tags <= flabel)
+    seen = jnp.sum(jnp.where(keep, states, 0.0), axis=0)
     if rows > 1:
-        pick = jnp.maximum if later else jnp.minimum
-        edge = tags[0]
-        for t in tags[1:]:
-            edge = pick(edge, t)
-        whole = sum(states)
-        edge_sum = sum(jnp.where(t == edge, s, 0.0) for t, s in zip(tags, states))
+        edge = jnp.max(tags, axis=0) if later else jnp.min(tags, axis=0)
+        whole = jnp.sum(states, axis=0)
+        edge_sum = jnp.sum(jnp.where(tags == edge[None], states, 0.0), axis=0)
         summary = jnp.stack(
             [jnp.concatenate([whole, edge], -1), jnp.concatenate([edge_sum, edge], -1)]
         )
-        for s in range(1, rows):
-            got = strided(summary, row, s)
-            source = (me - s) % rows
-            their_edge = got[1, ..., DH + 1 :]
-            full = (source > me) if later else (source < me)
-            part_only = ((source < me) if later else (source > me)) & (their_edge == flabel)
-            seen = (
-                seen
-                + jnp.where(full, got[0, ..., : DH + 1], 0.0)
-                + jnp.where(part_only, got[1, ..., : DH + 1], 0.0)
-            )
+        across = [list(range(j, total, row)) for j in range(row)]
+        got = lax.all_to_all(
+            jnp.broadcast_to(summary[None], (rows,) + summary.shape),
+            "tm", 0, 0, tiled=True, axis_index_groups=across,
+        )
+        source = jnp.arange(rows).reshape(rows, 1, 1, 1)
+        their_edge = got[:, 1, ..., DH + 1 :]
+        full = (source > me) if later else (source < me)
+        part_only = ((source < me) if later else (source > me)) & (their_edge == flabel)
+        seen = seen + jnp.sum(
+            jnp.where(full, got[:, 0, ..., : DH + 1], 0.0)
+            + jnp.where(part_only, got[:, 1, ..., : DH + 1], 0.0),
+            axis=0,
+        )
     return seen.astype(jnp.bfloat16)
 
 

time: 154 us -> 186 us (1.21)
  waiting for transfers between devices: 80.4 us -> 104 us
  blocking collectives: 0 us -> 17.1 us
  starting transfers between devices: 43 us -> 32.2 us
  local copies, waits for them, and re-layouts: 15.6 us -> 24.1 us
  other arithmetic: 10.8 us -> 4.61 us
    all_to_all x0 -> x3, waiting for transfers between devices: none -> 27.9 us  [the longest x2 17.1 us: visible(): lax.all_to_all(jnp.broadcast_to(summary[None], (rows,) + summary.shape),...]
    ppermute x20 -> x0, waiting for transfers between devices: 23.6 us -> none  [the longest x6 15.3 us: strided(): return lax.ppermute(value, 'tm', pairs)]
    ppermute x20 -> x0, starting transfers between devices: 22.3 us -> none  [the longest x14 14.7 us: shifted(): return lax.ppermute(value, 'tm', pairs)]
    all_to_all x0 -> x1, blocking collectives: none -> 17.1 us  [visible(): lax.all_to_all(jnp.broadcast_to(packed[None], (row,) + packed.shape), 'tm...]
    all_to_all x0 -> x3, starting transfers between devices: none -> 12.9 us  [the longest x2 7.97 us: visible(): lax.all_to_all(jnp.broadcast_to(summary[None], (rows,) + summary.shape),...]
    all_to_all x1, waiting for transfers between devices: 2.09 us -> 14.1 us  [to_rows(): returned = lax.all_to_all(leaving, 'inner', 0, 0, tiled=True)]
    all_to_all x2, waiting for transfers between devices: 40 us -> 49.4 us  [to_heads(): incoming = lax.all_to_all(outgoing, 'inner', 0, 0, tiled=True)]
    broadcast_in_dim x0 -> x8, local copies, waits for them, and re-layouts: none -> 3.11 us  [the longest x2 1.98 us: visible(): jnp.broadcast_to(summary[None], (rows,) + summary.shape)]
  transfers between devices with their start and end apart: 24 -> 7, of which waited for: 15 -> 7; matrix products, arithmetic and copies ran while one was open for 8% -> 7% of each run, Pallas kernels for 0% -> 0%
where the time goes in v9:
time: 186 us; the launch traced here: 185 us
  waiting for transfers between devices  104 us (56%)
  starting transfers between devices  32.2 us (17%)
  local copies, waits for them, and re-layouts  24.1 us (13%)
  blocking collectives  17.1 us (9%)
  other arithmetic  4.61 us (2%)
  matrix products  1.89 us (1%)
    all_to_all x2, waiting for transfers between devices, to_heads(): incoming = lax.all_to_all(outgoing, 'inner', 0, 0, tiled=True)  49.4 us
    all_to_all x2, waiting for transfers between devices, visible(): lax.all_to_all(jnp.broadcast_to(summary[None], (rows,) + summary.shape),...  17.1 us
    all_to_all x1, blocking collectives, visible(): lax.all_to_all(jnp.broadcast_to(packed[None], (row,) + packed.shape), 'tm...  17.1 us
    all_to_all x1, waiting for transfers between devices, to_rows(): returned = lax.all_to_all(leaving, 'inner', 0, 0, tiled=True)  14.1 us
    all_to_all x1, waiting for transfers between devices, local(): lax.all_to_all(copies, 'inner', 0, 0, tiled=True)  12.5 us
    all_to_all x2, starting transfers between devices, to_heads(): incoming = lax.all_to_all(outgoing, 'inner', 0, 0, tiled=True)  12 us
    all_to_all x1, waiting for transfers between devices, visible(): lax.all_to_all(jnp.broadcast_to(packed[None], (row,) + packed.shape), 'tm...  10.7 us
    unnamed x33, local copies, waits for them, and re-layouts  10.1 us
  transfers between devices with their start and end apart: 7, of which 7 were waited for; matrix products, arithmetic and copies ran while one was open for 7% of the time, Pallas kernels for 0%

profile of v9, /device:TPU:2, one launch (start us, length us, event | category | flops | bytes accessed | tf_op | source)
XLA Modules:
  0.0 184.9 jit_solution(10668431477906670805)
XLA Ops:
  0.6 1.3 copy.95
  2.8 1.0 copy.96
  3.8 8.5 %all-to-all-start.1 = ((bf16[8,2,128,224]{2,3,1,0:T(8,128)(2,1)}), bf16[8,2,128,224]{2,3,1,0:T(8,128)(2,1)S(1)}, u32[]{:S(2)}, u32[]{:S(2)}) async-start(bf16[8,2,128,224]{2,3,1,0:T(8,128)(2,1)} %copy.96), calls=%async_computation.1 | async-start | bytes 1835008 | tf_op jit(solution)/shard_map/all_to_all | solution.py:84
  13.0 25.2 %all-to-all-done.1 = bf16[8,2,128,224]{2,3,1,0:T(8,128)(2,1)S(1)} async-done(((bf16[8,2,128,224]{2,3,1,0:T(8,128)(2,1)}), bf16[8,2,128,224]{2,3,1,0:T(8,128)(2,1)S(1)}, u32[]{:S(2)}, u32[]{:S(2)}) %all-to-all-start.1) | async-done | bytes 917536 | tf_op jit(solution)/shard_map/all_to_all | solution.py:84
  39.4 1.0 broadcast_in_dim.119
  40.4 5.0 %all-to-all-start.2 = ((f32[8,2,112,114]{3,2,1,0:T(8,128)}), f32[8,2,112,114]{3,2,1,0:T(8,128)S(1)}, u32[]{:S(2)}, u32[]{:S(2)}) async-start(f32[8,2,112,114]{3,2,1,0:T(8,128)} %broadcast_in_dim.119), calls=%async_computation.2 | async-start | bytes 1835008 | tf_op jit(solution)/shard_map/all_to_all | solution.py:42
  45.6 0.8 copy-done.5
  46.7 1.0 copy.92
  47.7 10.7 %all-to-all-done.2 = f32[8,2,112,114]{3,2,1,0:T(8,128)S(1)} async-done(((f32[8,2,112,114]{3,2,1,0:T(8,128)}), f32[8,2,112,114]{3,2,1,0:T(8,128)S(1)}, u32[]{:S(2)}, u32[]{:S(2)}) %all-to-all-start.2) | async-done | bytes 817184 | tf_op jit(solution)/shard_map/all_to_all | solution.py:42
  58.5 3.6 %all-to-all-start = ((bf16[8,2,128,224]{2,3,1,0:T(8,128)(2,1)}), bf16[8,2,128,224]{2,3,1,0:T(8,128)(2,1)S(1)}, u32[]{:S(2)}, u32[]{:S(2)}) async-start(bf16[8,2,128,224]{2,3,1,0:T(8,128)(2,1)} %copy.92), calls=%async_computation | async-start | bytes 1835008 | tf_op jit(solution)/shard_map/all_to_all | solution.py:84
  63.7 24.2 %all-to-all-done = bf16[8,2,128,224]{2,3,1,0:T(8,128)(2,1)S(1)} async-done(((bf16[8,2,128,224]{2,3,1,0:T(8,128)(2,1)}), bf16[8,2,128,224]{2,3,1,0:T(8,128)(2,1)S(1)}, u32[]{:S(2)}, u32[]{:S(2)}) %all-to-all-start) | async-done | bytes 917536 | tf_op jit(solution)/shard_map/all_to_all | solution.py:84
  88.0 1.0 broadcast_in_dim.126
  88.9 4.5 %all-to-all-start.3 = ((f32[4,2,2,112,114]{4,3,2,1,0:T(8,128)}), f32[4,2,2,112,114]{4,3,2,1,0:T(8,128)S(1)}, u32[]{:S(2)}, u32[]{:S(2)}) async-start(f32[4,2,2,112,114]{4,3,2,1,0:T(8,128)} %broadcast_in_dim.126), calls=%async_computation.3 | async-start | bytes 1835008 | tf_op jit(solution)/shard_map/all_to_all | solution.py:58
  93.5 1.5 copy.111
  95.0 1.3 mul.22
  96.3 0.9 copy.112
  97.3 2.0 %max.21 = bf16[1024,2,112]{0,2,1:T(8,128)(2,1)} reshape(bf16[1,8,128,224]{2,1,3,0:T(8,128)(2,1)} %copy.112) | data formatting | bytes 917504 | tf_op jit(solution)/shard_map/max | solution.py:98
  99.3 5.8 %all-to-all-done.3 = f32[4,2,2,112,114]{4,3,2,1,0:T(8,128)S(1)} async-done(((f32[4,2,2,112,114]{4,3,2,1,0:T(8,128)}), f32[4,2,2,112,114]{4,3,2,1,0:T(8,128)S(1)}, u32[]{:S(2)}, u32[]{:S(2)}) %all-to-all-start.3) | async-done | bytes 817184 | tf_op jit(solution)/shard_map/all_to_all | solution.py:58
  105.8 0.8 copy-done.2
  108.0 17.1 %all_to_all.40 = f32[8,2,112,114]{3,2,1,0:T(8,128)S(1)} all-to-all(f32[8,2,112,114]{3,2,1,0:T(8,128)S(1)} %broadcast_in_dim.130), channel_id=1, replica_groups={{0,8,16,24,32,40,48,56},{64,72,80,88,96,104,112,120},{128,136,144,152,1..., dimensions={0} | all-to-all | bytes 1634304 | tf_op jit(solution)/shard_map/all_to_all | solution.py:42
  126.8 1.0 broadcast_in_dim.136
  127.8 3.5 %all-to-all-start.6 = ((f32[4,2,2,112,114]{4,3,2,1,0:T(8,128)}), f32[4,2,2,112,114]{4,3,2,1,0:T(8,128)S(1)}, u32[]{:S(2)}, u32[]{:S(2)}) async-start(f32[4,2,2,112,114]{4,3,2,1,0:T(8,128)} %broadcast_in_dim.136), calls=%async_computation.6 | async-start | bytes 1835008 | tf_op jit(solution)/shard_map/all_to_all | solution.py:58
  132.8 0.8 copy.113
  133.7 11.3 %all-to-all-done.6 = f32[4,2,2,112,114]{4,3,2,1,0:T(8,128)S(1)} async-done(((f32[4,2,2,112,114]{4,3,2,1,0:T(8,128)}), f32[4,2,2,112,114]{4,3,2,1,0:T(8,128)S(1)}, u32[]{:S(2)}, u32[]{:S(2)}) %all-to-all-start.6) | async-done | bytes 817184 | tf_op jit(solution)/shard_map/all_to_all | solution.py:58
  145.0 3.8 %all-to-all-start.4 = ((bf16[8,1,128,224]{2,3,1,0:T(8,128)(2,1)}), bf16[8,1,128,224]{2,3,1,0:T(8,128)(2,1)S(1)}, u32[]{:S(2)}, u32[]{:S(2)}) async-start(bf16[8,1,128,224]{2,3,1,0:T(8,128)(2,1)} %copy.113), calls=%async_computation.4 | async-start | bytes 917504 | tf_op jit(solution)/shard_map/all_to_all | solution.py:91
  149.8 14.1 %all-to-all-done.4 = bf16[8,1,128,224]{2,3,1,0:T(8,128)(2,1)S(1)} async-done(((bf16[8,1,128,224]{2,3,1,0:T(8,128)(2,1)}), bf16[8,1,128,224]{2,3,1,0:T(8,128)(2,1)S(1)}, u32[]{:S(2)}, u32[]{:S(2)}) %all-to-all-start.4) | async-done | bytes 458784 | tf_op jit(solution)/shard_map/all_to_all | solution.py:91
  163.8 0.8 broadcast_in_dim.138
  164.6 3.5 %all-to-all-start.7 = ((bf16[8,2,112,113]{3,2,1,0:T(8,128)(2,1)}), bf16[8,2,112,113]{3,2,1,0:T(8,128)(2,1)S(1)}, u32[]{:S(2)}, u32[]{:S(2)}) async-start(bf16[8,2,112,113]{3,2,1,0:T(8,128)(2,1)} %broadcast_in_dim.138), calls=%async_computation.7 | async-start | bytes 917504 | tf_op jit(solution)/shard_map/all_to_all | solution.py:125
  168.3 1.0 copy.131
  169.3 12.5 %all-to-all-done.7 = bf16[8,2,112,113]{3,2,1,0:T(8,128)(2,1)S(1)} async-done(((bf16[8,2,112,113]{3,2,1,0:T(8,128)(2,1)}), bf16[8,2,112,113]{3,2,1,0:T(8,128)(2,1)S(1)}, u32[]{:S(2)}, u32[]{:S(2)}) %all-to-all-start.7) | async-done | bytes 405024 | tf_op jit(solution)/shard_map/all_to_all | solution.py:125
  182.6 1.0 copy.132
  183.9 1.0 copy.133
  (84 shorter events, 12.4 us)
Async XLA Ops:
  0.6 1.3 copy-start.3
  2.0 0.8 copy-start
  3.8 34.4 %all-to-all-start.1 = ((bf16[8,2,128,224]{2,3,1,0:T(8,128)(2,1)}), bf16[8,2,128,224]{2,3,1,0:T(8,128)(2,1)S(1)}, u32[]{:S(2)}, u32[]{:S(2)}) async-start(bf16[8,2,128,224]{2,3,1,0:T(8,128)(2,1)} %copy.96), calls=%async_computation.1 | async-start | bytes 1835008 | tf_op jit(solution)/shard_map/all_to_all | solution.py:84
  12.3 0.7 copy-start.8
  40.4 5.0 %copy-start.4 = (bf16[128,1792]{1,0:T(8,128)(2,1)S(1)}, bf16[128,1792]{1,0:T(8,128)(2,1)}, u32[]{:S(2)}) copy-start(bf16[128,1792]{1,0:T(8,128)(2,1)} %param.8) | copy-start | bytes 1376260
  40.4 18.1 %all-to-all-start.2 = ((f32[8,2,112,114]{3,2,1,0:T(8,128)}), f32[8,2,112,114]{3,2,1,0:T(8,128)S(1)}, u32[]{:S(2)}, u32[]{:S(2)}) async-start(f32[8,2,112,114]{3,2,1,0:T(8,128)} %broadcast_in_dim.119), calls=%async_computation.2 | async-start | bytes 1835008 | tf_op jit(solution)/shard_map/all_to_all | solution.py:42
  45.4 1.0 copy-start.5
  58.5 29.5 %all-to-all-start = ((bf16[8,2,128,224]{2,3,1,0:T(8,128)(2,1)}), bf16[8,2,128,224]{2,3,1,0:T(8,128)(2,1)S(1)}, u32[]{:S(2)}, u32[]{:S(2)}) async-start(bf16[8,2,128,224]{2,3,1,0:T(8,128)(2,1)} %copy.92), calls=%async_computation | async-start | bytes 1835008 | tf_op jit(solution)/shard_map/all_to_all | solution.py:84
  88.9 16.2 %all-to-all-start.3 = ((f32[4,2,2,112,114]{4,3,2,1,0:T(8,128)}), f32[4,2,2,112,114]{4,3,2,1,0:T(8,128)S(1)}, u32[]{:S(2)}, u32[]{:S(2)}) async-start(f32[4,2,2,112,114]{4,3,2,1,0:T(8,128)} %broadcast_in_dim.126), calls=%async_computation.3 | async-start | bytes 1835008 | tf_op jit(solution)/shard_map/all_to_all | solution.py:58
  105.5 1.0 copy-start.2
  107.2 0.8 copy-start.6
  127.8 17.3 %all-to-all-start.6 = ((f32[4,2,2,112,114]{4,3,2,1,0:T(8,128)}), f32[4,2,2,112,114]{4,3,2,1,0:T(8,128)S(1)}, u32[]{:S(2)}, u32[]{:S(2)}) async-start(f32[4,2,2,112,114]{4,3,2,1,0:T(8,128)} %broadcast_in_dim.136), calls=%async_computation.6 | async-start | bytes 1835008 | tf_op jit(solution)/shard_map/all_to_all | solution.py:58
  131.4 1.0 copy-start.7
  145.0 18.8 %all-to-all-start.4 = ((bf16[8,1,128,224]{2,3,1,0:T(8,128)(2,1)}), bf16[8,1,128,224]{2,3,1,0:T(8,128)(2,1)S(1)}, u32[]{:S(2)}, u32[]{:S(2)}) async-start(bf16[8,1,128,224]{2,3,1,0:T(8,128)(2,1)} %copy.113), calls=%async_computation.4 | async-start | bytes 917504 | tf_op jit(solution)/shard_map/all_to_all | solution.py:91
  164.6 17.2 %all-to-all-start.7 = ((bf16[8,2,112,113]{3,2,1,0:T(8,128)(2,1)}), bf16[8,2,112,113]{3,2,1,0:T(8,128)(2,1)S(1)}, u32[]{:S(2)}, u32[]{:S(2)}) async-start(bf16[8,2,112,113]{3,2,1,0:T(8,128)(2,1)} %broadcast_in_dim.138), calls=%async_computation.7 | async-start | bytes 917504 | tf_op jit(solution)/shard_map/all_to_all | solution.py:125
  169.3 12.9 %copy-start.1 = (bf16[128,1792]{0,1:T(8,128)(2,1)S(1)}, bf16[128,1792]{0,1:T(8,128)(2,1)}, u32[]{:S(2)}) copy-start(bf16[128,1792]{0,1:T(8,128)(2,1)} %copy-done) | copy-start | bytes 1376260

commit v10 on v8

--- a/solution.py
+++ b/solution.py
@@ -88,17 +88,25 @@
         merged = returned.transpose(1, 2, 0, 3).reshape(count, rows, columns)
         return [merged[i] for i in range(count)]
 
-    key_heads, value_heads = to_heads([key_input, value_input])
+    all_heads = groups * heads
+    own_key = key_input.reshape(rows, all_heads, DH)
+    own_value = value_input.reshape(rows, all_heads, DH)
+    own_feat_key = jnp.maximum(own_key, 0)
+    own_ones = jnp.ones((rows, all_heads, 1), jnp.bfloat16)
+    own_state = jnp.einsum(
+        "thk,thv->hkv",
+        own_feat_key,
+        jnp.concatenate([own_value, own_ones], axis=-1),
+        preferred_element_type=jnp.float32,
+    )
+    pieces = own_state.astype(jnp.bfloat16).reshape(groups, heads, DH, DH + 1)
+    state_part = jnp.sum(
+        lax.all_to_all(pieces, "inner", 0, 0, tiled=True).astype(jnp.float32), axis=0
+    )
     query_heads, cotangent_heads = to_heads([query_input, cotangent])
 
     feat_query = jnp.maximum(query_heads, 0)
-    feat_key = jnp.maximum(key_heads, 0)
     label = span_labels[0]
-    ones = jnp.ones((tokens, heads, 1), jnp.bfloat16)
-    value_aug = jnp.concatenate([value_heads, ones], axis=-1)
-    state_part = jnp.einsum(
-        "thk,thv->hkv", feat_key, value_aug, preferred_element_type=jnp.float32
-    )
     state_vis = visible(state_part, label, False)
     both = jnp.einsum("thk,hkv->thv", feat_query, state_vis, preferred_element_type=jnp.float32)
     numerator = both[..., :DH]
@@ -121,10 +129,6 @@
     adjoint_all = lax.all_to_all(copies, "inner", 0, 0, tiled=True).reshape(
         groups * heads, DH, DH + 1
     )
-    all_heads = groups * heads
-    own_key = key_input.reshape(rows, all_heads, DH)
-    own_value = value_input.reshape(rows, all_heads, DH)
-    own_feat_key = jnp.maximum(own_key, 0)
     key_feat = jnp.einsum(
         "thv,hkv->thk", own_value, adjoint_all[..., :DH], preferred_element_type=jnp.float32
     ) + adjoint_all[..., DH].astype(jnp.float32)[None]

time: 154 us -> 147 us (0.955)
  the two profiles are of different devices: /device:TPU:2 before, /device:TPU:5 now
where the time goes in v10:
time: 147 us; the launch traced here: 146 us
  starting transfers between devices  61.3 us (42%)
  waiting for transfers between devices  60.6 us (41%)
  local copies, waits for them, and re-layouts  14.5 us (10%)
  other arithmetic  5.95 us (4%)
  matrix products  2.79 us (2%)
    ppermute x14, starting transfers between devices, shifted(): return lax.ppermute(value, 'tm', pairs)  33.1 us
    ppermute x6, waiting for transfers between devices, strided(): return lax.ppermute(value, 'tm', pairs)  22.3 us
    all_to_all x1, waiting for transfers between devices, local(): lax.all_to_all(pieces, 'inner', 0, 0, tiled=True).astype(jnp.float32)  16.4 us
    all_to_all x1, waiting for transfers between devices, local(): lax.all_to_all(copies, 'inner', 0, 0, tiled=True)  15.4 us
    all_to_all x1, starting transfers between devices, local(): lax.all_to_all(pieces, 'inner', 0, 0, tiled=True).astype(jnp.float32)  8.32 us
    ppermute x6, starting transfers between devices, strided(): return lax.ppermute(value, 'tm', pairs)  8.16 us
    unnamed x25, local copies, waits for them, and re-layouts  6.53 us
    all_to_all x1, starting transfers between devices, local(): lax.all_to_all(copies, 'inner', 0, 0, tiled=True)  4.68 us
  transfers between devices with their start and end apart: 24, of which 10 were waited for; matrix products, arithmetic and copies ran while one was open for 5% of the time, Pallas kernels for 0%

profile of v10, /device:TPU:5, one launch (start us, length us, event | category | flops | bytes accessed | tf_op | source)
XLA Modules:
  0.0 146.2 jit_solution(5546610055045066405)
XLA Ops:
  0.6 1.3 copy.35
  3.2 1.2 convolution_convert_fusion.1
  4.4 8.3 %all-to-all-start.1 = ((bf16[8,2,112,113]{3,2,1,0:T(8,128)(2,1)}), bf16[8,2,112,113]{3,2,1,0:T(8,128)(2,1)S(1)}, u32[]{:S(2)}, u32[]{:S(2)}) async-start(bf16[8,2,112,113]{3,2,1,0:T(8,128)(2,1)} %bitcast.7), calls=%async_computation.1 | async-start | bytes 917504 | tf_op jit(solution)/shard_map/all_to_all | solution.py:104
  12.8 16.4 %all-to-all-done.1 = bf16[8,2,112,113]{3,2,1,0:T(8,128)(2,1)S(1)} async-done(((bf16[8,2,112,113]{3,2,1,0:T(8,128)(2,1)}), bf16[8,2,112,113]{3,2,1,0:T(8,128)(2,1)S(1)}, u32[]{:S(2)}, u32[]{:S(2)}) %all-to-all-start.1) | async-done | bytes 405024 | tf_op jit(solution)/shard_map/all_to_all | solution.py:104
  30.7 2.8 %collective-permute-start.4 = (f32[2,112,114]{2,1,0:T(8,128)S(1)}, f32[2,112,114]{2,1,0:T(8,128)S(1)}, u32[]{:S(2)}, u32[]{:S(2)}) collective-permute-start(f32[2,112,114]{2,1,0:T(8,128)S(1)} %concatenate.26), channel_id=1, source_target_pairs={{0,40},{8,48},{16,56},{24,0},{32,8},{40,16},{48,24},{56,32},{64,10... | collective-permute-start | bytes 306440 | tf_op jit(solution)/shard_map/ppermute | solution.py:20
  34.0 2.7 %collective-permute-start.2 = (f32[2,112,114]{2,1,0:T(8,128)S(1)}, f32[2,112,114]{2,1,0:T(8,128)S(1)}, u32[]{:S(2)}, u32[]{:S(2)}) collective-permute-start(f32[2,112,114]{2,1,0:T(8,128)S(1)} %concatenate.26), channel_id=1, source_target_pairs={{0,24},{8,32},{16,40},{24,48},{32,56},{40,0},{48,8},{56,16},{64,88... | collective-permute-start | bytes 306440 | tf_op jit(solution)/shard_map/ppermute | solution.py:20
  36.8 7.9 %collective-permute-start = (f32[2,112,114]{2,1,0:T(8,128)S(1)}, f32[2,112,114]{2,1,0:T(8,128)S(1)}, u32[]{:S(2)}, u32[]{:S(2)}) collective-permute-start(f32[2,112,114]{2,1,0:T(8,128)S(1)} %concatenate.26), channel_id=1, source_target_pairs={{0,8},{8,16},{16,24},{24,32},{32,40},{40,48},{48,56},{56,0},{64,72... | collective-permute-start | bytes 306440 | tf_op jit(solution)/shard_map/ppermute | solution.py:20
  44.9 1.0 copy.33
  45.9 3.6 %all-to-all-start = ((bf16[8,2,128,224]{2,3,1,0:T(8,128)(2,1)}), bf16[8,2,128,224]{2,3,1,0:T(8,128)(2,1)S(1)}, u32[]{:S(2)}, u32[]{:S(2)}) async-start(bf16[8,2,128,224]{2,3,1,0:T(8,128)(2,1)} %copy.33), calls=%async_computation | async-start | bytes 1835008 | tf_op jit(solution)/shard_map/all_to_all | solution.py:80
  50.8 2.8 %collective-permute-start.9 = (f32[2,2,112,114]{3,2,1,0:T(8,128)S(1)}, f32[2,2,112,114]{3,2,1,0:T(8,128)S(1)}, u32[]{:S(2)}, u32[]{:S(2)}) collective-permute-start(f32[2,2,112,114]{3,2,1,0:T(8,128)S(1)} %pad_maximum_fusion.3), channel_id=1, source_target_pairs={{0,192},{8,200},{16,208},{24,216},{32,224},{40,232},{48,240},{56,2... | collective-permute-start | bytes 612872 | tf_op jit(solution)/shard_map/ppermute | solution.py:30
  54.7 6.5 %collective-permute-done.9 = f32[2,2,112,114]{3,2,1,0:T(8,128)S(1)} collective-permute-done((f32[2,2,112,114]{3,2,1,0:T(8,128)S(1)}, f32[2,2,112,114]{3,2,1,0:T(8,128)S(1)}, u32[]{:S(2)}, u32[]{:S(2)}) %collective-permute-start.9) | collective-permute-done | bytes 204320 | tf_op jit(solution)/shard_map/ppermute | solution.py:30
  61.4 1.4 collective-permute-done.8
  63.0 2.1 %collective-permute-done.7 = f32[2,2,112,114]{3,2,1,0:T(8,128)S(1)} collective-permute-done((f32[2,2,112,114]{3,2,1,0:T(8,128)S(1)}, f32[2,2,112,114]{3,2,1,0:T(8,128)S(1)}, u32[]{:S(2)}, u32[]{:S(2)}) %collective-permute-start.7) | collective-permute-done | bytes 204320 | tf_op jit(solution)/shard_map/ppermute | solution.py:30
  65.8 3.4 %all-to-all-done = bf16[8,2,128,224]{2,3,1,0:T(8,128)(2,1)S(1)} async-done(((bf16[8,2,128,224]{2,3,1,0:T(8,128)(2,1)}), bf16[8,2,128,224]{2,3,1,0:T(8,128)(2,1)S(1)}, u32[]{:S(2)}, u32[]{:S(2)}) %all-to-all-start) | async-done | bytes 917536 | tf_op jit(solution)/shard_map/all_to_all | solution.py:80
  69.3 1.5 %copy.37 = f32[1,8,128,224]{2,1,3,0:T(8,128)} copy(f32[1,8,128,224]{2,3,0,1:T(8,128)S(1)} %convert_multiply_fusion) | data formatting | bytes 1835008 | tf_op jit(solution)/shard_map/mul | solution.py:116
  70.8 1.3 mul.22
  73.1 1.2 max.36
  75.7 1.5 collective-permute-start.15
  77.1 4.6 %collective-permute-start.14 = (f32[2,112,114]{2,1,0:T(8,128)S(1)}, f32[2,112,114]{2,1,0:T(8,128)S(1)}, u32[]{:S(2)}, u32[]{:S(2)}) collective-permute-start(f32[2,112,114]{2,1,0:T(8,128)S(1)} %concatenate.30), channel_id=1, source_target_pairs={{0,40},{8,48},{16,56},{24,0},{32,8},{40,16},{48,24},{56,32},{64,10... | collective-permute-start | bytes 306440 | tf_op jit(solution)/shard_map/ppermute | solution.py:20
  81.8 2.1 %collective-permute-start.13 = (f32[2,112,114]{2,1,0:T(8,128)S(1)}, f32[2,112,114]{2,1,0:T(8,128)S(1)}, u32[]{:S(2)}, u32[]{:S(2)}) collective-permute-start(f32[2,112,114]{2,1,0:T(8,128)S(1)} %concatenate.30), channel_id=1, source_target_pairs={{0,32},{8,40},{16,48},{24,56},{32,0},{40,8},{48,16},{56,24},{64,96... | collective-permute-start | bytes 306440 | tf_op jit(solution)/shard_map/ppermute | solution.py:20
  83.8 3.3 %collective-permute-start.12 = (f32[2,112,114]{2,1,0:T(8,128)S(1)}, f32[2,112,114]{2,1,0:T(8,128)S(1)}, u32[]{:S(2)}, u32[]{:S(2)}) collective-permute-start(f32[2,112,114]{2,1,0:T(8,128)S(1)} %concatenate.30), channel_id=1, source_target_pairs={{0,24},{8,32},{16,40},{24,48},{32,56},{40,0},{48,8},{56,16},{64,88... | collective-permute-start | bytes 306440 | tf_op jit(solution)/shard_map/ppermute | solution.py:20
  87.1 6.7 %collective-permute-start.10 = (f32[2,112,114]{2,1,0:T(8,128)S(1)}, f32[2,112,114]{2,1,0:T(8,128)S(1)}, u32[]{:S(2)}, u32[]{:S(2)}) collective-permute-start(f32[2,112,114]{2,1,0:T(8,128)S(1)} %concatenate.30), channel_id=1, source_target_pairs={{0,8},{8,16},{16,24},{24,32},{32,40},{40,48},{48,56},{56,0},{64,72... | collective-permute-start | bytes 306440 | tf_op jit(solution)/shard_map/ppermute | solution.py:20
  94.4 1.3 collective-permute-done.10
  97.0 2.8 %collective-permute-start.19 = (f32[2,2,112,114]{3,2,1,0:T(8,128)S(1)}, f32[2,2,112,114]{3,2,1,0:T(8,128)S(1)}, u32[]{:S(2)}, u32[]{:S(2)}) collective-permute-start(f32[2,2,112,114]{3,2,1,0:T(8,128)S(1)} %pad_maximum_fusion.4), channel_id=1, source_target_pairs={{0,192},{8,200},{16,208},{24,216},{32,224},{40,232},{48,240},{56,2... | collective-permute-start | bytes 612872 | tf_op jit(solution)/shard_map/ppermute | solution.py:30
  101.0 3.5 %all-to-all-start.2 = ((bf16[8,1,128,224]{2,3,1,0:T(8,128)(2,1)}), bf16[8,1,128,224]{2,3,1,0:T(8,128)(2,1)S(1)}, u32[]{:S(2)}, u32[]{:S(2)}) async-start(bf16[8,1,128,224]{2,3,1,0:T(8,128)(2,1)} %copy.39), calls=%async_computation.2 | async-start | bytes 917504 | tf_op jit(solution)/shard_map/all_to_all | solution.py:87
  104.5 1.1 collective-permute-start.18
  106.2 7.0 %collective-permute-done.18 = f32[2,2,112,114]{3,2,1,0:T(8,128)S(1)} collective-permute-done((f32[2,2,112,114]{3,2,1,0:T(8,128)S(1)}, f32[2,2,112,114]{3,2,1,0:T(8,128)S(1)}, u32[]{:S(2)}, u32[]{:S(2)}) %collective-permute-start.18) | collective-permute-done | bytes 204320 | tf_op jit(solution)/shard_map/ppermute | solution.py:30
  113.3 5.3 %collective-permute-done.17 = f32[2,2,112,114]{3,2,1,0:T(8,128)S(1)} collective-permute-done((f32[2,2,112,114]{3,2,1,0:T(8,128)S(1)}, f32[2,2,112,114]{3,2,1,0:T(8,128)S(1)}, u32[]{:S(2)}, u32[]{:S(2)}) %collective-permute-start.17) | collective-permute-done | bytes 204320 | tf_op jit(solution)/shard_map/ppermute | solution.py:30
  119.3 1.8 %all-to-all-done.2 = bf16[8,1,128,224]{2,3,1,0:T(8,128)(2,1)S(1)} async-done(((bf16[8,1,128,224]{2,3,1,0:T(8,128)(2,1)}), bf16[8,1,128,224]{2,3,1,0:T(8,128)(2,1)S(1)}, u32[]{:S(2)}, u32[]{:S(2)}) %all-to-all-start.2) | async-done | bytes 458784 | tf_op jit(solution)/shard_map/all_to_all | solution.py:87
  121.9 4.7 %all-to-all-start.3 = ((bf16[8,2,112,113]{3,2,1,0:T(8,128)(2,1)}), bf16[8,2,112,113]{3,2,1,0:T(8,128)(2,1)S(1)}, u32[]{:S(2)}, u32[]{:S(2)}) async-start(bf16[8,2,112,113]{3,2,1,0:T(8,128)(2,1)} %broadcast_in_dim.401), calls=%async_computation.3 | async-start | bytes 917504 | tf_op jit(solution)/shard_map/all_to_all | solution.py:129
  126.7 1.0 copy.43
  127.7 15.4 %all-to-all-done.3 = bf16[8,2,112,113]{3,2,1,0:T(8,128)(2,1)S(1)} async-done(((bf16[8,2,112,113]{3,2,1,0:T(8,128)(2,1)}), bf16[8,2,112,113]{3,2,1,0:T(8,128)(2,1)S(1)}, u32[]{:S(2)}, u32[]{:S(2)}) %all-to-all-start.3) | async-done | bytes 405024 | tf_op jit(solution)/shard_map/all_to_all | solution.py:129
  (88 shorter events, 17.8 us)
Async XLA Ops:
  1.9 1.0 copy-start.2
  3.2 1.2 copy-start
  4.4 8.3 %copy-start.7 = (s32[128]{0:T(128)S(1)}, s32[128]{0:T(128)}, u32[]{:S(2)}) copy-start(s32[128]{0:T(128)} %param.9) | copy-start | bytes 1540
  4.4 24.8 %all-to-all-start.1 = ((bf16[8,2,112,113]{3,2,1,0:T(8,128)(2,1)}), bf16[8,2,112,113]{3,2,1,0:T(8,128)(2,1)S(1)}, u32[]{:S(2)}, u32[]{:S(2)}) async-start(bf16[8,2,112,113]{3,2,1,0:T(8,128)(2,1)} %bitcast.7), calls=%async_computation.1 | async-start | bytes 917504 | tf_op jit(solution)/shard_map/all_to_all | solution.py:104
  12.7 17.5 %copy-start.3 = (bf16[128,1792]{1,0:T(8,128)(2,1)S(1)}, bf16[128,1792]{1,0:T(8,128)(2,1)}, u32[]{:S(2)}) copy-start(bf16[128,1792]{1,0:T(8,128)(2,1)} %param.5) | copy-start | bytes 1376260
  29.3 1.1 copy-start.4
  29.3 7.4 %collective-permute-start.6 = (f32[2,112,114]{2,1,0:T(8,128)S(1)}, f32[2,112,114]{2,1,0:T(8,128)S(1)}, u32[]{:S(2)}, u32[]{:S(2)}) collective-permute-start(f32[2,112,114]{2,1,0:T(8,128)S(1)} %concatenate.26), channel_id=1, source_target_pairs={{0,56},{8,0},{16,8},{24,16},{32,24},{40,32},{48,40},{56,48},{64,12... | collective-permute-start | bytes 306440 | tf_op jit(solution)/shard_map/ppermute | solution.py:20
  29.9 7.0 %collective-permute-start.5 = (f32[2,112,114]{2,1,0:T(8,128)S(1)}, f32[2,112,114]{2,1,0:T(8,128)S(1)}, u32[]{:S(2)}, u32[]{:S(2)}) collective-permute-start(f32[2,112,114]{2,1,0:T(8,128)S(1)} %concatenate.26), channel_id=1, source_target_pairs={{0,48},{8,56},{16,0},{24,8},{32,16},{40,24},{48,32},{56,40},{64,11... | collective-permute-start | bytes 306440 | tf_op jit(solution)/shard_map/ppermute | solution.py:20
  30.7 18.8 %collective-permute-start.4 = (f32[2,112,114]{2,1,0:T(8,128)S(1)}, f32[2,112,114]{2,1,0:T(8,128)S(1)}, u32[]{:S(2)}, u32[]{:S(2)}) collective-permute-start(f32[2,112,114]{2,1,0:T(8,128)S(1)} %concatenate.26), channel_id=1, source_target_pairs={{0,40},{8,48},{16,56},{24,0},{32,8},{40,16},{48,24},{56,32},{64,10... | collective-permute-start | bytes 306440 | tf_op jit(solution)/shard_map/ppermute | solution.py:20
  33.4 16.0 %collective-permute-start.3 = (f32[2,112,114]{2,1,0:T(8,128)S(1)}, f32[2,112,114]{2,1,0:T(8,128)S(1)}, u32[]{:S(2)}, u32[]{:S(2)}) collective-permute-start(f32[2,112,114]{2,1,0:T(8,128)S(1)} %concatenate.26), channel_id=1, source_target_pairs={{0,32},{8,40},{16,48},{24,56},{32,0},{40,8},{48,16},{56,24},{64,96... | collective-permute-start | bytes 306440 | tf_op jit(solution)/shard_map/ppermute | solution.py:20
  34.0 15.4 %collective-permute-start.2 = (f32[2,112,114]{2,1,0:T(8,128)S(1)}, f32[2,112,114]{2,1,0:T(8,128)S(1)}, u32[]{:S(2)}, u32[]{:S(2)}) collective-permute-start(f32[2,112,114]{2,1,0:T(8,128)S(1)} %concatenate.26), channel_id=1, source_target_pairs={{0,24},{8,32},{16,40},{24,48},{32,56},{40,0},{48,8},{56,16},{64,88... | collective-permute-start | bytes 306440 | tf_op jit(solution)/shard_map/ppermute | solution.py:20
  36.7 12.7 %collective-permute-start.1 = (f32[2,112,114]{2,1,0:T(8,128)S(1)}, f32[2,112,114]{2,1,0:T(8,128)S(1)}, u32[]{:S(2)}, u32[]{:S(2)}) collective-permute-start(f32[2,112,114]{2,1,0:T(8,128)S(1)} %concatenate.26), channel_id=1, source_target_pairs={{0,16},{8,24},{16,32},{24,40},{32,48},{40,56},{48,0},{56,8},{64,80... | collective-permute-start | bytes 306440 | tf_op jit(solution)/shard_map/ppermute | solution.py:20
  36.8 12.6 %collective-permute-start = (f32[2,112,114]{2,1,0:T(8,128)S(1)}, f32[2,112,114]{2,1,0:T(8,128)S(1)}, u32[]{:S(2)}, u32[]{:S(2)}) collective-permute-start(f32[2,112,114]{2,1,0:T(8,128)S(1)} %concatenate.26), channel_id=1, source_target_pairs={{0,8},{8,16},{16,24},{24,32},{32,40},{40,48},{48,56},{56,0},{64,72... | collective-permute-start | bytes 306440 | tf_op jit(solution)/shard_map/ppermute | solution.py:20
  45.9 23.4 %all-to-all-start = ((bf16[8,2,128,224]{2,3,1,0:T(8,128)(2,1)}), bf16[8,2,128,224]{2,3,1,0:T(8,128)(2,1)S(1)}, u32[]{:S(2)}, u32[]{:S(2)}) async-start(bf16[8,2,128,224]{2,3,1,0:T(8,128)(2,1)} %copy.33), calls=%async_computation | async-start | bytes 1835008 | tf_op jit(solution)/shard_map/all_to_all | solution.py:80
  50.8 10.4 %collective-permute-start.9 = (f32[2,2,112,114]{3,2,1,0:T(8,128)S(1)}, f32[2,2,112,114]{3,2,1,0:T(8,128)S(1)}, u32[]{:S(2)}, u32[]{:S(2)}) collective-permute-start(f32[2,2,112,114]{3,2,1,0:T(8,128)S(1)} %pad_maximum_fusion.3), channel_id=1, source_target_pairs={{0,192},{8,200},{16,208},{24,216},{32,224},{40,232},{48,240},{56,2... | collective-permute-start | bytes 612872 | tf_op jit(solution)/shard_map/ppermute | solution.py:30
  53.7 9.1 %collective-permute-start.8 = (f32[2,2,112,114]{3,2,1,0:T(8,128)S(1)}, f32[2,2,112,114]{3,2,1,0:T(8,128)S(1)}, u32[]{:S(2)}, u32[]{:S(2)}) collective-permute-start(f32[2,2,112,114]{3,2,1,0:T(8,128)S(1)} %pad_maximum_fusion.3), channel_id=1, source_target_pairs={{0,128},{8,136},{16,144},{24,152},{32,160},{40,168},{48,176},{56,1... | collective-permute-start | bytes 612872 | tf_op jit(solution)/shard_map/ppermute | solution.py:30
  54.0 11.1 %collective-permute-start.7 = (f32[2,2,112,114]{3,2,1,0:T(8,128)S(1)}, f32[2,2,112,114]{3,2,1,0:T(8,128)S(1)}, u32[]{:S(2)}, u32[]{:S(2)}) collective-permute-start(f32[2,2,112,114]{3,2,1,0:T(8,128)S(1)} %pad_maximum_fusion.3), channel_id=1, source_target_pairs={{0,64},{8,72},{16,80},{24,88},{32,96},{40,104},{48,112},{56,120},{... | collective-permute-start | bytes 612872 | tf_op jit(solution)/shard_map/ppermute | solution.py:30
  74.9 0.8 copy-start.5
  75.7 11.5 %collective-permute-start.16 = (f32[2,112,114]{2,1,0:T(8,128)S(1)}, f32[2,112,114]{2,1,0:T(8,128)S(1)}, u32[]{:S(2)}, u32[]{:S(2)}) collective-permute-start(f32[2,112,114]{2,1,0:T(8,128)S(1)} %concatenate.30), channel_id=1, source_target_pairs={{0,56},{8,0},{16,8},{24,16},{32,24},{40,32},{48,40},{56,48},{64,12... | collective-permute-start | bytes 306440 | tf_op jit(solution)/shard_map/ppermute | solution.py:20
  75.7 11.4 %collective-permute-start.15 = (f32[2,112,114]{2,1,0:T(8,128)S(1)}, f32[2,112,114]{2,1,0:T(8,128)S(1)}, u32[]{:S(2)}, u32[]{:S(2)}) collective-permute-start(f32[2,112,114]{2,1,0:T(8,128)S(1)} %concatenate.30), channel_id=1, source_target_pairs={{0,48},{8,56},{16,0},{24,8},{32,16},{40,24},{48,32},{56,40},{64,11... | collective-permute-start | bytes 306440 | tf_op jit(solution)/shard_map/ppermute | solution.py:20
  77.1 17.2 %collective-permute-start.14 = (f32[2,112,114]{2,1,0:T(8,128)S(1)}, f32[2,112,114]{2,1,0:T(8,128)S(1)}, u32[]{:S(2)}, u32[]{:S(2)}) collective-permute-start(f32[2,112,114]{2,1,0:T(8,128)S(1)} %concatenate.30), channel_id=1, source_target_pairs={{0,40},{8,48},{16,56},{24,0},{32,8},{40,16},{48,24},{56,32},{64,10... | collective-permute-start | bytes 306440 | tf_op jit(solution)/shard_map/ppermute | solution.py:20
  81.8 12.6 %collective-permute-start.13 = (f32[2,112,114]{2,1,0:T(8,128)S(1)}, f32[2,112,114]{2,1,0:T(8,128)S(1)}, u32[]{:S(2)}, u32[]{:S(2)}) collective-permute-start(f32[2,112,114]{2,1,0:T(8,128)S(1)} %concatenate.30), channel_id=1, source_target_pairs={{0,32},{8,40},{16,48},{24,56},{32,0},{40,8},{48,16},{56,24},{64,96... | collective-permute-start | bytes 306440 | tf_op jit(solution)/shard_map/ppermute | solution.py:20
  83.8 10.5 %collective-permute-start.12 = (f32[2,112,114]{2,1,0:T(8,128)S(1)}, f32[2,112,114]{2,1,0:T(8,128)S(1)}, u32[]{:S(2)}, u32[]{:S(2)}) collective-permute-start(f32[2,112,114]{2,1,0:T(8,128)S(1)} %concatenate.30), channel_id=1, source_target_pairs={{0,24},{8,32},{16,40},{24,48},{32,56},{40,0},{48,8},{56,16},{64,88... | collective-permute-start | bytes 306440 | tf_op jit(solution)/shard_map/ppermute | solution.py:20
  87.1 7.3 %collective-permute-start.11 = (f32[2,112,114]{2,1,0:T(8,128)S(1)}, f32[2,112,114]{2,1,0:T(8,128)S(1)}, u32[]{:S(2)}, u32[]{:S(2)}) collective-permute-start(f32[2,112,114]{2,1,0:T(8,128)S(1)} %concatenate.30), channel_id=1, source_target_pairs={{0,16},{8,24},{16,32},{24,40},{32,48},{40,56},{48,0},{56,8},{64,80... | collective-permute-start | bytes 306440 | tf_op jit(solution)/shard_map/ppermute | solution.py:20
  87.1 8.5 %collective-permute-start.10 = (f32[2,112,114]{2,1,0:T(8,128)S(1)}, f32[2,112,114]{2,1,0:T(8,128)S(1)}, u32[]{:S(2)}, u32[]{:S(2)}) collective-permute-start(f32[2,112,114]{2,1,0:T(8,128)S(1)} %concatenate.30), channel_id=1, source_target_pairs={{0,8},{8,16},{16,24},{24,32},{32,40},{40,48},{48,56},{56,0},{64,72... | collective-permute-start | bytes 306440 | tf_op jit(solution)/shard_map/ppermute | solution.py:20
  96.9 3.0 %copy-start.6 = (bf16[1024,2,112]{0,2,1:T(8,128)(2,1)S(1)}, bf16[1024,2,112]{0,2,1:T(8,128)(2,1)}, u32[]{:S(2)}) copy-start(bf16[1024,2,112]{0,2,1:T(8,128)(2,1)} %copy-done.5) | copy-start | bytes 1376260
  97.0 9.0 %collective-permute-start.19 = (f32[2,2,112,114]{3,2,1,0:T(8,128)S(1)}, f32[2,2,112,114]{3,2,1,0:T(8,128)S(1)}, u32[]{:S(2)}, u32[]{:S(2)}) collective-permute-start(f32[2,2,112,114]{3,2,1,0:T(8,128)S(1)} %pad_maximum_fusion.4), channel_id=1, source_target_pairs={{0,192},{8,200},{16,208},{24,216},{32,224},{40,232},{48,240},{56,2... | collective-permute-start | bytes 612872 | tf_op jit(solution)/shard_map/ppermute | solution.py:30
  101.0 20.0 %all-to-all-start.2 = ((bf16[8,1,128,224]{2,3,1,0:T(8,128)(2,1)}), bf16[8,1,128,224]{2,3,1,0:T(8,128)(2,1)S(1)}, u32[]{:S(2)}, u32[]{:S(2)}) async-start(bf16[8,1,128,224]{2,3,1,0:T(8,128)(2,1)} %copy.39), calls=%async_computation.2 | async-start | bytes 917504 | tf_op jit(solution)/shard_map/all_to_all | solution.py:87
  104.5 8.6 %collective-permute-start.18 = (f32[2,2,112,114]{3,2,1,0:T(8,128)S(1)}, f32[2,2,112,114]{3,2,1,0:T(8,128)S(1)}, u32[]{:S(2)}, u32[]{:S(2)}) collective-permute-start(f32[2,2,112,114]{3,2,1,0:T(8,128)S(1)} %pad_maximum_fusion.4), channel_id=1, source_target_pairs={{0,128},{8,136},{16,144},{24,152},{32,160},{40,168},{48,176},{56,1... | collective-permute-start | bytes 612872 | tf_op jit(solution)/shard_map/ppermute | solution.py:30
  105.6 13.0 %collective-permute-start.17 = (f32[2,2,112,114]{3,2,1,0:T(8,128)S(1)}, f32[2,2,112,114]{3,2,1,0:T(8,128)S(1)}, u32[]{:S(2)}, u32[]{:S(2)}) collective-permute-start(f32[2,2,112,114]{3,2,1,0:T(8,128)S(1)} %pad_maximum_fusion.4), channel_id=1, source_target_pairs={{0,64},{8,72},{16,80},{24,88},{32,96},{40,104},{48,112},{56,120},{... | collective-permute-start | bytes 612872 | tf_op jit(solution)/shard_map/ppermute | solution.py:30
  121.9 21.2 %all-to-all-start.3 = ((bf16[8,2,112,113]{3,2,1,0:T(8,128)(2,1)}), bf16[8,2,112,113]{3,2,1,0:T(8,128)(2,1)S(1)}, u32[]{:S(2)}, u32[]{:S(2)}) async-start(bf16[8,2,112,113]{3,2,1,0:T(8,128)(2,1)} %broadcast_in_dim.401), calls=%async_computation.3 | async-start | bytes 917504 | tf_op jit(solution)/shard_map/all_to_all | solution.py:129
  143.8 1.0 copy-start.1

commit v11 on v10

--- a/solution.py
+++ b/solution.py
@@ -50,20 +50,16 @@
             edge = pick(edge, t)
         whole = sum(states)
         edge_sum = sum(jnp.where(t == edge, s, 0.0) for t, s in zip(tags, states))
-        summary = jnp.stack(
-            [jnp.concatenate([whole, edge], -1), jnp.concatenate([edge_sum, edge], -1)]
-        )
+        whole = jnp.concatenate([whole, edge], -1)
+        edge_sum = jnp.concatenate([edge_sum, edge], -1)
         for s in range(1, rows):
-            got = strided(summary, row, s)
+            target = (me + s) % rows
+            sends_whole = (target < me) if later else (target > me)
+            got = strided(jnp.where(sends_whole, whole, edge_sum), row, s)
             source = (me - s) % rows
-            their_edge = got[1, ..., DH + 1 :]
-            full = (source > me) if later else (source < me)
-            part_only = ((source < me) if later else (source > me)) & (their_edge == flabel)
-            seen = (
-                seen
-                + jnp.where(full, got[0, ..., : DH + 1], 0.0)
-                + jnp.where(part_only, got[1, ..., : DH + 1], 0.0)
-            )
+            is_whole = (source > me) if later else (source < me)
+            take = is_whole | (got[..., DH + 1 :] == flabel)
+            seen = seen + jnp.where(take, got[..., : DH + 1], 0.0)
     return seen.astype(jnp.bfloat16)
 
 

time: 147 us -> 137 us (0.932)
  the two profiles are of different devices: /device:TPU:5 before, /device:TPU:2 now
where the time goes in v11:
time: 137 us; the launch traced here: 135 us
  waiting for transfers between devices  60.4 us (44%)
  starting transfers between devices  49.9 us (36%)
  local copies, waits for them, and re-layouts  14.5 us (11%)
  other arithmetic  5.92 us (4%)
  matrix products  2.78 us (2%)
    ppermute x14, starting transfers between devices, shifted(): return lax.ppermute(value, 'tm', pairs)  20.2 us
    all_to_all x1, waiting for transfers between devices, local(): lax.all_to_all(pieces, 'inner', 0, 0, tiled=True).astype(jnp.float32)  16 us
    all_to_all x1, waiting for transfers between devices, local(): lax.all_to_all(copies, 'inner', 0, 0, tiled=True)  15.4 us
    all_to_all x1, waiting for transfers between devices, to_heads(): incoming = lax.all_to_all(outgoing, 'inner', 0, 0, tiled=True)  12.1 us
    ppermute x6, starting transfers between devices, strided(): return lax.ppermute(value, 'tm', pairs)  10.6 us
    all_to_all x1, starting transfers between devices, local(): lax.all_to_all(pieces, 'inner', 0, 0, tiled=True).astype(jnp.float32)  8.6 us
    ppermute x6, waiting for transfers between devices, strided(): return lax.ppermute(value, 'tm', pairs)  7.85 us
    unnamed x25, local copies, waits for them, and re-layouts  6.53 us
  transfers between devices with their start and end apart: 24, of which 13 were waited for; matrix products, arithmetic and copies ran while one was open for 7% of the time, Pallas kernels for 0%

profile of v11, /device:TPU:2, one launch (start us, length us, event | category | flops | bytes accessed | tf_op | source)
XLA Modules:
  0.0 134.6 jit_solution(2138176729635121564)
XLA Ops:
  0.6 1.3 copy.35
  3.2 1.2 convolution_convert_fusion.1
  4.4 8.6 %all-to-all-start.1 = ((bf16[8,2,112,113]{3,2,1,0:T(8,128)(2,1)}), bf16[8,2,112,113]{3,2,1,0:T(8,128)(2,1)S(1)}, u32[]{:S(2)}, u32[]{:S(2)}) async-start(bf16[8,2,112,113]{3,2,1,0:T(8,128)(2,1)} %bitcast.7), calls=%async_computation.1 | async-start | bytes 917504 | tf_op jit(solution)/shard_map/all_to_all | solution.py:100
  13.0 16.0 %all-to-all-done.1 = bf16[8,2,112,113]{3,2,1,0:T(8,128)(2,1)S(1)} async-done(((bf16[8,2,112,113]{3,2,1,0:T(8,128)(2,1)}), bf16[8,2,112,113]{3,2,1,0:T(8,128)(2,1)S(1)}, u32[]{:S(2)}, u32[]{:S(2)}) %all-to-all-start.1) | async-done | bytes 405024 | tf_op jit(solution)/shard_map/all_to_all | solution.py:100
  29.3 2.8 %collective-permute-start.5 = (f32[2,112,114]{2,1,0:T(8,128)S(1)}, f32[2,112,114]{2,1,0:T(8,128)S(1)}, u32[]{:S(2)}, u32[]{:S(2)}) collective-permute-start(f32[2,112,114]{2,1,0:T(8,128)S(1)} %concatenate.26), channel_id=1, source_target_pairs={{0,48},{8,56},{16,0},{24,8},{32,16},{40,24},{48,32},{56,40},{64,11... | collective-permute-start | bytes 306440 | tf_op jit(solution)/shard_map/ppermute | solution.py:20
  33.7 1.2 collective-permute-start.2
  34.9 2.1 %collective-permute-start.1 = (f32[2,112,114]{2,1,0:T(8,128)S(1)}, f32[2,112,114]{2,1,0:T(8,128)S(1)}, u32[]{:S(2)}, u32[]{:S(2)}) collective-permute-start(f32[2,112,114]{2,1,0:T(8,128)S(1)} %concatenate.26), channel_id=1, source_target_pairs={{0,16},{8,24},{16,32},{24,40},{32,48},{40,56},{48,0},{56,8},{64,80... | collective-permute-start | bytes 306440 | tf_op jit(solution)/shard_map/ppermute | solution.py:20
  38.9 3.6 %all-to-all-start = ((bf16[8,2,128,224]{2,3,1,0:T(8,128)(2,1)}), bf16[8,2,128,224]{2,3,1,0:T(8,128)(2,1)S(1)}, u32[]{:S(2)}, u32[]{:S(2)}) async-start(bf16[8,2,128,224]{2,3,1,0:T(8,128)(2,1)} %copy.33), calls=%async_computation | async-start | bytes 1835008 | tf_op jit(solution)/shard_map/all_to_all | solution.py:76
  43.1 2.3 %collective-permute-done.1 = f32[2,112,114]{2,1,0:T(8,128)S(1)} collective-permute-done((f32[2,112,114]{2,1,0:T(8,128)S(1)}, f32[2,112,114]{2,1,0:T(8,128)S(1)}, u32[]{:S(2)}, u32[]{:S(2)}) %collective-permute-start.1) | collective-permute-done | bytes 102176 | tf_op jit(solution)/shard_map/ppermute | solution.py:20
  47.4 1.7 %collective-permute-start.7 = (f32[2,112,114]{2,1,0:T(8,128)S(1)}, f32[2,112,114]{2,1,0:T(8,128)S(1)}, u32[]{:S(2)}, u32[]{:S(2)}) collective-permute-start(f32[2,112,114]{2,1,0:T(8,128)S(1)} %get-tuple-element.49), channel_id=1, source_target_pairs={{0,64},{8,72},{16,80},{24,88},{32,96},{40,104},{48,112},{56,120},{... | collective-permute-start | bytes 306440 | tf_op jit(solution)/shard_map/ppermute | solution.py:30
  49.0 1.7 %collective-permute-start.9 = (f32[2,112,114]{2,1,0:T(8,128)S(1)}, f32[2,112,114]{2,1,0:T(8,128)S(1)}, u32[]{:S(2)}, u32[]{:S(2)}) collective-permute-start(f32[2,112,114]{2,1,0:T(8,128)S(1)} %get-tuple-element.50), channel_id=1, source_target_pairs={{0,192},{8,200},{16,208},{24,216},{32,224},{40,232},{48,240},{56,2... | collective-permute-start | bytes 306440 | tf_op jit(solution)/shard_map/ppermute | solution.py:30
  50.7 2.0 %collective-permute-start.8 = (f32[2,112,114]{2,1,0:T(8,128)S(1)}, f32[2,112,114]{2,1,0:T(8,128)S(1)}, u32[]{:S(2)}, u32[]{:S(2)}) collective-permute-start(f32[2,112,114]{2,1,0:T(8,128)S(1)} %get-tuple-element.51), channel_id=1, source_target_pairs={{0,128},{8,136},{16,144},{24,152},{32,160},{40,168},{48,176},{56,1... | collective-permute-start | bytes 306440 | tf_op jit(solution)/shard_map/ppermute | solution.py:30
  52.7 1.3 collective-permute-done.7
  54.7 2.3 %collective-permute-done.8 = f32[2,112,114]{2,1,0:T(8,128)S(1)} collective-permute-done((f32[2,112,114]{2,1,0:T(8,128)S(1)}, f32[2,112,114]{2,1,0:T(8,128)S(1)}, u32[]{:S(2)}, u32[]{:S(2)}) %collective-permute-start.8) | collective-permute-done | bytes 102176 | tf_op jit(solution)/shard_map/ppermute | solution.py:30
  57.7 12.1 %all-to-all-done = bf16[8,2,128,224]{2,3,1,0:T(8,128)(2,1)S(1)} async-done(((bf16[8,2,128,224]{2,3,1,0:T(8,128)(2,1)}), bf16[8,2,128,224]{2,3,1,0:T(8,128)(2,1)S(1)}, u32[]{:S(2)}, u32[]{:S(2)}) %all-to-all-start) | async-done | bytes 917536 | tf_op jit(solution)/shard_map/all_to_all | solution.py:76
  69.9 1.5 %copy.37 = f32[1,8,128,224]{2,1,3,0:T(8,128)} copy(f32[1,8,128,224]{2,3,0,1:T(8,128)S(1)} %convert_multiply_fusion) | data formatting | bytes 1835008 | tf_op jit(solution)/shard_map/mul | solution.py:112
  71.3 1.3 mul.22
  73.6 1.2 max.36
  76.2 4.7 %collective-permute-start.15 = (f32[2,112,114]{2,1,0:T(8,128)S(1)}, f32[2,112,114]{2,1,0:T(8,128)S(1)}, u32[]{:S(2)}, u32[]{:S(2)}) collective-permute-start(f32[2,112,114]{2,1,0:T(8,128)S(1)} %concatenate.30), channel_id=1, source_target_pairs={{0,48},{8,56},{16,0},{24,8},{32,16},{40,24},{48,32},{56,40},{64,11... | collective-permute-start | bytes 306440 | tf_op jit(solution)/shard_map/ppermute | solution.py:20
  81.1 1.6 %collective-permute-start.14 = (f32[2,112,114]{2,1,0:T(8,128)S(1)}, f32[2,112,114]{2,1,0:T(8,128)S(1)}, u32[]{:S(2)}, u32[]{:S(2)}) collective-permute-start(f32[2,112,114]{2,1,0:T(8,128)S(1)} %concatenate.30), channel_id=1, source_target_pairs={{0,40},{8,48},{16,56},{24,0},{32,8},{40,16},{48,24},{56,32},{64,10... | collective-permute-start | bytes 306440 | tf_op jit(solution)/shard_map/ppermute | solution.py:20
  82.9 2.0 %collective-permute-start.12 = (f32[2,112,114]{2,1,0:T(8,128)S(1)}, f32[2,112,114]{2,1,0:T(8,128)S(1)}, u32[]{:S(2)}, u32[]{:S(2)}) collective-permute-start(f32[2,112,114]{2,1,0:T(8,128)S(1)} %concatenate.30), channel_id=1, source_target_pairs={{0,24},{8,32},{16,40},{24,48},{32,56},{40,0},{48,8},{56,16},{64,88... | collective-permute-start | bytes 306440 | tf_op jit(solution)/shard_map/ppermute | solution.py:20
  85.3 2.7 %collective-permute-start.11 = (f32[2,112,114]{2,1,0:T(8,128)S(1)}, f32[2,112,114]{2,1,0:T(8,128)S(1)}, u32[]{:S(2)}, u32[]{:S(2)}) collective-permute-start(f32[2,112,114]{2,1,0:T(8,128)S(1)} %concatenate.30), channel_id=1, source_target_pairs={{0,16},{8,24},{16,32},{24,40},{32,48},{40,56},{48,0},{56,8},{64,80... | collective-permute-start | bytes 306440 | tf_op jit(solution)/shard_map/ppermute | solution.py:20
  90.0 3.5 %all-to-all-start.2 = ((bf16[8,1,128,224]{2,3,1,0:T(8,128)(2,1)}), bf16[8,1,128,224]{2,3,1,0:T(8,128)(2,1)S(1)}, u32[]{:S(2)}, u32[]{:S(2)}) async-start(bf16[8,1,128,224]{2,3,1,0:T(8,128)(2,1)} %copy.39), calls=%async_computation.2 | async-start | bytes 917504 | tf_op jit(solution)/shard_map/all_to_all | solution.py:83
  93.5 2.4 %collective-permute-done.11 = f32[2,112,114]{2,1,0:T(8,128)S(1)} collective-permute-done((f32[2,112,114]{2,1,0:T(8,128)S(1)}, f32[2,112,114]{2,1,0:T(8,128)S(1)}, u32[]{:S(2)}, u32[]{:S(2)}) %collective-permute-start.11) | collective-permute-done | bytes 102176 | tf_op jit(solution)/shard_map/ppermute | solution.py:20
  97.3 1.7 %collective-permute-start.17 = (f32[2,112,114]{2,1,0:T(8,128)S(1)}, f32[2,112,114]{2,1,0:T(8,128)S(1)}, u32[]{:S(2)}, u32[]{:S(2)}) collective-permute-start(f32[2,112,114]{2,1,0:T(8,128)S(1)} %get-tuple-element.46), channel_id=1, source_target_pairs={{0,64},{8,72},{16,80},{24,88},{32,96},{40,104},{48,112},{56,120},{... | collective-permute-start | bytes 306440 | tf_op jit(solution)/shard_map/ppermute | solution.py:30
  99.0 1.6 %collective-permute-start.19 = (f32[2,112,114]{2,1,0:T(8,128)S(1)}, f32[2,112,114]{2,1,0:T(8,128)S(1)}, u32[]{:S(2)}, u32[]{:S(2)}) collective-permute-start(f32[2,112,114]{2,1,0:T(8,128)S(1)} %get-tuple-element.47), channel_id=1, source_target_pairs={{0,192},{8,200},{16,208},{24,216},{32,224},{40,232},{48,240},{56,2... | collective-permute-start | bytes 306440 | tf_op jit(solution)/shard_map/ppermute | solution.py:30
  100.6 2.0 %collective-permute-start.18 = (f32[2,112,114]{2,1,0:T(8,128)S(1)}, f32[2,112,114]{2,1,0:T(8,128)S(1)}, u32[]{:S(2)}, u32[]{:S(2)}) collective-permute-start(f32[2,112,114]{2,1,0:T(8,128)S(1)} %get-tuple-element.48), channel_id=1, source_target_pairs={{0,128},{8,136},{16,144},{24,152},{32,160},{40,168},{48,176},{56,1... | collective-permute-start | bytes 306440 | tf_op jit(solution)/shard_map/ppermute | solution.py:30
  102.7 1.9 %collective-permute-done.17 = f32[2,112,114]{2,1,0:T(8,128)S(1)} collective-permute-done((f32[2,112,114]{2,1,0:T(8,128)S(1)}, f32[2,112,114]{2,1,0:T(8,128)S(1)}, u32[]{:S(2)}, u32[]{:S(2)}) %collective-permute-start.17) | collective-permute-done | bytes 102176 | tf_op jit(solution)/shard_map/ppermute | solution.py:30
  104.9 2.0 %collective-permute-done.18 = f32[2,112,114]{2,1,0:T(8,128)S(1)} collective-permute-done((f32[2,112,114]{2,1,0:T(8,128)S(1)}, f32[2,112,114]{2,1,0:T(8,128)S(1)}, u32[]{:S(2)}, u32[]{:S(2)}) %collective-permute-start.18) | collective-permute-done | bytes 102176 | tf_op jit(solution)/shard_map/ppermute | solution.py:30
  107.6 3.0 %all-to-all-done.2 = bf16[8,1,128,224]{2,3,1,0:T(8,128)(2,1)S(1)} async-done(((bf16[8,1,128,224]{2,3,1,0:T(8,128)(2,1)}), bf16[8,1,128,224]{2,3,1,0:T(8,128)(2,1)S(1)}, u32[]{:S(2)}, u32[]{:S(2)}) %all-to-all-start.2) | async-done | bytes 458784 | tf_op jit(solution)/shard_map/all_to_all | solution.py:83
  111.5 3.5 %all-to-all-start.3 = ((bf16[8,2,112,113]{3,2,1,0:T(8,128)(2,1)}), bf16[8,2,112,113]{3,2,1,0:T(8,128)(2,1)S(1)}, u32[]{:S(2)}, u32[]{:S(2)}) async-start(bf16[8,2,112,113]{3,2,1,0:T(8,128)(2,1)} %broadcast_in_dim.406), calls=%async_computation.3 | async-start | bytes 917504 | tf_op jit(solution)/shard_map/all_to_all | solution.py:125
  116.1 15.4 %all-to-all-done.3 = bf16[8,2,112,113]{3,2,1,0:T(8,128)(2,1)S(1)} async-done(((bf16[8,2,112,113]{3,2,1,0:T(8,128)(2,1)}), bf16[8,2,112,113]{3,2,1,0:T(8,128)(2,1)S(1)}, u32[]{:S(2)}, u32[]{:S(2)}) %all-to-all-start.3) | async-done | bytes 405024 | tf_op jit(solution)/shard_map/all_to_all | solution.py:125
  (86 shorter events, 21.4 us)
Async XLA Ops:
  1.9 1.0 copy-start.2
  3.2 1.2 copy-start
  4.4 8.6 %copy-start.7 = (s32[128]{0:T(128)S(1)}, s32[128]{0:T(128)}, u32[]{:S(2)}) copy-start(s32[128]{0:T(128)} %param.9) | copy-start | bytes 1540
  4.4 24.7 %all-to-all-start.1 = ((bf16[8,2,112,113]{3,2,1,0:T(8,128)(2,1)}), bf16[8,2,112,113]{3,2,1,0:T(8,128)(2,1)S(1)}, u32[]{:S(2)}, u32[]{:S(2)}) async-start(bf16[8,2,112,113]{3,2,1,0:T(8,128)(2,1)} %bitcast.7), calls=%async_computation.1 | async-start | bytes 917504 | tf_op jit(solution)/shard_map/all_to_all | solution.py:100
  13.0 19.0 %copy-start.3 = (bf16[128,1792]{1,0:T(8,128)(2,1)S(1)}, bf16[128,1792]{1,0:T(8,128)(2,1)}, u32[]{:S(2)}) copy-start(bf16[128,1792]{1,0:T(8,128)(2,1)} %param.5) | copy-start | bytes 1376260
  29.2 3.1 %copy-start.4 = (bf16[128,1792]{1,0:T(8,128)(2,1)S(1)}, bf16[128,1792]{1,0:T(8,128)(2,1)}, u32[]{:S(2)}) copy-start(bf16[128,1792]{1,0:T(8,128)(2,1)} %param.8) | copy-start | bytes 1376260
  29.2 5.7 %collective-permute-start.6 = (f32[2,112,114]{2,1,0:T(8,128)S(1)}, f32[2,112,114]{2,1,0:T(8,128)S(1)}, u32[]{:S(2)}, u32[]{:S(2)}) collective-permute-start(f32[2,112,114]{2,1,0:T(8,128)S(1)} %concatenate.26), channel_id=1, source_target_pairs={{0,56},{8,0},{16,8},{24,16},{32,24},{40,32},{48,40},{56,48},{64,12... | collective-permute-start | bytes 306440 | tf_op jit(solution)/shard_map/ppermute | solution.py:20
  29.3 7.7 %collective-permute-start.5 = (f32[2,112,114]{2,1,0:T(8,128)S(1)}, f32[2,112,114]{2,1,0:T(8,128)S(1)}, u32[]{:S(2)}, u32[]{:S(2)}) collective-permute-start(f32[2,112,114]{2,1,0:T(8,128)S(1)} %concatenate.26), channel_id=1, source_target_pairs={{0,48},{8,56},{16,0},{24,8},{32,16},{40,24},{48,32},{56,40},{64,11... | collective-permute-start | bytes 306440 | tf_op jit(solution)/shard_map/ppermute | solution.py:20
  32.5 10.0 %collective-permute-start.4 = (f32[2,112,114]{2,1,0:T(8,128)S(1)}, f32[2,112,114]{2,1,0:T(8,128)S(1)}, u32[]{:S(2)}, u32[]{:S(2)}) collective-permute-start(f32[2,112,114]{2,1,0:T(8,128)S(1)} %concatenate.26), channel_id=1, source_target_pairs={{0,40},{8,48},{16,56},{24,0},{32,8},{40,16},{48,24},{56,32},{64,10... | collective-permute-start | bytes 306440 | tf_op jit(solution)/shard_map/ppermute | solution.py:20
  32.6 10.4 %collective-permute-start.3 = (f32[2,112,114]{2,1,0:T(8,128)S(1)}, f32[2,112,114]{2,1,0:T(8,128)S(1)}, u32[]{:S(2)}, u32[]{:S(2)}) collective-permute-start(f32[2,112,114]{2,1,0:T(8,128)S(1)} %concatenate.26), channel_id=1, source_target_pairs={{0,32},{8,40},{16,48},{24,56},{32,0},{40,8},{48,16},{56,24},{64,96... | collective-permute-start | bytes 306440 | tf_op jit(solution)/shard_map/ppermute | solution.py:20
  33.7 9.4 %collective-permute-start.2 = (f32[2,112,114]{2,1,0:T(8,128)S(1)}, f32[2,112,114]{2,1,0:T(8,128)S(1)}, u32[]{:S(2)}, u32[]{:S(2)}) collective-permute-start(f32[2,112,114]{2,1,0:T(8,128)S(1)} %concatenate.26), channel_id=1, source_target_pairs={{0,24},{8,32},{16,40},{24,48},{32,56},{40,0},{48,8},{56,16},{64,88... | collective-permute-start | bytes 306440 | tf_op jit(solution)/shard_map/ppermute | solution.py:20
  34.9 10.4 %collective-permute-start.1 = (f32[2,112,114]{2,1,0:T(8,128)S(1)}, f32[2,112,114]{2,1,0:T(8,128)S(1)}, u32[]{:S(2)}, u32[]{:S(2)}) collective-permute-start(f32[2,112,114]{2,1,0:T(8,128)S(1)} %concatenate.26), channel_id=1, source_target_pairs={{0,16},{8,24},{16,32},{24,40},{32,48},{40,56},{48,0},{56,8},{64,80... | collective-permute-start | bytes 306440 | tf_op jit(solution)/shard_map/ppermute | solution.py:20
  37.0 9.0 %collective-permute-start = (f32[2,112,114]{2,1,0:T(8,128)S(1)}, f32[2,112,114]{2,1,0:T(8,128)S(1)}, u32[]{:S(2)}, u32[]{:S(2)}) collective-permute-start(f32[2,112,114]{2,1,0:T(8,128)S(1)} %concatenate.26), channel_id=1, source_target_pairs={{0,8},{8,16},{16,24},{24,32},{32,40},{40,48},{48,56},{56,0},{64,72... | collective-permute-start | bytes 306440 | tf_op jit(solution)/shard_map/ppermute | solution.py:20
  38.9 30.9 %all-to-all-start = ((bf16[8,2,128,224]{2,3,1,0:T(8,128)(2,1)}), bf16[8,2,128,224]{2,3,1,0:T(8,128)(2,1)S(1)}, u32[]{:S(2)}, u32[]{:S(2)}) async-start(bf16[8,2,128,224]{2,3,1,0:T(8,128)(2,1)} %copy.33), calls=%async_computation | async-start | bytes 1835008 | tf_op jit(solution)/shard_map/all_to_all | solution.py:76
  47.4 6.7 %collective-permute-start.7 = (f32[2,112,114]{2,1,0:T(8,128)S(1)}, f32[2,112,114]{2,1,0:T(8,128)S(1)}, u32[]{:S(2)}, u32[]{:S(2)}) collective-permute-start(f32[2,112,114]{2,1,0:T(8,128)S(1)} %get-tuple-element.49), channel_id=1, source_target_pairs={{0,64},{8,72},{16,80},{24,88},{32,96},{40,104},{48,112},{56,120},{... | collective-permute-start | bytes 306440 | tf_op jit(solution)/shard_map/ppermute | solution.py:30
  49.0 5.5 %collective-permute-start.9 = (f32[2,112,114]{2,1,0:T(8,128)S(1)}, f32[2,112,114]{2,1,0:T(8,128)S(1)}, u32[]{:S(2)}, u32[]{:S(2)}) collective-permute-start(f32[2,112,114]{2,1,0:T(8,128)S(1)} %get-tuple-element.50), channel_id=1, source_target_pairs={{0,192},{8,200},{16,208},{24,216},{32,224},{40,232},{48,240},{56,2... | collective-permute-start | bytes 306440 | tf_op jit(solution)/shard_map/ppermute | solution.py:30
  50.7 6.3 %collective-permute-start.8 = (f32[2,112,114]{2,1,0:T(8,128)S(1)}, f32[2,112,114]{2,1,0:T(8,128)S(1)}, u32[]{:S(2)}, u32[]{:S(2)}) collective-permute-start(f32[2,112,114]{2,1,0:T(8,128)S(1)} %get-tuple-element.51), channel_id=1, source_target_pairs={{0,128},{8,136},{16,144},{24,152},{32,160},{40,168},{48,176},{56,1... | collective-permute-start | bytes 306440 | tf_op jit(solution)/shard_map/ppermute | solution.py:30
  75.4 0.8 copy-start.5
  76.2 9.1 %collective-permute-start.16 = (f32[2,112,114]{2,1,0:T(8,128)S(1)}, f32[2,112,114]{2,1,0:T(8,128)S(1)}, u32[]{:S(2)}, u32[]{:S(2)}) collective-permute-start(f32[2,112,114]{2,1,0:T(8,128)S(1)} %concatenate.30), channel_id=1, source_target_pairs={{0,56},{8,0},{16,8},{24,16},{32,24},{40,32},{48,40},{56,48},{64,12... | collective-permute-start | bytes 306440 | tf_op jit(solution)/shard_map/ppermute | solution.py:20
  76.2 11.8 %collective-permute-start.15 = (f32[2,112,114]{2,1,0:T(8,128)S(1)}, f32[2,112,114]{2,1,0:T(8,128)S(1)}, u32[]{:S(2)}, u32[]{:S(2)}) collective-permute-start(f32[2,112,114]{2,1,0:T(8,128)S(1)} %concatenate.30), channel_id=1, source_target_pairs={{0,48},{8,56},{16,0},{24,8},{32,16},{40,24},{48,32},{56,40},{64,11... | collective-permute-start | bytes 306440 | tf_op jit(solution)/shard_map/ppermute | solution.py:20
  81.1 7.8 %copy-start.6 = (bf16[1024,2,112]{0,2,1:T(8,128)(2,1)S(1)}, bf16[1024,2,112]{0,2,1:T(8,128)(2,1)}, u32[]{:S(2)}) copy-start(bf16[1024,2,112]{0,2,1:T(8,128)(2,1)} %copy-done.5) | copy-start | bytes 1376260
  81.1 12.4 %collective-permute-start.14 = (f32[2,112,114]{2,1,0:T(8,128)S(1)}, f32[2,112,114]{2,1,0:T(8,128)S(1)}, u32[]{:S(2)}, u32[]{:S(2)}) collective-permute-start(f32[2,112,114]{2,1,0:T(8,128)S(1)} %concatenate.30), channel_id=1, source_target_pairs={{0,40},{8,48},{16,56},{24,0},{32,8},{40,16},{48,24},{56,32},{64,10... | collective-permute-start | bytes 306440 | tf_op jit(solution)/shard_map/ppermute | solution.py:20
  82.7 10.9 %collective-permute-start.13 = (f32[2,112,114]{2,1,0:T(8,128)S(1)}, f32[2,112,114]{2,1,0:T(8,128)S(1)}, u32[]{:S(2)}, u32[]{:S(2)}) collective-permute-start(f32[2,112,114]{2,1,0:T(8,128)S(1)} %concatenate.30), channel_id=1, source_target_pairs={{0,32},{8,40},{16,48},{24,56},{32,0},{40,8},{48,16},{56,24},{64,96... | collective-permute-start | bytes 306440 | tf_op jit(solution)/shard_map/ppermute | solution.py:20
  82.9 10.6 %collective-permute-start.12 = (f32[2,112,114]{2,1,0:T(8,128)S(1)}, f32[2,112,114]{2,1,0:T(8,128)S(1)}, u32[]{:S(2)}, u32[]{:S(2)}) collective-permute-start(f32[2,112,114]{2,1,0:T(8,128)S(1)} %concatenate.30), channel_id=1, source_target_pairs={{0,24},{8,32},{16,40},{24,48},{32,56},{40,0},{48,8},{56,16},{64,88... | collective-permute-start | bytes 306440 | tf_op jit(solution)/shard_map/ppermute | solution.py:20
  85.3 10.7 %collective-permute-start.11 = (f32[2,112,114]{2,1,0:T(8,128)S(1)}, f32[2,112,114]{2,1,0:T(8,128)S(1)}, u32[]{:S(2)}, u32[]{:S(2)}) collective-permute-start(f32[2,112,114]{2,1,0:T(8,128)S(1)} %concatenate.30), channel_id=1, source_target_pairs={{0,16},{8,24},{16,32},{24,40},{32,48},{40,56},{48,0},{56,8},{64,80... | collective-permute-start | bytes 306440 | tf_op jit(solution)/shard_map/ppermute | solution.py:20
  88.0 8.0 %collective-permute-start.10 = (f32[2,112,114]{2,1,0:T(8,128)S(1)}, f32[2,112,114]{2,1,0:T(8,128)S(1)}, u32[]{:S(2)}, u32[]{:S(2)}) collective-permute-start(f32[2,112,114]{2,1,0:T(8,128)S(1)} %concatenate.30), channel_id=1, source_target_pairs={{0,8},{8,16},{16,24},{24,32},{32,40},{40,48},{48,56},{56,0},{64,72... | collective-permute-start | bytes 306440 | tf_op jit(solution)/shard_map/ppermute | solution.py:20
  90.0 20.6 %all-to-all-start.2 = ((bf16[8,1,128,224]{2,3,1,0:T(8,128)(2,1)}), bf16[8,1,128,224]{2,3,1,0:T(8,128)(2,1)S(1)}, u32[]{:S(2)}, u32[]{:S(2)}) async-start(bf16[8,1,128,224]{2,3,1,0:T(8,128)(2,1)} %copy.39), calls=%async_computation.2 | async-start | bytes 917504 | tf_op jit(solution)/shard_map/all_to_all | solution.py:83
  97.3 7.2 %collective-permute-start.17 = (f32[2,112,114]{2,1,0:T(8,128)S(1)}, f32[2,112,114]{2,1,0:T(8,128)S(1)}, u32[]{:S(2)}, u32[]{:S(2)}) collective-permute-start(f32[2,112,114]{2,1,0:T(8,128)S(1)} %get-tuple-element.46), channel_id=1, source_target_pairs={{0,64},{8,72},{16,80},{24,88},{32,96},{40,104},{48,112},{56,120},{... | collective-permute-start | bytes 306440 | tf_op jit(solution)/shard_map/ppermute | solution.py:30
  99.0 5.7 %collective-permute-start.19 = (f32[2,112,114]{2,1,0:T(8,128)S(1)}, f32[2,112,114]{2,1,0:T(8,128)S(1)}, u32[]{:S(2)}, u32[]{:S(2)}) collective-permute-start(f32[2,112,114]{2,1,0:T(8,128)S(1)} %get-tuple-element.47), channel_id=1, source_target_pairs={{0,192},{8,200},{16,208},{24,216},{32,224},{40,232},{48,240},{56,2... | collective-permute-start | bytes 306440 | tf_op jit(solution)/shard_map/ppermute | solution.py:30
  100.6 6.3 %collective-permute-start.18 = (f32[2,112,114]{2,1,0:T(8,128)S(1)}, f32[2,112,114]{2,1,0:T(8,128)S(1)}, u32[]{:S(2)}, u32[]{:S(2)}) collective-permute-start(f32[2,112,114]{2,1,0:T(8,128)S(1)} %get-tuple-element.48), channel_id=1, source_target_pairs={{0,128},{8,136},{16,144},{24,152},{32,160},{40,168},{48,176},{56,1... | collective-permute-start | bytes 306440 | tf_op jit(solution)/shard_map/ppermute | solution.py:30
  111.5 20.0 %all-to-all-start.3 = ((bf16[8,2,112,113]{3,2,1,0:T(8,128)(2,1)}), bf16[8,2,112,113]{3,2,1,0:T(8,128)(2,1)S(1)}, u32[]{:S(2)}, u32[]{:S(2)}) async-start(bf16[8,2,112,113]{3,2,1,0:T(8,128)(2,1)} %broadcast_in_dim.406), calls=%async_computation.3 | async-start | bytes 917504 | tf_op jit(solution)/shard_map/all_to_all | solution.py:125
  132.2 1.0 copy-start.1

commit v12 on v11

--- a/solution.py
+++ b/solution.py
@@ -99,9 +99,10 @@
     state_part = jnp.sum(
         lax.all_to_all(pieces, "inner", 0, 0, tiled=True).astype(jnp.float32), axis=0
     )
-    query_heads, cotangent_heads = to_heads([query_input, cotangent])
+    feat_query, scaled_heads = to_heads(
+        [jnp.maximum(query_input, 0), cotangent * jnp.asarray(loss_scale, jnp.bfloat16)]
+    )
 
-    feat_query = jnp.maximum(query_heads, 0)
     label = span_labels[0]
     state_vis = visible(state_part, label, False)
     both = jnp.einsum("thk,hkv->thv", feat_query, state_vis, preferred_element_type=jnp.float32)
@@ -109,7 +110,7 @@
     weight = both[..., DH]
     denominator = weight / DH + 1.0
     output = numerator / (DH * denominator[..., None])
-    scaled = cotangent_heads.astype(jnp.float32) * loss_scale
+    scaled = scaled_heads.astype(jnp.float32)
     numer_back = (scaled / (DH * denominator[..., None])).astype(jnp.bfloat16)
     weight_back = (-jnp.sum(scaled * output, axis=-1) / (DH * denominator)).astype(jnp.bfloat16)
     back_aug = jnp.concatenate([numer_back, weight_back[..., None]], axis=-1)
@@ -117,7 +118,7 @@
         "thk,thv->hkv", feat_query, back_aug, preferred_element_type=jnp.float32
     )
     query_feat = jnp.einsum("thv,hkv->thk", back_aug, state_vis, preferred_element_type=jnp.float32)
-    query_back = jnp.where(query_heads > 0, query_feat, 0.0).astype(jnp.bfloat16)
+    query_back = jnp.where(feat_query > 0, query_feat, 0.0).astype(jnp.bfloat16)
     adjoint_vis = visible(adjoint_part, label, True)
     (query_out,) = to_rows([query_back])
 

time: 137 us -> 134 us (0.978)
  the two profiles are of different devices: /device:TPU:2 before, /device:TPU:22 now
where the time goes in v12:
time: 134 us
  waiting for transfers between devices  71.4 us (53%)
  starting transfers between devices  39.6 us (30%)
  local copies, waits for them, and re-layouts  12.1 us (9%)
  other arithmetic  6.64 us (5%)
  matrix products  2.79 us (2%)
    all_to_all x1, waiting for transfers between devices, to_heads(): incoming = lax.all_to_all(outgoing, 'inner', 0, 0, tiled=True)  15.2 us
    all_to_all x1, waiting for transfers between devices, local(): lax.all_to_all(copies, 'inner', 0, 0, tiled=True)  14.7 us
    all_to_all x1, waiting for transfers between devices, local(): lax.all_to_all(pieces, 'inner', 0, 0, tiled=True).astype(jnp.float32)  14.1 us
    ppermute x14, starting transfers between devices, shifted(): return lax.ppermute(value, 'tm', pairs)  13.3 us
    ppermute x14, waiting for transfers between devices, shifted(): return lax.ppermute(value, 'tm', pairs)  13.2 us
    ppermute x6, waiting for transfers between devices, strided(): return lax.ppermute(value, 'tm', pairs)  8.8 us
    all_to_all x1, starting transfers between devices, local(): lax.all_to_all(pieces, 'inner', 0, 0, tiled=True).astype(jnp.float32)  8.6 us
    unnamed x23, local copies, waits for them, and re-layouts  8.36 us
  transfers between devices with their start and end apart: 24, of which 12 were waited for; matrix products, arithmetic and copies ran while one was open for 6% of the time, Pallas kernels for 0%

profile of v12, /device:TPU:22, one launch (start us, length us, event | category | flops | bytes accessed | tf_op | source)
XLA Modules:
  0.0 133.8 jit_solution(6812665263276855522)
XLA Ops:
  0.6 1.3 copy.34
  2.0 1.0 copy-done.3
  3.2 1.2 convolution_convert_fusion.1
  4.4 8.6 %all-to-all-start.1 = ((bf16[8,2,112,113]{3,2,1,0:T(8,128)(2,1)}), bf16[8,2,112,113]{3,2,1,0:T(8,128)(2,1)S(1)}, u32[]{:S(2)}, u32[]{:S(2)}) async-start(bf16[8,2,112,113]{3,2,1,0:T(8,128)(2,1)} %bitcast.7), calls=%async_computation.1 | async-start | bytes 917504 | tf_op jit(solution)/shard_map/all_to_all | solution.py:100
  15.0 14.1 %all-to-all-done.1 = bf16[8,2,112,113]{3,2,1,0:T(8,128)(2,1)S(1)} async-done(((bf16[8,2,112,113]{3,2,1,0:T(8,128)(2,1)}), bf16[8,2,112,113]{3,2,1,0:T(8,128)(2,1)S(1)}, u32[]{:S(2)}, u32[]{:S(2)}) %all-to-all-start.1) | async-done | bytes 405024 | tf_op jit(solution)/shard_map/all_to_all | solution.py:100
  30.2 0.9 collective-permute-start.4
  31.1 2.6 %collective-permute-start.3 = (f32[2,112,114]{2,1,0:T(8,128)S(1)}, f32[2,112,114]{2,1,0:T(8,128)S(1)}, u32[]{:S(2)}, u32[]{:S(2)}) collective-permute-start(f32[2,112,114]{2,1,0:T(8,128)S(1)} %concatenate.26), channel_id=1, source_target_pairs={{0,32},{8,40},{16,48},{24,56},{32,0},{40,8},{48,16},{56,24},{64,96... | collective-permute-start | bytes 306440 | tf_op jit(solution)/shard_map/ppermute | solution.py:20
  33.6 2.0 %collective-permute-start.2 = (f32[2,112,114]{2,1,0:T(8,128)S(1)}, f32[2,112,114]{2,1,0:T(8,128)S(1)}, u32[]{:S(2)}, u32[]{:S(2)}) collective-permute-start(f32[2,112,114]{2,1,0:T(8,128)S(1)} %concatenate.26), channel_id=1, source_target_pairs={{0,24},{8,32},{16,40},{24,48},{32,56},{40,0},{48,8},{56,16},{64,88... | collective-permute-start | bytes 306440 | tf_op jit(solution)/shard_map/ppermute | solution.py:20
  35.9 7.4 %collective-permute-done.5 = f32[2,112,114]{2,1,0:T(8,128)S(1)} collective-permute-done((f32[2,112,114]{2,1,0:T(8,128)S(1)}, f32[2,112,114]{2,1,0:T(8,128)S(1)}, u32[]{:S(2)}, u32[]{:S(2)}) %collective-permute-start.5) | collective-permute-done | bytes 102176 | tf_op jit(solution)/shard_map/ppermute | solution.py:20
  43.4 1.0 copy.32
  44.4 3.6 %all-to-all-start = ((bf16[8,2,128,224]{2,3,1,0:T(8,128)(2,1)}), bf16[8,2,128,224]{2,3,1,0:T(8,128)(2,1)S(1)}, u32[]{:S(2)}, u32[]{:S(2)}) async-start(bf16[8,2,128,224]{2,3,1,0:T(8,128)(2,1)} %copy.32), calls=%async_computation | async-start | bytes 1835008 | tf_op jit(solution)/shard_map/all_to_all | solution.py:76
  49.4 1.4 %collective-permute-start.7 = (f32[2,112,114]{2,1,0:T(8,128)S(1)}, f32[2,112,114]{2,1,0:T(8,128)S(1)}, u32[]{:S(2)}, u32[]{:S(2)}) collective-permute-start(f32[2,112,114]{2,1,0:T(8,128)S(1)} %get-tuple-element.51), channel_id=1, source_target_pairs={{0,64},{8,72},{16,80},{24,88},{32,96},{40,104},{48,112},{56,120},{... | collective-permute-start | bytes 306440 | tf_op jit(solution)/shard_map/ppermute | solution.py:30
  51.5 1.5 %collective-permute-start.8 = (f32[2,112,114]{2,1,0:T(8,128)S(1)}, f32[2,112,114]{2,1,0:T(8,128)S(1)}, u32[]{:S(2)}, u32[]{:S(2)}) collective-permute-start(f32[2,112,114]{2,1,0:T(8,128)S(1)} %get-tuple-element.53), channel_id=1, source_target_pairs={{0,128},{8,136},{16,144},{24,152},{32,160},{40,168},{48,176},{56,1... | collective-permute-start | bytes 306440 | tf_op jit(solution)/shard_map/ppermute | solution.py:30
  53.1 1.2 collective-permute-done.7
  54.5 1.8 %collective-permute-done.9 = f32[2,112,114]{2,1,0:T(8,128)S(1)} collective-permute-done((f32[2,112,114]{2,1,0:T(8,128)S(1)}, f32[2,112,114]{2,1,0:T(8,128)S(1)}, u32[]{:S(2)}, u32[]{:S(2)}) %collective-permute-start.9) | collective-permute-done | bytes 102176 | tf_op jit(solution)/shard_map/ppermute | solution.py:30
  56.5 1.3 %collective-permute-done.8 = f32[2,112,114]{2,1,0:T(8,128)S(1)} collective-permute-done((f32[2,112,114]{2,1,0:T(8,128)S(1)}, f32[2,112,114]{2,1,0:T(8,128)S(1)}, u32[]{:S(2)}, u32[]{:S(2)}) %collective-permute-start.8) | collective-permute-done | bytes 102176 | tf_op jit(solution)/shard_map/ppermute | solution.py:30
  58.5 15.2 %all-to-all-done = bf16[8,2,128,224]{2,3,1,0:T(8,128)(2,1)S(1)} async-done(((bf16[8,2,128,224]{2,3,1,0:T(8,128)(2,1)}), bf16[8,2,128,224]{2,3,1,0:T(8,128)(2,1)S(1)}, u32[]{:S(2)}, u32[]{:S(2)}) %all-to-all-start) | async-done | bytes 917536 | tf_op jit(solution)/shard_map/all_to_all | solution.py:76
  77.9 3.3 %collective-permute-start.13 = (f32[2,112,114]{2,1,0:T(8,128)S(1)}, f32[2,112,114]{2,1,0:T(8,128)S(1)}, u32[]{:S(2)}, u32[]{:S(2)}) collective-permute-start(f32[2,112,114]{2,1,0:T(8,128)S(1)} %concatenate.30), channel_id=1, source_target_pairs={{0,32},{8,40},{16,48},{24,56},{32,0},{40,8},{48,16},{56,24},{64,96... | collective-permute-start | bytes 306440 | tf_op jit(solution)/shard_map/ppermute | solution.py:20
  81.8 2.4 %collective-permute-start.11 = (f32[2,112,114]{2,1,0:T(8,128)S(1)}, f32[2,112,114]{2,1,0:T(8,128)S(1)}, u32[]{:S(2)}, u32[]{:S(2)}) collective-permute-start(f32[2,112,114]{2,1,0:T(8,128)S(1)} %concatenate.30), channel_id=1, source_target_pairs={{0,16},{8,24},{16,32},{24,40},{32,48},{40,56},{48,0},{56,8},{64,80... | collective-permute-start | bytes 306440 | tf_op jit(solution)/shard_map/ppermute | solution.py:20
  84.1 5.8 %collective-permute-done.15 = f32[2,112,114]{2,1,0:T(8,128)S(1)} collective-permute-done((f32[2,112,114]{2,1,0:T(8,128)S(1)}, f32[2,112,114]{2,1,0:T(8,128)S(1)}, u32[]{:S(2)}, u32[]{:S(2)}) %collective-permute-start.15) | collective-permute-done | bytes 102176 | tf_op jit(solution)/shard_map/ppermute | solution.py:20
  91.1 3.5 %all-to-all-start.2 = ((bf16[8,1,128,224]{2,3,1,0:T(8,128)(2,1)}), bf16[8,1,128,224]{2,3,1,0:T(8,128)(2,1)S(1)}, u32[]{:S(2)}, u32[]{:S(2)}) async-start(bf16[8,1,128,224]{2,3,1,0:T(8,128)(2,1)} %copy.37), calls=%async_computation.2 | async-start | bytes 917504 | tf_op jit(solution)/shard_map/all_to_all | solution.py:83
  96.0 1.4 %collective-permute-start.17 = (f32[2,112,114]{2,1,0:T(8,128)S(1)}, f32[2,112,114]{2,1,0:T(8,128)S(1)}, u32[]{:S(2)}, u32[]{:S(2)}) collective-permute-start(f32[2,112,114]{2,1,0:T(8,128)S(1)} %get-tuple-element.48), channel_id=1, source_target_pairs={{0,64},{8,72},{16,80},{24,88},{32,96},{40,104},{48,112},{56,120},{... | collective-permute-start | bytes 306440 | tf_op jit(solution)/shard_map/ppermute | solution.py:30
  98.1 1.5 %collective-permute-start.18 = (f32[2,112,114]{2,1,0:T(8,128)S(1)}, f32[2,112,114]{2,1,0:T(8,128)S(1)}, u32[]{:S(2)}, u32[]{:S(2)}) collective-permute-start(f32[2,112,114]{2,1,0:T(8,128)S(1)} %get-tuple-element.50), channel_id=1, source_target_pairs={{0,128},{8,136},{16,144},{24,152},{32,160},{40,168},{48,176},{56,1... | collective-permute-start | bytes 306440 | tf_op jit(solution)/shard_map/ppermute | solution.py:30
  99.6 1.2 collective-permute-done.17
  101.0 1.8 %collective-permute-done.19 = f32[2,112,114]{2,1,0:T(8,128)S(1)} collective-permute-done((f32[2,112,114]{2,1,0:T(8,128)S(1)}, f32[2,112,114]{2,1,0:T(8,128)S(1)}, u32[]{:S(2)}, u32[]{:S(2)}) %collective-permute-start.19) | collective-permute-done | bytes 102176 | tf_op jit(solution)/shard_map/ppermute | solution.py:30
  103.0 1.3 %collective-permute-done.18 = f32[2,112,114]{2,1,0:T(8,128)S(1)} collective-permute-done((f32[2,112,114]{2,1,0:T(8,128)S(1)}, f32[2,112,114]{2,1,0:T(8,128)S(1)}, u32[]{:S(2)}, u32[]{:S(2)}) %collective-permute-start.18) | collective-permute-done | bytes 102176 | tf_op jit(solution)/shard_map/ppermute | solution.py:30
  105.1 5.5 %all-to-all-done.2 = bf16[8,1,128,224]{2,3,1,0:T(8,128)(2,1)S(1)} async-done(((bf16[8,1,128,224]{2,3,1,0:T(8,128)(2,1)}), bf16[8,1,128,224]{2,3,1,0:T(8,128)(2,1)S(1)}, u32[]{:S(2)}, u32[]{:S(2)}) %all-to-all-start.2) | async-done | bytes 458784 | tf_op jit(solution)/shard_map/all_to_all | solution.py:83
  111.4 3.5 %all-to-all-start.3 = ((bf16[8,2,112,113]{3,2,1,0:T(8,128)(2,1)}), bf16[8,2,112,113]{3,2,1,0:T(8,128)(2,1)S(1)}, u32[]{:S(2)}, u32[]{:S(2)}) async-start(bf16[8,2,112,113]{3,2,1,0:T(8,128)(2,1)} %broadcast_in_dim.406), calls=%async_computation.3 | async-start | bytes 917504 | tf_op jit(solution)/shard_map/all_to_all | solution.py:126
  115.0 1.0 copy.41
  116.0 14.7 %all-to-all-done.3 = bf16[8,2,112,113]{3,2,1,0:T(8,128)(2,1)S(1)} async-done(((bf16[8,2,112,113]{3,2,1,0:T(8,128)(2,1)}), bf16[8,2,112,113]{3,2,1,0:T(8,128)(2,1)S(1)}, u32[]{:S(2)}, u32[]{:S(2)}) %all-to-all-start.3) | async-done | bytes 405024 | tf_op jit(solution)/shard_map/all_to_all | solution.py:126
  131.4 1.0 copy.43
  132.8 1.0 copy.42
  (82 shorter events, 17.9 us)
Async XLA Ops:
  1.9 1.0 copy-start.3
  3.2 1.2 copy-start
  4.4 9.3 %copy-start.4 = (bf16[128,1792]{1,0:T(8,128)(2,1)S(1)}, bf16[128,1792]{1,0:T(8,128)(2,1)}, u32[]{:S(2)}) copy-start(bf16[128,1792]{1,0:T(8,128)(2,1)} %param.5) | copy-start | bytes 1376260
  4.4 24.7 %all-to-all-start.1 = ((bf16[8,2,112,113]{3,2,1,0:T(8,128)(2,1)}), bf16[8,2,112,113]{3,2,1,0:T(8,128)(2,1)S(1)}, u32[]{:S(2)}, u32[]{:S(2)}) async-start(bf16[8,2,112,113]{3,2,1,0:T(8,128)(2,1)} %bitcast.7), calls=%async_computation.1 | async-start | bytes 917504 | tf_op jit(solution)/shard_map/all_to_all | solution.py:100
  13.0 0.7 copy-start.6
  13.7 1.0 copy-start.5
  29.2 6.4 %collective-permute-start.6 = (f32[2,112,114]{2,1,0:T(8,128)S(1)}, f32[2,112,114]{2,1,0:T(8,128)S(1)}, u32[]{:S(2)}, u32[]{:S(2)}) collective-permute-start(f32[2,112,114]{2,1,0:T(8,128)S(1)} %concatenate.26), channel_id=1, source_target_pairs={{0,56},{8,0},{16,8},{24,16},{32,24},{40,32},{48,40},{56,48},{64,12... | collective-permute-start | bytes 306440 | tf_op jit(solution)/shard_map/ppermute | solution.py:20
  29.5 13.8 %collective-permute-start.5 = (f32[2,112,114]{2,1,0:T(8,128)S(1)}, f32[2,112,114]{2,1,0:T(8,128)S(1)}, u32[]{:S(2)}, u32[]{:S(2)}) collective-permute-start(f32[2,112,114]{2,1,0:T(8,128)S(1)} %concatenate.26), channel_id=1, source_target_pairs={{0,48},{8,56},{16,0},{24,8},{32,16},{40,24},{48,32},{56,40},{64,11... | collective-permute-start | bytes 306440 | tf_op jit(solution)/shard_map/ppermute | solution.py:20
  30.2 17.9 %collective-permute-start.4 = (f32[2,112,114]{2,1,0:T(8,128)S(1)}, f32[2,112,114]{2,1,0:T(8,128)S(1)}, u32[]{:S(2)}, u32[]{:S(2)}) collective-permute-start(f32[2,112,114]{2,1,0:T(8,128)S(1)} %concatenate.26), channel_id=1, source_target_pairs={{0,40},{8,48},{16,56},{24,0},{32,8},{40,16},{48,24},{56,32},{64,10... | collective-permute-start | bytes 306440 | tf_op jit(solution)/shard_map/ppermute | solution.py:20
  31.1 16.9 %collective-permute-start.3 = (f32[2,112,114]{2,1,0:T(8,128)S(1)}, f32[2,112,114]{2,1,0:T(8,128)S(1)}, u32[]{:S(2)}, u32[]{:S(2)}) collective-permute-start(f32[2,112,114]{2,1,0:T(8,128)S(1)} %concatenate.26), channel_id=1, source_target_pairs={{0,32},{8,40},{16,48},{24,56},{32,0},{40,8},{48,16},{56,24},{64,96... | collective-permute-start | bytes 306440 | tf_op jit(solution)/shard_map/ppermute | solution.py:20
  33.6 14.4 %collective-permute-start.2 = (f32[2,112,114]{2,1,0:T(8,128)S(1)}, f32[2,112,114]{2,1,0:T(8,128)S(1)}, u32[]{:S(2)}, u32[]{:S(2)}) collective-permute-start(f32[2,112,114]{2,1,0:T(8,128)S(1)} %concatenate.26), channel_id=1, source_target_pairs={{0,24},{8,32},{16,40},{24,48},{32,56},{40,0},{48,8},{56,16},{64,88... | collective-permute-start | bytes 306440 | tf_op jit(solution)/shard_map/ppermute | solution.py:20
  35.6 12.4 %collective-permute-start.1 = (f32[2,112,114]{2,1,0:T(8,128)S(1)}, f32[2,112,114]{2,1,0:T(8,128)S(1)}, u32[]{:S(2)}, u32[]{:S(2)}) collective-permute-start(f32[2,112,114]{2,1,0:T(8,128)S(1)} %concatenate.26), channel_id=1, source_target_pairs={{0,16},{8,24},{16,32},{24,40},{32,48},{40,56},{48,0},{56,8},{64,80... | collective-permute-start | bytes 306440 | tf_op jit(solution)/shard_map/ppermute | solution.py:20
  43.3 4.8 %collective-permute-start = (f32[2,112,114]{2,1,0:T(8,128)S(1)}, f32[2,112,114]{2,1,0:T(8,128)S(1)}, u32[]{:S(2)}, u32[]{:S(2)}) collective-permute-start(f32[2,112,114]{2,1,0:T(8,128)S(1)} %concatenate.26), channel_id=1, source_target_pairs={{0,8},{8,16},{16,24},{24,32},{32,40},{40,48},{48,56},{56,0},{64,72... | collective-permute-start | bytes 306440 | tf_op jit(solution)/shard_map/ppermute | solution.py:20
  44.4 29.4 %all-to-all-start = ((bf16[8,2,128,224]{2,3,1,0:T(8,128)(2,1)}), bf16[8,2,128,224]{2,3,1,0:T(8,128)(2,1)S(1)}, u32[]{:S(2)}, u32[]{:S(2)}) async-start(bf16[8,2,128,224]{2,3,1,0:T(8,128)(2,1)} %copy.32), calls=%async_computation | async-start | bytes 1835008 | tf_op jit(solution)/shard_map/all_to_all | solution.py:76
  49.4 4.9 %collective-permute-start.7 = (f32[2,112,114]{2,1,0:T(8,128)S(1)}, f32[2,112,114]{2,1,0:T(8,128)S(1)}, u32[]{:S(2)}, u32[]{:S(2)}) collective-permute-start(f32[2,112,114]{2,1,0:T(8,128)S(1)} %get-tuple-element.51), channel_id=1, source_target_pairs={{0,64},{8,72},{16,80},{24,88},{32,96},{40,104},{48,112},{56,120},{... | collective-permute-start | bytes 306440 | tf_op jit(solution)/shard_map/ppermute | solution.py:30
  50.8 5.5 %collective-permute-start.9 = (f32[2,112,114]{2,1,0:T(8,128)S(1)}, f32[2,112,114]{2,1,0:T(8,128)S(1)}, u32[]{:S(2)}, u32[]{:S(2)}) collective-permute-start(f32[2,112,114]{2,1,0:T(8,128)S(1)} %get-tuple-element.52), channel_id=1, source_target_pairs={{0,192},{8,200},{16,208},{24,216},{32,224},{40,232},{48,240},{56,2... | collective-permute-start | bytes 306440 | tf_op jit(solution)/shard_map/ppermute | solution.py:30
  51.5 6.3 %collective-permute-start.8 = (f32[2,112,114]{2,1,0:T(8,128)S(1)}, f32[2,112,114]{2,1,0:T(8,128)S(1)}, u32[]{:S(2)}, u32[]{:S(2)}) collective-permute-start(f32[2,112,114]{2,1,0:T(8,128)S(1)} %get-tuple-element.53), channel_id=1, source_target_pairs={{0,128},{8,136},{16,144},{24,152},{32,160},{40,168},{48,176},{56,1... | collective-permute-start | bytes 306440 | tf_op jit(solution)/shard_map/ppermute | solution.py:30
  75.1 1.0 copy-start.2
  77.5 4.2 %collective-permute-start.16 = (f32[2,112,114]{2,1,0:T(8,128)S(1)}, f32[2,112,114]{2,1,0:T(8,128)S(1)}, u32[]{:S(2)}, u32[]{:S(2)}) collective-permute-start(f32[2,112,114]{2,1,0:T(8,128)S(1)} %concatenate.30), channel_id=1, source_target_pairs={{0,56},{8,0},{16,8},{24,16},{32,24},{40,32},{48,40},{56,48},{64,12... | collective-permute-start | bytes 306440 | tf_op jit(solution)/shard_map/ppermute | solution.py:20
  77.5 12.4 %collective-permute-start.15 = (f32[2,112,114]{2,1,0:T(8,128)S(1)}, f32[2,112,114]{2,1,0:T(8,128)S(1)}, u32[]{:S(2)}, u32[]{:S(2)}) collective-permute-start(f32[2,112,114]{2,1,0:T(8,128)S(1)} %concatenate.30), channel_id=1, source_target_pairs={{0,48},{8,56},{16,0},{24,8},{32,16},{40,24},{48,32},{56,40},{64,11... | collective-permute-start | bytes 306440 | tf_op jit(solution)/shard_map/ppermute | solution.py:20
  77.8 16.8 %collective-permute-start.14 = (f32[2,112,114]{2,1,0:T(8,128)S(1)}, f32[2,112,114]{2,1,0:T(8,128)S(1)}, u32[]{:S(2)}, u32[]{:S(2)}) collective-permute-start(f32[2,112,114]{2,1,0:T(8,128)S(1)} %concatenate.30), channel_id=1, source_target_pairs={{0,40},{8,48},{16,56},{24,0},{32,8},{40,16},{48,24},{56,32},{64,10... | collective-permute-start | bytes 306440 | tf_op jit(solution)/shard_map/ppermute | solution.py:20
  77.9 16.7 %collective-permute-start.13 = (f32[2,112,114]{2,1,0:T(8,128)S(1)}, f32[2,112,114]{2,1,0:T(8,128)S(1)}, u32[]{:S(2)}, u32[]{:S(2)}) collective-permute-start(f32[2,112,114]{2,1,0:T(8,128)S(1)} %concatenate.30), channel_id=1, source_target_pairs={{0,32},{8,40},{16,48},{24,56},{32,0},{40,8},{48,16},{56,24},{64,96... | collective-permute-start | bytes 306440 | tf_op jit(solution)/shard_map/ppermute | solution.py:20
  81.2 13.4 %collective-permute-start.12 = (f32[2,112,114]{2,1,0:T(8,128)S(1)}, f32[2,112,114]{2,1,0:T(8,128)S(1)}, u32[]{:S(2)}, u32[]{:S(2)}) collective-permute-start(f32[2,112,114]{2,1,0:T(8,128)S(1)} %concatenate.30), channel_id=1, source_target_pairs={{0,24},{8,32},{16,40},{24,48},{32,56},{40,0},{48,8},{56,16},{64,88... | collective-permute-start | bytes 306440 | tf_op jit(solution)/shard_map/ppermute | solution.py:20
  81.8 12.9 %collective-permute-start.11 = (f32[2,112,114]{2,1,0:T(8,128)S(1)}, f32[2,112,114]{2,1,0:T(8,128)S(1)}, u32[]{:S(2)}, u32[]{:S(2)}) collective-permute-start(f32[2,112,114]{2,1,0:T(8,128)S(1)} %concatenate.30), channel_id=1, source_target_pairs={{0,16},{8,24},{16,32},{24,40},{32,48},{40,56},{48,0},{56,8},{64,80... | collective-permute-start | bytes 306440 | tf_op jit(solution)/shard_map/ppermute | solution.py:20
  89.9 4.7 %collective-permute-start.10 = (f32[2,112,114]{2,1,0:T(8,128)S(1)}, f32[2,112,114]{2,1,0:T(8,128)S(1)}, u32[]{:S(2)}, u32[]{:S(2)}) collective-permute-start(f32[2,112,114]{2,1,0:T(8,128)S(1)} %concatenate.30), channel_id=1, source_target_pairs={{0,8},{8,16},{16,24},{24,32},{32,40},{40,48},{48,56},{56,0},{64,72... | collective-permute-start | bytes 306440 | tf_op jit(solution)/shard_map/ppermute | solution.py:20
  91.1 19.4 %all-to-all-start.2 = ((bf16[8,1,128,224]{2,3,1,0:T(8,128)(2,1)}), bf16[8,1,128,224]{2,3,1,0:T(8,128)(2,1)S(1)}, u32[]{:S(2)}, u32[]{:S(2)}) async-start(bf16[8,1,128,224]{2,3,1,0:T(8,128)(2,1)} %copy.37), calls=%async_computation.2 | async-start | bytes 917504 | tf_op jit(solution)/shard_map/all_to_all | solution.py:83
  96.0 4.9 %collective-permute-start.17 = (f32[2,112,114]{2,1,0:T(8,128)S(1)}, f32[2,112,114]{2,1,0:T(8,128)S(1)}, u32[]{:S(2)}, u32[]{:S(2)}) collective-permute-start(f32[2,112,114]{2,1,0:T(8,128)S(1)} %get-tuple-element.48), channel_id=1, source_target_pairs={{0,64},{8,72},{16,80},{24,88},{32,96},{40,104},{48,112},{56,120},{... | collective-permute-start | bytes 306440 | tf_op jit(solution)/shard_map/ppermute | solution.py:30
  97.3 5.5 %collective-permute-start.19 = (f32[2,112,114]{2,1,0:T(8,128)S(1)}, f32[2,112,114]{2,1,0:T(8,128)S(1)}, u32[]{:S(2)}, u32[]{:S(2)}) collective-permute-start(f32[2,112,114]{2,1,0:T(8,128)S(1)} %get-tuple-element.49), channel_id=1, source_target_pairs={{0,192},{8,200},{16,208},{24,216},{32,224},{40,232},{48,240},{56,2... | collective-permute-start | bytes 306440 | tf_op jit(solution)/shard_map/ppermute | solution.py:30
  98.1 6.3 %collective-permute-start.18 = (f32[2,112,114]{2,1,0:T(8,128)S(1)}, f32[2,112,114]{2,1,0:T(8,128)S(1)}, u32[]{:S(2)}, u32[]{:S(2)}) collective-permute-start(f32[2,112,114]{2,1,0:T(8,128)S(1)} %get-tuple-element.50), channel_id=1, source_target_pairs={{0,128},{8,136},{16,144},{24,152},{32,160},{40,168},{48,176},{56,1... | collective-permute-start | bytes 306440 | tf_op jit(solution)/shard_map/ppermute | solution.py:30
  111.4 19.3 %all-to-all-start.3 = ((bf16[8,2,112,113]{3,2,1,0:T(8,128)(2,1)}), bf16[8,2,112,113]{3,2,1,0:T(8,128)(2,1)S(1)}, u32[]{:S(2)}, u32[]{:S(2)}) async-start(bf16[8,2,112,113]{3,2,1,0:T(8,128)(2,1)} %broadcast_in_dim.406), calls=%async_computation.3 | async-start | bytes 917504 | tf_op jit(solution)/shard_map/all_to_all | solution.py:126
  131.4 1.0 copy-start.1

commit v13 on v12

--- a/solution.py
+++ b/solution.py
@@ -96,11 +96,17 @@
         preferred_element_type=jnp.float32,
     )
     pieces = own_state.astype(jnp.bfloat16).reshape(groups, heads, DH, DH + 1)
-    state_part = jnp.sum(
-        lax.all_to_all(pieces, "inner", 0, 0, tiled=True).astype(jnp.float32), axis=0
-    )
+    place = lax.axis_index("inner")
+    state_part = lax.dynamic_index_in_dim(pieces, place, 0, False).astype(jnp.float32)
+    for s in range(1, groups):
+        sent = lax.dynamic_index_in_dim(pieces, (place + s) % groups, 0, False)
+        got = lax.ppermute(sent, "inner", [(i, (i + s) % groups) for i in range(groups)])
+        state_part = state_part + got.astype(jnp.float32)
     feat_query, scaled_heads = to_heads(
         [jnp.maximum(query_input, 0), cotangent * jnp.asarray(loss_scale, jnp.bfloat16)]
+    )
+    state_part, feat_query, scaled_heads = lax.optimization_barrier(
+        (state_part, feat_query, scaled_heads)
     )
 
     label = span_labels[0]

time: 134 us -> 138 us (1.030)
  the two profiles are of different devices: /device:TPU:22 before, /device:TPU:2 now
where the time goes in v13:
time: 138 us; the launch traced here: 135 us
  starting transfers between devices  61.5 us (45%)
  waiting for transfers between devices  48.7 us (35%)
  local copies, waits for them, and re-layouts  11.7 us (8%)
  other arithmetic  10.4 us (8%)
  matrix products  2.01 us (1%)
    ppermute x7, starting transfers between devices, local(): lax.ppermute(sent, 'inner', [(i, (i + s) % groups) for i in range(groups)])  18.5 us
    all_to_all x1, waiting for transfers between devices, local(): lax.all_to_all(copies, 'inner', 0, 0, tiled=True)  14.5 us
    ppermute x14, starting transfers between devices, shifted(): return lax.ppermute(value, 'tm', pairs)  14.2 us
    ppermute x7, waiting for transfers between devices, local(): lax.ppermute(sent, 'inner', [(i, (i + s) % groups) for i in range(groups)])  13.5 us
    ppermute x14, waiting for transfers between devices, shifted(): return lax.ppermute(value, 'tm', pairs)  10.6 us
    ppermute x6, starting transfers between devices, strided(): return lax.ppermute(value, 'tm', pairs)  9.31 us
    ppermute x6, waiting for transfers between devices, strided(): return lax.ppermute(value, 'tm', pairs)  9.1 us
    all_to_all x1, starting transfers between devices, to_heads(): incoming = lax.all_to_all(outgoing, 'inner', 0, 0, tiled=True)  8.6 us
  transfers between devices with their start and end apart: 30, of which 22 were waited for; matrix products, arithmetic and copies ran while one was open for 7% of the time, Pallas kernels for 0%

profile of v13, /device:TPU:2, one launch (start us, length us, event | category | flops | bytes accessed | tf_op | source)
XLA Modules:
  0.0 135.4 jit_solution(9883590201141287971)
XLA Ops:
  0.6 1.3 copy.32
  4.3 8.6 %all-to-all-start = ((bf16[8,2,128,224]{2,3,1,0:T(8,128)(2,1)}), bf16[8,2,128,224]{2,3,1,0:T(8,128)(2,1)S(1)}, u32[]{:S(2)}, u32[]{:S(2)}) async-start(bf16[8,2,128,224]{2,3,1,0:T(8,128)(2,1)} %copy.34), calls=%async_computation | async-start | bytes 1835008 | tf_op jit(solution)/shard_map/all_to_all | solution.py:76
  14.7 2.1 %collective-permute-start = (bf16[2,112,113]{2,1,0:T(8,128)(2,1)S(1)}, bf16[2,112,113]{2,1,0:T(8,128)(2,1)S(1)}, u32[]{:S(2)}, u32[]{:S(2)}) collective-permute-start(bf16[2,112,113]{2,1,0:T(8,128)(2,1)S(1)} %get-tuple-element.54), channel_id=1, source_target_pairs={{0,1},{1,2},{2,3},{3,4},{4,5},{5,6},{6,7},{7,0},{8,9},{9,10},{10,1... | collective-permute-start | bytes 151880 | tf_op jit(solution)/shard_map/ppermute | solution.py:103
  16.8 1.3 collective-permute-start.6
  18.1 2.8 %collective-permute-start.5 = (bf16[2,112,113]{2,1,0:T(8,128)(2,1)S(1)}, bf16[2,112,113]{2,1,0:T(8,128)(2,1)S(1)}, u32[]{:S(2)}, u32[]{:S(2)}) collective-permute-start(bf16[2,112,113]{2,1,0:T(8,128)(2,1)S(1)} %get-tuple-element.56), channel_id=1, source_target_pairs={{0,6},{1,7},{2,0},{3,1},{4,2},{5,3},{6,4},{7,5},{8,14},{9,15},{10,... | collective-permute-start | bytes 151880 | tf_op jit(solution)/shard_map/ppermute | solution.py:103
  21.0 3.0 %collective-permute-start.4 = (bf16[2,112,113]{2,1,0:T(8,128)(2,1)S(1)}, bf16[2,112,113]{2,1,0:T(8,128)(2,1)S(1)}, u32[]{:S(2)}, u32[]{:S(2)}) collective-permute-start(bf16[2,112,113]{2,1,0:T(8,128)(2,1)S(1)} %get-tuple-element.57), channel_id=1, source_target_pairs={{0,5},{1,6},{2,7},{3,0},{4,1},{5,2},{6,3},{7,4},{8,13},{9,14},{10,... | collective-permute-start | bytes 151880 | tf_op jit(solution)/shard_map/ppermute | solution.py:103
  24.0 2.0 %collective-permute-start.3 = (bf16[2,112,113]{2,1,0:T(8,128)(2,1)S(1)}, bf16[2,112,113]{2,1,0:T(8,128)(2,1)S(1)}, u32[]{:S(2)}, u32[]{:S(2)}) collective-permute-start(bf16[2,112,113]{2,1,0:T(8,128)(2,1)S(1)} %get-tuple-element.58), channel_id=1, source_target_pairs={{0,4},{1,5},{2,6},{3,7},{4,0},{5,1},{6,2},{7,3},{8,12},{9,13},{10,... | collective-permute-start | bytes 151880 | tf_op jit(solution)/shard_map/ppermute | solution.py:103
  26.0 8.7 %collective-permute-done = bf16[2,112,113]{2,1,0:T(8,128)(2,1)S(1)} collective-permute-done((bf16[2,112,113]{2,1,0:T(8,128)(2,1)S(1)}, bf16[2,112,113]{2,1,0:T(8,128)(2,1)S(1)}, u32[]{:S(2)}, u32[]{:S(2)}) %collective-permute-start) | collective-permute-done | bytes 50656 | tf_op jit(solution)/shard_map/ppermute | solution.py:103
  34.7 5.3 %collective-permute-start.2 = (bf16[2,112,113]{2,1,0:T(8,128)(2,1)S(1)}, bf16[2,112,113]{2,1,0:T(8,128)(2,1)S(1)}, u32[]{:S(2)}, u32[]{:S(2)}) collective-permute-start(bf16[2,112,113]{2,1,0:T(8,128)(2,1)S(1)} %get-tuple-element.59), channel_id=1, source_target_pairs={{0,3},{1,4},{2,5},{3,6},{4,7},{5,0},{6,1},{7,2},{8,11},{9,12},{10,... | collective-permute-start | bytes 151880 | tf_op jit(solution)/shard_map/ppermute | solution.py:103
  40.2 2.0 %collective-permute-start.1 = (bf16[2,112,113]{2,1,0:T(8,128)(2,1)S(1)}, bf16[2,112,113]{2,1,0:T(8,128)(2,1)S(1)}, u32[]{:S(2)}, u32[]{:S(2)}) collective-permute-start(bf16[2,112,113]{2,1,0:T(8,128)(2,1)S(1)} %get-tuple-element.60), channel_id=1, source_target_pairs={{0,2},{1,3},{2,4},{3,5},{4,6},{5,7},{6,0},{7,1},{8,10},{9,11},{10,... | collective-permute-start | bytes 151880 | tf_op jit(solution)/shard_map/ppermute | solution.py:103
  43.3 3.6 %collective-permute-done.2 = bf16[2,112,113]{2,1,0:T(8,128)(2,1)S(1)} collective-permute-done((bf16[2,112,113]{2,1,0:T(8,128)(2,1)S(1)}, bf16[2,112,113]{2,1,0:T(8,128)(2,1)S(1)}, u32[]{:S(2)}, u32[]{:S(2)}) %collective-permute-start.2) | collective-permute-done | bytes 50656 | tf_op jit(solution)/shard_map/ppermute | solution.py:103
  48.4 2.1 %collective-permute-start.12 = (f32[2,112,114]{2,1,0:T(8,128)S(1)}, f32[2,112,114]{2,1,0:T(8,128)S(1)}, u32[]{:S(2)}, u32[]{:S(2)}) collective-permute-start(f32[2,112,114]{2,1,0:T(8,128)S(1)} %concatenate.26), channel_id=1, source_target_pairs={{0,48},{8,56},{16,0},{24,8},{32,16},{40,24},{48,32},{56,40},{64,11... | collective-permute-start | bytes 306440 | tf_op jit(solution)/shard_map/ppermute | solution.py:20
  53.5 1.8 %collective-permute-start.8 = (f32[2,112,114]{2,1,0:T(8,128)S(1)}, f32[2,112,114]{2,1,0:T(8,128)S(1)}, u32[]{:S(2)}, u32[]{:S(2)}) collective-permute-start(f32[2,112,114]{2,1,0:T(8,128)S(1)} %concatenate.26), channel_id=1, source_target_pairs={{0,16},{8,24},{16,32},{24,40},{32,48},{40,56},{48,0},{56,8},{64,80... | collective-permute-start | bytes 306440 | tf_op jit(solution)/shard_map/ppermute | solution.py:20
  56.5 5.1 %collective-permute-done.10 = f32[2,112,114]{2,1,0:T(8,128)S(1)} collective-permute-done((f32[2,112,114]{2,1,0:T(8,128)S(1)}, f32[2,112,114]{2,1,0:T(8,128)S(1)}, u32[]{:S(2)}, u32[]{:S(2)}) %collective-permute-start.10) | collective-permute-done | bytes 102176 | tf_op jit(solution)/shard_map/ppermute | solution.py:20
  61.9 1.8 %collective-permute-done.8 = f32[2,112,114]{2,1,0:T(8,128)S(1)} collective-permute-done((f32[2,112,114]{2,1,0:T(8,128)S(1)}, f32[2,112,114]{2,1,0:T(8,128)S(1)}, u32[]{:S(2)}, u32[]{:S(2)}) %collective-permute-start.8) | collective-permute-done | bytes 102176 | tf_op jit(solution)/shard_map/ppermute | solution.py:20
  64.1 1.4 %compare_reduce_fusion.29 = (pred[2,112]{1,0:T(4,128)(4,1)}, pred[2,112]{1,0:T(4,128)(4,1)S(1)}, pred[2,112]{1,0:T(4,128)(4,1)S(1)}, pred[2,112]{1,0:T(4,128)(4,...) fusion(f32[2,112,114]{2,1,0:T(8,128)S(1)} %collective-permute-d, ...), kind=kLoop, calls=%fused_computation.98 | loop fusion | flops 4928 | bytes 10532 | tf_op jit(solution)/shard_map/le | solution.py:44
  66.5 1.6 %collective-permute-start.14 = (f32[2,112,114]{2,1,0:T(8,128)}, f32[2,112,114]{2,1,0:T(8,128)S(1)}, u32[]{:S(2)}, u32[]{:S(2)}) collective-permute-start(f32[2,112,114]{2,1,0:T(8,128)} %get-tuple-element.64), channel_id=1, source_target_pairs={{0,64},{8,72},{16,80},{24,88},{32,96},{40,104},{48,112},{56,120},{... | collective-permute-start | bytes 306440 | tf_op jit(solution)/shard_map/ppermute | solution.py:30
  68.1 1.7 %collective-permute-start.16 = (f32[2,112,114]{2,1,0:T(8,128)S(1)}, f32[2,112,114]{2,1,0:T(8,128)S(1)}, u32[]{:S(2)}, u32[]{:S(2)}) collective-permute-start(f32[2,112,114]{2,1,0:T(8,128)S(1)} %get-tuple-element.65), channel_id=1, source_target_pairs={{0,192},{8,200},{16,208},{24,216},{32,224},{40,232},{48,240},{56,2... | collective-permute-start | bytes 306440 | tf_op jit(solution)/shard_map/ppermute | solution.py:30
  69.7 2.0 %collective-permute-start.15 = (f32[2,112,114]{2,1,0:T(8,128)S(1)}, f32[2,112,114]{2,1,0:T(8,128)S(1)}, u32[]{:S(2)}, u32[]{:S(2)}) collective-permute-start(f32[2,112,114]{2,1,0:T(8,128)S(1)} %get-tuple-element.66), channel_id=1, source_target_pairs={{0,128},{8,136},{16,144},{24,152},{32,160},{40,168},{48,176},{56,1... | collective-permute-start | bytes 306440 | tf_op jit(solution)/shard_map/ppermute | solution.py:30
  71.7 1.7 %collective-permute-done.14 = f32[2,112,114]{2,1,0:T(8,128)S(1)} collective-permute-done((f32[2,112,114]{2,1,0:T(8,128)}, f32[2,112,114]{2,1,0:T(8,128)S(1)}, u32[]{:S(2)}, u32[]{:S(2)}) %collective-permute-start.14) | collective-permute-done | bytes 102176 | tf_op jit(solution)/shard_map/ppermute | solution.py:30
  74.1 2.0 %collective-permute-done.15 = f32[2,112,114]{2,1,0:T(8,128)S(1)} collective-permute-done((f32[2,112,114]{2,1,0:T(8,128)S(1)}, f32[2,112,114]{2,1,0:T(8,128)S(1)}, u32[]{:S(2)}, u32[]{:S(2)}) %collective-permute-start.15) | collective-permute-done | bytes 102176 | tf_op jit(solution)/shard_map/ppermute | solution.py:30
  78.4 2.5 %collective-permute-start.22 = (f32[2,112,114]{2,1,0:T(8,128)S(1)}, f32[2,112,114]{2,1,0:T(8,128)S(1)}, u32[]{:S(2)}, u32[]{:S(2)}) collective-permute-start(f32[2,112,114]{2,1,0:T(8,128)S(1)} %concatenate.30), channel_id=1, source_target_pairs={{0,48},{8,56},{16,0},{24,8},{32,16},{40,24},{48,32},{56,40},{64,11... | collective-permute-start | bytes 306440 | tf_op jit(solution)/shard_map/ppermute | solution.py:20
  81.1 3.2 %collective-permute-start.20 = (f32[2,112,114]{2,1,0:T(8,128)S(1)}, f32[2,112,114]{2,1,0:T(8,128)S(1)}, u32[]{:S(2)}, u32[]{:S(2)}) collective-permute-start(f32[2,112,114]{2,1,0:T(8,128)S(1)} %concatenate.30), channel_id=1, source_target_pairs={{0,32},{8,40},{16,48},{24,56},{32,0},{40,8},{48,16},{56,24},{64,96... | collective-permute-start | bytes 306440 | tf_op jit(solution)/shard_map/ppermute | solution.py:20
  87.5 5.6 %all-to-all-start.1 = ((bf16[8,1,128,224]{2,3,1,0:T(8,128)(2,1)}), bf16[8,1,128,224]{2,3,1,0:T(8,128)(2,1)S(1)}, u32[]{:S(2)}, u32[]{:S(2)}) async-start(bf16[8,1,128,224]{2,3,1,0:T(8,128)(2,1)} %copy.37), calls=%async_computation.1 | async-start | bytes 917504 | tf_op jit(solution)/shard_map/all_to_all | solution.py:83
  95.4 1.7 %compare_reduce_fusion.14 = (pred[2,112]{1,0:T(4,128)(4,1)S(1)}, pred[2,112]{1,0:T(4,128)(4,1)S(1)}, pred[2,112]{1,0:T(4,128)(4,1)S(1)}, pred[2,112]{1,0:T(4,128...) fusion(f32[2,112,114]{2,1,0:T(8,128)} %collective-permute-done., ...), kind=kLoop, calls=%fused_computation.83 | loop fusion | flops 4928 | bytes 10532 | tf_op jit(solution)/shard_map/ge | solution.py:44
  99.0 2.9 %collective-permute-start.26 = (f32[2,112,114]{2,1,0:T(8,128)S(1)}, f32[2,112,114]{2,1,0:T(8,128)S(1)}, u32[]{:S(2)}, u32[]{:S(2)}) collective-permute-start(f32[2,112,114]{2,1,0:T(8,128)S(1)} %get-tuple-element.62), channel_id=1, source_target_pairs={{0,192},{8,200},{16,208},{24,216},{32,224},{40,232},{48,240},{56,2... | collective-permute-start | bytes 306440 | tf_op jit(solution)/shard_map/ppermute | solution.py:30
  102.6 2.0 %collective-permute-done.24 = f32[2,112,114]{2,1,0:T(8,128)S(1)} collective-permute-done((f32[2,112,114]{2,1,0:T(8,128)S(1)}, f32[2,112,114]{2,1,0:T(8,128)S(1)}, u32[]{:S(2)}, u32[]{:S(2)}) %collective-permute-start.24) | collective-permute-done | bytes 102176 | tf_op jit(solution)/shard_map/ppermute | solution.py:30
  104.8 1.5 %collective-permute-done.26 = f32[2,112,114]{2,1,0:T(8,128)S(1)} collective-permute-done((f32[2,112,114]{2,1,0:T(8,128)S(1)}, f32[2,112,114]{2,1,0:T(8,128)S(1)}, u32[]{:S(2)}, u32[]{:S(2)}) %collective-permute-start.26) | collective-permute-done | bytes 102176 | tf_op jit(solution)/shard_map/ppermute | solution.py:30
  106.5 1.7 %collective-permute-done.25 = f32[2,112,114]{2,1,0:T(8,128)S(1)} collective-permute-done((f32[2,112,114]{2,1,0:T(8,128)S(1)}, f32[2,112,114]{2,1,0:T(8,128)S(1)}, u32[]{:S(2)}, u32[]{:S(2)}) %collective-permute-start.25) | collective-permute-done | bytes 102176 | tf_op jit(solution)/shard_map/ppermute | solution.py:30
  108.3 1.3 fusion.12
  111.5 5.3 %all-to-all-start.2 = ((bf16[8,2,112,113]{3,2,1,0:T(8,128)(2,1)}), bf16[8,2,112,113]{3,2,1,0:T(8,128)(2,1)S(1)}, u32[]{:S(2)}, u32[]{:S(2)}) async-start(bf16[8,2,112,113]{3,2,1,0:T(8,128)(2,1)} %broadcast_in_dim.406), calls=%async_computation.2 | async-start | bytes 917504 | tf_op jit(solution)/shard_map/all_to_all | solution.py:132
  117.9 14.5 %all-to-all-done.2 = bf16[8,2,112,113]{3,2,1,0:T(8,128)(2,1)S(1)} async-done(((bf16[8,2,112,113]{3,2,1,0:T(8,128)(2,1)}), bf16[8,2,112,113]{3,2,1,0:T(8,128)(2,1)S(1)}, u32[]{:S(2)}, u32[]{:S(2)}) %all-to-all-start.2) | async-done | bytes 405024 | tf_op jit(solution)/shard_map/all_to_all | solution.py:132
  (103 shorter events, 30.4 us)
Async XLA Ops:
  1.9 1.0 copy-start
  4.3 8.6 %copy-start.1 = (bf16[128,1792]{1,0:T(8,128)(2,1)S(1)}, bf16[128,1792]{1,0:T(8,128)(2,1)}, u32[]{:S(2)}) copy-start(bf16[128,1792]{1,0:T(8,128)(2,1)} %param.6) | copy-start | bytes 1376260
  4.3 43.2 %all-to-all-start = ((bf16[8,2,128,224]{2,3,1,0:T(8,128)(2,1)}), bf16[8,2,128,224]{2,3,1,0:T(8,128)(2,1)S(1)}, u32[]{:S(2)}, u32[]{:S(2)}) async-start(bf16[8,2,128,224]{2,3,1,0:T(8,128)(2,1)} %copy.34), calls=%async_computation | async-start | bytes 1835008 | tf_op jit(solution)/shard_map/all_to_all | solution.py:76
  14.7 20.0 %collective-permute-start = (bf16[2,112,113]{2,1,0:T(8,128)(2,1)S(1)}, bf16[2,112,113]{2,1,0:T(8,128)(2,1)S(1)}, u32[]{:S(2)}, u32[]{:S(2)}) collective-permute-start(bf16[2,112,113]{2,1,0:T(8,128)(2,1)S(1)} %get-tuple-element.54), channel_id=1, source_target_pairs={{0,1},{1,2},{2,3},{3,4},{4,5},{5,6},{6,7},{7,0},{8,9},{9,10},{10,1... | collective-permute-start | bytes 151880 | tf_op jit(solution)/shard_map/ppermute | solution.py:103
  16.8 23.3 %collective-permute-start.6 = (bf16[2,112,113]{2,1,0:T(8,128)(2,1)S(1)}, bf16[2,112,113]{2,1,0:T(8,128)(2,1)S(1)}, u32[]{:S(2)}, u32[]{:S(2)}) collective-permute-start(bf16[2,112,113]{2,1,0:T(8,128)(2,1)S(1)} %get-tuple-element.55), channel_id=1, source_target_pairs={{0,7},{1,0},{2,1},{3,2},{4,3},{5,4},{6,5},{7,6},{8,15},{9,8},{10,9... | collective-permute-start | bytes 151880 | tf_op jit(solution)/shard_map/ppermute | solution.py:103
  18.1 24.7 %collective-permute-start.5 = (bf16[2,112,113]{2,1,0:T(8,128)(2,1)S(1)}, bf16[2,112,113]{2,1,0:T(8,128)(2,1)S(1)}, u32[]{:S(2)}, u32[]{:S(2)}) collective-permute-start(bf16[2,112,113]{2,1,0:T(8,128)(2,1)S(1)} %get-tuple-element.56), channel_id=1, source_target_pairs={{0,6},{1,7},{2,0},{3,1},{4,2},{5,3},{6,4},{7,5},{8,14},{9,15},{10,... | collective-permute-start | bytes 151880 | tf_op jit(solution)/shard_map/ppermute | solution.py:103
  21.0 21.9 %collective-permute-start.4 = (bf16[2,112,113]{2,1,0:T(8,128)(2,1)S(1)}, bf16[2,112,113]{2,1,0:T(8,128)(2,1)S(1)}, u32[]{:S(2)}, u32[]{:S(2)}) collective-permute-start(bf16[2,112,113]{2,1,0:T(8,128)(2,1)S(1)} %get-tuple-element.57), channel_id=1, source_target_pairs={{0,5},{1,6},{2,7},{3,0},{4,1},{5,2},{6,3},{7,4},{8,13},{9,14},{10,... | collective-permute-start | bytes 151880 | tf_op jit(solution)/shard_map/ppermute | solution.py:103
  24.0 19.3 %collective-permute-start.3 = (bf16[2,112,113]{2,1,0:T(8,128)(2,1)S(1)}, bf16[2,112,113]{2,1,0:T(8,128)(2,1)S(1)}, u32[]{:S(2)}, u32[]{:S(2)}) collective-permute-start(bf16[2,112,113]{2,1,0:T(8,128)(2,1)S(1)} %get-tuple-element.58), channel_id=1, source_target_pairs={{0,4},{1,5},{2,6},{3,7},{4,0},{5,1},{6,2},{7,3},{8,12},{9,13},{10,... | collective-permute-start | bytes 151880 | tf_op jit(solution)/shard_map/ppermute | solution.py:103
  34.7 12.2 %collective-permute-start.2 = (bf16[2,112,113]{2,1,0:T(8,128)(2,1)S(1)}, bf16[2,112,113]{2,1,0:T(8,128)(2,1)S(1)}, u32[]{:S(2)}, u32[]{:S(2)}) collective-permute-start(bf16[2,112,113]{2,1,0:T(8,128)(2,1)S(1)} %get-tuple-element.59), channel_id=1, source_target_pairs={{0,3},{1,4},{2,5},{3,6},{4,7},{5,0},{6,1},{7,2},{8,11},{9,12},{10,... | collective-permute-start | bytes 151880 | tf_op jit(solution)/shard_map/ppermute | solution.py:103
  40.2 7.3 %collective-permute-start.1 = (bf16[2,112,113]{2,1,0:T(8,128)(2,1)S(1)}, bf16[2,112,113]{2,1,0:T(8,128)(2,1)S(1)}, u32[]{:S(2)}, u32[]{:S(2)}) collective-permute-start(bf16[2,112,113]{2,1,0:T(8,128)(2,1)S(1)} %get-tuple-element.60), channel_id=1, source_target_pairs={{0,2},{1,3},{2,4},{3,5},{4,6},{5,7},{6,0},{7,1},{8,10},{9,11},{10,... | collective-permute-start | bytes 151880 | tf_op jit(solution)/shard_map/ppermute | solution.py:103
  48.4 5.1 %collective-permute-start.13 = (f32[2,112,114]{2,1,0:T(8,128)S(1)}, f32[2,112,114]{2,1,0:T(8,128)S(1)}, u32[]{:S(2)}, u32[]{:S(2)}) collective-permute-start(f32[2,112,114]{2,1,0:T(8,128)S(1)} %concatenate.26), channel_id=1, source_target_pairs={{0,56},{8,0},{16,8},{24,16},{32,24},{40,32},{48,40},{56,48},{64,12... | collective-permute-start | bytes 306440 | tf_op jit(solution)/shard_map/ppermute | solution.py:20
  48.4 7.8 %collective-permute-start.12 = (f32[2,112,114]{2,1,0:T(8,128)S(1)}, f32[2,112,114]{2,1,0:T(8,128)S(1)}, u32[]{:S(2)}, u32[]{:S(2)}) collective-permute-start(f32[2,112,114]{2,1,0:T(8,128)S(1)} %concatenate.26), channel_id=1, source_target_pairs={{0,48},{8,56},{16,0},{24,8},{32,16},{40,24},{48,32},{56,40},{64,11... | collective-permute-start | bytes 306440 | tf_op jit(solution)/shard_map/ppermute | solution.py:20
  50.5 6.0 %collective-permute-start.11 = (f32[2,112,114]{2,1,0:T(8,128)S(1)}, f32[2,112,114]{2,1,0:T(8,128)S(1)}, u32[]{:S(2)}, u32[]{:S(2)}) collective-permute-start(f32[2,112,114]{2,1,0:T(8,128)S(1)} %concatenate.26), channel_id=1, source_target_pairs={{0,40},{8,48},{16,56},{24,0},{32,8},{40,16},{48,24},{56,32},{64,10... | collective-permute-start | bytes 306440 | tf_op jit(solution)/shard_map/ppermute | solution.py:20
  51.2 10.4 %collective-permute-start.10 = (f32[2,112,114]{2,1,0:T(8,128)S(1)}, f32[2,112,114]{2,1,0:T(8,128)S(1)}, u32[]{:S(2)}, u32[]{:S(2)}) collective-permute-start(f32[2,112,114]{2,1,0:T(8,128)S(1)} %concatenate.26), channel_id=1, source_target_pairs={{0,32},{8,40},{16,48},{24,56},{32,0},{40,8},{48,16},{56,24},{64,96... | collective-permute-start | bytes 306440 | tf_op jit(solution)/shard_map/ppermute | solution.py:20
  52.3 9.6 %collective-permute-start.9 = (f32[2,112,114]{2,1,0:T(8,128)S(1)}, f32[2,112,114]{2,1,0:T(8,128)S(1)}, u32[]{:S(2)}, u32[]{:S(2)}) collective-permute-start(f32[2,112,114]{2,1,0:T(8,128)S(1)} %concatenate.26), channel_id=1, source_target_pairs={{0,24},{8,32},{16,40},{24,48},{32,56},{40,0},{48,8},{56,16},{64,88... | collective-permute-start | bytes 306440 | tf_op jit(solution)/shard_map/ppermute | solution.py:20
  53.5 10.2 %collective-permute-start.8 = (f32[2,112,114]{2,1,0:T(8,128)S(1)}, f32[2,112,114]{2,1,0:T(8,128)S(1)}, u32[]{:S(2)}, u32[]{:S(2)}) collective-permute-start(f32[2,112,114]{2,1,0:T(8,128)S(1)} %concatenate.26), channel_id=1, source_target_pairs={{0,16},{8,24},{16,32},{24,40},{32,48},{40,56},{48,0},{56,8},{64,80... | collective-permute-start | bytes 306440 | tf_op jit(solution)/shard_map/ppermute | solution.py:20
  56.3 7.7 %collective-permute-start.7 = (f32[2,112,114]{2,1,0:T(8,128)S(1)}, f32[2,112,114]{2,1,0:T(8,128)S(1)}, u32[]{:S(2)}, u32[]{:S(2)}) collective-permute-start(f32[2,112,114]{2,1,0:T(8,128)S(1)} %concatenate.26), channel_id=1, source_target_pairs={{0,8},{8,16},{16,24},{24,32},{32,40},{40,48},{48,56},{56,0},{64,72... | collective-permute-start | bytes 306440 | tf_op jit(solution)/shard_map/ppermute | solution.py:20
  66.5 6.9 %collective-permute-start.14 = (f32[2,112,114]{2,1,0:T(8,128)}, f32[2,112,114]{2,1,0:T(8,128)S(1)}, u32[]{:S(2)}, u32[]{:S(2)}) collective-permute-start(f32[2,112,114]{2,1,0:T(8,128)} %get-tuple-element.64), channel_id=1, source_target_pairs={{0,64},{8,72},{16,80},{24,88},{32,96},{40,104},{48,112},{56,120},{... | collective-permute-start | bytes 306440 | tf_op jit(solution)/shard_map/ppermute | solution.py:30
  68.1 5.8 %collective-permute-start.16 = (f32[2,112,114]{2,1,0:T(8,128)S(1)}, f32[2,112,114]{2,1,0:T(8,128)S(1)}, u32[]{:S(2)}, u32[]{:S(2)}) collective-permute-start(f32[2,112,114]{2,1,0:T(8,128)S(1)} %get-tuple-element.65), channel_id=1, source_target_pairs={{0,192},{8,200},{16,208},{24,216},{32,224},{40,232},{48,240},{56,2... | collective-permute-start | bytes 306440 | tf_op jit(solution)/shard_map/ppermute | solution.py:30
  69.7 6.3 %collective-permute-start.15 = (f32[2,112,114]{2,1,0:T(8,128)S(1)}, f32[2,112,114]{2,1,0:T(8,128)S(1)}, u32[]{:S(2)}, u32[]{:S(2)}) collective-permute-start(f32[2,112,114]{2,1,0:T(8,128)S(1)} %get-tuple-element.66), channel_id=1, source_target_pairs={{0,128},{8,136},{16,144},{24,152},{32,160},{40,168},{48,176},{56,1... | collective-permute-start | bytes 306440 | tf_op jit(solution)/shard_map/ppermute | solution.py:30
  78.4 5.9 %collective-permute-start.23 = (f32[2,112,114]{2,1,0:T(8,128)S(1)}, f32[2,112,114]{2,1,0:T(8,128)S(1)}, u32[]{:S(2)}, u32[]{:S(2)}) collective-permute-start(f32[2,112,114]{2,1,0:T(8,128)S(1)} %concatenate.30), channel_id=1, source_target_pairs={{0,56},{8,0},{16,8},{24,16},{32,24},{40,32},{48,40},{56,48},{64,12... | collective-permute-start | bytes 306440 | tf_op jit(solution)/shard_map/ppermute | solution.py:20
  78.4 7.5 %collective-permute-start.22 = (f32[2,112,114]{2,1,0:T(8,128)S(1)}, f32[2,112,114]{2,1,0:T(8,128)S(1)}, u32[]{:S(2)}, u32[]{:S(2)}) collective-permute-start(f32[2,112,114]{2,1,0:T(8,128)S(1)} %concatenate.30), channel_id=1, source_target_pairs={{0,48},{8,56},{16,0},{24,8},{32,16},{40,24},{48,32},{56,40},{64,11... | collective-permute-start | bytes 306440 | tf_op jit(solution)/shard_map/ppermute | solution.py:20
  81.0 12.1 %collective-permute-start.21 = (f32[2,112,114]{2,1,0:T(8,128)S(1)}, f32[2,112,114]{2,1,0:T(8,128)S(1)}, u32[]{:S(2)}, u32[]{:S(2)}) collective-permute-start(f32[2,112,114]{2,1,0:T(8,128)S(1)} %concatenate.30), channel_id=1, source_target_pairs={{0,40},{8,48},{16,56},{24,0},{32,8},{40,16},{48,24},{56,32},{64,10... | collective-permute-start | bytes 306440 | tf_op jit(solution)/shard_map/ppermute | solution.py:20
  81.1 12.0 %collective-permute-start.20 = (f32[2,112,114]{2,1,0:T(8,128)S(1)}, f32[2,112,114]{2,1,0:T(8,128)S(1)}, u32[]{:S(2)}, u32[]{:S(2)}) collective-permute-start(f32[2,112,114]{2,1,0:T(8,128)S(1)} %concatenate.30), channel_id=1, source_target_pairs={{0,32},{8,40},{16,48},{24,56},{32,0},{40,8},{48,16},{56,24},{64,96... | collective-permute-start | bytes 306440 | tf_op jit(solution)/shard_map/ppermute | solution.py:20
  84.3 8.9 %collective-permute-start.19 = (f32[2,112,114]{2,1,0:T(8,128)S(1)}, f32[2,112,114]{2,1,0:T(8,128)S(1)}, u32[]{:S(2)}, u32[]{:S(2)}) collective-permute-start(f32[2,112,114]{2,1,0:T(8,128)S(1)} %concatenate.30), channel_id=1, source_target_pairs={{0,24},{8,32},{16,40},{24,48},{32,56},{40,0},{48,8},{56,16},{64,88... | collective-permute-start | bytes 306440 | tf_op jit(solution)/shard_map/ppermute | solution.py:20
  84.3 9.7 %collective-permute-start.18 = (f32[2,112,114]{2,1,0:T(8,128)S(1)}, f32[2,112,114]{2,1,0:T(8,128)S(1)}, u32[]{:S(2)}, u32[]{:S(2)}) collective-permute-start(f32[2,112,114]{2,1,0:T(8,128)S(1)} %concatenate.30), channel_id=1, source_target_pairs={{0,16},{8,24},{16,32},{24,40},{32,48},{40,56},{48,0},{56,8},{64,80... | collective-permute-start | bytes 306440 | tf_op jit(solution)/shard_map/ppermute | solution.py:20
  86.0 8.5 %collective-permute-start.17 = (f32[2,112,114]{2,1,0:T(8,128)S(1)}, f32[2,112,114]{2,1,0:T(8,128)}, u32[]{:S(2)}, u32[]{:S(2)}) collective-permute-start(f32[2,112,114]{2,1,0:T(8,128)S(1)} %concatenate.30), channel_id=1, source_target_pairs={{0,8},{8,16},{16,24},{24,32},{32,40},{40,48},{48,56},{56,0},{64,72... | collective-permute-start | bytes 306440 | tf_op jit(solution)/shard_map/ppermute | solution.py:20
  87.5 23.1 %all-to-all-start.1 = ((bf16[8,1,128,224]{2,3,1,0:T(8,128)(2,1)}), bf16[8,1,128,224]{2,3,1,0:T(8,128)(2,1)S(1)}, u32[]{:S(2)}, u32[]{:S(2)}) async-start(bf16[8,1,128,224]{2,3,1,0:T(8,128)(2,1)} %copy.37), calls=%async_computation.1 | async-start | bytes 917504 | tf_op jit(solution)/shard_map/all_to_all | solution.py:83
  98.5 6.1 %collective-permute-start.24 = (f32[2,112,114]{2,1,0:T(8,128)S(1)}, f32[2,112,114]{2,1,0:T(8,128)S(1)}, u32[]{:S(2)}, u32[]{:S(2)}) collective-permute-start(f32[2,112,114]{2,1,0:T(8,128)S(1)} %get-tuple-element.61), channel_id=1, source_target_pairs={{0,64},{8,72},{16,80},{24,88},{32,96},{40,104},{48,112},{56,120},{... | collective-permute-start | bytes 306440 | tf_op jit(solution)/shard_map/ppermute | solution.py:30
  99.0 7.3 %collective-permute-start.26 = (f32[2,112,114]{2,1,0:T(8,128)S(1)}, f32[2,112,114]{2,1,0:T(8,128)S(1)}, u32[]{:S(2)}, u32[]{:S(2)}) collective-permute-start(f32[2,112,114]{2,1,0:T(8,128)S(1)} %get-tuple-element.62), channel_id=1, source_target_pairs={{0,192},{8,200},{16,208},{24,216},{32,224},{40,232},{48,240},{56,2... | collective-permute-start | bytes 306440 | tf_op jit(solution)/shard_map/ppermute | solution.py:30
  101.8 6.3 %collective-permute-start.25 = (f32[2,112,114]{2,1,0:T(8,128)S(1)}, f32[2,112,114]{2,1,0:T(8,128)S(1)}, u32[]{:S(2)}, u32[]{:S(2)}) collective-permute-start(f32[2,112,114]{2,1,0:T(8,128)S(1)} %get-tuple-element.63), channel_id=1, source_target_pairs={{0,128},{8,136},{16,144},{24,152},{32,160},{40,168},{48,176},{56,1... | collective-permute-start | bytes 306440 | tf_op jit(solution)/shard_map/ppermute | solution.py:30
  111.5 20.9 %all-to-all-start.2 = ((bf16[8,2,112,113]{3,2,1,0:T(8,128)(2,1)}), bf16[8,2,112,113]{3,2,1,0:T(8,128)(2,1)S(1)}, u32[]{:S(2)}, u32[]{:S(2)}) async-start(bf16[8,2,112,113]{3,2,1,0:T(8,128)(2,1)} %broadcast_in_dim.406), calls=%async_computation.2 | async-start | bytes 917504 | tf_op jit(solution)/shard_map/all_to_all | solution.py:132
  (9 other events, 6.3 us)

commit v14 on v12

--- a/solution.py
+++ b/solution.py
@@ -90,18 +90,19 @@
     own_feat_key = jnp.maximum(own_key, 0)
     own_ones = jnp.ones((rows, all_heads, 1), jnp.bfloat16)
     own_state = jnp.einsum(
-        "thk,thv->hkv",
+        "thv,thk->vhk",
+        jnp.concatenate([own_value, own_ones], axis=-1),
         own_feat_key,
-        jnp.concatenate([own_value, own_ones], axis=-1),
         preferred_element_type=jnp.float32,
     )
-    pieces = own_state.astype(jnp.bfloat16).reshape(groups, heads, DH, DH + 1)
-    state_part = jnp.sum(
-        lax.all_to_all(pieces, "inner", 0, 0, tiled=True).astype(jnp.float32), axis=0
-    )
-    feat_query, scaled_heads = to_heads(
-        [jnp.maximum(query_input, 0), cotangent * jnp.asarray(loss_scale, jnp.bfloat16)]
-    )
+    state_rows = own_state.astype(jnp.bfloat16).reshape(DH + 1, groups, width)
+    query_rows = jnp.maximum(query_input, 0).reshape(rows, groups, width)
+    outgoing = jnp.concatenate([state_rows, query_rows], axis=0).transpose(1, 0, 2)
+    incoming = lax.all_to_all(outgoing, "inner", 0, 0, tiled=True)
+    summed = jnp.sum(incoming[:, : DH + 1].astype(jnp.float32), axis=0)
+    state_part = summed.reshape(DH + 1, heads, DH).transpose(1, 2, 0)
+    feat_query = incoming[:, DH + 1 :].reshape(tokens, heads, DH)
+    (scaled_heads,) = to_heads([cotangent * jnp.asarray(loss_scale, jnp.bfloat16)])
 
     label = span_labels[0]
     state_vis = visible(state_part, label, False)

time: 134 us -> 147 us (1.097)
  the two profiles are of different devices: /device:TPU:22 before, /device:TPU:2 now
where the time goes in v14:
time: 147 us; the launch traced here: 146 us
  waiting for transfers between devices  66.7 us (45%)
  starting transfers between devices  49.6 us (34%)
  other arithmetic  13.7 us (9%)
  local copies, waits for them, and re-layouts  11.6 us (8%)
  matrix products  3.04 us (2%)
    all_to_all x1, waiting for transfers between devices, local(): incoming = lax.all_to_all(outgoing, 'inner', 0, 0, tiled=True)  25.9 us
    ppermute x14, starting transfers between devices, shifted(): return lax.ppermute(value, 'tm', pairs)  20.7 us
    all_to_all x1, waiting for transfers between devices, local(): lax.all_to_all(copies, 'inner', 0, 0, tiled=True)  15.4 us
    ppermute x6, starting transfers between devices, strided(): return lax.ppermute(value, 'tm', pairs)  9.87 us
    ppermute x6, waiting for transfers between devices, strided(): return lax.ppermute(value, 'tm', pairs)  9.56 us
    all_to_all x1, starting transfers between devices, local(): incoming = lax.all_to_all(outgoing, 'inner', 0, 0, tiled=True)  8.6 us
    unnamed x31, local copies, waits for them, and re-layouts  6.28 us
    all_to_all x1, waiting for transfers between devices, to_heads(): incoming = lax.all_to_all(outgoing, 'inner', 0, 0, tiled=True)  6.01 us
  transfers between devices with their start and end apart: 24, of which 13 were waited for; matrix products, arithmetic and copies ran while one was open for 11% of the time, Pallas kernels for 0%

profile of v14, /device:TPU:2, one launch (start us, length us, event | category | flops | bytes accessed | tf_op | source)
XLA Modules:
  0.0 145.8 jit_solution(14491350869240982269)
XLA Ops:
  0.6 1.3 copy.31
  3.7 1.3 maximum_bitcast_fusion
  5.0 8.6 %all-to-all-start = ((bf16[8,241,224]{1,2,0:T(8,128)(2,1)}), bf16[8,241,224]{1,2,0:T(8,128)(2,1)S(1)}, u32[]{:S(2)}, u32[]{:S(2)}) async-start(bf16[8,241,224]{1,2,0:T(8,128)(2,1)} %maximum_bitcast_fusion), calls=%async_computation | async-start | bytes 1835008 | tf_op jit(solution)/shard_map/all_to_all | solution.py:101
  13.7 25.9 %all-to-all-done = bf16[8,241,224]{1,2,0:T(8,128)(2,1)S(1)} async-done(((bf16[8,241,224]{1,2,0:T(8,128)(2,1)}), bf16[8,241,224]{1,2,0:T(8,128)(2,1)S(1)}, u32[]{:S(2)}, u32[]{:S(2)}) %all-to-all-start) | async-done | bytes 863776 | tf_op jit(solution)/shard_map/all_to_all | solution.py:101
  40.5 2.8 %collective-permute-start.5 = (f32[2,112,114]{2,1,0:T(8,128)}, f32[2,112,114]{2,1,0:T(8,128)S(1)}, u32[]{:S(2)}, u32[]{:S(2)}) collective-permute-start(f32[2,112,114]{2,1,0:T(8,128)} %concatenate.29), channel_id=1, source_target_pairs={{0,48},{8,56},{16,0},{24,8},{32,16},{40,24},{48,32},{56,40},{64,11... | collective-permute-start | bytes 306440 | tf_op jit(solution)/shard_map/ppermute | solution.py:20
  44.5 1.3 collective-permute-start.2
  45.8 2.1 %collective-permute-start.1 = (f32[2,112,114]{2,1,0:T(8,128)}, f32[2,112,114]{2,1,0:T(8,128)S(1)}, u32[]{:S(2)}, u32[]{:S(2)}) collective-permute-start(f32[2,112,114]{2,1,0:T(8,128)} %concatenate.29), channel_id=1, source_target_pairs={{0,16},{8,24},{16,32},{24,40},{32,48},{40,56},{48,0},{56,8},{64,80... | collective-permute-start | bytes 306440 | tf_op jit(solution)/shard_map/ppermute | solution.py:20
  49.4 3.5 %all-to-all-start.1 = ((bf16[8,1,128,224]{2,3,1,0:T(8,128)(2,1)}), bf16[8,1,128,224]{2,3,1,0:T(8,128)(2,1)S(1)}, u32[]{:S(2)}, u32[]{:S(2)}) async-start(bf16[8,1,128,224]{2,3,1,0:T(8,128)(2,1)} %bitcast.12), calls=%async_computation.1 | async-start | bytes 917504 | tf_op jit(solution)/shard_map/all_to_all | solution.py:76
  53.0 1.4 collective-permute-done.3
  54.4 2.0 %collective-permute-done.1 = f32[2,112,114]{2,1,0:T(8,128)S(1)} collective-permute-done((f32[2,112,114]{2,1,0:T(8,128)}, f32[2,112,114]{2,1,0:T(8,128)S(1)}, u32[]{:S(2)}, u32[]{:S(2)}) %collective-permute-start.1) | collective-permute-done | bytes 102176 | tf_op jit(solution)/shard_map/ppermute | solution.py:20
  57.3 2.3 %compare_reduce_fusion.29 = (pred[2,112]{1,0:T(4,128)(4,1)}, pred[2,112]{1,0:T(4,128)(4,1)S(1)}, pred[2,112]{1,0:T(4,128)(4,1)S(1)}, pred[2,112]{1,0:T(4,128)(4,...) fusion(f32[2,112,114]{2,1,0:T(8,128)} %collective-permute-done,, ...), kind=kLoop, calls=%fused_computation.91 | loop fusion | flops 4928 | bytes 10532 | tf_op jit(solution)/shard_map/le | solution.py:44
  62.7 1.6 %collective-permute-start.7 = (f32[2,112,114]{2,1,0:T(8,128)}, f32[2,112,114]{2,1,0:T(8,128)}, u32[]{:S(2)}, u32[]{:S(2)}) collective-permute-start(f32[2,112,114]{2,1,0:T(8,128)} %get-tuple-element.49), channel_id=1, source_target_pairs={{0,64},{8,72},{16,80},{24,88},{32,96},{40,104},{48,112},{56,120},{... | collective-permute-start | bytes 306440 | tf_op jit(solution)/shard_map/ppermute | solution.py:30
  64.2 6.0 %all-to-all-done.1 = bf16[8,1,128,224]{2,3,1,0:T(8,128)(2,1)S(1)} async-done(((bf16[8,1,128,224]{2,3,1,0:T(8,128)(2,1)}), bf16[8,1,128,224]{2,3,1,0:T(8,128)(2,1)S(1)}, u32[]{:S(2)}, u32[]{:S(2)}) %all-to-all-start.1) | async-done | bytes 458784 | tf_op jit(solution)/shard_map/all_to_all | solution.py:76
  71.3 1.3 reshape.63
  73.2 3.1 %collective-permute-start.9 = (f32[2,112,114]{2,1,0:T(8,128)}, f32[2,112,114]{2,1,0:T(8,128)S(1)}, u32[]{:S(2)}, u32[]{:S(2)}) collective-permute-start(f32[2,112,114]{2,1,0:T(8,128)} %get-tuple-element.50), channel_id=1, source_target_pairs={{0,192},{8,200},{16,208},{24,216},{32,224},{40,232},{48,240},{56,2... | collective-permute-start | bytes 306440 | tf_op jit(solution)/shard_map/ppermute | solution.py:30
  78.1 3.7 %collective-permute-done.9 = f32[2,112,114]{2,1,0:T(8,128)S(1)} collective-permute-done((f32[2,112,114]{2,1,0:T(8,128)}, f32[2,112,114]{2,1,0:T(8,128)S(1)}, u32[]{:S(2)}, u32[]{:S(2)}) %collective-permute-start.9) | collective-permute-done | bytes 102176 | tf_op jit(solution)/shard_map/ppermute | solution.py:30
  83.1 1.5 %fusion.16 = bf16[2,112,113]{2,1,0:T(8,128)(2,1)S(1)} fusion(f32[2,112,114]{2,1,0:T(8,128)S(1)} %collective-permute-done.9, f32[2,112,114]{2,1,0:T(8,128)S(1)} %collective-permute-done.8, f32[2,112,114]{2,1,0:T(8,128)} %collective-permute-done.7, f32[2,112,113]{2,1,0:T(8,128)S(1)} %bitcast.74, f32[2,112,114]{2,1,0:T(8,128)S(1)} %collective-permute-done.6, ...), kind=kLoop, calls=%fused_computation.38 | loop fusion | flops 556864 | bytes 1166593 | tf_op jit(solution)/shard_map/convert_element_type | solution.py:63
  86.0 6.2 %collective-permute-start.15 = (f32[2,112,114]{2,1,0:T(8,128)S(1)}, f32[2,112,114]{2,1,0:T(8,128)S(1)}, u32[]{:S(2)}, u32[]{:S(2)}) collective-permute-start(f32[2,112,114]{2,1,0:T(8,128)S(1)} %concatenate.33), channel_id=1, source_target_pairs={{0,48},{8,56},{16,0},{24,8},{32,16},{40,24},{48,32},{56,40},{64,11... | collective-permute-start | bytes 306440 | tf_op jit(solution)/shard_map/ppermute | solution.py:20
  93.1 2.0 %collective-permute-start.12 = (f32[2,112,114]{2,1,0:T(8,128)S(1)}, f32[2,112,114]{2,1,0:T(8,128)S(1)}, u32[]{:S(2)}, u32[]{:S(2)}) collective-permute-start(f32[2,112,114]{2,1,0:T(8,128)S(1)} %concatenate.33), channel_id=1, source_target_pairs={{0,24},{8,32},{16,40},{24,48},{32,56},{40,0},{48,8},{56,16},{64,88... | collective-permute-start | bytes 306440 | tf_op jit(solution)/shard_map/ppermute | solution.py:20
  95.1 2.5 %collective-permute-start.11 = (f32[2,112,114]{2,1,0:T(8,128)S(1)}, f32[2,112,114]{2,1,0:T(8,128)S(1)}, u32[]{:S(2)}, u32[]{:S(2)}) collective-permute-start(f32[2,112,114]{2,1,0:T(8,128)S(1)} %concatenate.33), channel_id=1, source_target_pairs={{0,16},{8,24},{16,32},{24,40},{32,48},{40,56},{48,0},{56,8},{64,80... | collective-permute-start | bytes 306440 | tf_op jit(solution)/shard_map/ppermute | solution.py:20
  98.7 1.3 fusion.4
  101.0 3.5 %all-to-all-start.2 = ((bf16[8,1,128,224]{2,3,1,0:T(8,128)(2,1)}), bf16[8,1,128,224]{2,3,1,0:T(8,128)(2,1)S(1)}, u32[]{:S(2)}, u32[]{:S(2)}) async-start(bf16[8,1,128,224]{2,3,1,0:T(8,128)(2,1)} %copy.38), calls=%async_computation.2 | async-start | bytes 917504 | tf_op jit(solution)/shard_map/all_to_all | solution.py:83
  104.5 1.5 %collective-permute-done.11 = f32[2,112,114]{2,1,0:T(8,128)S(1)} collective-permute-done((f32[2,112,114]{2,1,0:T(8,128)S(1)}, f32[2,112,114]{2,1,0:T(8,128)S(1)}, u32[]{:S(2)}, u32[]{:S(2)}) %collective-permute-start.11) | collective-permute-done | bytes 102176 | tf_op jit(solution)/shard_map/ppermute | solution.py:20
  107.3 1.2 collective-permute-start.17
  108.5 2.1 %collective-permute-start.19 = (f32[2,112,114]{2,1,0:T(8,128)S(1)}, f32[2,112,114]{2,1,0:T(8,128)S(1)}, u32[]{:S(2)}, u32[]{:S(2)}) collective-permute-start(f32[2,112,114]{2,1,0:T(8,128)S(1)} %get-tuple-element.47), channel_id=1, source_target_pairs={{0,192},{8,200},{16,208},{24,216},{32,224},{40,232},{48,240},{56,2... | collective-permute-start | bytes 306440 | tf_op jit(solution)/shard_map/ppermute | solution.py:30
  110.6 1.3 collective-permute-start.18
  111.9 1.6 %collective-permute-done.17 = f32[2,112,114]{2,1,0:T(8,128)S(1)} collective-permute-done((f32[2,112,114]{2,1,0:T(8,128)S(1)}, f32[2,112,114]{2,1,0:T(8,128)S(1)}, u32[]{:S(2)}, u32[]{:S(2)}) %collective-permute-start.17) | collective-permute-done | bytes 102176 | tf_op jit(solution)/shard_map/ppermute | solution.py:30
  113.7 1.8 %collective-permute-done.19 = f32[2,112,114]{2,1,0:T(8,128)S(1)} collective-permute-done((f32[2,112,114]{2,1,0:T(8,128)S(1)}, f32[2,112,114]{2,1,0:T(8,128)S(1)}, u32[]{:S(2)}, u32[]{:S(2)}) %collective-permute-start.19) | collective-permute-done | bytes 102176 | tf_op jit(solution)/shard_map/ppermute | solution.py:30
  115.6 1.5 %collective-permute-done.18 = f32[2,112,114]{2,1,0:T(8,128)S(1)} collective-permute-done((f32[2,112,114]{2,1,0:T(8,128)S(1)}, f32[2,112,114]{2,1,0:T(8,128)S(1)}, u32[]{:S(2)}, u32[]{:S(2)}) %collective-permute-start.18) | collective-permute-done | bytes 102176 | tf_op jit(solution)/shard_map/ppermute | solution.py:30
  117.8 4.1 %all-to-all-done.2 = bf16[8,1,128,224]{2,3,1,0:T(8,128)(2,1)S(1)} async-done(((bf16[8,1,128,224]{2,3,1,0:T(8,128)(2,1)}), bf16[8,1,128,224]{2,3,1,0:T(8,128)(2,1)S(1)}, u32[]{:S(2)}, u32[]{:S(2)}) %all-to-all-start.2) | async-done | bytes 458784 | tf_op jit(solution)/shard_map/all_to_all | solution.py:83
  122.7 3.5 %all-to-all-start.3 = ((bf16[8,2,112,113]{3,2,1,0:T(8,128)(2,1)}), bf16[8,2,112,113]{3,2,1,0:T(8,128)(2,1)S(1)}, u32[]{:S(2)}, u32[]{:S(2)}) async-start(bf16[8,2,112,113]{3,2,1,0:T(8,128)(2,1)} %broadcast_in_dim.406), calls=%async_computation.3 | async-start | bytes 917504 | tf_op jit(solution)/shard_map/all_to_all | solution.py:127
  127.3 15.4 %all-to-all-done.3 = bf16[8,2,112,113]{3,2,1,0:T(8,128)(2,1)S(1)} async-done(((bf16[8,2,112,113]{3,2,1,0:T(8,128)(2,1)}), bf16[8,2,112,113]{3,2,1,0:T(8,128)(2,1)S(1)}, u32[]{:S(2)}, u32[]{:S(2)}) %all-to-all-start.3) | async-done | bytes 405024 | tf_op jit(solution)/shard_map/all_to_all | solution.py:127
  (89 shorter events, 25.5 us)
Async XLA Ops:
  0.6 1.4 copy-start.4
  5.0 8.6 %copy-start.10 = (s32[128]{0:T(128)S(1)}, s32[128]{0:T(128)}, u32[]{:S(2)}) copy-start(s32[128]{0:T(128)} %param.9) | copy-start | bytes 1540
  5.0 38.2 %copy-start.6 = (bf16[128,1792]{1,0:T(8,128)(2,1)S(1)}, bf16[128,1792]{1,0:T(8,128)(2,1)}, u32[]{:S(2)}) copy-start(bf16[128,1792]{1,0:T(8,128)(2,1)} %param.8) | copy-start | bytes 1376260
  5.0 34.5 %all-to-all-start = ((bf16[8,241,224]{1,2,0:T(8,128)(2,1)}), bf16[8,241,224]{1,2,0:T(8,128)(2,1)S(1)}, u32[]{:S(2)}, u32[]{:S(2)}) async-start(bf16[8,241,224]{1,2,0:T(8,128)(2,1)} %maximum_bitcast_fusion), calls=%async_computation | async-start | bytes 1835008 | tf_op jit(solution)/shard_map/all_to_all | solution.py:101
  40.3 5.5 %collective-permute-start.6 = (f32[2,112,114]{2,1,0:T(8,128)}, f32[2,112,114]{2,1,0:T(8,128)S(1)}, u32[]{:S(2)}, u32[]{:S(2)}) collective-permute-start(f32[2,112,114]{2,1,0:T(8,128)} %concatenate.29), channel_id=1, source_target_pairs={{0,56},{8,0},{16,8},{24,16},{32,24},{40,32},{48,40},{56,48},{64,12... | collective-permute-start | bytes 306440 | tf_op jit(solution)/shard_map/ppermute | solution.py:20
  40.5 7.5 %collective-permute-start.5 = (f32[2,112,114]{2,1,0:T(8,128)}, f32[2,112,114]{2,1,0:T(8,128)S(1)}, u32[]{:S(2)}, u32[]{:S(2)}) collective-permute-start(f32[2,112,114]{2,1,0:T(8,128)} %concatenate.29), channel_id=1, source_target_pairs={{0,48},{8,56},{16,0},{24,8},{32,16},{40,24},{48,32},{56,40},{64,11... | collective-permute-start | bytes 306440 | tf_op jit(solution)/shard_map/ppermute | solution.py:20
  43.5 9.5 %collective-permute-start.4 = (f32[2,112,114]{2,1,0:T(8,128)}, f32[2,112,114]{2,1,0:T(8,128)S(1)}, u32[]{:S(2)}, u32[]{:S(2)}) collective-permute-start(f32[2,112,114]{2,1,0:T(8,128)} %concatenate.29), channel_id=1, source_target_pairs={{0,40},{8,48},{16,56},{24,0},{32,8},{40,16},{48,24},{56,32},{64,10... | collective-permute-start | bytes 306440 | tf_op jit(solution)/shard_map/ppermute | solution.py:20
  43.6 10.8 %collective-permute-start.3 = (f32[2,112,114]{2,1,0:T(8,128)}, f32[2,112,114]{2,1,0:T(8,128)S(1)}, u32[]{:S(2)}, u32[]{:S(2)}) collective-permute-start(f32[2,112,114]{2,1,0:T(8,128)} %concatenate.29), channel_id=1, source_target_pairs={{0,32},{8,40},{16,48},{24,56},{32,0},{40,8},{48,16},{56,24},{64,96... | collective-permute-start | bytes 306440 | tf_op jit(solution)/shard_map/ppermute | solution.py:20
  44.5 9.8 %collective-permute-start.2 = (f32[2,112,114]{2,1,0:T(8,128)}, f32[2,112,114]{2,1,0:T(8,128)S(1)}, u32[]{:S(2)}, u32[]{:S(2)}) collective-permute-start(f32[2,112,114]{2,1,0:T(8,128)} %concatenate.29), channel_id=1, source_target_pairs={{0,24},{8,32},{16,40},{24,48},{32,56},{40,0},{48,8},{56,16},{64,88... | collective-permute-start | bytes 306440 | tf_op jit(solution)/shard_map/ppermute | solution.py:20
  45.8 10.6 %collective-permute-start.1 = (f32[2,112,114]{2,1,0:T(8,128)}, f32[2,112,114]{2,1,0:T(8,128)S(1)}, u32[]{:S(2)}, u32[]{:S(2)}) collective-permute-start(f32[2,112,114]{2,1,0:T(8,128)} %concatenate.29), channel_id=1, source_target_pairs={{0,16},{8,24},{16,32},{24,40},{32,48},{40,56},{48,0},{56,8},{64,80... | collective-permute-start | bytes 306440 | tf_op jit(solution)/shard_map/ppermute | solution.py:20
  47.9 9.4 %collective-permute-start = (f32[2,112,114]{2,1,0:T(8,128)}, f32[2,112,114]{2,1,0:T(8,128)}, u32[]{:S(2)}, u32[]{:S(2)}) collective-permute-start(f32[2,112,114]{2,1,0:T(8,128)} %concatenate.29), channel_id=1, source_target_pairs={{0,8},{8,16},{16,24},{24,32},{32,40},{40,48},{48,56},{56,0},{64,72... | collective-permute-start | bytes 306440 | tf_op jit(solution)/shard_map/ppermute | solution.py:20
  49.4 20.8 %all-to-all-start.1 = ((bf16[8,1,128,224]{2,3,1,0:T(8,128)(2,1)}), bf16[8,1,128,224]{2,3,1,0:T(8,128)(2,1)S(1)}, u32[]{:S(2)}, u32[]{:S(2)}) async-start(bf16[8,1,128,224]{2,3,1,0:T(8,128)(2,1)} %bitcast.12), calls=%async_computation.1 | async-start | bytes 917504 | tf_op jit(solution)/shard_map/all_to_all | solution.py:76
  53.0 7.6 %copy-start = (f32[2,112,114]{2,1,0:T(8,128)}, f32[2,112,114]{2,1,0:T(8,128)S(1)}, u32[]{:S(2)}) copy-start(f32[2,112,114]{2,1,0:T(8,128)S(1)} %collective-permute-done.4) | copy-start | bytes 306436
  54.4 6.2 %copy-start.1 = (f32[2,112,114]{2,1,0:T(8,128)}, f32[2,112,114]{2,1,0:T(8,128)S(1)}, u32[]{:S(2)}) copy-start(f32[2,112,114]{2,1,0:T(8,128)S(1)} %collective-permute-done.3) | copy-start | bytes 306436
  54.4 6.2 %copy-start.2 = (f32[2,112,114]{2,1,0:T(8,128)}, f32[2,112,114]{2,1,0:T(8,128)S(1)}, u32[]{:S(2)}) copy-start(f32[2,112,114]{2,1,0:T(8,128)S(1)} %collective-permute-done.2) | copy-start | bytes 306436
  56.4 4.2 %copy-start.3 = (f32[2,112,114]{2,1,0:T(8,128)}, f32[2,112,114]{2,1,0:T(8,128)S(1)}, u32[]{:S(2)}) copy-start(f32[2,112,114]{2,1,0:T(8,128)S(1)} %collective-permute-done.1) | copy-start | bytes 306436
  62.7 14.3 %collective-permute-start.7 = (f32[2,112,114]{2,1,0:T(8,128)}, f32[2,112,114]{2,1,0:T(8,128)}, u32[]{:S(2)}, u32[]{:S(2)}) collective-permute-start(f32[2,112,114]{2,1,0:T(8,128)} %get-tuple-element.49), channel_id=1, source_target_pairs={{0,64},{8,72},{16,80},{24,88},{32,96},{40,104},{48,112},{56,120},{... | collective-permute-start | bytes 306440 | tf_op jit(solution)/shard_map/ppermute | solution.py:30
  73.2 8.6 %collective-permute-start.9 = (f32[2,112,114]{2,1,0:T(8,128)}, f32[2,112,114]{2,1,0:T(8,128)S(1)}, u32[]{:S(2)}, u32[]{:S(2)}) collective-permute-start(f32[2,112,114]{2,1,0:T(8,128)} %get-tuple-element.50), channel_id=1, source_target_pairs={{0,192},{8,200},{16,208},{24,216},{32,224},{40,232},{48,240},{56,2... | collective-permute-start | bytes 306440 | tf_op jit(solution)/shard_map/ppermute | solution.py:30
  76.3 6.6 %collective-permute-start.8 = (f32[2,112,114]{2,1,0:T(8,128)}, f32[2,112,114]{2,1,0:T(8,128)S(1)}, u32[]{:S(2)}, u32[]{:S(2)}) collective-permute-start(f32[2,112,114]{2,1,0:T(8,128)} %get-tuple-element.51), channel_id=1, source_target_pairs={{0,128},{8,136},{16,144},{24,152},{32,160},{40,168},{48,176},{56,1... | collective-permute-start | bytes 306440 | tf_op jit(solution)/shard_map/ppermute | solution.py:30
  85.3 13.5 %copy-start.9 = (bf16[2,112,113]{2,1,0:T(8,128)(2,1)S(1)}, bf16[2,112,113]{2,1,0:T(8,128)(2,1)}, u32[]{:S(2)}) copy-start(bf16[2,112,113]{2,1,0:T(8,128)(2,1)} %copy-done.8) | copy-start | bytes 151876
  86.0 9.1 %collective-permute-start.16 = (f32[2,112,114]{2,1,0:T(8,128)S(1)}, f32[2,112,114]{2,1,0:T(8,128)S(1)}, u32[]{:S(2)}, u32[]{:S(2)}) collective-permute-start(f32[2,112,114]{2,1,0:T(8,128)S(1)} %concatenate.33), channel_id=1, source_target_pairs={{0,56},{8,0},{16,8},{24,16},{32,24},{40,32},{48,40},{56,48},{64,12... | collective-permute-start | bytes 306440 | tf_op jit(solution)/shard_map/ppermute | solution.py:20
  86.0 11.6 %collective-permute-start.15 = (f32[2,112,114]{2,1,0:T(8,128)S(1)}, f32[2,112,114]{2,1,0:T(8,128)S(1)}, u32[]{:S(2)}, u32[]{:S(2)}) collective-permute-start(f32[2,112,114]{2,1,0:T(8,128)S(1)} %concatenate.33), channel_id=1, source_target_pairs={{0,48},{8,56},{16,0},{24,8},{32,16},{40,24},{48,32},{56,40},{64,11... | collective-permute-start | bytes 306440 | tf_op jit(solution)/shard_map/ppermute | solution.py:20
  92.3 12.2 %collective-permute-start.14 = (f32[2,112,114]{2,1,0:T(8,128)S(1)}, f32[2,112,114]{2,1,0:T(8,128)S(1)}, u32[]{:S(2)}, u32[]{:S(2)}) collective-permute-start(f32[2,112,114]{2,1,0:T(8,128)S(1)} %concatenate.33), channel_id=1, source_target_pairs={{0,40},{8,48},{16,56},{24,0},{32,8},{40,16},{48,24},{56,32},{64,10... | collective-permute-start | bytes 306440 | tf_op jit(solution)/shard_map/ppermute | solution.py:20
  93.0 11.4 %collective-permute-start.13 = (f32[2,112,114]{2,1,0:T(8,128)S(1)}, f32[2,112,114]{2,1,0:T(8,128)S(1)}, u32[]{:S(2)}, u32[]{:S(2)}) collective-permute-start(f32[2,112,114]{2,1,0:T(8,128)S(1)} %concatenate.33), channel_id=1, source_target_pairs={{0,32},{8,40},{16,48},{24,56},{32,0},{40,8},{48,16},{56,24},{64,96... | collective-permute-start | bytes 306440 | tf_op jit(solution)/shard_map/ppermute | solution.py:20
  93.1 11.4 %collective-permute-start.12 = (f32[2,112,114]{2,1,0:T(8,128)S(1)}, f32[2,112,114]{2,1,0:T(8,128)S(1)}, u32[]{:S(2)}, u32[]{:S(2)}) collective-permute-start(f32[2,112,114]{2,1,0:T(8,128)S(1)} %concatenate.33), channel_id=1, source_target_pairs={{0,24},{8,32},{16,40},{24,48},{32,56},{40,0},{48,8},{56,16},{64,88... | collective-permute-start | bytes 306440 | tf_op jit(solution)/shard_map/ppermute | solution.py:20
  95.1 10.8 %collective-permute-start.11 = (f32[2,112,114]{2,1,0:T(8,128)S(1)}, f32[2,112,114]{2,1,0:T(8,128)S(1)}, u32[]{:S(2)}, u32[]{:S(2)}) collective-permute-start(f32[2,112,114]{2,1,0:T(8,128)S(1)} %concatenate.33), channel_id=1, source_target_pairs={{0,16},{8,24},{16,32},{24,40},{32,48},{40,56},{48,0},{56,8},{64,80... | collective-permute-start | bytes 306440 | tf_op jit(solution)/shard_map/ppermute | solution.py:20
  97.6 8.3 %collective-permute-start.10 = (f32[2,112,114]{2,1,0:T(8,128)S(1)}, f32[2,112,114]{2,1,0:T(8,128)S(1)}, u32[]{:S(2)}, u32[]{:S(2)}) collective-permute-start(f32[2,112,114]{2,1,0:T(8,128)S(1)} %concatenate.33), channel_id=1, source_target_pairs={{0,8},{8,16},{16,24},{24,32},{32,40},{40,48},{48,56},{56,0},{64,72... | collective-permute-start | bytes 306440 | tf_op jit(solution)/shard_map/ppermute | solution.py:20
  101.0 20.9 %all-to-all-start.2 = ((bf16[8,1,128,224]{2,3,1,0:T(8,128)(2,1)}), bf16[8,1,128,224]{2,3,1,0:T(8,128)(2,1)S(1)}, u32[]{:S(2)}, u32[]{:S(2)}) async-start(bf16[8,1,128,224]{2,3,1,0:T(8,128)(2,1)} %copy.38), calls=%async_computation.2 | async-start | bytes 917504 | tf_op jit(solution)/shard_map/all_to_all | solution.py:83
  107.3 6.2 %collective-permute-start.17 = (f32[2,112,114]{2,1,0:T(8,128)S(1)}, f32[2,112,114]{2,1,0:T(8,128)S(1)}, u32[]{:S(2)}, u32[]{:S(2)}) collective-permute-start(f32[2,112,114]{2,1,0:T(8,128)S(1)} %get-tuple-element.46), channel_id=1, source_target_pairs={{0,64},{8,72},{16,80},{24,88},{32,96},{40,104},{48,112},{56,120},{... | collective-permute-start | bytes 306440 | tf_op jit(solution)/shard_map/ppermute | solution.py:30
  108.5 6.9 %collective-permute-start.19 = (f32[2,112,114]{2,1,0:T(8,128)S(1)}, f32[2,112,114]{2,1,0:T(8,128)S(1)}, u32[]{:S(2)}, u32[]{:S(2)}) collective-permute-start(f32[2,112,114]{2,1,0:T(8,128)S(1)} %get-tuple-element.47), channel_id=1, source_target_pairs={{0,192},{8,200},{16,208},{24,216},{32,224},{40,232},{48,240},{56,2... | collective-permute-start | bytes 306440 | tf_op jit(solution)/shard_map/ppermute | solution.py:30
  110.6 6.5 %collective-permute-start.18 = (f32[2,112,114]{2,1,0:T(8,128)S(1)}, f32[2,112,114]{2,1,0:T(8,128)S(1)}, u32[]{:S(2)}, u32[]{:S(2)}) collective-permute-start(f32[2,112,114]{2,1,0:T(8,128)S(1)} %get-tuple-element.48), channel_id=1, source_target_pairs={{0,128},{8,136},{16,144},{24,152},{32,160},{40,168},{48,176},{56,1... | collective-permute-start | bytes 306440 | tf_op jit(solution)/shard_map/ppermute | solution.py:30
  122.7 20.0 %all-to-all-start.3 = ((bf16[8,2,112,113]{3,2,1,0:T(8,128)(2,1)}), bf16[8,2,112,113]{3,2,1,0:T(8,128)(2,1)S(1)}, u32[]{:S(2)}, u32[]{:S(2)}) async-start(bf16[8,2,112,113]{3,2,1,0:T(8,128)(2,1)} %broadcast_in_dim.406), calls=%async_computation.3 | async-start | bytes 917504 | tf_op jit(solution)/shard_map/all_to_all | solution.py:127
  (3 other events, 2.4 us)

commit v15 on v12

--- a/solution.py
+++ b/solution.py
@@ -84,20 +84,13 @@
         merged = returned.transpose(1, 2, 0, 3).reshape(count, rows, columns)
         return [merged[i] for i in range(count)]
 
-    all_heads = groups * heads
-    own_key = key_input.reshape(rows, all_heads, DH)
-    own_value = value_input.reshape(rows, all_heads, DH)
-    own_feat_key = jnp.maximum(own_key, 0)
-    own_ones = jnp.ones((rows, all_heads, 1), jnp.bfloat16)
-    own_state = jnp.einsum(
+    key_heads, value_heads = to_heads([key_input, value_input])
+    ones = jnp.ones((tokens, heads, 1), jnp.bfloat16)
+    state_part = jnp.einsum(
         "thk,thv->hkv",
-        own_feat_key,
-        jnp.concatenate([own_value, own_ones], axis=-1),
+        jnp.maximum(key_heads, 0),
+        jnp.concatenate([value_heads, ones], axis=-1),
         preferred_element_type=jnp.float32,
-    )
-    pieces = own_state.astype(jnp.bfloat16).reshape(groups, heads, DH, DH + 1)
-    state_part = jnp.sum(
-        lax.all_to_all(pieces, "inner", 0, 0, tiled=True).astype(jnp.float32), axis=0
     )
     feat_query, scaled_heads = to_heads(
         [jnp.maximum(query_input, 0), cotangent * jnp.asarray(loss_scale, jnp.bfloat16)]
@@ -126,6 +119,10 @@
     adjoint_all = lax.all_to_all(copies, "inner", 0, 0, tiled=True).reshape(
         groups * heads, DH, DH + 1
     )
+    all_heads = groups * heads
+    own_key = key_input.reshape(rows, all_heads, DH)
+    own_value = value_input.reshape(rows, all_heads, DH)
+    own_feat_key = jnp.maximum(own_key, 0)
     key_feat = jnp.einsum(
         "thv,hkv->thk", own_value, adjoint_all[..., :DH], preferred_element_type=jnp.float32
     ) + adjoint_all[..., DH].astype(jnp.float32)[None]

time: 134 us -> 138 us (1.030)
  the two profiles are of different devices: /device:TPU:22 before, /device:TPU:2 now
where the time goes in v15:
time: 138 us; the launch traced here: 137 us
  waiting for transfers between devices  64.3 us (47%)
  starting transfers between devices  45.4 us (33%)
  local copies, waits for them, and re-layouts  14.7 us (11%)
  other arithmetic  9 us (7%)
  matrix products  1.9 us (1%)
    all_to_all x2, waiting for transfers between devices, to_heads(): incoming = lax.all_to_all(outgoing, 'inner', 0, 0, tiled=True)  26.5 us
    ppermute x14, starting transfers between devices, shifted(): return lax.ppermute(value, 'tm', pairs)  17.2 us
    all_to_all x1, waiting for transfers between devices, local(): lax.all_to_all(copies, 'inner', 0, 0, tiled=True)  15.3 us
    all_to_all x2, starting transfers between devices, to_heads(): incoming = lax.all_to_all(outgoing, 'inner', 0, 0, tiled=True)  12.1 us
    ppermute x6, waiting for transfers between devices, strided(): return lax.ppermute(value, 'tm', pairs)  10.7 us
    ppermute x14, waiting for transfers between devices, shifted(): return lax.ppermute(value, 'tm', pairs)  9.51 us
    ppermute x6, starting transfers between devices, strided(): return lax.ppermute(value, 'tm', pairs)  9.13 us
    unnamed x61, local copies, waits for them, and re-layouts  8.43 us
  transfers between devices with their start and end apart: 24, of which 14 were waited for; matrix products, arithmetic and copies ran while one was open for 10% of the time, Pallas kernels for 0%

profile of v15, /device:TPU:2, one launch (start us, length us, event | category | flops | bytes accessed | tf_op | source)
XLA Modules:
  0.0 136.5 jit_solution(6230825220073202126)
XLA Ops:
  0.6 1.3 copy.40
  3.9 8.6 %all-to-all-start.1 = ((bf16[8,2,128,224]{2,3,1,0:T(8,128)(2,1)}), bf16[8,2,128,224]{2,3,1,0:T(8,128)(2,1)S(1)}, u32[]{:S(2)}, u32[]{:S(2)}) async-start(bf16[8,2,128,224]{2,3,1,0:T(8,128)(2,1)} %copy.41), calls=%async_computation.1 | async-start | bytes 1835008 | tf_op jit(solution)/shard_map/all_to_all | solution.py:76
  14.9 23.5 %all-to-all-done.1 = bf16[8,2,128,224]{2,3,1,0:T(8,128)(2,1)S(1)} async-done(((bf16[8,2,128,224]{2,3,1,0:T(8,128)(2,1)}), bf16[8,2,128,224]{2,3,1,0:T(8,128)(2,1)S(1)}, u32[]{:S(2)}, u32[]{:S(2)}) %all-to-all-start.1) | async-done | bytes 917536 | tf_op jit(solution)/shard_map/all_to_all | solution.py:76
  38.4 3.6 %all-to-all-start = ((bf16[8,2,128,224]{2,3,1,0:T(8,128)(2,1)}), bf16[8,2,128,224]{2,3,1,0:T(8,128)(2,1)S(1)}, u32[]{:S(2)}, u32[]{:S(2)}) async-start(bf16[8,2,128,224]{2,3,1,0:T(8,128)(2,1)} %copy.37), calls=%async_computation | async-start | bytes 1835008 | tf_op jit(solution)/shard_map/all_to_all | solution.py:76
  43.8 1.7 %collective-permute-start.6 = (f32[2,112,114]{2,1,0:T(8,128)S(1)}, f32[2,112,114]{2,1,0:T(8,128)S(1)}, u32[]{:S(2)}, u32[]{:S(2)}) collective-permute-start(f32[2,112,114]{2,1,0:T(8,128)S(1)} %concatenate.27), channel_id=1, source_target_pairs={{0,56},{8,0},{16,8},{24,16},{32,24},{40,32},{48,40},{56,48},{64,12... | collective-permute-start | bytes 306440 | tf_op jit(solution)/shard_map/ppermute | solution.py:20
  45.6 1.7 %collective-permute-start.5 = (f32[2,112,114]{2,1,0:T(8,128)S(1)}, f32[2,112,114]{2,1,0:T(8,128)S(1)}, u32[]{:S(2)}, u32[]{:S(2)}) collective-permute-start(f32[2,112,114]{2,1,0:T(8,128)S(1)} %concatenate.27), channel_id=1, source_target_pairs={{0,48},{8,56},{16,0},{24,8},{32,16},{40,24},{48,32},{56,40},{64,11... | collective-permute-start | bytes 306440 | tf_op jit(solution)/shard_map/ppermute | solution.py:20
  47.4 1.4 %collective-permute-start.3 = (f32[2,112,114]{2,1,0:T(8,128)S(1)}, f32[2,112,114]{2,1,0:T(8,128)S(1)}, u32[]{:S(2)}, u32[]{:S(2)}) collective-permute-start(f32[2,112,114]{2,1,0:T(8,128)S(1)} %concatenate.27), channel_id=1, source_target_pairs={{0,32},{8,40},{16,48},{24,56},{32,0},{40,8},{48,16},{56,24},{64,96... | collective-permute-start | bytes 306440 | tf_op jit(solution)/shard_map/ppermute | solution.py:20
  48.9 1.8 %collective-permute-start.2 = (f32[2,112,114]{2,1,0:T(8,128)S(1)}, f32[2,112,114]{2,1,0:T(8,128)S(1)}, u32[]{:S(2)}, u32[]{:S(2)}) collective-permute-start(f32[2,112,114]{2,1,0:T(8,128)S(1)} %concatenate.27), channel_id=1, source_target_pairs={{0,24},{8,32},{16,40},{24,48},{32,56},{40,0},{48,8},{56,16},{64,88... | collective-permute-start | bytes 306440 | tf_op jit(solution)/shard_map/ppermute | solution.py:20
  50.6 1.8 %collective-permute-start.1 = (f32[2,112,114]{2,1,0:T(8,128)S(1)}, f32[2,112,114]{2,1,0:T(8,128)S(1)}, u32[]{:S(2)}, u32[]{:S(2)}) collective-permute-start(f32[2,112,114]{2,1,0:T(8,128)S(1)} %concatenate.27), channel_id=1, source_target_pairs={{0,16},{8,24},{16,32},{24,40},{32,48},{40,56},{48,0},{56,8},{64,80... | collective-permute-start | bytes 306440 | tf_op jit(solution)/shard_map/ppermute | solution.py:20
  53.0 5.5 %collective-permute-done.3 = f32[2,112,114]{2,1,0:T(8,128)S(1)} collective-permute-done((f32[2,112,114]{2,1,0:T(8,128)S(1)}, f32[2,112,114]{2,1,0:T(8,128)S(1)}, u32[]{:S(2)}, u32[]{:S(2)}) %collective-permute-start.3) | collective-permute-done | bytes 102176 | tf_op jit(solution)/shard_map/ppermute | solution.py:20
  59.5 1.4 %compare_reduce_fusion.29 = (pred[2,112]{1,0:T(4,128)(4,1)}, pred[2,112]{1,0:T(4,128)(4,1)S(1)}, pred[2,112]{1,0:T(4,128)(4,1)S(1)}, pred[2,112]{1,0:T(4,128)(4,...) fusion(f32[2,112,114]{2,1,0:T(8,128)S(1)} %collective-permute-d, ...), kind=kLoop, calls=%fused_computation.93 | loop fusion | flops 4928 | bytes 10532 | tf_op jit(solution)/shard_map/le | solution.py:44
  62.2 3.0 %collective-permute-start.9 = (f32[2,112,114]{2,1,0:T(8,128)}, f32[2,112,114]{2,1,0:T(8,128)}, u32[]{:S(2)}, u32[]{:S(2)}) collective-permute-start(f32[2,112,114]{2,1,0:T(8,128)} %get-tuple-element.54), channel_id=1, source_target_pairs={{0,192},{8,200},{16,208},{24,216},{32,224},{40,232},{48,240},{56,2... | collective-permute-start | bytes 306440 | tf_op jit(solution)/shard_map/ppermute | solution.py:30
  65.2 3.0 %all-to-all-done = bf16[8,2,128,224]{2,3,1,0:T(8,128)(2,1)S(1)} async-done(((bf16[8,2,128,224]{2,3,1,0:T(8,128)(2,1)}), bf16[8,2,128,224]{2,3,1,0:T(8,128)(2,1)S(1)}, u32[]{:S(2)}, u32[]{:S(2)}) %all-to-all-start) | async-done | bytes 917536 | tf_op jit(solution)/shard_map/all_to_all | solution.py:76
  70.9 3.2 %collective-permute-start.8 = (f32[2,112,114]{2,1,0:T(8,128)S(1)}, f32[2,112,114]{2,1,0:T(8,128)S(1)}, u32[]{:S(2)}, u32[]{:S(2)}) collective-permute-start(f32[2,112,114]{2,1,0:T(8,128)S(1)} %copy-done.17), channel_id=1, source_target_pairs={{0,128},{8,136},{16,144},{24,152},{32,160},{40,168},{48,176},{56,1... | collective-permute-start | bytes 306440 | tf_op jit(solution)/shard_map/ppermute | solution.py:30
  74.8 1.1 fusion.29
  75.9 1.4 %collective-permute-done.8 = f32[2,112,114]{2,1,0:T(8,128)S(1)} collective-permute-done((f32[2,112,114]{2,1,0:T(8,128)S(1)}, f32[2,112,114]{2,1,0:T(8,128)S(1)}, u32[]{:S(2)}, u32[]{:S(2)}) %collective-permute-start.8) | collective-permute-done | bytes 102176 | tf_op jit(solution)/shard_map/ppermute | solution.py:30
  77.5 2.6 %collective-permute-done.7 = f32[2,112,114]{2,1,0:T(8,128)S(1)} collective-permute-done((f32[2,112,114]{2,1,0:T(8,128)S(1)}, f32[2,112,114]{2,1,0:T(8,128)S(1)}, u32[]{:S(2)}, u32[]{:S(2)}) %collective-permute-start.7) | collective-permute-done | bytes 102176 | tf_op jit(solution)/shard_map/ppermute | solution.py:30
  81.0 1.4 fusion.17
  83.4 1.7 %collective-permute-start.16 = (f32[2,112,114]{2,1,0:T(8,128)S(1)}, f32[2,112,114]{2,1,0:T(8,128)S(1)}, u32[]{:S(2)}, u32[]{:S(2)}) collective-permute-start(f32[2,112,114]{2,1,0:T(8,128)S(1)} %concatenate.31), channel_id=1, source_target_pairs={{0,56},{8,0},{16,8},{24,16},{32,24},{40,32},{48,40},{56,48},{64,12... | collective-permute-start | bytes 306440 | tf_op jit(solution)/shard_map/ppermute | solution.py:20
  85.1 1.7 %collective-permute-start.15 = (f32[2,112,114]{2,1,0:T(8,128)S(1)}, f32[2,112,114]{2,1,0:T(8,128)S(1)}, u32[]{:S(2)}, u32[]{:S(2)}) collective-permute-start(f32[2,112,114]{2,1,0:T(8,128)S(1)} %concatenate.31), channel_id=1, source_target_pairs={{0,48},{8,56},{16,0},{24,8},{32,16},{40,24},{48,32},{56,40},{64,11... | collective-permute-start | bytes 306440 | tf_op jit(solution)/shard_map/ppermute | solution.py:20
  87.0 1.4 %collective-permute-start.13 = (f32[2,112,114]{2,1,0:T(8,128)S(1)}, f32[2,112,114]{2,1,0:T(8,128)S(1)}, u32[]{:S(2)}, u32[]{:S(2)}) collective-permute-start(f32[2,112,114]{2,1,0:T(8,128)S(1)} %concatenate.31), channel_id=1, source_target_pairs={{0,32},{8,40},{16,48},{24,56},{32,0},{40,8},{48,16},{56,24},{64,96... | collective-permute-start | bytes 306440 | tf_op jit(solution)/shard_map/ppermute | solution.py:20
  88.4 1.7 %collective-permute-start.12 = (f32[2,112,114]{2,1,0:T(8,128)S(1)}, f32[2,112,114]{2,1,0:T(8,128)S(1)}, u32[]{:S(2)}, u32[]{:S(2)}) collective-permute-start(f32[2,112,114]{2,1,0:T(8,128)S(1)} %concatenate.31), channel_id=1, source_target_pairs={{0,24},{8,32},{16,40},{24,48},{32,56},{40,0},{48,8},{56,16},{64,88... | collective-permute-start | bytes 306440 | tf_op jit(solution)/shard_map/ppermute | solution.py:20
  90.1 1.8 %collective-permute-start.11 = (f32[2,112,114]{2,1,0:T(8,128)S(1)}, f32[2,112,114]{2,1,0:T(8,128)S(1)}, u32[]{:S(2)}, u32[]{:S(2)}) collective-permute-start(f32[2,112,114]{2,1,0:T(8,128)S(1)} %concatenate.31), channel_id=1, source_target_pairs={{0,16},{8,24},{16,32},{24,40},{32,48},{40,56},{48,0},{56,8},{64,80... | collective-permute-start | bytes 306440 | tf_op jit(solution)/shard_map/ppermute | solution.py:20
  93.1 3.5 %all-to-all-start.2 = ((bf16[8,1,128,224]{2,3,1,0:T(8,128)(2,1)}), bf16[8,1,128,224]{2,3,1,0:T(8,128)(2,1)S(1)}, u32[]{:S(2)}, u32[]{:S(2)}) async-start(bf16[8,1,128,224]{2,3,1,0:T(8,128)(2,1)} %copy.45), calls=%async_computation.2 | async-start | bytes 917504 | tf_op jit(solution)/shard_map/all_to_all | solution.py:83
  96.6 1.4 %collective-permute-done.13 = f32[2,112,114]{2,1,0:T(8,128)S(1)} collective-permute-done((f32[2,112,114]{2,1,0:T(8,128)S(1)}, f32[2,112,114]{2,1,0:T(8,128)S(1)}, u32[]{:S(2)}, u32[]{:S(2)}) %collective-permute-start.13) | collective-permute-done | bytes 102176 | tf_op jit(solution)/shard_map/ppermute | solution.py:20
  100.8 1.8 %collective-permute-start.18 = (f32[2,112,114]{2,1,0:T(8,128)S(1)}, f32[2,112,114]{2,1,0:T(8,128)S(1)}, u32[]{:S(2)}, u32[]{:S(2)}) collective-permute-start(f32[2,112,114]{2,1,0:T(8,128)S(1)} %get-tuple-element.52), channel_id=1, source_target_pairs={{0,128},{8,136},{16,144},{24,152},{32,160},{40,168},{48,176},{56,1... | collective-permute-start | bytes 306440 | tf_op jit(solution)/shard_map/ppermute | solution.py:30
  102.6 3.8 %collective-permute-done.19 = f32[2,112,114]{2,1,0:T(8,128)S(1)} collective-permute-done((f32[2,112,114]{2,1,0:T(8,128)S(1)}, f32[2,112,114]{2,1,0:T(8,128)S(1)}, u32[]{:S(2)}, u32[]{:S(2)}) %collective-permute-start.19) | collective-permute-done | bytes 102176 | tf_op jit(solution)/shard_map/ppermute | solution.py:30
  106.6 1.1 collective-permute-done.18
  107.9 1.7 %collective-permute-done.17 = f32[2,112,114]{2,1,0:T(8,128)S(1)} collective-permute-done((f32[2,112,114]{2,1,0:T(8,128)S(1)}, f32[2,112,114]{2,1,0:T(8,128)S(1)}, u32[]{:S(2)}, u32[]{:S(2)}) %collective-permute-start.17) | collective-permute-done | bytes 102176 | tf_op jit(solution)/shard_map/ppermute | solution.py:30
  110.3 2.3 %all-to-all-done.2 = bf16[8,1,128,224]{2,3,1,0:T(8,128)(2,1)S(1)} async-done(((bf16[8,1,128,224]{2,3,1,0:T(8,128)(2,1)}), bf16[8,1,128,224]{2,3,1,0:T(8,128)(2,1)S(1)}, u32[]{:S(2)}, u32[]{:S(2)}) %all-to-all-start.2) | async-done | bytes 458784 | tf_op jit(solution)/shard_map/all_to_all | solution.py:83
  113.5 3.5 %all-to-all-start.3 = ((bf16[8,2,112,113]{3,2,1,0:T(8,128)(2,1)}), bf16[8,2,112,113]{3,2,1,0:T(8,128)(2,1)S(1)}, u32[]{:S(2)}, u32[]{:S(2)}) async-start(bf16[8,2,112,113]{3,2,1,0:T(8,128)(2,1)} %broadcast_in_dim.406), calls=%async_computation.3 | async-start | bytes 917504 | tf_op jit(solution)/shard_map/all_to_all | solution.py:119
  118.2 15.3 %all-to-all-done.3 = bf16[8,2,112,113]{3,2,1,0:T(8,128)(2,1)S(1)} async-done(((bf16[8,2,112,113]{3,2,1,0:T(8,128)(2,1)}), bf16[8,2,112,113]{3,2,1,0:T(8,128)(2,1)S(1)}, u32[]{:S(2)}, u32[]{:S(2)}) %all-to-all-start.3) | async-done | bytes 405024 | tf_op jit(solution)/shard_map/all_to_all | solution.py:119
  (126 shorter events, 24.4 us)
Async XLA Ops:
  3.9 8.6 %copy-start.14 = (bf16[128,1792]{1,0:T(8,128)(2,1)S(1)}, bf16[128,1792]{1,0:T(8,128)(2,1)}, u32[]{:S(2)}) copy-start(bf16[128,1792]{1,0:T(8,128)(2,1)} %param.8) | copy-start | bytes 1376260
  3.9 34.5 %all-to-all-start.1 = ((bf16[8,2,128,224]{2,3,1,0:T(8,128)(2,1)}), bf16[8,2,128,224]{2,3,1,0:T(8,128)(2,1)S(1)}, u32[]{:S(2)}, u32[]{:S(2)}) async-start(bf16[8,2,128,224]{2,3,1,0:T(8,128)(2,1)} %copy.41), calls=%async_computation.1 | async-start | bytes 1835008 | tf_op jit(solution)/shard_map/all_to_all | solution.py:76
  38.4 29.9 %all-to-all-start = ((bf16[8,2,128,224]{2,3,1,0:T(8,128)(2,1)}), bf16[8,2,128,224]{2,3,1,0:T(8,128)(2,1)S(1)}, u32[]{:S(2)}, u32[]{:S(2)}) async-start(bf16[8,2,128,224]{2,3,1,0:T(8,128)(2,1)} %copy.37), calls=%async_computation | async-start | bytes 1835008 | tf_op jit(solution)/shard_map/all_to_all | solution.py:76
  43.8 5.0 %collective-permute-start = (f32[2,112,114]{2,1,0:T(8,128)S(1)}, f32[2,112,114]{2,1,0:T(8,128)S(1)}, u32[]{:S(2)}, u32[]{:S(2)}) collective-permute-start(f32[2,112,114]{2,1,0:T(8,128)S(1)} %concatenate.27), channel_id=1, source_target_pairs={{0,8},{8,16},{16,24},{24,32},{32,40},{40,48},{48,56},{56,0},{64,72... | collective-permute-start | bytes 306440 | tf_op jit(solution)/shard_map/ppermute | solution.py:20
  43.8 6.8 %collective-permute-start.6 = (f32[2,112,114]{2,1,0:T(8,128)S(1)}, f32[2,112,114]{2,1,0:T(8,128)S(1)}, u32[]{:S(2)}, u32[]{:S(2)}) collective-permute-start(f32[2,112,114]{2,1,0:T(8,128)S(1)} %concatenate.27), channel_id=1, source_target_pairs={{0,56},{8,0},{16,8},{24,16},{32,24},{40,32},{48,40},{56,48},{64,12... | collective-permute-start | bytes 306440 | tf_op jit(solution)/shard_map/ppermute | solution.py:20
  45.6 7.4 %collective-permute-start.5 = (f32[2,112,114]{2,1,0:T(8,128)S(1)}, f32[2,112,114]{2,1,0:T(8,128)S(1)}, u32[]{:S(2)}, u32[]{:S(2)}) collective-permute-start(f32[2,112,114]{2,1,0:T(8,128)S(1)} %concatenate.27), channel_id=1, source_target_pairs={{0,48},{8,56},{16,0},{24,8},{32,16},{40,24},{48,32},{56,40},{64,11... | collective-permute-start | bytes 306440 | tf_op jit(solution)/shard_map/ppermute | solution.py:20
  47.3 5.7 %collective-permute-start.4 = (f32[2,112,114]{2,1,0:T(8,128)S(1)}, f32[2,112,114]{2,1,0:T(8,128)S(1)}, u32[]{:S(2)}, u32[]{:S(2)}) collective-permute-start(f32[2,112,114]{2,1,0:T(8,128)S(1)} %concatenate.27), channel_id=1, source_target_pairs={{0,40},{8,48},{16,56},{24,0},{32,8},{40,16},{48,24},{56,32},{64,10... | collective-permute-start | bytes 306440 | tf_op jit(solution)/shard_map/ppermute | solution.py:20
  47.4 11.1 %collective-permute-start.3 = (f32[2,112,114]{2,1,0:T(8,128)S(1)}, f32[2,112,114]{2,1,0:T(8,128)S(1)}, u32[]{:S(2)}, u32[]{:S(2)}) collective-permute-start(f32[2,112,114]{2,1,0:T(8,128)S(1)} %concatenate.27), channel_id=1, source_target_pairs={{0,32},{8,40},{16,48},{24,56},{32,0},{40,8},{48,16},{56,24},{64,96... | collective-permute-start | bytes 306440 | tf_op jit(solution)/shard_map/ppermute | solution.py:20
  48.9 9.7 %collective-permute-start.2 = (f32[2,112,114]{2,1,0:T(8,128)S(1)}, f32[2,112,114]{2,1,0:T(8,128)S(1)}, u32[]{:S(2)}, u32[]{:S(2)}) collective-permute-start(f32[2,112,114]{2,1,0:T(8,128)S(1)} %concatenate.27), channel_id=1, source_target_pairs={{0,24},{8,32},{16,40},{24,48},{32,56},{40,0},{48,8},{56,16},{64,88... | collective-permute-start | bytes 306440 | tf_op jit(solution)/shard_map/ppermute | solution.py:20
  50.6 8.9 %collective-permute-start.1 = (f32[2,112,114]{2,1,0:T(8,128)S(1)}, f32[2,112,114]{2,1,0:T(8,128)S(1)}, u32[]{:S(2)}, u32[]{:S(2)}) collective-permute-start(f32[2,112,114]{2,1,0:T(8,128)S(1)} %concatenate.27), channel_id=1, source_target_pairs={{0,16},{8,24},{16,32},{24,40},{32,48},{40,56},{48,0},{56,8},{64,80... | collective-permute-start | bytes 306440 | tf_op jit(solution)/shard_map/ppermute | solution.py:20
  53.0 8.0 %copy-start.3 = (f32[2,112,114]{2,1,0:T(8,128)}, f32[2,112,114]{2,1,0:T(8,128)S(1)}, u32[]{:S(2)}) copy-start(f32[2,112,114]{2,1,0:T(8,128)S(1)} %collective-permute-done.5) | copy-start | bytes 306436
  53.0 8.0 %copy-start.5 = (f32[2,112,114]{2,1,0:T(8,128)}, f32[2,112,114]{2,1,0:T(8,128)S(1)}, u32[]{:S(2)}) copy-start(f32[2,112,114]{2,1,0:T(8,128)S(1)} %collective-permute-done.4) | copy-start | bytes 306436
  62.2 12.6 %collective-permute-start.9 = (f32[2,112,114]{2,1,0:T(8,128)}, f32[2,112,114]{2,1,0:T(8,128)}, u32[]{:S(2)}, u32[]{:S(2)}) collective-permute-start(f32[2,112,114]{2,1,0:T(8,128)} %get-tuple-element.54), channel_id=1, source_target_pairs={{0,192},{8,200},{16,208},{24,216},{32,224},{40,232},{48,240},{56,2... | collective-permute-start | bytes 306440 | tf_op jit(solution)/shard_map/ppermute | solution.py:30
  70.0 10.3 %copy-start.10 = (f32[2,112,114]{2,1,0:T(8,128)S(1)}, f32[2,112,114]{2,1,0:T(8,128)}, u32[]{:S(2)}) copy-start(f32[2,112,114]{2,1,0:T(8,128)} %copy-done.9) | copy-start | bytes 306436
  70.1 10.3 %copy-start.12 = (f32[2,112,114]{2,1,0:T(8,128)S(1)}, f32[2,112,114]{2,1,0:T(8,128)}, u32[]{:S(2)}) copy-start(f32[2,112,114]{2,1,0:T(8,128)} %copy-done.11) | copy-start | bytes 306436
  70.9 6.4 %collective-permute-start.8 = (f32[2,112,114]{2,1,0:T(8,128)S(1)}, f32[2,112,114]{2,1,0:T(8,128)S(1)}, u32[]{:S(2)}, u32[]{:S(2)}) collective-permute-start(f32[2,112,114]{2,1,0:T(8,128)S(1)} %copy-done.17), channel_id=1, source_target_pairs={{0,128},{8,136},{16,144},{24,152},{32,160},{40,168},{48,176},{56,1... | collective-permute-start | bytes 306440 | tf_op jit(solution)/shard_map/ppermute | solution.py:30
  74.1 6.0 %collective-permute-start.7 = (f32[2,112,114]{2,1,0:T(8,128)S(1)}, f32[2,112,114]{2,1,0:T(8,128)S(1)}, u32[]{:S(2)}, u32[]{:S(2)}) collective-permute-start(f32[2,112,114]{2,1,0:T(8,128)S(1)} %copy-done.16), channel_id=1, source_target_pairs={{0,64},{8,72},{16,80},{24,88},{32,96},{40,104},{48,112},{56,120},{... | collective-permute-start | bytes 306440 | tf_op jit(solution)/shard_map/ppermute | solution.py:30
  74.8 5.6 %copy-start.8 = (f32[2,112,114]{2,1,0:T(8,128)S(1)}, f32[2,112,114]{2,1,0:T(8,128)}, u32[]{:S(2)}) copy-start(f32[2,112,114]{2,1,0:T(8,128)} %copy-done.7) | copy-start | bytes 306436
  75.9 4.5 %copy-start.4 = (f32[2,112,114]{2,1,0:T(8,128)S(1)}, f32[2,112,114]{2,1,0:T(8,128)}, u32[]{:S(2)}) copy-start(f32[2,112,114]{2,1,0:T(8,128)} %copy-done.3) | copy-start | bytes 306436
  83.3 5.0 %collective-permute-start.10 = (f32[2,112,114]{2,1,0:T(8,128)S(1)}, f32[2,112,114]{2,1,0:T(8,128)S(1)}, u32[]{:S(2)}, u32[]{:S(2)}) collective-permute-start(f32[2,112,114]{2,1,0:T(8,128)S(1)} %concatenate.31), channel_id=1, source_target_pairs={{0,8},{8,16},{16,24},{24,32},{32,40},{40,48},{48,56},{56,0},{64,72... | collective-permute-start | bytes 306440 | tf_op jit(solution)/shard_map/ppermute | solution.py:20
  83.4 6.8 %collective-permute-start.16 = (f32[2,112,114]{2,1,0:T(8,128)S(1)}, f32[2,112,114]{2,1,0:T(8,128)S(1)}, u32[]{:S(2)}, u32[]{:S(2)}) collective-permute-start(f32[2,112,114]{2,1,0:T(8,128)S(1)} %concatenate.31), channel_id=1, source_target_pairs={{0,56},{8,0},{16,8},{24,16},{32,24},{40,32},{48,40},{56,48},{64,12... | collective-permute-start | bytes 306440 | tf_op jit(solution)/shard_map/ppermute | solution.py:20
  85.1 11.5 %collective-permute-start.15 = (f32[2,112,114]{2,1,0:T(8,128)S(1)}, f32[2,112,114]{2,1,0:T(8,128)S(1)}, u32[]{:S(2)}, u32[]{:S(2)}) collective-permute-start(f32[2,112,114]{2,1,0:T(8,128)S(1)} %concatenate.31), channel_id=1, source_target_pairs={{0,48},{8,56},{16,0},{24,8},{32,16},{40,24},{48,32},{56,40},{64,11... | collective-permute-start | bytes 306440 | tf_op jit(solution)/shard_map/ppermute | solution.py:20
  86.8 9.8 %collective-permute-start.14 = (f32[2,112,114]{2,1,0:T(8,128)S(1)}, f32[2,112,114]{2,1,0:T(8,128)S(1)}, u32[]{:S(2)}, u32[]{:S(2)}) collective-permute-start(f32[2,112,114]{2,1,0:T(8,128)S(1)} %concatenate.31), channel_id=1, source_target_pairs={{0,40},{8,48},{16,56},{24,0},{32,8},{40,16},{48,24},{56,32},{64,10... | collective-permute-start | bytes 306440 | tf_op jit(solution)/shard_map/ppermute | solution.py:20
  87.0 11.1 %collective-permute-start.13 = (f32[2,112,114]{2,1,0:T(8,128)S(1)}, f32[2,112,114]{2,1,0:T(8,128)S(1)}, u32[]{:S(2)}, u32[]{:S(2)}) collective-permute-start(f32[2,112,114]{2,1,0:T(8,128)S(1)} %concatenate.31), channel_id=1, source_target_pairs={{0,32},{8,40},{16,48},{24,56},{32,0},{40,8},{48,16},{56,24},{64,96... | collective-permute-start | bytes 306440 | tf_op jit(solution)/shard_map/ppermute | solution.py:20
  88.4 9.7 %collective-permute-start.12 = (f32[2,112,114]{2,1,0:T(8,128)S(1)}, f32[2,112,114]{2,1,0:T(8,128)S(1)}, u32[]{:S(2)}, u32[]{:S(2)}) collective-permute-start(f32[2,112,114]{2,1,0:T(8,128)S(1)} %concatenate.31), channel_id=1, source_target_pairs={{0,24},{8,32},{16,40},{24,48},{32,56},{40,0},{48,8},{56,16},{64,88... | collective-permute-start | bytes 306440 | tf_op jit(solution)/shard_map/ppermute | solution.py:20
  90.1 8.9 %collective-permute-start.11 = (f32[2,112,114]{2,1,0:T(8,128)S(1)}, f32[2,112,114]{2,1,0:T(8,128)S(1)}, u32[]{:S(2)}, u32[]{:S(2)}) collective-permute-start(f32[2,112,114]{2,1,0:T(8,128)S(1)} %concatenate.31), channel_id=1, source_target_pairs={{0,16},{8,24},{16,32},{24,40},{32,48},{40,56},{48,0},{56,8},{64,80... | collective-permute-start | bytes 306440 | tf_op jit(solution)/shard_map/ppermute | solution.py:20
  93.1 19.6 %all-to-all-start.2 = ((bf16[8,1,128,224]{2,3,1,0:T(8,128)(2,1)}), bf16[8,1,128,224]{2,3,1,0:T(8,128)(2,1)S(1)}, u32[]{:S(2)}, u32[]{:S(2)}) async-start(bf16[8,1,128,224]{2,3,1,0:T(8,128)(2,1)} %copy.45), calls=%async_computation.2 | async-start | bytes 917504 | tf_op jit(solution)/shard_map/all_to_all | solution.py:83
  100.4 6.1 %collective-permute-start.19 = (f32[2,112,114]{2,1,0:T(8,128)S(1)}, f32[2,112,114]{2,1,0:T(8,128)S(1)}, u32[]{:S(2)}, u32[]{:S(2)}) collective-permute-start(f32[2,112,114]{2,1,0:T(8,128)S(1)} %get-tuple-element.51), channel_id=1, source_target_pairs={{0,192},{8,200},{16,208},{24,216},{32,224},{40,232},{48,240},{56,2... | collective-permute-start | bytes 306440 | tf_op jit(solution)/shard_map/ppermute | solution.py:30
  100.8 6.9 %collective-permute-start.18 = (f32[2,112,114]{2,1,0:T(8,128)S(1)}, f32[2,112,114]{2,1,0:T(8,128)S(1)}, u32[]{:S(2)}, u32[]{:S(2)}) collective-permute-start(f32[2,112,114]{2,1,0:T(8,128)S(1)} %get-tuple-element.52), channel_id=1, source_target_pairs={{0,128},{8,136},{16,144},{24,152},{32,160},{40,168},{48,176},{56,1... | collective-permute-start | bytes 306440 | tf_op jit(solution)/shard_map/ppermute | solution.py:30
  102.6 7.1 %collective-permute-start.17 = (f32[2,112,114]{2,1,0:T(8,128)S(1)}, f32[2,112,114]{2,1,0:T(8,128)S(1)}, u32[]{:S(2)}, u32[]{:S(2)}) collective-permute-start(f32[2,112,114]{2,1,0:T(8,128)S(1)} %get-tuple-element.50), channel_id=1, source_target_pairs={{0,64},{8,72},{16,80},{24,88},{32,96},{40,104},{48,112},{56,120},{... | collective-permute-start | bytes 306440 | tf_op jit(solution)/shard_map/ppermute | solution.py:30
  113.5 19.9 %all-to-all-start.3 = ((bf16[8,2,112,113]{3,2,1,0:T(8,128)(2,1)}), bf16[8,2,112,113]{3,2,1,0:T(8,128)(2,1)S(1)}, u32[]{:S(2)}, u32[]{:S(2)}) async-start(bf16[8,2,112,113]{3,2,1,0:T(8,128)(2,1)} %broadcast_in_dim.406), calls=%async_computation.3 | async-start | bytes 917504 | tf_op jit(solution)/shard_map/all_to_all | solution.py:119
  118.2 15.7 %copy-start.1 = (bf16[128,1792]{0,1:T(8,128)(2,1)S(1)}, bf16[128,1792]{0,1:T(8,128)(2,1)}, u32[]{:S(2)}) copy-start(bf16[128,1792]{0,1:T(8,128)(2,1)} %copy-done) | copy-start | bytes 1376260
  (18 other events, 25.8 us)

commit v16 on v12

--- a/solution.py
+++ b/solution.py
@@ -8,7 +8,7 @@
 loss_scale = 1024.0
 
 
-ROW = 8
+ROW = 4
 
 
 def shifted(value, count, step):

time: 134 us -> 120 us (0.90)
  the two profiles are of different devices: /device:TPU:22 before, /device:TPU:2 now
where the time goes in v16:
time: 120 us; the launch traced here: 119 us
  starting transfers between devices  58.5 us (49%)
  waiting for transfers between devices  39.2 us (33%)
  local copies, waits for them, and re-layouts  10.7 us (9%)
  other arithmetic  6.3 us (5%)
  matrix products  2.78 us (2%)
  between operations  1.39 us (1%)
    ppermute x14, starting transfers between devices, strided(): return lax.ppermute(value, 'tm', pairs)  33 us
    all_to_all x1, waiting for transfers between devices, local(): lax.all_to_all(pieces, 'inner', 0, 0, tiled=True).astype(jnp.float32)  14.5 us
    all_to_all x1, waiting for transfers between devices, local(): lax.all_to_all(copies, 'inner', 0, 0, tiled=True)  13.4 us
    all_to_all x1, starting transfers between devices, local(): lax.all_to_all(pieces, 'inner', 0, 0, tiled=True).astype(jnp.float32)  8.6 us
    unnamed x21, local copies, waits for them, and re-layouts  7.03 us
    all_to_all x1, starting transfers between devices, local(): lax.all_to_all(copies, 'inner', 0, 0, tiled=True)  6.44 us
    ppermute x14, waiting for transfers between devices, strided(): return lax.ppermute(value, 'tm', pairs)  4.29 us
    all_to_all x1, waiting for transfers between devices, to_heads(): incoming = lax.all_to_all(outgoing, 'inner', 0, 0, tiled=True)  3.89 us
  transfers between devices with their start and end apart: 24, of which 7 were waited for; matrix products, arithmetic and copies ran while one was open for 8% of the time, Pallas kernels for 0%

profile of v16, /device:TPU:2, one launch (start us, length us, event | category | flops | bytes accessed | tf_op | source)
XLA Modules:
  0.0 118.9 jit_solution(14443790017536564607)
XLA Ops:
  0.6 1.3 %copy.34 = bf16[128,1792]{0,1:T(8,128)(2,1)S(1)} copy(bf16[128,1792]{1,0:T(8,128)(2,1)} %param.6) | data formatting | bytes 917504 | tf_op args[1]
  2.0 1.0 copy-done.2
  3.2 1.2 convolution_convert_fusion.1
  4.4 8.6 %all-to-all-start.1 = ((bf16[8,2,112,113]{3,2,1,0:T(8,128)(2,1)}), bf16[8,2,112,113]{3,2,1,0:T(8,128)(2,1)S(1)}, u32[]{:S(2)}, u32[]{:S(2)}) async-start(bf16[8,2,112,113]{3,2,1,0:T(8,128)(2,1)} %bitcast.7), calls=%async_computation.1 | async-start | bytes 917504 | tf_op jit(solution)/shard_map/all_to_all | solution.py:100
  14.6 14.5 %all-to-all-done.1 = bf16[8,2,112,113]{3,2,1,0:T(8,128)(2,1)S(1)} async-done(((bf16[8,2,112,113]{3,2,1,0:T(8,128)(2,1)}), bf16[8,2,112,113]{3,2,1,0:T(8,128)(2,1)S(1)}, u32[]{:S(2)}, u32[]{:S(2)}) %all-to-all-start.1) | async-done | bytes 405024 | tf_op jit(solution)/shard_map/all_to_all | solution.py:100
  29.3 1.5 %collective-permute-start.1 = (f32[2,112,114]{2,1,0:T(8,128)S(1)}, f32[2,112,114]{2,1,0:T(8,128)S(1)}, u32[]{:S(2)}, u32[]{:S(2)}) collective-permute-start(f32[2,112,114]{2,1,0:T(8,128)S(1)} %concatenate.26), channel_id=1, source_target_pairs={{0,16},{8,24},{16,0},{24,8},{32,48},{40,56},{48,32},{56,40},{64,80... | collective-permute-start | bytes 306440 | tf_op jit(solution)/shard_map/ppermute | solution.py:20
  30.9 1.0 copy.32
  31.9 3.6 %all-to-all-start = ((bf16[8,2,128,224]{2,3,1,0:T(8,128)(2,1)}), bf16[8,2,128,224]{2,3,1,0:T(8,128)(2,1)S(1)}, u32[]{:S(2)}, u32[]{:S(2)}) async-start(bf16[8,2,128,224]{2,3,1,0:T(8,128)(2,1)} %copy.32), calls=%async_computation | async-start | bytes 1835008 | tf_op jit(solution)/shard_map/all_to_all | solution.py:76
  35.8 1.5 %collective-permute-done.1 = f32[2,112,114]{2,1,0:T(8,128)S(1)} collective-permute-done((f32[2,112,114]{2,1,0:T(8,128)S(1)}, f32[2,112,114]{2,1,0:T(8,128)S(1)}, u32[]{:S(2)}, u32[]{:S(2)}) %collective-permute-start.1) | collective-permute-done | bytes 102176 | tf_op jit(solution)/shard_map/ppermute | solution.py:20
  38.0 2.2 %collective-permute-start.3 = (f32[2,112,114]{2,1,0:T(8,128)S(1)}, f32[2,112,114]{2,1,0:T(8,128)S(1)}, u32[]{:S(2)}, u32[]{:S(2)}) collective-permute-start(f32[2,112,114]{2,1,0:T(8,128)S(1)} %get-tuple-element.30), channel_id=1, source_target_pairs={{0,32},{8,40},{16,48},{24,56},{32,64},{40,72},{48,80},{56,88},{64,... | collective-permute-start | bytes 306440 | tf_op jit(solution)/shard_map/ppermute | solution.py:30
  40.3 1.7 %collective-permute-start.4 = (f32[2,112,114]{2,1,0:T(8,128)S(1)}, f32[2,112,114]{2,1,0:T(8,128)S(1)}, u32[]{:S(2)}, u32[]{:S(2)}) collective-permute-start(f32[2,112,114]{2,1,0:T(8,128)S(1)} %get-tuple-element.48), channel_id=1, source_target_pairs={{0,64},{8,72},{16,80},{24,88},{32,96},{40,104},{48,112},{56,120},{... | collective-permute-start | bytes 306440 | tf_op jit(solution)/shard_map/ppermute | solution.py:30
  41.9 1.6 %collective-permute-start.8 = (f32[2,112,114]{2,1,0:T(8,128)S(1)}, f32[2,112,114]{2,1,0:T(8,128)S(1)}, u32[]{:S(2)}, u32[]{:S(2)}) collective-permute-start(f32[2,112,114]{2,1,0:T(8,128)S(1)} %get-tuple-element.49), channel_id=1, source_target_pairs={{0,192},{8,200},{16,208},{24,216},{32,224},{40,232},{48,240},{56,2... | collective-permute-start | bytes 306440 | tf_op jit(solution)/shard_map/ppermute | solution.py:30
  43.6 3.5 %collective-permute-start.7 = (f32[2,112,114]{2,1,0:T(8,128)S(1)}, f32[2,112,114]{2,1,0:T(8,128)S(1)}, u32[]{:S(2)}, u32[]{:S(2)}) collective-permute-start(f32[2,112,114]{2,1,0:T(8,128)S(1)} %get-tuple-element.50), channel_id=1, source_target_pairs={{0,160},{8,168},{16,176},{24,184},{32,192},{40,200},{48,208},{56,2... | collective-permute-start | bytes 306440 | tf_op jit(solution)/shard_map/ppermute | solution.py:30
  47.1 1.8 %collective-permute-start.6 = (f32[2,112,114]{2,1,0:T(8,128)S(1)}, f32[2,112,114]{2,1,0:T(8,128)S(1)}, u32[]{:S(2)}, u32[]{:S(2)}) collective-permute-start(f32[2,112,114]{2,1,0:T(8,128)S(1)} %get-tuple-element.51), channel_id=1, source_target_pairs={{0,128},{8,136},{16,144},{24,152},{32,160},{40,168},{48,176},{56,1... | collective-permute-start | bytes 306440 | tf_op jit(solution)/shard_map/ppermute | solution.py:30
  49.6 5.3 %collective-permute-start.9 = (f32[2,112,114]{2,1,0:T(8,128)S(1)}, f32[2,112,114]{2,1,0:T(8,128)S(1)}, u32[]{:S(2)}, u32[]{:S(2)}) collective-permute-start(f32[2,112,114]{2,1,0:T(8,128)S(1)} %get-tuple-element.53), channel_id=1, source_target_pairs={{0,224},{8,232},{16,240},{24,248},{32,0},{40,8},{48,16},{56,24},{6... | collective-permute-start | bytes 306440 | tf_op jit(solution)/shard_map/ppermute | solution.py:30
  55.6 2.0 %collective-permute-done.5 = f32[2,112,114]{2,1,0:T(8,128)S(1)} collective-permute-done((f32[2,112,114]{2,1,0:T(8,128)S(1)}, f32[2,112,114]{2,1,0:T(8,128)S(1)}, u32[]{:S(2)}, u32[]{:S(2)}) %collective-permute-start.5) | collective-permute-done | bytes 102176 | tf_op jit(solution)/shard_map/ppermute | solution.py:30
  58.6 3.9 %all-to-all-done = bf16[8,2,128,224]{2,3,1,0:T(8,128)(2,1)S(1)} async-done(((bf16[8,2,128,224]{2,3,1,0:T(8,128)(2,1)}), bf16[8,2,128,224]{2,3,1,0:T(8,128)(2,1)S(1)}, u32[]{:S(2)}, u32[]{:S(2)}) %all-to-all-start) | async-done | bytes 917536 | tf_op jit(solution)/shard_map/all_to_all | solution.py:76
  65.4 1.0 collective-permute-start.11
  67.6 3.5 %all-to-all-start.2 = ((bf16[8,1,128,224]{2,3,1,0:T(8,128)(2,1)}), bf16[8,1,128,224]{2,3,1,0:T(8,128)(2,1)S(1)}, u32[]{:S(2)}, u32[]{:S(2)}) async-start(bf16[8,1,128,224]{2,3,1,0:T(8,128)(2,1)} %copy.37), calls=%async_computation.2 | async-start | bytes 917504 | tf_op jit(solution)/shard_map/all_to_all | solution.py:83
  71.1 1.6 %collective-permute-done.11 = f32[2,112,114]{2,1,0:T(8,128)S(1)} collective-permute-done((f32[2,112,114]{2,1,0:T(8,128)S(1)}, f32[2,112,114]{2,1,0:T(8,128)S(1)}, u32[]{:S(2)}, u32[]{:S(2)}) %collective-permute-start.11) | collective-permute-done | bytes 102176 | tf_op jit(solution)/shard_map/ppermute | solution.py:20
  73.5 2.5 %collective-permute-start.13 = (f32[2,112,114]{2,1,0:T(8,128)S(1)}, f32[2,112,114]{2,1,0:T(8,128)S(1)}, u32[]{:S(2)}, u32[]{:S(2)}) collective-permute-start(f32[2,112,114]{2,1,0:T(8,128)S(1)} %get-tuple-element.26), channel_id=1, source_target_pairs={{0,32},{8,40},{16,48},{24,56},{32,64},{40,72},{48,80},{56,88},{64,... | collective-permute-start | bytes 306440 | tf_op jit(solution)/shard_map/ppermute | solution.py:30
  76.0 1.6 %collective-permute-start.14 = (f32[2,112,114]{2,1,0:T(8,128)S(1)}, f32[2,112,114]{2,1,0:T(8,128)S(1)}, u32[]{:S(2)}, u32[]{:S(2)}) collective-permute-start(f32[2,112,114]{2,1,0:T(8,128)S(1)} %get-tuple-element.42), channel_id=1, source_target_pairs={{0,64},{8,72},{16,80},{24,88},{32,96},{40,104},{48,112},{56,120},{... | collective-permute-start | bytes 306440 | tf_op jit(solution)/shard_map/ppermute | solution.py:30
  77.7 1.7 %collective-permute-start.18 = (f32[2,112,114]{2,1,0:T(8,128)S(1)}, f32[2,112,114]{2,1,0:T(8,128)S(1)}, u32[]{:S(2)}, u32[]{:S(2)}) collective-permute-start(f32[2,112,114]{2,1,0:T(8,128)S(1)} %get-tuple-element.43), channel_id=1, source_target_pairs={{0,192},{8,200},{16,208},{24,216},{32,224},{40,232},{48,240},{56,2... | collective-permute-start | bytes 306440 | tf_op jit(solution)/shard_map/ppermute | solution.py:30
  79.3 3.2 %collective-permute-start.17 = (f32[2,112,114]{2,1,0:T(8,128)S(1)}, f32[2,112,114]{2,1,0:T(8,128)S(1)}, u32[]{:S(2)}, u32[]{:S(2)}) collective-permute-start(f32[2,112,114]{2,1,0:T(8,128)S(1)} %get-tuple-element.44), channel_id=1, source_target_pairs={{0,160},{8,168},{16,176},{24,184},{32,192},{40,200},{48,208},{56,2... | collective-permute-start | bytes 306440 | tf_op jit(solution)/shard_map/ppermute | solution.py:30
  82.6 1.8 %collective-permute-start.16 = (f32[2,112,114]{2,1,0:T(8,128)S(1)}, f32[2,112,114]{2,1,0:T(8,128)S(1)}, u32[]{:S(2)}, u32[]{:S(2)}) collective-permute-start(f32[2,112,114]{2,1,0:T(8,128)S(1)} %get-tuple-element.45), channel_id=1, source_target_pairs={{0,128},{8,136},{16,144},{24,152},{32,160},{40,168},{48,176},{56,1... | collective-permute-start | bytes 306440 | tf_op jit(solution)/shard_map/ppermute | solution.py:30
  85.3 4.8 %collective-permute-start.19 = (f32[2,112,114]{2,1,0:T(8,128)S(1)}, f32[2,112,114]{2,1,0:T(8,128)S(1)}, u32[]{:S(2)}, u32[]{:S(2)}) collective-permute-start(f32[2,112,114]{2,1,0:T(8,128)S(1)} %get-tuple-element.47), channel_id=1, source_target_pairs={{0,224},{8,232},{16,240},{24,248},{32,0},{40,8},{48,16},{56,24},{6... | collective-permute-start | bytes 306440 | tf_op jit(solution)/shard_map/ppermute | solution.py:30
  90.9 2.2 %collective-permute-done.15 = f32[2,112,114]{2,1,0:T(8,128)S(1)} collective-permute-done((f32[2,112,114]{2,1,0:T(8,128)S(1)}, f32[2,112,114]{2,1,0:T(8,128)S(1)}, u32[]{:S(2)}, u32[]{:S(2)}) %collective-permute-start.15) | collective-permute-done | bytes 102176 | tf_op jit(solution)/shard_map/ppermute | solution.py:30
  94.8 6.4 %all-to-all-start.3 = ((bf16[8,2,112,113]{3,2,1,0:T(8,128)(2,1)}), bf16[8,2,112,113]{3,2,1,0:T(8,128)(2,1)S(1)}, u32[]{:S(2)}, u32[]{:S(2)}) async-start(bf16[8,2,112,113]{3,2,1,0:T(8,128)(2,1)} %broadcast_in_dim.326), calls=%async_computation.3 | async-start | bytes 917504 | tf_op jit(solution)/shard_map/all_to_all | solution.py:126
  101.4 1.0 copy.41
  102.4 13.4 %all-to-all-done.3 = bf16[8,2,112,113]{3,2,1,0:T(8,128)(2,1)S(1)} async-done(((bf16[8,2,112,113]{3,2,1,0:T(8,128)(2,1)}), bf16[8,2,112,113]{3,2,1,0:T(8,128)(2,1)S(1)}, u32[]{:S(2)}, u32[]{:S(2)}) %all-to-all-start.3) | async-done | bytes 405024 | tf_op jit(solution)/shard_map/all_to_all | solution.py:126
  116.5 1.0 copy.43
  117.9 1.0 copy.42
  (88 shorter events, 14.6 us)
Async XLA Ops:
  1.9 1.0 copy-start.2
  3.2 1.2 %copy-start = (bf16[128,1792]{0,1:T(8,128)(2,1)}, bf16[128,1792]{0,1:T(8,128)(2,1)S(1)}, u32[]{:S(2)}) copy-start(bf16[128,1792]{0,1:T(8,128)(2,1)S(1)} %copy.35) | copy-start | bytes 1376260
  4.4 8.6 %copy-start.3 = (bf16[128,1792]{1,0:T(8,128)(2,1)S(1)}, bf16[128,1792]{1,0:T(8,128)(2,1)}, u32[]{:S(2)}) copy-start(bf16[128,1792]{1,0:T(8,128)(2,1)} %param.5) | copy-start | bytes 1376260
  4.4 24.7 %all-to-all-start.1 = ((bf16[8,2,112,113]{3,2,1,0:T(8,128)(2,1)}), bf16[8,2,112,113]{3,2,1,0:T(8,128)(2,1)S(1)}, u32[]{:S(2)}, u32[]{:S(2)}) async-start(bf16[8,2,112,113]{3,2,1,0:T(8,128)(2,1)} %bitcast.7), calls=%async_computation.1 | async-start | bytes 917504 | tf_op jit(solution)/shard_map/all_to_all | solution.py:100
  13.2 1.0 copy-start.4
  13.3 0.7 copy-start.5
  29.2 6.6 %collective-permute-start.2 = (f32[2,112,114]{2,1,0:T(8,128)S(1)}, f32[2,112,114]{2,1,0:T(8,128)S(1)}, u32[]{:S(2)}, u32[]{:S(2)}) collective-permute-start(f32[2,112,114]{2,1,0:T(8,128)S(1)} %concatenate.26), channel_id=1, source_target_pairs={{0,24},{8,0},{16,8},{24,16},{32,56},{40,32},{48,40},{56,48},{64,88... | collective-permute-start | bytes 306440 | tf_op jit(solution)/shard_map/ppermute | solution.py:20
  29.3 7.9 %collective-permute-start.1 = (f32[2,112,114]{2,1,0:T(8,128)S(1)}, f32[2,112,114]{2,1,0:T(8,128)S(1)}, u32[]{:S(2)}, u32[]{:S(2)}) collective-permute-start(f32[2,112,114]{2,1,0:T(8,128)S(1)} %concatenate.26), channel_id=1, source_target_pairs={{0,16},{8,24},{16,0},{24,8},{32,48},{40,56},{48,32},{56,40},{64,80... | collective-permute-start | bytes 306440 | tf_op jit(solution)/shard_map/ppermute | solution.py:20
  30.8 6.5 %collective-permute-start = (f32[2,112,114]{2,1,0:T(8,128)S(1)}, f32[2,112,114]{2,1,0:T(8,128)S(1)}, u32[]{:S(2)}, u32[]{:S(2)}) collective-permute-start(f32[2,112,114]{2,1,0:T(8,128)S(1)} %concatenate.26), channel_id=1, source_target_pairs={{0,8},{8,16},{16,24},{24,0},{32,40},{40,48},{48,56},{56,32},{64,72... | collective-permute-start | bytes 306440 | tf_op jit(solution)/shard_map/ppermute | solution.py:20
  31.9 30.6 %all-to-all-start = ((bf16[8,2,128,224]{2,3,1,0:T(8,128)(2,1)}), bf16[8,2,128,224]{2,3,1,0:T(8,128)(2,1)S(1)}, u32[]{:S(2)}, u32[]{:S(2)}) async-start(bf16[8,2,128,224]{2,3,1,0:T(8,128)(2,1)} %copy.32), calls=%async_computation | async-start | bytes 1835008 | tf_op jit(solution)/shard_map/all_to_all | solution.py:76
  38.0 11.0 %collective-permute-start.3 = (f32[2,112,114]{2,1,0:T(8,128)S(1)}, f32[2,112,114]{2,1,0:T(8,128)S(1)}, u32[]{:S(2)}, u32[]{:S(2)}) collective-permute-start(f32[2,112,114]{2,1,0:T(8,128)S(1)} %get-tuple-element.30), channel_id=1, source_target_pairs={{0,32},{8,40},{16,48},{24,56},{32,64},{40,72},{48,80},{56,88},{64,... | collective-permute-start | bytes 306440 | tf_op jit(solution)/shard_map/ppermute | solution.py:30
  40.3 9.3 %collective-permute-start.4 = (f32[2,112,114]{2,1,0:T(8,128)S(1)}, f32[2,112,114]{2,1,0:T(8,128)S(1)}, u32[]{:S(2)}, u32[]{:S(2)}) collective-permute-start(f32[2,112,114]{2,1,0:T(8,128)S(1)} %get-tuple-element.48), channel_id=1, source_target_pairs={{0,64},{8,72},{16,80},{24,88},{32,96},{40,104},{48,112},{56,120},{... | collective-permute-start | bytes 306440 | tf_op jit(solution)/shard_map/ppermute | solution.py:30
  41.9 13.1 %collective-permute-start.8 = (f32[2,112,114]{2,1,0:T(8,128)S(1)}, f32[2,112,114]{2,1,0:T(8,128)S(1)}, u32[]{:S(2)}, u32[]{:S(2)}) collective-permute-start(f32[2,112,114]{2,1,0:T(8,128)S(1)} %get-tuple-element.49), channel_id=1, source_target_pairs={{0,192},{8,200},{16,208},{24,216},{32,224},{40,232},{48,240},{56,2... | collective-permute-start | bytes 306440 | tf_op jit(solution)/shard_map/ppermute | solution.py:30
  43.6 11.7 %collective-permute-start.7 = (f32[2,112,114]{2,1,0:T(8,128)S(1)}, f32[2,112,114]{2,1,0:T(8,128)S(1)}, u32[]{:S(2)}, u32[]{:S(2)}) collective-permute-start(f32[2,112,114]{2,1,0:T(8,128)S(1)} %get-tuple-element.50), channel_id=1, source_target_pairs={{0,160},{8,168},{16,176},{24,184},{32,192},{40,200},{48,208},{56,2... | collective-permute-start | bytes 306440 | tf_op jit(solution)/shard_map/ppermute | solution.py:30
  47.1 8.3 %collective-permute-start.6 = (f32[2,112,114]{2,1,0:T(8,128)S(1)}, f32[2,112,114]{2,1,0:T(8,128)S(1)}, u32[]{:S(2)}, u32[]{:S(2)}) collective-permute-start(f32[2,112,114]{2,1,0:T(8,128)S(1)} %get-tuple-element.51), channel_id=1, source_target_pairs={{0,128},{8,136},{16,144},{24,152},{32,160},{40,168},{48,176},{56,1... | collective-permute-start | bytes 306440 | tf_op jit(solution)/shard_map/ppermute | solution.py:30
  49.0 8.7 %collective-permute-start.5 = (f32[2,112,114]{2,1,0:T(8,128)S(1)}, f32[2,112,114]{2,1,0:T(8,128)S(1)}, u32[]{:S(2)}, u32[]{:S(2)}) collective-permute-start(f32[2,112,114]{2,1,0:T(8,128)S(1)} %get-tuple-element.52), channel_id=1, source_target_pairs={{0,96},{8,104},{16,112},{24,120},{32,128},{40,136},{48,144},{56,15... | collective-permute-start | bytes 306440 | tf_op jit(solution)/shard_map/ppermute | solution.py:30
  49.6 8.3 %collective-permute-start.9 = (f32[2,112,114]{2,1,0:T(8,128)S(1)}, f32[2,112,114]{2,1,0:T(8,128)S(1)}, u32[]{:S(2)}, u32[]{:S(2)}) collective-permute-start(f32[2,112,114]{2,1,0:T(8,128)S(1)} %get-tuple-element.53), channel_id=1, source_target_pairs={{0,224},{8,232},{16,240},{24,248},{32,0},{40,8},{48,16},{56,24},{6... | collective-permute-start | bytes 306440 | tf_op jit(solution)/shard_map/ppermute | solution.py:30
  64.6 6.5 %collective-permute-start.12 = (f32[2,112,114]{2,1,0:T(8,128)S(1)}, f32[2,112,114]{2,1,0:T(8,128)S(1)}, u32[]{:S(2)}, u32[]{:S(2)}) collective-permute-start(f32[2,112,114]{2,1,0:T(8,128)S(1)} %concatenate.30), channel_id=1, source_target_pairs={{0,24},{8,0},{16,8},{24,16},{32,56},{40,32},{48,40},{56,48},{64,88... | collective-permute-start | bytes 306440 | tf_op jit(solution)/shard_map/ppermute | solution.py:20
  65.4 7.3 %collective-permute-start.11 = (f32[2,112,114]{2,1,0:T(8,128)S(1)}, f32[2,112,114]{2,1,0:T(8,128)S(1)}, u32[]{:S(2)}, u32[]{:S(2)}) collective-permute-start(f32[2,112,114]{2,1,0:T(8,128)S(1)} %concatenate.30), channel_id=1, source_target_pairs={{0,16},{8,24},{16,0},{24,8},{32,48},{40,56},{48,32},{56,40},{64,80... | collective-permute-start | bytes 306440 | tf_op jit(solution)/shard_map/ppermute | solution.py:20
  66.4 6.3 %collective-permute-start.10 = (f32[2,112,114]{2,1,0:T(8,128)S(1)}, f32[2,112,114]{2,1,0:T(8,128)S(1)}, u32[]{:S(2)}, u32[]{:S(2)}) collective-permute-start(f32[2,112,114]{2,1,0:T(8,128)S(1)} %concatenate.30), channel_id=1, source_target_pairs={{0,8},{8,16},{16,24},{24,0},{32,40},{40,48},{48,56},{56,32},{64,72... | collective-permute-start | bytes 306440 | tf_op jit(solution)/shard_map/ppermute | solution.py:20
  67.6 26.4 %all-to-all-start.2 = ((bf16[8,1,128,224]{2,3,1,0:T(8,128)(2,1)}), bf16[8,1,128,224]{2,3,1,0:T(8,128)(2,1)S(1)}, u32[]{:S(2)}, u32[]{:S(2)}) async-start(bf16[8,1,128,224]{2,3,1,0:T(8,128)(2,1)} %copy.37), calls=%async_computation.2 | async-start | bytes 917504 | tf_op jit(solution)/shard_map/all_to_all | solution.py:83
  73.5 11.0 %collective-permute-start.13 = (f32[2,112,114]{2,1,0:T(8,128)S(1)}, f32[2,112,114]{2,1,0:T(8,128)S(1)}, u32[]{:S(2)}, u32[]{:S(2)}) collective-permute-start(f32[2,112,114]{2,1,0:T(8,128)S(1)} %get-tuple-element.26), channel_id=1, source_target_pairs={{0,32},{8,40},{16,48},{24,56},{32,64},{40,72},{48,80},{56,88},{64,... | collective-permute-start | bytes 306440 | tf_op jit(solution)/shard_map/ppermute | solution.py:30
  76.0 9.3 %collective-permute-start.14 = (f32[2,112,114]{2,1,0:T(8,128)S(1)}, f32[2,112,114]{2,1,0:T(8,128)S(1)}, u32[]{:S(2)}, u32[]{:S(2)}) collective-permute-start(f32[2,112,114]{2,1,0:T(8,128)S(1)} %get-tuple-element.42), channel_id=1, source_target_pairs={{0,64},{8,72},{16,80},{24,88},{32,96},{40,104},{48,112},{56,120},{... | collective-permute-start | bytes 306440 | tf_op jit(solution)/shard_map/ppermute | solution.py:30
  77.7 12.7 %collective-permute-start.18 = (f32[2,112,114]{2,1,0:T(8,128)S(1)}, f32[2,112,114]{2,1,0:T(8,128)S(1)}, u32[]{:S(2)}, u32[]{:S(2)}) collective-permute-start(f32[2,112,114]{2,1,0:T(8,128)S(1)} %get-tuple-element.43), channel_id=1, source_target_pairs={{0,192},{8,200},{16,208},{24,216},{32,224},{40,232},{48,240},{56,2... | collective-permute-start | bytes 306440 | tf_op jit(solution)/shard_map/ppermute | solution.py:30
  79.3 11.2 %collective-permute-start.17 = (f32[2,112,114]{2,1,0:T(8,128)S(1)}, f32[2,112,114]{2,1,0:T(8,128)S(1)}, u32[]{:S(2)}, u32[]{:S(2)}) collective-permute-start(f32[2,112,114]{2,1,0:T(8,128)S(1)} %get-tuple-element.44), channel_id=1, source_target_pairs={{0,160},{8,168},{16,176},{24,184},{32,192},{40,200},{48,208},{56,2... | collective-permute-start | bytes 306440 | tf_op jit(solution)/shard_map/ppermute | solution.py:30
  82.6 8.1 %collective-permute-start.16 = (f32[2,112,114]{2,1,0:T(8,128)S(1)}, f32[2,112,114]{2,1,0:T(8,128)S(1)}, u32[]{:S(2)}, u32[]{:S(2)}) collective-permute-start(f32[2,112,114]{2,1,0:T(8,128)S(1)} %get-tuple-element.45), channel_id=1, source_target_pairs={{0,128},{8,136},{16,144},{24,152},{32,160},{40,168},{48,176},{56,1... | collective-permute-start | bytes 306440 | tf_op jit(solution)/shard_map/ppermute | solution.py:30
  84.4 8.7 %collective-permute-start.15 = (f32[2,112,114]{2,1,0:T(8,128)S(1)}, f32[2,112,114]{2,1,0:T(8,128)S(1)}, u32[]{:S(2)}, u32[]{:S(2)}) collective-permute-start(f32[2,112,114]{2,1,0:T(8,128)S(1)} %get-tuple-element.46), channel_id=1, source_target_pairs={{0,96},{8,104},{16,112},{24,120},{32,128},{40,136},{48,144},{56,15... | collective-permute-start | bytes 306440 | tf_op jit(solution)/shard_map/ppermute | solution.py:30
  85.3 8.0 %collective-permute-start.19 = (f32[2,112,114]{2,1,0:T(8,128)S(1)}, f32[2,112,114]{2,1,0:T(8,128)S(1)}, u32[]{:S(2)}, u32[]{:S(2)}) collective-permute-start(f32[2,112,114]{2,1,0:T(8,128)S(1)} %get-tuple-element.47), channel_id=1, source_target_pairs={{0,224},{8,232},{16,240},{24,248},{32,0},{40,8},{48,16},{56,24},{6... | collective-permute-start | bytes 306440 | tf_op jit(solution)/shard_map/ppermute | solution.py:30
  94.8 20.9 %all-to-all-start.3 = ((bf16[8,2,112,113]{3,2,1,0:T(8,128)(2,1)}), bf16[8,2,112,113]{3,2,1,0:T(8,128)(2,1)S(1)}, u32[]{:S(2)}, u32[]{:S(2)}) async-start(bf16[8,2,112,113]{3,2,1,0:T(8,128)(2,1)} %broadcast_in_dim.326), calls=%async_computation.3 | async-start | bytes 917504 | tf_op jit(solution)/shard_map/all_to_all | solution.py:126
  116.5 1.0 copy-start.1

commit v17 on v15

--- a/solution.py
+++ b/solution.py
@@ -8,7 +8,7 @@
 loss_scale = 1024.0
 
 
-ROW = 8
+ROW = 4
 
 
 def shifted(value, count, step):

time: 138 us -> 152 us (1.10)
  starting transfers between devices: 45.4 us -> 56.2 us
  waiting for transfers between devices: 64.3 us -> 68.1 us
    ppermute x6 -> x14, starting transfers between devices: 9.13 us -> 28.6 us  [strided(): return lax.ppermute(value, 'tm', pairs)]
    ppermute x14 -> x6, starting transfers between devices: 17.2 us -> 4.87 us  [shifted(): return lax.ppermute(value, 'tm', pairs)]
    all_to_all x2, waiting for transfers between devices: 26.5 us -> 32.4 us  [to_heads(): incoming = lax.all_to_all(outgoing, 'inner', 0, 0, tiled=True)]
    all_to_all x1, waiting for transfers between devices: 15.3 us -> 11.4 us  [local(): lax.all_to_all(copies, 'inner', 0, 0, tiled=True)]
    all_to_all x1, starting transfers between devices: 3.47 us -> 7.11 us  [local(): lax.all_to_all(copies, 'inner', 0, 0, tiled=True)]
    ppermute x6 -> x14, waiting for transfers between devices: 10.7 us -> 13.2 us  [strided(): return lax.ppermute(value, 'tm', pairs)]
    all_to_all x1, waiting for transfers between devices: 2.34 us -> 0.01 us  [to_rows(): returned = lax.all_to_all(leaving, 'inner', 0, 0, tiled=True)]
    ppermute x14 -> x6, waiting for transfers between devices: 9.51 us -> 11.1 us  [shifted(): return lax.ppermute(value, 'tm', pairs)]
  transfers between devices with their start and end apart: 24 -> 24, of which waited for: 14 -> 16; matrix products, arithmetic and copies ran while one was open for 10% -> 9% of each run, Pallas kernels for 0% -> 0%
where the time goes in v17:
time: 152 us
  waiting for transfers between devices  68.1 us (45%)
  starting transfers between devices  56.2 us (37%)
  local copies, waits for them, and re-layouts  14 us (9%)
  other arithmetic  10.2 us (7%)
  matrix products  1.9 us (1%)
    all_to_all x2, waiting for transfers between devices, to_heads(): incoming = lax.all_to_all(outgoing, 'inner', 0, 0, tiled=True)  32.4 us
    ppermute x14, starting transfers between devices, strided(): return lax.ppermute(value, 'tm', pairs)  28.6 us
    ppermute x14, waiting for transfers between devices, strided(): return lax.ppermute(value, 'tm', pairs)  13.2 us
    all_to_all x2, starting transfers between devices, to_heads(): incoming = lax.all_to_all(outgoing, 'inner', 0, 0, tiled=True)  12.1 us
    all_to_all x1, waiting for transfers between devices, local(): lax.all_to_all(copies, 'inner', 0, 0, tiled=True)  11.4 us
    ppermute x6, waiting for transfers between devices, shifted(): return lax.ppermute(value, 'tm', pairs)  11.1 us
    unnamed x43, local copies, waits for them, and re-layouts  7.74 us
    all_to_all x1, starting transfers between devices, local(): lax.all_to_all(copies, 'inner', 0, 0, tiled=True)  7.11 us
  transfers between devices with their start and end apart: 24, of which 16 were waited for; matrix products, arithmetic and copies ran while one was open for 9% of the time, Pallas kernels for 0%

profile of v17, /device:TPU:2, one launch (start us, length us, event | category | flops | bytes accessed | tf_op | source)
XLA Modules:
  0.0 151.6 jit_solution(12968765808102714148)
XLA Ops:
  0.6 1.3 copy.40
  2.8 1.0 copy.41
  3.9 8.6 %all-to-all-start.1 = ((bf16[8,2,128,224]{2,3,1,0:T(8,128)(2,1)}), bf16[8,2,128,224]{2,3,1,0:T(8,128)(2,1)S(1)}, u32[]{:S(2)}, u32[]{:S(2)}) async-start(bf16[8,2,128,224]{2,3,1,0:T(8,128)(2,1)} %copy.41), calls=%async_computation.1 | async-start | bytes 1835008 | tf_op jit(solution)/shard_map/all_to_all | solution.py:76
  14.9 23.5 %all-to-all-done.1 = bf16[8,2,128,224]{2,3,1,0:T(8,128)(2,1)S(1)} async-done(((bf16[8,2,128,224]{2,3,1,0:T(8,128)(2,1)}), bf16[8,2,128,224]{2,3,1,0:T(8,128)(2,1)S(1)}, u32[]{:S(2)}, u32[]{:S(2)}) %all-to-all-start.1) | async-done | bytes 917536 | tf_op jit(solution)/shard_map/all_to_all | solution.py:76
  38.4 3.6 %all-to-all-start = ((bf16[8,2,128,224]{2,3,1,0:T(8,128)(2,1)}), bf16[8,2,128,224]{2,3,1,0:T(8,128)(2,1)S(1)}, u32[]{:S(2)}, u32[]{:S(2)}) async-start(bf16[8,2,128,224]{2,3,1,0:T(8,128)(2,1)} %copy.37), calls=%async_computation | async-start | bytes 1835008 | tf_op jit(solution)/shard_map/all_to_all | solution.py:76
  43.9 1.7 %collective-permute-start.2 = (f32[2,112,114]{2,1,0:T(8,128)S(1)}, f32[2,112,114]{2,1,0:T(8,128)S(1)}, u32[]{:S(2)}, u32[]{:S(2)}) collective-permute-start(f32[2,112,114]{2,1,0:T(8,128)S(1)} %concatenate.27), channel_id=1, source_target_pairs={{0,24},{8,0},{16,8},{24,16},{32,56},{40,32},{48,40},{56,48},{64,88... | collective-permute-start | bytes 306440 | tf_op jit(solution)/shard_map/ppermute | solution.py:20
  46.2 2.4 %collective-permute-done = f32[2,112,114]{2,1,0:T(8,128)S(1)} collective-permute-done((f32[2,112,114]{2,1,0:T(8,128)S(1)}, f32[2,112,114]{2,1,0:T(8,128)S(1)}, u32[]{:S(2)}, u32[]{:S(2)}) %collective-permute-start) | collective-permute-done | bytes 102176 | tf_op jit(solution)/shard_map/ppermute | solution.py:20
  48.6 3.2 %collective-permute-done.1 = f32[2,112,114]{2,1,0:T(8,128)S(1)} collective-permute-done((f32[2,112,114]{2,1,0:T(8,128)S(1)}, f32[2,112,114]{2,1,0:T(8,128)S(1)}, u32[]{:S(2)}, u32[]{:S(2)}) %collective-permute-start.1) | collective-permute-done | bytes 102176 | tf_op jit(solution)/shard_map/ppermute | solution.py:20
  54.7 4.6 %collective-permute-start.9 = (f32[2,112,114]{2,1,0:T(8,128)}, f32[2,112,114]{2,1,0:T(8,128)}, u32[]{:S(2)}, u32[]{:S(2)}) collective-permute-start(f32[2,112,114]{2,1,0:T(8,128)} %get-tuple-element.55), channel_id=1, source_target_pairs={{0,224},{8,232},{16,240},{24,248},{32,0},{40,8},{48,16},{56,24},{6... | collective-permute-start | bytes 306440 | tf_op jit(solution)/shard_map/ppermute | solution.py:30
  59.3 9.0 %all-to-all-done = bf16[8,2,128,224]{2,3,1,0:T(8,128)(2,1)S(1)} async-done(((bf16[8,2,128,224]{2,3,1,0:T(8,128)(2,1)}), bf16[8,2,128,224]{2,3,1,0:T(8,128)(2,1)S(1)}, u32[]{:S(2)}, u32[]{:S(2)}) %all-to-all-start) | async-done | bytes 917536 | tf_op jit(solution)/shard_map/all_to_all | solution.py:76
  70.2 3.1 %collective-permute-start.8 = (f32[2,112,114]{2,1,0:T(8,128)}, f32[2,112,114]{2,1,0:T(8,128)S(1)}, u32[]{:S(2)}, u32[]{:S(2)}) collective-permute-start(f32[2,112,114]{2,1,0:T(8,128)} %get-tuple-element.51), channel_id=1, source_target_pairs={{0,192},{8,200},{16,208},{24,216},{32,224},{40,232},{48,240},{56,2... | collective-permute-start | bytes 306440 | tf_op jit(solution)/shard_map/ppermute | solution.py:30
  73.3 2.4 %collective-permute-start.7 = (f32[2,112,114]{2,1,0:T(8,128)S(1)}, f32[2,112,114]{2,1,0:T(8,128)S(1)}, u32[]{:S(2)}, u32[]{:S(2)}) collective-permute-start(f32[2,112,114]{2,1,0:T(8,128)S(1)} %copy-done.12), channel_id=1, source_target_pairs={{0,160},{8,168},{16,176},{24,184},{32,192},{40,200},{48,208},{56,2... | collective-permute-start | bytes 306440 | tf_op jit(solution)/shard_map/ppermute | solution.py:30
  75.7 2.7 %collective-permute-start.6 = (f32[2,112,114]{2,1,0:T(8,128)S(1)}, f32[2,112,114]{2,1,0:T(8,128)S(1)}, u32[]{:S(2)}, u32[]{:S(2)}) collective-permute-start(f32[2,112,114]{2,1,0:T(8,128)S(1)} %copy-done.11), channel_id=1, source_target_pairs={{0,128},{8,136},{16,144},{24,152},{32,160},{40,168},{48,176},{56,1... | collective-permute-start | bytes 306440 | tf_op jit(solution)/shard_map/ppermute | solution.py:30
  78.4 1.5 %collective-permute-start.4 = (f32[2,112,114]{2,1,0:T(8,128)S(1)}, f32[2,112,114]{2,1,0:T(8,128)S(1)}, u32[]{:S(2)}, u32[]{:S(2)}) collective-permute-start(f32[2,112,114]{2,1,0:T(8,128)S(1)} %copy-done.9), channel_id=1, source_target_pairs={{0,64},{8,72},{16,80},{24,88},{32,96},{40,104},{48,112},{56,120},{... | collective-permute-start | bytes 306440 | tf_op jit(solution)/shard_map/ppermute | solution.py:30
  80.0 1.1 fusion.49
  81.1 3.3 %collective-permute-start.3 = (f32[2,112,114]{2,1,0:T(8,128)S(1)}, f32[2,112,114]{2,1,0:T(8,128)S(1)}, u32[]{:S(2)}, u32[]{:S(2)}) collective-permute-start(f32[2,112,114]{2,1,0:T(8,128)S(1)} %copy-done.8), channel_id=1, source_target_pairs={{0,32},{8,40},{16,48},{24,56},{32,64},{40,72},{48,80},{56,88},{64,... | collective-permute-start | bytes 306440 | tf_op jit(solution)/shard_map/ppermute | solution.py:30
  84.9 2.5 %collective-permute-done.5 = f32[2,112,114]{2,1,0:T(8,128)S(1)} collective-permute-done((f32[2,112,114]{2,1,0:T(8,128)S(1)}, f32[2,112,114]{2,1,0:T(8,128)S(1)}, u32[]{:S(2)}, u32[]{:S(2)}) %collective-permute-start.5) | collective-permute-done | bytes 102176 | tf_op jit(solution)/shard_map/ppermute | solution.py:30
  87.8 2.0 %collective-permute-done.3 = f32[2,112,114]{2,1,0:T(8,128)S(1)} collective-permute-done((f32[2,112,114]{2,1,0:T(8,128)S(1)}, f32[2,112,114]{2,1,0:T(8,128)S(1)}, u32[]{:S(2)}, u32[]{:S(2)}) %collective-permute-start.3) | collective-permute-done | bytes 102176 | tf_op jit(solution)/shard_map/ppermute | solution.py:30
  90.6 1.3 fusion.21
  93.0 1.7 %collective-permute-start.12 = (f32[2,112,114]{2,1,0:T(8,128)S(1)}, f32[2,112,114]{2,1,0:T(8,128)S(1)}, u32[]{:S(2)}, u32[]{:S(2)}) collective-permute-start(f32[2,112,114]{2,1,0:T(8,128)S(1)} %concatenate.31), channel_id=1, source_target_pairs={{0,24},{8,0},{16,8},{24,16},{32,56},{40,32},{48,40},{56,48},{64,88... | collective-permute-start | bytes 306440 | tf_op jit(solution)/shard_map/ppermute | solution.py:20
  95.5 2.0 %collective-permute-done.10 = f32[2,112,114]{2,1,0:T(8,128)S(1)} collective-permute-done((f32[2,112,114]{2,1,0:T(8,128)S(1)}, f32[2,112,114]{2,1,0:T(8,128)S(1)}, u32[]{:S(2)}, u32[]{:S(2)}) %collective-permute-start.10) | collective-permute-done | bytes 102176 | tf_op jit(solution)/shard_map/ppermute | solution.py:20
  97.9 3.0 %collective-permute-done.11 = f32[2,112,114]{2,1,0:T(8,128)S(1)} collective-permute-done((f32[2,112,114]{2,1,0:T(8,128)S(1)}, f32[2,112,114]{2,1,0:T(8,128)S(1)}, u32[]{:S(2)}, u32[]{:S(2)}) %collective-permute-start.11) | collective-permute-done | bytes 102176 | tf_op jit(solution)/shard_map/ppermute | solution.py:20
  101.7 2.9 %collective-permute-start.19 = (f32[2,112,114]{2,1,0:T(8,128)S(1)}, f32[2,112,114]{2,1,0:T(8,128)S(1)}, u32[]{:S(2)}, u32[]{:S(2)}) collective-permute-start(f32[2,112,114]{2,1,0:T(8,128)S(1)} %get-tuple-element.49), channel_id=1, source_target_pairs={{0,224},{8,232},{16,240},{24,248},{32,0},{40,8},{48,16},{56,24},{6... | collective-permute-start | bytes 306440 | tf_op jit(solution)/shard_map/ppermute | solution.py:30
  105.8 3.5 %all-to-all-start.2 = ((bf16[8,1,128,224]{2,3,1,0:T(8,128)(2,1)}), bf16[8,1,128,224]{2,3,1,0:T(8,128)(2,1)S(1)}, u32[]{:S(2)}, u32[]{:S(2)}) async-start(bf16[8,1,128,224]{2,3,1,0:T(8,128)(2,1)} %copy.45), calls=%async_computation.2 | async-start | bytes 917504 | tf_op jit(solution)/shard_map/all_to_all | solution.py:83
  109.4 2.9 %collective-permute-start.17 = (f32[2,112,114]{2,1,0:T(8,128)S(1)}, f32[2,112,114]{2,1,0:T(8,128)S(1)}, u32[]{:S(2)}, u32[]{:S(2)}) collective-permute-start(f32[2,112,114]{2,1,0:T(8,128)S(1)} %get-tuple-element.46), channel_id=1, source_target_pairs={{0,160},{8,168},{16,176},{24,184},{32,192},{40,200},{48,208},{56,2... | collective-permute-start | bytes 306440 | tf_op jit(solution)/shard_map/ppermute | solution.py:30
  112.3 1.6 %collective-permute-start.16 = (f32[2,112,114]{2,1,0:T(8,128)S(1)}, f32[2,112,114]{2,1,0:T(8,128)S(1)}, u32[]{:S(2)}, u32[]{:S(2)}) collective-permute-start(f32[2,112,114]{2,1,0:T(8,128)S(1)} %get-tuple-element.47), channel_id=1, source_target_pairs={{0,128},{8,136},{16,144},{24,152},{32,160},{40,168},{48,176},{56,1... | collective-permute-start | bytes 306440 | tf_op jit(solution)/shard_map/ppermute | solution.py:30
  114.8 2.5 %collective-permute-start.14 = (f32[2,112,114]{2,1,0:T(8,128)S(1)}, f32[2,112,114]{2,1,0:T(8,128)S(1)}, u32[]{:S(2)}, u32[]{:S(2)}) collective-permute-start(f32[2,112,114]{2,1,0:T(8,128)S(1)} %get-tuple-element.44), channel_id=1, source_target_pairs={{0,64},{8,72},{16,80},{24,88},{32,96},{40,104},{48,112},{56,120},{... | collective-permute-start | bytes 306440 | tf_op jit(solution)/shard_map/ppermute | solution.py:30
  117.5 1.4 collective-permute-done.18
  120.2 3.8 %collective-permute-done.15 = f32[2,112,114]{2,1,0:T(8,128)S(1)} collective-permute-done((f32[2,112,114]{2,1,0:T(8,128)S(1)}, f32[2,112,114]{2,1,0:T(8,128)S(1)}, u32[]{:S(2)}, u32[]{:S(2)}) %collective-permute-start.15) | collective-permute-done | bytes 102176 | tf_op jit(solution)/shard_map/ppermute | solution.py:30
  124.9 2.4 %collective-permute-done.13 = f32[2,112,114]{2,1,0:T(8,128)S(1)} collective-permute-done((f32[2,112,114]{2,1,0:T(8,128)S(1)}, f32[2,112,114]{2,1,0:T(8,128)S(1)}, u32[]{:S(2)}, u32[]{:S(2)}) %collective-permute-start.13) | collective-permute-done | bytes 102176 | tf_op jit(solution)/shard_map/ppermute | solution.py:30
  128.9 7.1 %all-to-all-start.3 = ((bf16[8,2,112,113]{3,2,1,0:T(8,128)(2,1)}), bf16[8,2,112,113]{3,2,1,0:T(8,128)(2,1)S(1)}, u32[]{:S(2)}, u32[]{:S(2)}) async-start(bf16[8,2,112,113]{3,2,1,0:T(8,128)(2,1)} %broadcast_in_dim.326), calls=%async_computation.3 | async-start | bytes 917504 | tf_op jit(solution)/shard_map/all_to_all | solution.py:119
  137.1 11.4 %all-to-all-done.3 = bf16[8,2,112,113]{3,2,1,0:T(8,128)(2,1)S(1)} async-done(((bf16[8,2,112,113]{3,2,1,0:T(8,128)(2,1)}), bf16[8,2,112,113]{3,2,1,0:T(8,128)(2,1)S(1)}, u32[]{:S(2)}, u32[]{:S(2)}) %all-to-all-start.3) | async-done | bytes 405024 | tf_op jit(solution)/shard_map/all_to_all | solution.py:119
  (116 shorter events, 25.6 us)
Async XLA Ops:
  3.9 8.6 %copy-start.6 = (bf16[128,1792]{1,0:T(8,128)(2,1)S(1)}, bf16[128,1792]{1,0:T(8,128)(2,1)}, u32[]{:S(2)}) copy-start(bf16[128,1792]{1,0:T(8,128)(2,1)} %param.8) | copy-start | bytes 1376260
  3.9 34.5 %all-to-all-start.1 = ((bf16[8,2,128,224]{2,3,1,0:T(8,128)(2,1)}), bf16[8,2,128,224]{2,3,1,0:T(8,128)(2,1)S(1)}, u32[]{:S(2)}, u32[]{:S(2)}) async-start(bf16[8,2,128,224]{2,3,1,0:T(8,128)(2,1)} %copy.41), calls=%async_computation.1 | async-start | bytes 1835008 | tf_op jit(solution)/shard_map/all_to_all | solution.py:76
  38.4 29.9 %all-to-all-start = ((bf16[8,2,128,224]{2,3,1,0:T(8,128)(2,1)}), bf16[8,2,128,224]{2,3,1,0:T(8,128)(2,1)S(1)}, u32[]{:S(2)}, u32[]{:S(2)}) async-start(bf16[8,2,128,224]{2,3,1,0:T(8,128)(2,1)} %copy.37), calls=%async_computation | async-start | bytes 1835008 | tf_op jit(solution)/shard_map/all_to_all | solution.py:76
  43.8 4.7 %collective-permute-start = (f32[2,112,114]{2,1,0:T(8,128)S(1)}, f32[2,112,114]{2,1,0:T(8,128)S(1)}, u32[]{:S(2)}, u32[]{:S(2)}) collective-permute-start(f32[2,112,114]{2,1,0:T(8,128)S(1)} %concatenate.27), channel_id=1, source_target_pairs={{0,8},{8,16},{16,24},{24,0},{32,40},{40,48},{48,56},{56,32},{64,72... | collective-permute-start | bytes 306440 | tf_op jit(solution)/shard_map/ppermute | solution.py:20
  43.9 4.7 %collective-permute-start.2 = (f32[2,112,114]{2,1,0:T(8,128)S(1)}, f32[2,112,114]{2,1,0:T(8,128)S(1)}, u32[]{:S(2)}, u32[]{:S(2)}) collective-permute-start(f32[2,112,114]{2,1,0:T(8,128)S(1)} %concatenate.27), channel_id=1, source_target_pairs={{0,24},{8,0},{16,8},{24,16},{32,56},{40,32},{48,40},{56,48},{64,88... | collective-permute-start | bytes 306440 | tf_op jit(solution)/shard_map/ppermute | solution.py:20
  45.6 6.2 %collective-permute-start.1 = (f32[2,112,114]{2,1,0:T(8,128)S(1)}, f32[2,112,114]{2,1,0:T(8,128)S(1)}, u32[]{:S(2)}, u32[]{:S(2)}) collective-permute-start(f32[2,112,114]{2,1,0:T(8,128)S(1)} %concatenate.27), channel_id=1, source_target_pairs={{0,16},{8,24},{16,0},{24,8},{32,48},{40,56},{48,32},{56,40},{64,80... | collective-permute-start | bytes 306440 | tf_op jit(solution)/shard_map/ppermute | solution.py:20
  54.7 23.7 %collective-permute-start.9 = (f32[2,112,114]{2,1,0:T(8,128)}, f32[2,112,114]{2,1,0:T(8,128)}, u32[]{:S(2)}, u32[]{:S(2)}) collective-permute-start(f32[2,112,114]{2,1,0:T(8,128)} %get-tuple-element.55), channel_id=1, source_target_pairs={{0,224},{8,232},{16,240},{24,248},{32,0},{40,8},{48,16},{56,24},{6... | collective-permute-start | bytes 306440 | tf_op jit(solution)/shard_map/ppermute | solution.py:30
  70.0 3.3 %copy-start.12 = (f32[2,112,114]{2,1,0:T(8,128)S(1)}, f32[2,112,114]{2,1,0:T(8,128)}, u32[]{:S(2)}) copy-start(f32[2,112,114]{2,1,0:T(8,128)} %get-tuple-element.52) | copy-start | bytes 306436
  70.0 5.6 %copy-start.11 = (f32[2,112,114]{2,1,0:T(8,128)S(1)}, f32[2,112,114]{2,1,0:T(8,128)}, u32[]{:S(2)}) copy-start(f32[2,112,114]{2,1,0:T(8,128)} %get-tuple-element.53) | copy-start | bytes 306436
  70.0 8.4 %copy-start.10 = (f32[2,112,114]{2,1,0:T(8,128)S(1)}, f32[2,112,114]{2,1,0:T(8,128)}, u32[]{:S(2)}) copy-start(f32[2,112,114]{2,1,0:T(8,128)} %get-tuple-element.54) | copy-start | bytes 306436
  70.1 8.4 %copy-start.9 = (f32[2,112,114]{2,1,0:T(8,128)S(1)}, f32[2,112,114]{2,1,0:T(8,128)}, u32[]{:S(2)}) copy-start(f32[2,112,114]{2,1,0:T(8,128)} %get-tuple-element.50) | copy-start | bytes 306436
  70.2 10.8 %copy-start.8 = (f32[2,112,114]{2,1,0:T(8,128)S(1)}, f32[2,112,114]{2,1,0:T(8,128)}, u32[]{:S(2)}) copy-start(f32[2,112,114]{2,1,0:T(8,128)} %get-tuple-element.30) | copy-start | bytes 306436
  70.2 10.8 %collective-permute-start.8 = (f32[2,112,114]{2,1,0:T(8,128)}, f32[2,112,114]{2,1,0:T(8,128)S(1)}, u32[]{:S(2)}, u32[]{:S(2)}) collective-permute-start(f32[2,112,114]{2,1,0:T(8,128)} %get-tuple-element.51), channel_id=1, source_target_pairs={{0,192},{8,200},{16,208},{24,216},{32,224},{40,232},{48,240},{56,2... | collective-permute-start | bytes 306440 | tf_op jit(solution)/shard_map/ppermute | solution.py:30
  73.3 11.2 %collective-permute-start.7 = (f32[2,112,114]{2,1,0:T(8,128)S(1)}, f32[2,112,114]{2,1,0:T(8,128)S(1)}, u32[]{:S(2)}, u32[]{:S(2)}) collective-permute-start(f32[2,112,114]{2,1,0:T(8,128)S(1)} %copy-done.12), channel_id=1, source_target_pairs={{0,160},{8,168},{16,176},{24,184},{32,192},{40,200},{48,208},{56,2... | collective-permute-start | bytes 306440 | tf_op jit(solution)/shard_map/ppermute | solution.py:30
  75.7 9.1 %collective-permute-start.6 = (f32[2,112,114]{2,1,0:T(8,128)S(1)}, f32[2,112,114]{2,1,0:T(8,128)S(1)}, u32[]{:S(2)}, u32[]{:S(2)}) collective-permute-start(f32[2,112,114]{2,1,0:T(8,128)S(1)} %copy-done.11), channel_id=1, source_target_pairs={{0,128},{8,136},{16,144},{24,152},{32,160},{40,168},{48,176},{56,1... | collective-permute-start | bytes 306440 | tf_op jit(solution)/shard_map/ppermute | solution.py:30
  78.4 9.0 %collective-permute-start.5 = (f32[2,112,114]{2,1,0:T(8,128)S(1)}, f32[2,112,114]{2,1,0:T(8,128)S(1)}, u32[]{:S(2)}, u32[]{:S(2)}) collective-permute-start(f32[2,112,114]{2,1,0:T(8,128)S(1)} %copy-done.10), channel_id=1, source_target_pairs={{0,96},{8,104},{16,112},{24,120},{32,128},{40,136},{48,144},{56,15... | collective-permute-start | bytes 306440 | tf_op jit(solution)/shard_map/ppermute | solution.py:30
  78.4 9.2 %collective-permute-start.4 = (f32[2,112,114]{2,1,0:T(8,128)S(1)}, f32[2,112,114]{2,1,0:T(8,128)S(1)}, u32[]{:S(2)}, u32[]{:S(2)}) collective-permute-start(f32[2,112,114]{2,1,0:T(8,128)S(1)} %copy-done.9), channel_id=1, source_target_pairs={{0,64},{8,72},{16,80},{24,88},{32,96},{40,104},{48,112},{56,120},{... | collective-permute-start | bytes 306440 | tf_op jit(solution)/shard_map/ppermute | solution.py:30
  81.1 8.7 %collective-permute-start.3 = (f32[2,112,114]{2,1,0:T(8,128)S(1)}, f32[2,112,114]{2,1,0:T(8,128)S(1)}, u32[]{:S(2)}, u32[]{:S(2)}) collective-permute-start(f32[2,112,114]{2,1,0:T(8,128)S(1)} %copy-done.8), channel_id=1, source_target_pairs={{0,32},{8,40},{16,48},{24,56},{32,64},{40,72},{48,80},{56,88},{64,... | collective-permute-start | bytes 306440 | tf_op jit(solution)/shard_map/ppermute | solution.py:30
  87.6 2.4 %copy-start.4 = (f32[2,112,114]{2,1,0:T(8,128)S(1)}, f32[2,112,114]{2,1,0:T(8,128)}, u32[]{:S(2)}) copy-start(f32[2,112,114]{2,1,0:T(8,128)} %copy-done.3) | copy-start | bytes 306436
  92.9 4.5 %collective-permute-start.10 = (f32[2,112,114]{2,1,0:T(8,128)S(1)}, f32[2,112,114]{2,1,0:T(8,128)S(1)}, u32[]{:S(2)}, u32[]{:S(2)}) collective-permute-start(f32[2,112,114]{2,1,0:T(8,128)S(1)} %concatenate.31), channel_id=1, source_target_pairs={{0,8},{8,16},{16,24},{24,0},{32,40},{40,48},{48,56},{56,32},{64,72... | collective-permute-start | bytes 306440 | tf_op jit(solution)/shard_map/ppermute | solution.py:20
  93.0 4.9 %collective-permute-start.12 = (f32[2,112,114]{2,1,0:T(8,128)S(1)}, f32[2,112,114]{2,1,0:T(8,128)S(1)}, u32[]{:S(2)}, u32[]{:S(2)}) collective-permute-start(f32[2,112,114]{2,1,0:T(8,128)S(1)} %concatenate.31), channel_id=1, source_target_pairs={{0,24},{8,0},{16,8},{24,16},{32,56},{40,32},{48,40},{56,48},{64,88... | collective-permute-start | bytes 306440 | tf_op jit(solution)/shard_map/ppermute | solution.py:20
  94.8 6.2 %collective-permute-start.11 = (f32[2,112,114]{2,1,0:T(8,128)S(1)}, f32[2,112,114]{2,1,0:T(8,128)S(1)}, u32[]{:S(2)}, u32[]{:S(2)}) collective-permute-start(f32[2,112,114]{2,1,0:T(8,128)S(1)} %concatenate.31), channel_id=1, source_target_pairs={{0,16},{8,24},{16,0},{24,8},{32,48},{40,56},{48,32},{56,40},{64,80... | collective-permute-start | bytes 306440 | tf_op jit(solution)/shard_map/ppermute | solution.py:20
  101.7 13.1 %collective-permute-start.19 = (f32[2,112,114]{2,1,0:T(8,128)S(1)}, f32[2,112,114]{2,1,0:T(8,128)S(1)}, u32[]{:S(2)}, u32[]{:S(2)}) collective-permute-start(f32[2,112,114]{2,1,0:T(8,128)S(1)} %get-tuple-element.49), channel_id=1, source_target_pairs={{0,224},{8,232},{16,240},{24,248},{32,0},{40,8},{48,16},{56,24},{6... | collective-permute-start | bytes 306440 | tf_op jit(solution)/shard_map/ppermute | solution.py:30
  105.8 22.2 %all-to-all-start.2 = ((bf16[8,1,128,224]{2,3,1,0:T(8,128)(2,1)}), bf16[8,1,128,224]{2,3,1,0:T(8,128)(2,1)S(1)}, u32[]{:S(2)}, u32[]{:S(2)}) async-start(bf16[8,1,128,224]{2,3,1,0:T(8,128)(2,1)} %copy.45), calls=%async_computation.2 | async-start | bytes 917504 | tf_op jit(solution)/shard_map/all_to_all | solution.py:83
  109.3 9.6 %collective-permute-start.18 = (f32[2,112,114]{2,1,0:T(8,128)S(1)}, f32[2,112,114]{2,1,0:T(8,128)S(1)}, u32[]{:S(2)}, u32[]{:S(2)}) collective-permute-start(f32[2,112,114]{2,1,0:T(8,128)S(1)} %get-tuple-element.45), channel_id=1, source_target_pairs={{0,192},{8,200},{16,208},{24,216},{32,224},{40,232},{48,240},{56,2... | collective-permute-start | bytes 306440 | tf_op jit(solution)/shard_map/ppermute | solution.py:30
  109.4 9.8 %collective-permute-start.17 = (f32[2,112,114]{2,1,0:T(8,128)S(1)}, f32[2,112,114]{2,1,0:T(8,128)S(1)}, u32[]{:S(2)}, u32[]{:S(2)}) collective-permute-start(f32[2,112,114]{2,1,0:T(8,128)S(1)} %get-tuple-element.46), channel_id=1, source_target_pairs={{0,160},{8,168},{16,176},{24,184},{32,192},{40,200},{48,208},{56,2... | collective-permute-start | bytes 306440 | tf_op jit(solution)/shard_map/ppermute | solution.py:30
  112.3 7.7 %collective-permute-start.16 = (f32[2,112,114]{2,1,0:T(8,128)S(1)}, f32[2,112,114]{2,1,0:T(8,128)S(1)}, u32[]{:S(2)}, u32[]{:S(2)}) collective-permute-start(f32[2,112,114]{2,1,0:T(8,128)S(1)} %get-tuple-element.47), channel_id=1, source_target_pairs={{0,128},{8,136},{16,144},{24,152},{32,160},{40,168},{48,176},{56,1... | collective-permute-start | bytes 306440 | tf_op jit(solution)/shard_map/ppermute | solution.py:30
  113.9 10.0 %collective-permute-start.15 = (f32[2,112,114]{2,1,0:T(8,128)S(1)}, f32[2,112,114]{2,1,0:T(8,128)S(1)}, u32[]{:S(2)}, u32[]{:S(2)}) collective-permute-start(f32[2,112,114]{2,1,0:T(8,128)S(1)} %get-tuple-element.48), channel_id=1, source_target_pairs={{0,96},{8,104},{16,112},{24,120},{32,128},{40,136},{48,144},{56,15... | collective-permute-start | bytes 306440 | tf_op jit(solution)/shard_map/ppermute | solution.py:30
  114.8 9.9 %collective-permute-start.14 = (f32[2,112,114]{2,1,0:T(8,128)S(1)}, f32[2,112,114]{2,1,0:T(8,128)S(1)}, u32[]{:S(2)}, u32[]{:S(2)}) collective-permute-start(f32[2,112,114]{2,1,0:T(8,128)S(1)} %get-tuple-element.44), channel_id=1, source_target_pairs={{0,64},{8,72},{16,80},{24,88},{32,96},{40,104},{48,112},{56,120},{... | collective-permute-start | bytes 306440 | tf_op jit(solution)/shard_map/ppermute | solution.py:30
  118.9 8.4 %collective-permute-start.13 = (f32[2,112,114]{2,1,0:T(8,128)S(1)}, f32[2,112,114]{2,1,0:T(8,128)S(1)}, u32[]{:S(2)}, u32[]{:S(2)}) collective-permute-start(f32[2,112,114]{2,1,0:T(8,128)S(1)} %get-tuple-element.26), channel_id=1, source_target_pairs={{0,32},{8,40},{16,48},{24,56},{32,64},{40,72},{48,80},{56,88},{64,... | collective-permute-start | bytes 306440 | tf_op jit(solution)/shard_map/ppermute | solution.py:30
  128.9 19.7 %all-to-all-start.3 = ((bf16[8,2,112,113]{3,2,1,0:T(8,128)(2,1)}), bf16[8,2,112,113]{3,2,1,0:T(8,128)(2,1)S(1)}, u32[]{:S(2)}, u32[]{:S(2)}) async-start(bf16[8,2,112,113]{3,2,1,0:T(8,128)(2,1)} %broadcast_in_dim.326), calls=%async_computation.3 | async-start | bytes 917504 | tf_op jit(solution)/shard_map/all_to_all | solution.py:119
  137.1 11.8 %copy-start.1 = (bf16[128,1792]{0,1:T(8,128)(2,1)S(1)}, bf16[128,1792]{0,1:T(8,128)(2,1)}, u32[]{:S(2)}) copy-start(bf16[128,1792]{0,1:T(8,128)(2,1)} %copy-done) | copy-start | bytes 1376260
  (9 other events, 8.2 us)

commit v18 on v16

--- a/solution.py
+++ b/solution.py
@@ -8,7 +8,7 @@
 loss_scale = 1024.0
 
 
-ROW = 4
+ROW = 2
 
 
 def shifted(value, count, step):

time: 120 us -> 173 us (1.44); the launches traced: 119 us -> 170 us
  starting transfers between devices: 58.5 us -> 94.5 us
  other arithmetic: 6.3 us -> 11.5 us
  waiting for transfers between devices: 39.2 us -> 44.4 us
  local copies, waits for them, and re-layouts: 10.7 us -> 14.7 us
    ppermute x14 -> x30, starting transfers between devices: 33 us -> 68.7 us  [strided(): return lax.ppermute(value, 'tm', pairs)]
    ppermute x14 -> x30, waiting for transfers between devices: 4.29 us -> 13.1 us  [strided(): return lax.ppermute(value, 'tm', pairs)]
    all_to_all x1, waiting for transfers between devices: 3.89 us -> 0.01 us  [to_heads(): incoming = lax.all_to_all(outgoing, 'inner', 0, 0, tiled=True)]
    ppermute x6 -> x2, starting transfers between devices: 3.43 us -> 0.19 us  [shifted(): return lax.ppermute(value, 'tm', pairs)]
    all_to_all x1, starting transfers between devices: 3.47 us -> 6.58 us  [to_rows(): returned = lax.all_to_all(leaving, 'inner', 0, 0, tiled=True)]
    or x14 -> x30, other arithmetic: 2.58 us -> 5.5 us  [visible(): take = is_whole | (got[..., DH + 1:] == flabel)]
    convert_element_type x2, local copies, waits for them, and re-layouts: 0.68 us -> 2.78 us  [local(): scaled = scaled_heads.astype(jnp.float32)]
    select_n x4, other arithmetic: 0.3 us -> 2.19 us  [visible(): got = strided(jnp.where(sends_whole, whole, edge_sum), row, s)]
  transfers between devices with their start and end apart: 24 -> 36, of which waited for: 7 -> 7; matrix products, arithmetic and copies ran while one was open for 8% -> 6% of each run, Pallas kernels for 0% -> 0%
where the time goes in v18:
time: 173 us; the launch traced here: 170 us
  starting transfers between devices  94.5 us (55%)
  waiting for transfers between devices  44.4 us (26%)
  local copies, waits for them, and re-layouts  14.7 us (8%)
  other arithmetic  11.5 us (7%)
  matrix products  2.8 us (2%)
  between operations  2.13 us (1%)
    ppermute x30, starting transfers between devices, strided(): return lax.ppermute(value, 'tm', pairs)  68.7 us
    all_to_all x1, waiting for transfers between devices, local(): lax.all_to_all(copies, 'inner', 0, 0, tiled=True)  15.2 us
    all_to_all x1, waiting for transfers between devices, local(): lax.all_to_all(pieces, 'inner', 0, 0, tiled=True).astype(jnp.float32)  14.1 us
    ppermute x30, waiting for transfers between devices, strided(): return lax.ppermute(value, 'tm', pairs)  13.1 us
    unnamed x45, local copies, waits for them, and re-layouts  8.85 us
    all_to_all x1, starting transfers between devices, local(): lax.all_to_all(pieces, 'inner', 0, 0, tiled=True).astype(jnp.float32)  8.6 us
    all_to_all x1, starting transfers between devices, local(): lax.all_to_all(copies, 'inner', 0, 0, tiled=True)  6.88 us
    all_to_all x1, starting transfers between devices, to_rows(): returned = lax.all_to_all(leaving, 'inner', 0, 0, tiled=True)  6.58 us
  transfers between devices with their start and end apart: 36, of which 7 were waited for; matrix products, arithmetic and copies ran while one was open for 6% of the time, Pallas kernels for 0%

profile of v18, /device:TPU:2, one launch (start us, length us, event | category | flops | bytes accessed | tf_op | source)
XLA Modules:
  0.0 170.0 jit_solution(16916180676865890032)
XLA Ops:
  0.6 1.3 copy.34
  4.4 8.6 %all-to-all-start.1 = ((bf16[8,2,112,113]{3,2,1,0:T(8,128)(2,1)}), bf16[8,2,112,113]{3,2,1,0:T(8,128)(2,1)S(1)}, u32[]{:S(2)}, u32[]{:S(2)}) async-start(bf16[8,2,112,113]{3,2,1,0:T(8,128)(2,1)} %bitcast.7), calls=%async_computation.1 | async-start | bytes 917504 | tf_op jit(solution)/shard_map/all_to_all | solution.py:100
  15.0 14.1 %all-to-all-done.1 = bf16[8,2,112,113]{3,2,1,0:T(8,128)(2,1)S(1)} async-done(((bf16[8,2,112,113]{3,2,1,0:T(8,128)(2,1)}), bf16[8,2,112,113]{3,2,1,0:T(8,128)(2,1)S(1)}, u32[]{:S(2)}, u32[]{:S(2)}) %all-to-all-start.1) | async-done | bytes 405024 | tf_op jit(solution)/shard_map/all_to_all | solution.py:100
  34.1 3.6 %all-to-all-start = ((bf16[8,2,128,224]{2,3,1,0:T(8,128)(2,1)}), bf16[8,2,128,224]{2,3,1,0:T(8,128)(2,1)S(1)}, u32[]{:S(2)}, u32[]{:S(2)}) async-start(bf16[8,2,128,224]{2,3,1,0:T(8,128)(2,1)} %copy.32), calls=%async_computation | async-start | bytes 1835008 | tf_op jit(solution)/shard_map/all_to_all | solution.py:76
  38.0 4.9 %collective-permute-start.14 = (f32[2,112,114]{2,1,0:T(8,128)S(1)}, f32[2,112,114]{2,1,0:T(8,128)S(1)}, u32[]{:S(2)}, u32[]{:S(2)}) collective-permute-start(f32[2,112,114]{2,1,0:T(8,128)S(1)} %get-tuple-element.47), channel_id=1, source_target_pairs={{0,224},{8,232},{16,240},{24,248},{32,0},{40,8},{48,16},{56,24},{6... | collective-permute-start | bytes 306440 | tf_op jit(solution)/shard_map/ppermute | solution.py:30
  43.0 2.0 %collective-permute-start.13 = (f32[2,112,114]{2,1,0:T(8,128)}, f32[2,112,114]{2,1,0:T(8,128)S(1)}, u32[]{:S(2)}, u32[]{:S(2)}) collective-permute-start(f32[2,112,114]{2,1,0:T(8,128)} %get-tuple-element.48), channel_id=1, source_target_pairs={{0,208},{8,216},{16,224},{24,232},{32,240},{40,248},{48,0},{56,8},... | collective-permute-start | bytes 306440 | tf_op jit(solution)/shard_map/ppermute | solution.py:30
  45.5 3.7 %collective-permute-start.10 = (f32[2,112,114]{2,1,0:T(8,128)}, f32[2,112,114]{2,1,0:T(8,128)S(1)}, u32[]{:S(2)}, u32[]{:S(2)}) collective-permute-start(f32[2,112,114]{2,1,0:T(8,128)} %get-tuple-element.51), channel_id=1, source_target_pairs={{0,160},{8,168},{16,176},{24,184},{32,192},{40,200},{48,208},{56,2... | collective-permute-start | bytes 306440 | tf_op jit(solution)/shard_map/ppermute | solution.py:30
  49.4 2.9 %collective-permute-start.9 = (f32[2,112,114]{2,1,0:T(8,128)}, f32[2,112,114]{2,1,0:T(8,128)S(1)}, u32[]{:S(2)}, u32[]{:S(2)}) collective-permute-start(f32[2,112,114]{2,1,0:T(8,128)} %get-tuple-element.52), channel_id=1, source_target_pairs={{0,144},{8,152},{16,160},{24,168},{32,176},{40,184},{48,192},{56,2... | collective-permute-start | bytes 306440 | tf_op jit(solution)/shard_map/ppermute | solution.py:30
  52.5 3.4 %collective-permute-start.8 = (f32[2,112,114]{2,1,0:T(8,128)S(1)}, f32[2,112,114]{2,1,0:T(8,128)S(1)}, u32[]{:S(2)}, u32[]{:S(2)}) collective-permute-start(f32[2,112,114]{2,1,0:T(8,128)S(1)} %copy-done.6), channel_id=1, source_target_pairs={{0,128},{8,136},{16,144},{24,152},{32,160},{40,168},{48,176},{56,1... | collective-permute-start | bytes 306440 | tf_op jit(solution)/shard_map/ppermute | solution.py:30
  56.1 2.6 %collective-permute-done.12 = f32[2,112,114]{2,1,0:T(8,128)S(1)} collective-permute-done((f32[2,112,114]{2,1,0:T(8,128)}, f32[2,112,114]{2,1,0:T(8,128)S(1)}, u32[]{:S(2)}, u32[]{:S(2)}) %collective-permute-start.12) | collective-permute-done | bytes 102176 | tf_op jit(solution)/shard_map/ppermute | solution.py:30
  59.0 8.4 %collective-permute-start.6 = (f32[2,112,114]{2,1,0:T(8,128)S(1)}, f32[2,112,114]{2,1,0:T(8,128)S(1)}, u32[]{:S(2)}, u32[]{:S(2)}) collective-permute-start(f32[2,112,114]{2,1,0:T(8,128)S(1)} %get-tuple-element.55), channel_id=1, source_target_pairs={{0,96},{8,104},{16,112},{24,120},{32,128},{40,136},{48,144},{56,15... | collective-permute-start | bytes 306440 | tf_op jit(solution)/shard_map/ppermute | solution.py:30
  67.6 1.3 collective-permute-start.5
  70.1 6.2 %collective-permute-start.2 = (f32[2,112,114]{2,1,0:T(8,128)S(1)}, f32[2,112,114]{2,1,0:T(8,128)S(1)}, u32[]{:S(2)}, u32[]{:S(2)}) collective-permute-start(f32[2,112,114]{2,1,0:T(8,128)S(1)} %get-tuple-element.46), channel_id=1, source_target_pairs={{0,32},{8,40},{16,48},{24,56},{32,64},{40,72},{48,80},{56,88},{64,... | collective-permute-start | bytes 306440 | tf_op jit(solution)/shard_map/ppermute | solution.py:30
  76.9 5.0 %collective-permute-done.4 = f32[2,112,114]{2,1,0:T(8,128)S(1)} collective-permute-done((f32[2,112,114]{2,1,0:T(8,128)S(1)}, f32[2,112,114]{2,1,0:T(8,128)S(1)}, u32[]{:S(2)}, u32[]{:S(2)}) %collective-permute-start.4) | collective-permute-done | bytes 102176 | tf_op jit(solution)/shard_map/ppermute | solution.py:30
  84.5 1.5 copy.36
  86.0 1.3 reshape.61
  91.2 1.7 collective-permute-start.31
  94.1 6.6 %all-to-all-start.2 = ((bf16[8,1,128,224]{2,3,1,0:T(8,128)(2,1)}), bf16[8,1,128,224]{2,3,1,0:T(8,128)(2,1)S(1)}, u32[]{:S(2)}, u32[]{:S(2)}) async-start(bf16[8,1,128,224]{2,3,1,0:T(8,128)(2,1)} %copy.37), calls=%async_computation.2 | async-start | bytes 917504 | tf_op jit(solution)/shard_map/all_to_all | solution.py:83
  101.3 2.0 %collective-permute-start.29 = (f32[2,112,114]{2,1,0:T(8,128)S(1)}, f32[2,112,114]{2,1,0:T(8,128)S(1)}, u32[]{:S(2)}, u32[]{:S(2)}) collective-permute-start(f32[2,112,114]{2,1,0:T(8,128)S(1)} %copy-done.14), channel_id=1, source_target_pairs={{0,208},{8,216},{16,224},{24,232},{32,240},{40,248},{48,0},{56,8},... | collective-permute-start | bytes 306440 | tf_op jit(solution)/shard_map/ppermute | solution.py:30
  103.3 3.2 %collective-permute-start.28 = (f32[2,112,114]{2,1,0:T(8,128)S(1)}, f32[2,112,114]{2,1,0:T(8,128)S(1)}, u32[]{:S(2)}, u32[]{:S(2)}) collective-permute-start(f32[2,112,114]{2,1,0:T(8,128)S(1)} %copy-done.13), channel_id=1, source_target_pairs={{0,192},{8,200},{16,208},{24,216},{32,224},{40,232},{48,240},{56,2... | collective-permute-start | bytes 306440 | tf_op jit(solution)/shard_map/ppermute | solution.py:30
  107.3 3.0 %collective-permute-start.26 = (f32[2,112,114]{2,1,0:T(8,128)S(1)}, f32[2,112,114]{2,1,0:T(8,128)S(1)}, u32[]{:S(2)}, u32[]{:S(2)}) collective-permute-start(f32[2,112,114]{2,1,0:T(8,128)S(1)} %copy-done.11), channel_id=1, source_target_pairs={{0,160},{8,168},{16,176},{24,184},{32,192},{40,200},{48,208},{56,2... | collective-permute-start | bytes 306440 | tf_op jit(solution)/shard_map/ppermute | solution.py:30
  110.5 3.1 %collective-permute-start.25 = (f32[2,112,114]{2,1,0:T(8,128)S(1)}, f32[2,112,114]{2,1,0:T(8,128)S(1)}, u32[]{:S(2)}, u32[]{:S(2)}) collective-permute-start(f32[2,112,114]{2,1,0:T(8,128)S(1)} %copy-done.10), channel_id=1, source_target_pairs={{0,144},{8,152},{16,160},{24,168},{32,176},{40,184},{48,192},{56,2... | collective-permute-start | bytes 306440 | tf_op jit(solution)/shard_map/ppermute | solution.py:30
  113.9 2.2 %collective-permute-start.24 = (f32[2,112,114]{2,1,0:T(8,128)S(1)}, f32[2,112,114]{2,1,0:T(8,128)S(1)}, u32[]{:S(2)}, u32[]{:S(2)}) collective-permute-start(f32[2,112,114]{2,1,0:T(8,128)S(1)} %copy-done.9), channel_id=1, source_target_pairs={{0,128},{8,136},{16,144},{24,152},{32,160},{40,168},{48,176},{56,1... | collective-permute-start | bytes 306440 | tf_op jit(solution)/shard_map/ppermute | solution.py:30
  116.3 3.1 %collective-permute-start.23 = (f32[2,112,114]{2,1,0:T(8,128)S(1)}, f32[2,112,114]{2,1,0:T(8,128)S(1)}, u32[]{:S(2)}, u32[]{:S(2)}) collective-permute-start(f32[2,112,114]{2,1,0:T(8,128)S(1)} %copy-done.8), channel_id=1, source_target_pairs={{0,112},{8,120},{16,128},{24,136},{32,144},{40,152},{48,160},{56,1... | collective-permute-start | bytes 306440 | tf_op jit(solution)/shard_map/ppermute | solution.py:30
  119.5 5.8 %collective-permute-start.22 = (f32[2,112,114]{2,1,0:T(8,128)S(1)}, f32[2,112,114]{2,1,0:T(8,128)S(1)}, u32[]{:S(2)}, u32[]{:S(2)}) collective-permute-start(f32[2,112,114]{2,1,0:T(8,128)S(1)} %copy-done.7), channel_id=1, source_target_pairs={{0,96},{8,104},{16,112},{24,120},{32,128},{40,136},{48,144},{56,15... | collective-permute-start | bytes 306440 | tf_op jit(solution)/shard_map/ppermute | solution.py:30
  125.5 2.0 %collective-permute-start.21 = (f32[2,112,114]{2,1,0:T(8,128)S(1)}, f32[2,112,114]{2,1,0:T(8,128)S(1)}, u32[]{:S(2)}, u32[]{:S(2)}) collective-permute-start(f32[2,112,114]{2,1,0:T(8,128)S(1)} %get-tuple-element.40), channel_id=1, source_target_pairs={{0,80},{8,88},{16,96},{24,104},{32,112},{40,120},{48,128},{56,136}... | collective-permute-start | bytes 306440 | tf_op jit(solution)/shard_map/ppermute | solution.py:30
  127.7 3.1 %collective-permute-start.20 = (f32[2,112,114]{2,1,0:T(8,128)S(1)}, f32[2,112,114]{2,1,0:T(8,128)S(1)}, u32[]{:S(2)}, u32[]{:S(2)}) collective-permute-start(f32[2,112,114]{2,1,0:T(8,128)S(1)} %get-tuple-element.41), channel_id=1, source_target_pairs={{0,64},{8,72},{16,80},{24,88},{32,96},{40,104},{48,112},{56,120},{... | collective-permute-start | bytes 306440 | tf_op jit(solution)/shard_map/ppermute | solution.py:30
  131.3 1.9 %collective-permute-start.18 = (f32[2,112,114]{2,1,0:T(8,128)S(1)}, f32[2,112,114]{2,1,0:T(8,128)S(1)}, u32[]{:S(2)}, u32[]{:S(2)}) collective-permute-start(f32[2,112,114]{2,1,0:T(8,128)S(1)} %get-tuple-element.30), channel_id=1, source_target_pairs={{0,32},{8,40},{16,48},{24,56},{32,64},{40,72},{48,80},{56,88},{64,... | collective-permute-start | bytes 306440 | tf_op jit(solution)/shard_map/ppermute | solution.py:30
  133.5 1.5 collective-permute-start.17
  135.3 5.4 %collective-permute-done.20 = f32[2,112,114]{2,1,0:T(8,128)S(1)} collective-permute-done((f32[2,112,114]{2,1,0:T(8,128)S(1)}, f32[2,112,114]{2,1,0:T(8,128)S(1)}, u32[]{:S(2)}, u32[]{:S(2)}) %collective-permute-start.20) | collective-permute-done | bytes 102176 | tf_op jit(solution)/shard_map/ppermute | solution.py:30
  143.0 6.9 %all-to-all-start.3 = ((bf16[8,2,112,113]{3,2,1,0:T(8,128)(2,1)}), bf16[8,2,112,113]{3,2,1,0:T(8,128)(2,1)S(1)}, u32[]{:S(2)}, u32[]{:S(2)}) async-start(bf16[8,2,112,113]{3,2,1,0:T(8,128)(2,1)} %broadcast_in_dim.406), calls=%async_computation.3 | async-start | bytes 917504 | tf_op jit(solution)/shard_map/all_to_all | solution.py:126
  151.0 15.2 %all-to-all-done.3 = bf16[8,2,112,113]{3,2,1,0:T(8,128)(2,1)S(1)} async-done(((bf16[8,2,112,113]{3,2,1,0:T(8,128)(2,1)}), bf16[8,2,112,113]{3,2,1,0:T(8,128)(2,1)S(1)}, u32[]{:S(2)}, u32[]{:S(2)}) %all-to-all-start.3) | async-done | bytes 405024 | tf_op jit(solution)/shard_map/all_to_all | solution.py:126
  (152 shorter events, 30.6 us)
Async XLA Ops:
  4.4 24.7 %all-to-all-start.1 = ((bf16[8,2,112,113]{3,2,1,0:T(8,128)(2,1)}), bf16[8,2,112,113]{3,2,1,0:T(8,128)(2,1)S(1)}, u32[]{:S(2)}, u32[]{:S(2)}) async-start(bf16[8,2,112,113]{3,2,1,0:T(8,128)(2,1)} %bitcast.7), calls=%async_computation.1 | async-start | bytes 917504 | tf_op jit(solution)/shard_map/all_to_all | solution.py:100
  32.5 13.0 %collective-permute-start.15 = (f32[2,112,114]{2,1,0:T(8,128)S(1)}, f32[2,112,114]{2,1,0:T(8,128)S(1)}, u32[]{:S(2)}, u32[]{:S(2)}) collective-permute-start(f32[2,112,114]{2,1,0:T(8,128)S(1)} %get-tuple-element.59), channel_id=1, source_target_pairs={{0,240},{8,248},{16,0},{24,8},{32,16},{40,24},{48,32},{56,40},{64,... | collective-permute-start | bytes 306440 | tf_op jit(solution)/shard_map/ppermute | solution.py:30
  34.1 49.9 %all-to-all-start = ((bf16[8,2,128,224]{2,3,1,0:T(8,128)(2,1)}), bf16[8,2,128,224]{2,3,1,0:T(8,128)(2,1)S(1)}, u32[]{:S(2)}, u32[]{:S(2)}) async-start(bf16[8,2,128,224]{2,3,1,0:T(8,128)(2,1)} %copy.32), calls=%async_computation | async-start | bytes 1835008 | tf_op jit(solution)/shard_map/all_to_all | solution.py:76
  38.0 11.4 %collective-permute-start.14 = (f32[2,112,114]{2,1,0:T(8,128)S(1)}, f32[2,112,114]{2,1,0:T(8,128)S(1)}, u32[]{:S(2)}, u32[]{:S(2)}) collective-permute-start(f32[2,112,114]{2,1,0:T(8,128)S(1)} %get-tuple-element.47), channel_id=1, source_target_pairs={{0,224},{8,232},{16,240},{24,248},{32,0},{40,8},{48,16},{56,24},{6... | collective-permute-start | bytes 306440 | tf_op jit(solution)/shard_map/ppermute | solution.py:30
  43.0 9.5 %collective-permute-start.13 = (f32[2,112,114]{2,1,0:T(8,128)}, f32[2,112,114]{2,1,0:T(8,128)S(1)}, u32[]{:S(2)}, u32[]{:S(2)}) collective-permute-start(f32[2,112,114]{2,1,0:T(8,128)} %get-tuple-element.48), channel_id=1, source_target_pairs={{0,208},{8,216},{16,224},{24,232},{32,240},{40,248},{48,0},{56,8},... | collective-permute-start | bytes 306440 | tf_op jit(solution)/shard_map/ppermute | solution.py:30
  45.0 13.8 %collective-permute-start.12 = (f32[2,112,114]{2,1,0:T(8,128)}, f32[2,112,114]{2,1,0:T(8,128)S(1)}, u32[]{:S(2)}, u32[]{:S(2)}) collective-permute-start(f32[2,112,114]{2,1,0:T(8,128)} %get-tuple-element.49), channel_id=1, source_target_pairs={{0,192},{8,200},{16,208},{24,216},{32,224},{40,232},{48,240},{56,2... | collective-permute-start | bytes 306440 | tf_op jit(solution)/shard_map/ppermute | solution.py:30
  45.4 13.5 %collective-permute-start.11 = (f32[2,112,114]{2,1,0:T(8,128)}, f32[2,112,114]{2,1,0:T(8,128)S(1)}, u32[]{:S(2)}, u32[]{:S(2)}) collective-permute-start(f32[2,112,114]{2,1,0:T(8,128)} %get-tuple-element.50), channel_id=1, source_target_pairs={{0,176},{8,184},{16,192},{24,200},{32,208},{40,216},{48,224},{56,2... | collective-permute-start | bytes 306440 | tf_op jit(solution)/shard_map/ppermute | solution.py:30
  45.5 22.0 %collective-permute-start.10 = (f32[2,112,114]{2,1,0:T(8,128)}, f32[2,112,114]{2,1,0:T(8,128)S(1)}, u32[]{:S(2)}, u32[]{:S(2)}) collective-permute-start(f32[2,112,114]{2,1,0:T(8,128)} %get-tuple-element.51), channel_id=1, source_target_pairs={{0,160},{8,168},{16,176},{24,184},{32,192},{40,200},{48,208},{56,2... | collective-permute-start | bytes 306440 | tf_op jit(solution)/shard_map/ppermute | solution.py:30
  49.4 19.6 %collective-permute-start.9 = (f32[2,112,114]{2,1,0:T(8,128)}, f32[2,112,114]{2,1,0:T(8,128)S(1)}, u32[]{:S(2)}, u32[]{:S(2)}) collective-permute-start(f32[2,112,114]{2,1,0:T(8,128)} %get-tuple-element.52), channel_id=1, source_target_pairs={{0,144},{8,152},{16,160},{24,168},{32,176},{40,184},{48,192},{56,2... | collective-permute-start | bytes 306440 | tf_op jit(solution)/shard_map/ppermute | solution.py:30
  52.5 16.9 %collective-permute-start.8 = (f32[2,112,114]{2,1,0:T(8,128)S(1)}, f32[2,112,114]{2,1,0:T(8,128)S(1)}, u32[]{:S(2)}, u32[]{:S(2)}) collective-permute-start(f32[2,112,114]{2,1,0:T(8,128)S(1)} %copy-done.6), channel_id=1, source_target_pairs={{0,128},{8,136},{16,144},{24,152},{32,160},{40,168},{48,176},{56,1... | collective-permute-start | bytes 306440 | tf_op jit(solution)/shard_map/ppermute | solution.py:30
  58.8 11.3 %collective-permute-start.7 = (f32[2,112,114]{2,1,0:T(8,128)S(1)}, f32[2,112,114]{2,1,0:T(8,128)S(1)}, u32[]{:S(2)}, u32[]{:S(2)}) collective-permute-start(f32[2,112,114]{2,1,0:T(8,128)S(1)} %copy-done.5), channel_id=1, source_target_pairs={{0,112},{8,120},{16,128},{24,136},{32,144},{40,152},{48,160},{56,1... | collective-permute-start | bytes 306440 | tf_op jit(solution)/shard_map/ppermute | solution.py:30
  59.0 17.5 %collective-permute-start.6 = (f32[2,112,114]{2,1,0:T(8,128)S(1)}, f32[2,112,114]{2,1,0:T(8,128)S(1)}, u32[]{:S(2)}, u32[]{:S(2)}) collective-permute-start(f32[2,112,114]{2,1,0:T(8,128)S(1)} %get-tuple-element.55), channel_id=1, source_target_pairs={{0,96},{8,104},{16,112},{24,120},{32,128},{40,136},{48,144},{56,15... | collective-permute-start | bytes 306440 | tf_op jit(solution)/shard_map/ppermute | solution.py:30
  67.6 9.2 %collective-permute-start.5 = (f32[2,112,114]{2,1,0:T(8,128)S(1)}, f32[2,112,114]{2,1,0:T(8,128)S(1)}, u32[]{:S(2)}, u32[]{:S(2)}) collective-permute-start(f32[2,112,114]{2,1,0:T(8,128)S(1)} %get-tuple-element.56), channel_id=1, source_target_pairs={{0,80},{8,88},{16,96},{24,104},{32,112},{40,120},{48,128},{56,136}... | collective-permute-start | bytes 306440 | tf_op jit(solution)/shard_map/ppermute | solution.py:30
  69.0 12.9 %collective-permute-start.4 = (f32[2,112,114]{2,1,0:T(8,128)S(1)}, f32[2,112,114]{2,1,0:T(8,128)S(1)}, u32[]{:S(2)}, u32[]{:S(2)}) collective-permute-start(f32[2,112,114]{2,1,0:T(8,128)S(1)} %get-tuple-element.57), channel_id=1, source_target_pairs={{0,64},{8,72},{16,80},{24,88},{32,96},{40,104},{48,112},{56,120},{... | collective-permute-start | bytes 306440 | tf_op jit(solution)/shard_map/ppermute | solution.py:30
  69.5 12.6 %collective-permute-start.3 = (f32[2,112,114]{2,1,0:T(8,128)S(1)}, f32[2,112,114]{2,1,0:T(8,128)S(1)}, u32[]{:S(2)}, u32[]{:S(2)}) collective-permute-start(f32[2,112,114]{2,1,0:T(8,128)S(1)} %get-tuple-element.58), channel_id=1, source_target_pairs={{0,48},{8,56},{16,64},{24,72},{32,80},{40,88},{48,96},{56,104},{64... | collective-permute-start | bytes 306440 | tf_op jit(solution)/shard_map/ppermute | solution.py:30
  70.1 12.2 %collective-permute-start.2 = (f32[2,112,114]{2,1,0:T(8,128)S(1)}, f32[2,112,114]{2,1,0:T(8,128)S(1)}, u32[]{:S(2)}, u32[]{:S(2)}) collective-permute-start(f32[2,112,114]{2,1,0:T(8,128)S(1)} %get-tuple-element.46), channel_id=1, source_target_pairs={{0,32},{8,40},{16,48},{24,56},{32,64},{40,72},{48,80},{56,88},{64,... | collective-permute-start | bytes 306440 | tf_op jit(solution)/shard_map/ppermute | solution.py:30
  91.2 16.1 %collective-permute-start.31 = (f32[2,112,114]{2,1,0:T(8,128)}, f32[2,112,114]{2,1,0:T(8,128)S(1)}, u32[]{:S(2)}, u32[]{:S(2)}) collective-permute-start(f32[2,112,114]{2,1,0:T(8,128)} %get-tuple-element.43), channel_id=1, source_target_pairs={{0,240},{8,248},{16,0},{24,8},{32,16},{40,24},{48,32},{56,40},{64,... | collective-permute-start | bytes 306440 | tf_op jit(solution)/shard_map/ppermute | solution.py:30
  94.1 48.1 %all-to-all-start.2 = ((bf16[8,1,128,224]{2,3,1,0:T(8,128)(2,1)}), bf16[8,1,128,224]{2,3,1,0:T(8,128)(2,1)S(1)}, u32[]{:S(2)}, u32[]{:S(2)}) async-start(bf16[8,1,128,224]{2,3,1,0:T(8,128)(2,1)} %copy.37), calls=%async_computation.2 | async-start | bytes 917504 | tf_op jit(solution)/shard_map/all_to_all | solution.py:83
  100.7 9.8 %collective-permute-start.30 = (f32[2,112,114]{2,1,0:T(8,128)S(1)}, f32[2,112,114]{2,1,0:T(8,128)S(1)}, u32[]{:S(2)}, u32[]{:S(2)}) collective-permute-start(f32[2,112,114]{2,1,0:T(8,128)S(1)} %copy-done.15), channel_id=1, source_target_pairs={{0,224},{8,232},{16,240},{24,248},{32,0},{40,8},{48,16},{56,24},{6... | collective-permute-start | bytes 306440 | tf_op jit(solution)/shard_map/ppermute | solution.py:30
  101.3 12.6 %collective-permute-start.29 = (f32[2,112,114]{2,1,0:T(8,128)S(1)}, f32[2,112,114]{2,1,0:T(8,128)S(1)}, u32[]{:S(2)}, u32[]{:S(2)}) collective-permute-start(f32[2,112,114]{2,1,0:T(8,128)S(1)} %copy-done.14), channel_id=1, source_target_pairs={{0,208},{8,216},{16,224},{24,232},{32,240},{40,248},{48,0},{56,8},... | collective-permute-start | bytes 306440 | tf_op jit(solution)/shard_map/ppermute | solution.py:30
  103.3 13.0 %collective-permute-start.28 = (f32[2,112,114]{2,1,0:T(8,128)S(1)}, f32[2,112,114]{2,1,0:T(8,128)S(1)}, u32[]{:S(2)}, u32[]{:S(2)}) collective-permute-start(f32[2,112,114]{2,1,0:T(8,128)S(1)} %copy-done.13), channel_id=1, source_target_pairs={{0,192},{8,200},{16,208},{24,216},{32,224},{40,232},{48,240},{56,2... | collective-permute-start | bytes 306440 | tf_op jit(solution)/shard_map/ppermute | solution.py:30
  106.5 13.0 %collective-permute-start.27 = (f32[2,112,114]{2,1,0:T(8,128)S(1)}, f32[2,112,114]{2,1,0:T(8,128)S(1)}, u32[]{:S(2)}, u32[]{:S(2)}) collective-permute-start(f32[2,112,114]{2,1,0:T(8,128)S(1)} %copy-done.12), channel_id=1, source_target_pairs={{0,176},{8,184},{16,192},{24,200},{32,208},{40,216},{48,224},{56,2... | collective-permute-start | bytes 306440 | tf_op jit(solution)/shard_map/ppermute | solution.py:30
  107.3 18.2 %collective-permute-start.26 = (f32[2,112,114]{2,1,0:T(8,128)S(1)}, f32[2,112,114]{2,1,0:T(8,128)S(1)}, u32[]{:S(2)}, u32[]{:S(2)}) collective-permute-start(f32[2,112,114]{2,1,0:T(8,128)S(1)} %copy-done.11), channel_id=1, source_target_pairs={{0,160},{8,168},{16,176},{24,184},{32,192},{40,200},{48,208},{56,2... | collective-permute-start | bytes 306440 | tf_op jit(solution)/shard_map/ppermute | solution.py:30
  110.5 17.2 %collective-permute-start.25 = (f32[2,112,114]{2,1,0:T(8,128)S(1)}, f32[2,112,114]{2,1,0:T(8,128)S(1)}, u32[]{:S(2)}, u32[]{:S(2)}) collective-permute-start(f32[2,112,114]{2,1,0:T(8,128)S(1)} %copy-done.10), channel_id=1, source_target_pairs={{0,144},{8,152},{16,160},{24,168},{32,176},{40,184},{48,192},{56,2... | collective-permute-start | bytes 306440 | tf_op jit(solution)/shard_map/ppermute | solution.py:30
  113.9 17.2 %collective-permute-start.24 = (f32[2,112,114]{2,1,0:T(8,128)S(1)}, f32[2,112,114]{2,1,0:T(8,128)S(1)}, u32[]{:S(2)}, u32[]{:S(2)}) collective-permute-start(f32[2,112,114]{2,1,0:T(8,128)S(1)} %copy-done.9), channel_id=1, source_target_pairs={{0,128},{8,136},{16,144},{24,152},{32,160},{40,168},{48,176},{56,1... | collective-permute-start | bytes 306440 | tf_op jit(solution)/shard_map/ppermute | solution.py:30
  116.3 15.1 %collective-permute-start.23 = (f32[2,112,114]{2,1,0:T(8,128)S(1)}, f32[2,112,114]{2,1,0:T(8,128)S(1)}, u32[]{:S(2)}, u32[]{:S(2)}) collective-permute-start(f32[2,112,114]{2,1,0:T(8,128)S(1)} %copy-done.8), channel_id=1, source_target_pairs={{0,112},{8,120},{16,128},{24,136},{32,144},{40,152},{48,160},{56,1... | collective-permute-start | bytes 306440 | tf_op jit(solution)/shard_map/ppermute | solution.py:30
  119.5 13.9 %collective-permute-start.22 = (f32[2,112,114]{2,1,0:T(8,128)S(1)}, f32[2,112,114]{2,1,0:T(8,128)S(1)}, u32[]{:S(2)}, u32[]{:S(2)}) collective-permute-start(f32[2,112,114]{2,1,0:T(8,128)S(1)} %copy-done.7), channel_id=1, source_target_pairs={{0,96},{8,104},{16,112},{24,120},{32,128},{40,136},{48,144},{56,15... | collective-permute-start | bytes 306440 | tf_op jit(solution)/shard_map/ppermute | solution.py:30
  125.5 9.6 %collective-permute-start.21 = (f32[2,112,114]{2,1,0:T(8,128)S(1)}, f32[2,112,114]{2,1,0:T(8,128)S(1)}, u32[]{:S(2)}, u32[]{:S(2)}) collective-permute-start(f32[2,112,114]{2,1,0:T(8,128)S(1)} %get-tuple-element.40), channel_id=1, source_target_pairs={{0,80},{8,88},{16,96},{24,104},{32,112},{40,120},{48,128},{56,136}... | collective-permute-start | bytes 306440 | tf_op jit(solution)/shard_map/ppermute | solution.py:30
  127.7 13.0 %collective-permute-start.20 = (f32[2,112,114]{2,1,0:T(8,128)S(1)}, f32[2,112,114]{2,1,0:T(8,128)S(1)}, u32[]{:S(2)}, u32[]{:S(2)}) collective-permute-start(f32[2,112,114]{2,1,0:T(8,128)S(1)} %get-tuple-element.41), channel_id=1, source_target_pairs={{0,64},{8,72},{16,80},{24,88},{32,96},{40,104},{48,112},{56,120},{... | collective-permute-start | bytes 306440 | tf_op jit(solution)/shard_map/ppermute | solution.py:30
  131.0 9.8 %collective-permute-start.19 = (f32[2,112,114]{2,1,0:T(8,128)S(1)}, f32[2,112,114]{2,1,0:T(8,128)S(1)}, u32[]{:S(2)}, u32[]{:S(2)}) collective-permute-start(f32[2,112,114]{2,1,0:T(8,128)S(1)} %get-tuple-element.42), channel_id=1, source_target_pairs={{0,48},{8,56},{16,64},{24,72},{32,80},{40,88},{48,96},{56,104},{64... | collective-permute-start | bytes 306440 | tf_op jit(solution)/shard_map/ppermute | solution.py:30
  131.3 9.7 %collective-permute-start.18 = (f32[2,112,114]{2,1,0:T(8,128)S(1)}, f32[2,112,114]{2,1,0:T(8,128)S(1)}, u32[]{:S(2)}, u32[]{:S(2)}) collective-permute-start(f32[2,112,114]{2,1,0:T(8,128)S(1)} %get-tuple-element.30), channel_id=1, source_target_pairs={{0,32},{8,40},{16,48},{24,56},{32,64},{40,72},{48,80},{56,88},{64,... | collective-permute-start | bytes 306440 | tf_op jit(solution)/shard_map/ppermute | solution.py:30
  143.0 23.1 %all-to-all-start.3 = ((bf16[8,2,112,113]{3,2,1,0:T(8,128)(2,1)}), bf16[8,2,112,113]{3,2,1,0:T(8,128)(2,1)S(1)}, u32[]{:S(2)}, u32[]{:S(2)}) async-start(bf16[8,2,112,113]{3,2,1,0:T(8,128)(2,1)} %broadcast_in_dim.406), calls=%async_computation.3 | async-start | bytes 917504 | tf_op jit(solution)/shard_map/all_to_all | solution.py:126
  (22 other events, 124.2 us)

commit v19 on v16

--- a/solution.py
+++ b/solution.py
@@ -88,12 +88,12 @@
     own_key = key_input.reshape(rows, all_heads, DH)
     own_value = value_input.reshape(rows, all_heads, DH)
     own_feat_key = jnp.maximum(own_key, 0)
-    own_ones = jnp.ones((rows, all_heads, 1), jnp.bfloat16)
-    own_state = jnp.einsum(
-        "thk,thv->hkv",
-        own_feat_key,
-        jnp.concatenate([own_value, own_ones], axis=-1),
-        preferred_element_type=jnp.float32,
+    own_state = jnp.concatenate(
+        [
+            jnp.einsum("thk,thv->hkv", own_feat_key, own_value, preferred_element_type=jnp.float32),
+            jnp.sum(own_feat_key, axis=0, dtype=jnp.float32)[..., None],
+        ],
+        axis=-1,
     )
     pieces = own_state.astype(jnp.bfloat16).reshape(groups, heads, DH, DH + 1)
     state_part = jnp.sum(

time: 120 us -> 121 us (level)
  other arithmetic: 6.3 us -> 7.51 us
where the time goes in v19:
time: 121 us; the launch traced here: 120 us
  starting transfers between devices  58.5 us (48%)
  waiting for transfers between devices  39.2 us (32%)
  local copies, waits for them, and re-layouts  11.1 us (9%)
  other arithmetic  7.51 us (6%)
  matrix products  2 us (2%)
  between operations  1.39 us (1%)
    ppermute x14, starting transfers between devices, strided(): return lax.ppermute(value, 'tm', pairs)  33 us
    all_to_all x1, waiting for transfers between devices, local(): lax.all_to_all(pieces, 'inner', 0, 0, tiled=True).astype(jnp.float32)  14.5 us
    all_to_all x1, waiting for transfers between devices, local(): lax.all_to_all(copies, 'inner', 0, 0, tiled=True)  13.4 us
    all_to_all x1, starting transfers between devices, local(): lax.all_to_all(pieces, 'inner', 0, 0, tiled=True).astype(jnp.float32)  8.6 us
    unnamed x21, local copies, waits for them, and re-layouts  6.55 us
    all_to_all x1, starting transfers between devices, local(): lax.all_to_all(copies, 'inner', 0, 0, tiled=True)  6.43 us
    ppermute x14, waiting for transfers between devices, strided(): return lax.ppermute(value, 'tm', pairs)  4.29 us
    all_to_all x1, waiting for transfers between devices, to_heads(): incoming = lax.all_to_all(outgoing, 'inner', 0, 0, tiled=True)  3.88 us
  transfers between devices with their start and end apart: 24, of which 7 were waited for; matrix products, arithmetic and copies ran while one was open for 8% of the time, Pallas kernels for 0%

profile of v19, /device:TPU:2, one launch (start us, length us, event | category | flops | bytes accessed | tf_op | source)
XLA Modules:
  0.0 119.7 jit_solution(15578709472924851745)
XLA Ops:
  0.6 1.3 %copy.36 = bf16[128,1792]{0,1:T(8,128)(2,1)S(1)} copy(bf16[128,1792]{1,0:T(8,128)(2,1)} %param.6) | data formatting | bytes 917504 | tf_op args[1]
  2.1 0.9 concatenate.41
  4.2 1.0 pad_maximum_fusion.1
  5.2 8.6 %all-to-all-start.1 = ((bf16[8,2,112,113]{3,2,1,0:T(8,128)(2,1)}), bf16[8,2,112,113]{3,2,1,0:T(8,128)(2,1)S(1)}, u32[]{:S(2)}, u32[]{:S(2)}) async-start(bf16[8,2,112,113]{3,2,1,0:T(8,128)(2,1)} %pad_maximum_fusion.1), calls=%async_computation.1 | async-start | bytes 917504 | tf_op jit(solution)/shard_map/all_to_all | solution.py:100
  15.4 14.5 %all-to-all-done.1 = bf16[8,2,112,113]{3,2,1,0:T(8,128)(2,1)S(1)} async-done(((bf16[8,2,112,113]{3,2,1,0:T(8,128)(2,1)}), bf16[8,2,112,113]{3,2,1,0:T(8,128)(2,1)S(1)}, u32[]{:S(2)}, u32[]{:S(2)}) %all-to-all-start.1) | async-done | bytes 405024 | tf_op jit(solution)/shard_map/all_to_all | solution.py:100
  30.2 1.5 %collective-permute-start.1 = (f32[2,112,114]{2,1,0:T(8,128)S(1)}, f32[2,112,114]{2,1,0:T(8,128)S(1)}, u32[]{:S(2)}, u32[]{:S(2)}) collective-permute-start(f32[2,112,114]{2,1,0:T(8,128)S(1)} %concatenate.34), channel_id=1, source_target_pairs={{0,16},{8,24},{16,0},{24,8},{32,48},{40,56},{48,32},{56,40},{64,80... | collective-permute-start | bytes 306440 | tf_op jit(solution)/shard_map/ppermute | solution.py:20
  31.7 1.0 copy.34
  32.7 3.6 %all-to-all-start = ((bf16[8,2,128,224]{2,3,1,0:T(8,128)(2,1)}), bf16[8,2,128,224]{2,3,1,0:T(8,128)(2,1)S(1)}, u32[]{:S(2)}, u32[]{:S(2)}) async-start(bf16[8,2,128,224]{2,3,1,0:T(8,128)(2,1)} %copy.34), calls=%async_computation | async-start | bytes 1835008 | tf_op jit(solution)/shard_map/all_to_all | solution.py:76
  36.6 1.5 %collective-permute-done.1 = f32[2,112,114]{2,1,0:T(8,128)S(1)} collective-permute-done((f32[2,112,114]{2,1,0:T(8,128)S(1)}, f32[2,112,114]{2,1,0:T(8,128)S(1)}, u32[]{:S(2)}, u32[]{:S(2)}) %collective-permute-start.1) | collective-permute-done | bytes 102176 | tf_op jit(solution)/shard_map/ppermute | solution.py:20
  38.9 2.2 %collective-permute-start.3 = (f32[2,112,114]{2,1,0:T(8,128)S(1)}, f32[2,112,114]{2,1,0:T(8,128)S(1)}, u32[]{:S(2)}, u32[]{:S(2)}) collective-permute-start(f32[2,112,114]{2,1,0:T(8,128)S(1)} %get-tuple-element.30), channel_id=1, source_target_pairs={{0,32},{8,40},{16,48},{24,56},{32,64},{40,72},{48,80},{56,88},{64,... | collective-permute-start | bytes 306440 | tf_op jit(solution)/shard_map/ppermute | solution.py:30
  41.1 1.7 %collective-permute-start.4 = (f32[2,112,114]{2,1,0:T(8,128)S(1)}, f32[2,112,114]{2,1,0:T(8,128)S(1)}, u32[]{:S(2)}, u32[]{:S(2)}) collective-permute-start(f32[2,112,114]{2,1,0:T(8,128)S(1)} %get-tuple-element.50), channel_id=1, source_target_pairs={{0,64},{8,72},{16,80},{24,88},{32,96},{40,104},{48,112},{56,120},{... | collective-permute-start | bytes 306440 | tf_op jit(solution)/shard_map/ppermute | solution.py:30
  42.8 1.7 %collective-permute-start.8 = (f32[2,112,114]{2,1,0:T(8,128)S(1)}, f32[2,112,114]{2,1,0:T(8,128)S(1)}, u32[]{:S(2)}, u32[]{:S(2)}) collective-permute-start(f32[2,112,114]{2,1,0:T(8,128)S(1)} %get-tuple-element.51), channel_id=1, source_target_pairs={{0,192},{8,200},{16,208},{24,216},{32,224},{40,232},{48,240},{56,2... | collective-permute-start | bytes 306440 | tf_op jit(solution)/shard_map/ppermute | solution.py:30
  44.4 3.5 %collective-permute-start.7 = (f32[2,112,114]{2,1,0:T(8,128)S(1)}, f32[2,112,114]{2,1,0:T(8,128)S(1)}, u32[]{:S(2)}, u32[]{:S(2)}) collective-permute-start(f32[2,112,114]{2,1,0:T(8,128)S(1)} %get-tuple-element.52), channel_id=1, source_target_pairs={{0,160},{8,168},{16,176},{24,184},{32,192},{40,200},{48,208},{56,2... | collective-permute-start | bytes 306440 | tf_op jit(solution)/shard_map/ppermute | solution.py:30
  48.0 1.8 %collective-permute-start.6 = (f32[2,112,114]{2,1,0:T(8,128)S(1)}, f32[2,112,114]{2,1,0:T(8,128)S(1)}, u32[]{:S(2)}, u32[]{:S(2)}) collective-permute-start(f32[2,112,114]{2,1,0:T(8,128)S(1)} %get-tuple-element.53), channel_id=1, source_target_pairs={{0,128},{8,136},{16,144},{24,152},{32,160},{40,168},{48,176},{56,1... | collective-permute-start | bytes 306440 | tf_op jit(solution)/shard_map/ppermute | solution.py:30
  50.4 5.3 %collective-permute-start.9 = (f32[2,112,114]{2,1,0:T(8,128)S(1)}, f32[2,112,114]{2,1,0:T(8,128)S(1)}, u32[]{:S(2)}, u32[]{:S(2)}) collective-permute-start(f32[2,112,114]{2,1,0:T(8,128)S(1)} %get-tuple-element.55), channel_id=1, source_target_pairs={{0,224},{8,232},{16,240},{24,248},{32,0},{40,8},{48,16},{56,24},{6... | collective-permute-start | bytes 306440 | tf_op jit(solution)/shard_map/ppermute | solution.py:30
  56.5 2.0 %collective-permute-done.5 = f32[2,112,114]{2,1,0:T(8,128)S(1)} collective-permute-done((f32[2,112,114]{2,1,0:T(8,128)S(1)}, f32[2,112,114]{2,1,0:T(8,128)S(1)}, u32[]{:S(2)}, u32[]{:S(2)}) %collective-permute-start.5) | collective-permute-done | bytes 102176 | tf_op jit(solution)/shard_map/ppermute | solution.py:30
  59.4 3.9 %all-to-all-done = bf16[8,2,128,224]{2,3,1,0:T(8,128)(2,1)S(1)} async-done(((bf16[8,2,128,224]{2,3,1,0:T(8,128)(2,1)}), bf16[8,2,128,224]{2,3,1,0:T(8,128)(2,1)S(1)}, u32[]{:S(2)}, u32[]{:S(2)}) %all-to-all-start) | async-done | bytes 917536 | tf_op jit(solution)/shard_map/all_to_all | solution.py:76
  66.2 1.0 collective-permute-start.11
  68.4 3.5 %all-to-all-start.2 = ((bf16[8,1,128,224]{2,3,1,0:T(8,128)(2,1)}), bf16[8,1,128,224]{2,3,1,0:T(8,128)(2,1)S(1)}, u32[]{:S(2)}, u32[]{:S(2)}) async-start(bf16[8,1,128,224]{2,3,1,0:T(8,128)(2,1)} %copy.40), calls=%async_computation.2 | async-start | bytes 917504 | tf_op jit(solution)/shard_map/all_to_all | solution.py:83
  71.9 1.6 %collective-permute-done.11 = f32[2,112,114]{2,1,0:T(8,128)S(1)} collective-permute-done((f32[2,112,114]{2,1,0:T(8,128)S(1)}, f32[2,112,114]{2,1,0:T(8,128)S(1)}, u32[]{:S(2)}, u32[]{:S(2)}) %collective-permute-start.11) | collective-permute-done | bytes 102176 | tf_op jit(solution)/shard_map/ppermute | solution.py:20
  74.3 2.5 %collective-permute-start.13 = (f32[2,112,114]{2,1,0:T(8,128)S(1)}, f32[2,112,114]{2,1,0:T(8,128)S(1)}, u32[]{:S(2)}, u32[]{:S(2)}) collective-permute-start(f32[2,112,114]{2,1,0:T(8,128)S(1)} %get-tuple-element.26), channel_id=1, source_target_pairs={{0,32},{8,40},{16,48},{24,56},{32,64},{40,72},{48,80},{56,88},{64,... | collective-permute-start | bytes 306440 | tf_op jit(solution)/shard_map/ppermute | solution.py:30
  76.8 1.7 %collective-permute-start.14 = (f32[2,112,114]{2,1,0:T(8,128)S(1)}, f32[2,112,114]{2,1,0:T(8,128)S(1)}, u32[]{:S(2)}, u32[]{:S(2)}) collective-permute-start(f32[2,112,114]{2,1,0:T(8,128)S(1)} %get-tuple-element.44), channel_id=1, source_target_pairs={{0,64},{8,72},{16,80},{24,88},{32,96},{40,104},{48,112},{56,120},{... | collective-permute-start | bytes 306440 | tf_op jit(solution)/shard_map/ppermute | solution.py:30
  78.5 1.7 %collective-permute-start.18 = (f32[2,112,114]{2,1,0:T(8,128)S(1)}, f32[2,112,114]{2,1,0:T(8,128)S(1)}, u32[]{:S(2)}, u32[]{:S(2)}) collective-permute-start(f32[2,112,114]{2,1,0:T(8,128)S(1)} %get-tuple-element.45), channel_id=1, source_target_pairs={{0,192},{8,200},{16,208},{24,216},{32,224},{40,232},{48,240},{56,2... | collective-permute-start | bytes 306440 | tf_op jit(solution)/shard_map/ppermute | solution.py:30
  80.2 3.2 %collective-permute-start.17 = (f32[2,112,114]{2,1,0:T(8,128)S(1)}, f32[2,112,114]{2,1,0:T(8,128)S(1)}, u32[]{:S(2)}, u32[]{:S(2)}) collective-permute-start(f32[2,112,114]{2,1,0:T(8,128)S(1)} %get-tuple-element.46), channel_id=1, source_target_pairs={{0,160},{8,168},{16,176},{24,184},{32,192},{40,200},{48,208},{56,2... | collective-permute-start | bytes 306440 | tf_op jit(solution)/shard_map/ppermute | solution.py:30
  83.4 1.8 %collective-permute-start.16 = (f32[2,112,114]{2,1,0:T(8,128)S(1)}, f32[2,112,114]{2,1,0:T(8,128)S(1)}, u32[]{:S(2)}, u32[]{:S(2)}) collective-permute-start(f32[2,112,114]{2,1,0:T(8,128)S(1)} %get-tuple-element.47), channel_id=1, source_target_pairs={{0,128},{8,136},{16,144},{24,152},{32,160},{40,168},{48,176},{56,1... | collective-permute-start | bytes 306440 | tf_op jit(solution)/shard_map/ppermute | solution.py:30
  86.2 4.8 %collective-permute-start.19 = (f32[2,112,114]{2,1,0:T(8,128)S(1)}, f32[2,112,114]{2,1,0:T(8,128)S(1)}, u32[]{:S(2)}, u32[]{:S(2)}) collective-permute-start(f32[2,112,114]{2,1,0:T(8,128)S(1)} %get-tuple-element.49), channel_id=1, source_target_pairs={{0,224},{8,232},{16,240},{24,248},{32,0},{40,8},{48,16},{56,24},{6... | collective-permute-start | bytes 306440 | tf_op jit(solution)/shard_map/ppermute | solution.py:30
  91.7 2.2 %collective-permute-done.15 = f32[2,112,114]{2,1,0:T(8,128)S(1)} collective-permute-done((f32[2,112,114]{2,1,0:T(8,128)S(1)}, f32[2,112,114]{2,1,0:T(8,128)S(1)}, u32[]{:S(2)}, u32[]{:S(2)}) %collective-permute-start.15) | collective-permute-done | bytes 102176 | tf_op jit(solution)/shard_map/ppermute | solution.py:30
  95.7 6.4 %all-to-all-start.3 = ((bf16[8,2,112,113]{3,2,1,0:T(8,128)(2,1)}), bf16[8,2,112,113]{3,2,1,0:T(8,128)(2,1)S(1)}, u32[]{:S(2)}, u32[]{:S(2)}) async-start(bf16[8,2,112,113]{3,2,1,0:T(8,128)(2,1)} %broadcast_in_dim.326), calls=%async_computation.3 | async-start | bytes 917504 | tf_op jit(solution)/shard_map/all_to_all | solution.py:126
  102.2 1.0 copy.44
  103.2 13.4 %all-to-all-done.3 = bf16[8,2,112,113]{3,2,1,0:T(8,128)(2,1)S(1)} async-done(((bf16[8,2,112,113]{3,2,1,0:T(8,128)(2,1)}), bf16[8,2,112,113]{3,2,1,0:T(8,128)(2,1)S(1)}, u32[]{:S(2)}, u32[]{:S(2)}) %all-to-all-start.3) | async-done | bytes 405024 | tf_op jit(solution)/shard_map/all_to_all | solution.py:126
  117.3 1.0 copy.46
  118.7 1.0 copy.45
  (90 shorter events, 15.7 us)
Async XLA Ops:
  2.1 1.0 copy-start.2
  3.4 0.8 copy-start
  5.2 8.6 %copy-start.3 = (bf16[128,1792]{1,0:T(8,128)(2,1)S(1)}, bf16[128,1792]{1,0:T(8,128)(2,1)}, u32[]{:S(2)}) copy-start(bf16[128,1792]{1,0:T(8,128)(2,1)} %param.5) | copy-start | bytes 1376260
  5.2 24.7 %all-to-all-start.1 = ((bf16[8,2,112,113]{3,2,1,0:T(8,128)(2,1)}), bf16[8,2,112,113]{3,2,1,0:T(8,128)(2,1)S(1)}, u32[]{:S(2)}, u32[]{:S(2)}) async-start(bf16[8,2,112,113]{3,2,1,0:T(8,128)(2,1)} %pad_maximum_fusion.1), calls=%async_computation.1 | async-start | bytes 917504 | tf_op jit(solution)/shard_map/all_to_all | solution.py:100
  14.1 1.0 copy-start.4
  14.1 0.7 copy-start.5
  30.0 6.6 %collective-permute-start.2 = (f32[2,112,114]{2,1,0:T(8,128)S(1)}, f32[2,112,114]{2,1,0:T(8,128)S(1)}, u32[]{:S(2)}, u32[]{:S(2)}) collective-permute-start(f32[2,112,114]{2,1,0:T(8,128)S(1)} %concatenate.34), channel_id=1, source_target_pairs={{0,24},{8,0},{16,8},{24,16},{32,56},{40,32},{48,40},{56,48},{64,88... | collective-permute-start | bytes 306440 | tf_op jit(solution)/shard_map/ppermute | solution.py:20
  30.2 7.9 %collective-permute-start.1 = (f32[2,112,114]{2,1,0:T(8,128)S(1)}, f32[2,112,114]{2,1,0:T(8,128)S(1)}, u32[]{:S(2)}, u32[]{:S(2)}) collective-permute-start(f32[2,112,114]{2,1,0:T(8,128)S(1)} %concatenate.34), channel_id=1, source_target_pairs={{0,16},{8,24},{16,0},{24,8},{32,48},{40,56},{48,32},{56,40},{64,80... | collective-permute-start | bytes 306440 | tf_op jit(solution)/shard_map/ppermute | solution.py:20
  31.6 6.5 %collective-permute-start = (f32[2,112,114]{2,1,0:T(8,128)S(1)}, f32[2,112,114]{2,1,0:T(8,128)S(1)}, u32[]{:S(2)}, u32[]{:S(2)}) collective-permute-start(f32[2,112,114]{2,1,0:T(8,128)S(1)} %concatenate.34), channel_id=1, source_target_pairs={{0,8},{8,16},{16,24},{24,0},{32,40},{40,48},{48,56},{56,32},{64,72... | collective-permute-start | bytes 306440 | tf_op jit(solution)/shard_map/ppermute | solution.py:20
  32.7 30.6 %all-to-all-start = ((bf16[8,2,128,224]{2,3,1,0:T(8,128)(2,1)}), bf16[8,2,128,224]{2,3,1,0:T(8,128)(2,1)S(1)}, u32[]{:S(2)}, u32[]{:S(2)}) async-start(bf16[8,2,128,224]{2,3,1,0:T(8,128)(2,1)} %copy.34), calls=%async_computation | async-start | bytes 1835008 | tf_op jit(solution)/shard_map/all_to_all | solution.py:76
  38.9 11.0 %collective-permute-start.3 = (f32[2,112,114]{2,1,0:T(8,128)S(1)}, f32[2,112,114]{2,1,0:T(8,128)S(1)}, u32[]{:S(2)}, u32[]{:S(2)}) collective-permute-start(f32[2,112,114]{2,1,0:T(8,128)S(1)} %get-tuple-element.30), channel_id=1, source_target_pairs={{0,32},{8,40},{16,48},{24,56},{32,64},{40,72},{48,80},{56,88},{64,... | collective-permute-start | bytes 306440 | tf_op jit(solution)/shard_map/ppermute | solution.py:30
  41.1 9.3 %collective-permute-start.4 = (f32[2,112,114]{2,1,0:T(8,128)S(1)}, f32[2,112,114]{2,1,0:T(8,128)S(1)}, u32[]{:S(2)}, u32[]{:S(2)}) collective-permute-start(f32[2,112,114]{2,1,0:T(8,128)S(1)} %get-tuple-element.50), channel_id=1, source_target_pairs={{0,64},{8,72},{16,80},{24,88},{32,96},{40,104},{48,112},{56,120},{... | collective-permute-start | bytes 306440 | tf_op jit(solution)/shard_map/ppermute | solution.py:30
  42.8 13.1 %collective-permute-start.8 = (f32[2,112,114]{2,1,0:T(8,128)S(1)}, f32[2,112,114]{2,1,0:T(8,128)S(1)}, u32[]{:S(2)}, u32[]{:S(2)}) collective-permute-start(f32[2,112,114]{2,1,0:T(8,128)S(1)} %get-tuple-element.51), channel_id=1, source_target_pairs={{0,192},{8,200},{16,208},{24,216},{32,224},{40,232},{48,240},{56,2... | collective-permute-start | bytes 306440 | tf_op jit(solution)/shard_map/ppermute | solution.py:30
  44.4 11.7 %collective-permute-start.7 = (f32[2,112,114]{2,1,0:T(8,128)S(1)}, f32[2,112,114]{2,1,0:T(8,128)S(1)}, u32[]{:S(2)}, u32[]{:S(2)}) collective-permute-start(f32[2,112,114]{2,1,0:T(8,128)S(1)} %get-tuple-element.52), channel_id=1, source_target_pairs={{0,160},{8,168},{16,176},{24,184},{32,192},{40,200},{48,208},{56,2... | collective-permute-start | bytes 306440 | tf_op jit(solution)/shard_map/ppermute | solution.py:30
  48.0 8.3 %collective-permute-start.6 = (f32[2,112,114]{2,1,0:T(8,128)S(1)}, f32[2,112,114]{2,1,0:T(8,128)S(1)}, u32[]{:S(2)}, u32[]{:S(2)}) collective-permute-start(f32[2,112,114]{2,1,0:T(8,128)S(1)} %get-tuple-element.53), channel_id=1, source_target_pairs={{0,128},{8,136},{16,144},{24,152},{32,160},{40,168},{48,176},{56,1... | collective-permute-start | bytes 306440 | tf_op jit(solution)/shard_map/ppermute | solution.py:30
  49.8 8.7 %collective-permute-start.5 = (f32[2,112,114]{2,1,0:T(8,128)S(1)}, f32[2,112,114]{2,1,0:T(8,128)S(1)}, u32[]{:S(2)}, u32[]{:S(2)}) collective-permute-start(f32[2,112,114]{2,1,0:T(8,128)S(1)} %get-tuple-element.54), channel_id=1, source_target_pairs={{0,96},{8,104},{16,112},{24,120},{32,128},{40,136},{48,144},{56,15... | collective-permute-start | bytes 306440 | tf_op jit(solution)/shard_map/ppermute | solution.py:30
  50.4 8.3 %collective-permute-start.9 = (f32[2,112,114]{2,1,0:T(8,128)S(1)}, f32[2,112,114]{2,1,0:T(8,128)S(1)}, u32[]{:S(2)}, u32[]{:S(2)}) collective-permute-start(f32[2,112,114]{2,1,0:T(8,128)S(1)} %get-tuple-element.55), channel_id=1, source_target_pairs={{0,224},{8,232},{16,240},{24,248},{32,0},{40,8},{48,16},{56,24},{6... | collective-permute-start | bytes 306440 | tf_op jit(solution)/shard_map/ppermute | solution.py:30
  65.4 6.5 %collective-permute-start.12 = (f32[2,112,114]{2,1,0:T(8,128)S(1)}, f32[2,112,114]{2,1,0:T(8,128)S(1)}, u32[]{:S(2)}, u32[]{:S(2)}) collective-permute-start(f32[2,112,114]{2,1,0:T(8,128)S(1)} %concatenate.38), channel_id=1, source_target_pairs={{0,24},{8,0},{16,8},{24,16},{32,56},{40,32},{48,40},{56,48},{64,88... | collective-permute-start | bytes 306440 | tf_op jit(solution)/shard_map/ppermute | solution.py:20
  66.2 7.3 %collective-permute-start.11 = (f32[2,112,114]{2,1,0:T(8,128)S(1)}, f32[2,112,114]{2,1,0:T(8,128)S(1)}, u32[]{:S(2)}, u32[]{:S(2)}) collective-permute-start(f32[2,112,114]{2,1,0:T(8,128)S(1)} %concatenate.38), channel_id=1, source_target_pairs={{0,16},{8,24},{16,0},{24,8},{32,48},{40,56},{48,32},{56,40},{64,80... | collective-permute-start | bytes 306440 | tf_op jit(solution)/shard_map/ppermute | solution.py:20
  67.2 6.3 %collective-permute-start.10 = (f32[2,112,114]{2,1,0:T(8,128)S(1)}, f32[2,112,114]{2,1,0:T(8,128)S(1)}, u32[]{:S(2)}, u32[]{:S(2)}) collective-permute-start(f32[2,112,114]{2,1,0:T(8,128)S(1)} %concatenate.38), channel_id=1, source_target_pairs={{0,8},{8,16},{16,24},{24,0},{32,40},{40,48},{48,56},{56,32},{64,72... | collective-permute-start | bytes 306440 | tf_op jit(solution)/shard_map/ppermute | solution.py:20
  68.4 26.4 %all-to-all-start.2 = ((bf16[8,1,128,224]{2,3,1,0:T(8,128)(2,1)}), bf16[8,1,128,224]{2,3,1,0:T(8,128)(2,1)S(1)}, u32[]{:S(2)}, u32[]{:S(2)}) async-start(bf16[8,1,128,224]{2,3,1,0:T(8,128)(2,1)} %copy.40), calls=%async_computation.2 | async-start | bytes 917504 | tf_op jit(solution)/shard_map/all_to_all | solution.py:83
  74.3 11.0 %collective-permute-start.13 = (f32[2,112,114]{2,1,0:T(8,128)S(1)}, f32[2,112,114]{2,1,0:T(8,128)S(1)}, u32[]{:S(2)}, u32[]{:S(2)}) collective-permute-start(f32[2,112,114]{2,1,0:T(8,128)S(1)} %get-tuple-element.26), channel_id=1, source_target_pairs={{0,32},{8,40},{16,48},{24,56},{32,64},{40,72},{48,80},{56,88},{64,... | collective-permute-start | bytes 306440 | tf_op jit(solution)/shard_map/ppermute | solution.py:30
  76.8 9.3 %collective-permute-start.14 = (f32[2,112,114]{2,1,0:T(8,128)S(1)}, f32[2,112,114]{2,1,0:T(8,128)S(1)}, u32[]{:S(2)}, u32[]{:S(2)}) collective-permute-start(f32[2,112,114]{2,1,0:T(8,128)S(1)} %get-tuple-element.44), channel_id=1, source_target_pairs={{0,64},{8,72},{16,80},{24,88},{32,96},{40,104},{48,112},{56,120},{... | collective-permute-start | bytes 306440 | tf_op jit(solution)/shard_map/ppermute | solution.py:30
  78.5 12.7 %collective-permute-start.18 = (f32[2,112,114]{2,1,0:T(8,128)S(1)}, f32[2,112,114]{2,1,0:T(8,128)S(1)}, u32[]{:S(2)}, u32[]{:S(2)}) collective-permute-start(f32[2,112,114]{2,1,0:T(8,128)S(1)} %get-tuple-element.45), channel_id=1, source_target_pairs={{0,192},{8,200},{16,208},{24,216},{32,224},{40,232},{48,240},{56,2... | collective-permute-start | bytes 306440 | tf_op jit(solution)/shard_map/ppermute | solution.py:30
  80.2 11.2 %collective-permute-start.17 = (f32[2,112,114]{2,1,0:T(8,128)S(1)}, f32[2,112,114]{2,1,0:T(8,128)S(1)}, u32[]{:S(2)}, u32[]{:S(2)}) collective-permute-start(f32[2,112,114]{2,1,0:T(8,128)S(1)} %get-tuple-element.46), channel_id=1, source_target_pairs={{0,160},{8,168},{16,176},{24,184},{32,192},{40,200},{48,208},{56,2... | collective-permute-start | bytes 306440 | tf_op jit(solution)/shard_map/ppermute | solution.py:30
  83.4 8.1 %collective-permute-start.16 = (f32[2,112,114]{2,1,0:T(8,128)S(1)}, f32[2,112,114]{2,1,0:T(8,128)S(1)}, u32[]{:S(2)}, u32[]{:S(2)}) collective-permute-start(f32[2,112,114]{2,1,0:T(8,128)S(1)} %get-tuple-element.47), channel_id=1, source_target_pairs={{0,128},{8,136},{16,144},{24,152},{32,160},{40,168},{48,176},{56,1... | collective-permute-start | bytes 306440 | tf_op jit(solution)/shard_map/ppermute | solution.py:30
  85.2 8.7 %collective-permute-start.15 = (f32[2,112,114]{2,1,0:T(8,128)S(1)}, f32[2,112,114]{2,1,0:T(8,128)S(1)}, u32[]{:S(2)}, u32[]{:S(2)}) collective-permute-start(f32[2,112,114]{2,1,0:T(8,128)S(1)} %get-tuple-element.48), channel_id=1, source_target_pairs={{0,96},{8,104},{16,112},{24,120},{32,128},{40,136},{48,144},{56,15... | collective-permute-start | bytes 306440 | tf_op jit(solution)/shard_map/ppermute | solution.py:30
  86.2 8.0 %collective-permute-start.19 = (f32[2,112,114]{2,1,0:T(8,128)S(1)}, f32[2,112,114]{2,1,0:T(8,128)S(1)}, u32[]{:S(2)}, u32[]{:S(2)}) collective-permute-start(f32[2,112,114]{2,1,0:T(8,128)S(1)} %get-tuple-element.49), channel_id=1, source_target_pairs={{0,224},{8,232},{16,240},{24,248},{32,0},{40,8},{48,16},{56,24},{6... | collective-permute-start | bytes 306440 | tf_op jit(solution)/shard_map/ppermute | solution.py:30
  95.7 20.9 %all-to-all-start.3 = ((bf16[8,2,112,113]{3,2,1,0:T(8,128)(2,1)}), bf16[8,2,112,113]{3,2,1,0:T(8,128)(2,1)S(1)}, u32[]{:S(2)}, u32[]{:S(2)}) async-start(bf16[8,2,112,113]{3,2,1,0:T(8,128)(2,1)} %broadcast_in_dim.326), calls=%async_computation.3 | async-start | bytes 917504 | tf_op jit(solution)/shard_map/all_to_all | solution.py:126
  117.3 1.0 copy-start.1
